TPU v7x, 256 devices: a whole 4x4x8 slice. The times are simulated.
256 devices in a mesh: row: 32 (over z, x_lo, core), feat: 8 (over y, x_hi).
Axes of the slice: x: 4 (x_hi: 2, x_lo: 2; x = x_hi * 2 + x_lo), y: 4, z: 8, core: 2. Of those that a mesh axis runs over, the one named last changes fastest.
Arguments:
- vectors: bfloat16 [81920, 1024], P('row', 'feat')
- rotation: bfloat16 [1024, 1024], P('feat')
- codes: int32 [81920, 64], P('row', 'feat'), may hold values from 0 to 255
- live_rows: int32 [32], P('row'), may hold values from 640 to 2560
Outputs:
- centroids: float32 [256, 1024], P('row', 'feat')
- grad_t: float32 [1024, 1024], P('row', 'feat')
All inputs are finite; a program needn't handle non-finite values.
Results may differ from a plain program's by a relative error of at most 0.00094.
Values may be sent and summed in bfloat16 or wider, within the bound.
No kernel may reach another device: no remote copies, remote signals or barrier semaphores. Data moves between devices by JAX's collectives and lax.ppermute only.
A program may use at most 64 MiB of HBM per device.

v0:
```python
import math

import jax
import jax.numpy as jnp
from jax import lax
from jax.sharding import PartitionSpec as P

K = 256


def make_hot(code_block, keeper):
    kinds = jnp.arange(K, dtype=jnp.int32)
    return (code_block[:, :, None] == kinds[None, None, :]).astype(jnp.bfloat16) * keeper[
        :, None, None
    ]


def rebuild(hot, table_part, groups, depth):
    rows = hot.shape[0]
    shaped = table_part.reshape(K, groups, depth)
    joined = jnp.einsum("nmk,kmd->nmd", hot, shaped, preferred_element_type=jnp.float32)
    return joined.reshape(rows, groups * depth).astype(jnp.bfloat16)


def blocked_sums(hot, rotated, groups, depth):
    rows = hot.shape[0]
    step_rows = math.gcd(rows, 512)
    turns = rows // step_rows

    def add_block(index, total):
        hot_block = lax.dynamic_slice_in_dim(hot, index * step_rows, step_rows, 0).astype(
            jnp.float32
        )
        rot_block = lax.dynamic_slice_in_dim(rotated, index * step_rows, step_rows, 0).reshape(
            step_rows, groups, depth
        )
        return total + jnp.einsum(
            "nmk,nmd->kmd", hot_block, rot_block, precision=lax.Precision.HIGHEST
        )

    start = jnp.zeros((K, groups, depth), jnp.float32)
    return lax.fori_loop(0, turns, add_block, start).reshape(K, groups * depth)


def shards(vectors, rotation, codes, live_rows):
    rows = vectors.shape[0]
    local = vectors.shape[1]
    groups = codes.shape[1]
    depth = local // groups
    keeper = (jnp.arange(rows, dtype=jnp.int32) < live_rows[0]).astype(jnp.bfloat16)
    hot = make_hot(codes, keeper)
    counts = jnp.sum(hot, axis=0, dtype=jnp.float32).T
    partial_value = jnp.dot(vectors, rotation, preferred_element_type=jnp.float32)
    rotated = lax.psum_scatter(partial_value, "feat", scatter_dimension=1, tiled=True)
    sums = blocked_sums(hot, rotated, groups, depth)
    share_sums, share_counts = (
        lax.psum_scatter(sums, "row", scatter_dimension=0, tiled=True),
        lax.psum_scatter(counts, "row", scatter_dimension=0, tiled=True),
    )
    centroids = share_sums / (jnp.repeat(share_counts, depth, axis=1) + 1.0)
    table = lax.all_gather(centroids.astype(jnp.bfloat16), "row", axis=0, tiled=True)
    local_recon = rebuild(hot, table, groups, depth)
    recon = lax.all_gather(local_recon, "feat", axis=1, tiled=True)
    inverse = 1.0 / (rows * lax.axis_size("row"))
    product = lax.dot_general(
        recon, vectors, (((0,), (0,)), ((), ())), preferred_element_type=jnp.float32
    )
    grad_t = lax.psum_scatter(product * inverse, "row", scatter_dimension=0, tiled=True)
    return (centroids, grad_t)


def solution(mesh):
    return jax.shard_map(
        shards,
        mesh=mesh,
        in_specs=(P("row", "feat"), P("feat", None), P("row", "feat"), P("row")),
        out_specs=(P("row", "feat"), P("row", "feat")),
        check_vma=False,
    )
```

profile of v0, /device:TPU:4, one launch (start us, length us, event | category | flops | bytes accessed | tf_op | source)
XLA Modules:
  0.0 625.4 jit_solution(6406891080240727840)
XLA Ops:
  7.2 1.0 copy-done
  8.3 6.4 %fusion.20 = f32[2560,1024]{1,0:T(8,128)} fusion(bf16[2560,128]{1,0:T(8,128)(2,1)S(1)} %copy-done, bf16[128,1024]{1,0:T(8,128)(2,1)} %param.7), kind=kOutput, calls=%fused_computation.20 | convolution fusion | flops 671088640 | bytes 11403264 | tf_op jit(solution)/shard_map/dot_general | solution.py:53
  15.4 5.4 fusion.9
  20.9 133.1 %reduce-scatter.5.cloned.1.call-done = f32[2560,128]{1,0:T(8,128)} async-done(((f32[2560,1024]{1,0:T(8,128)}), f32[2560,128]{1,0:T(8,128)}) %reduce-scatter.5.cloned.1.call-update) | async-done | bytes 1310736 | tf_op jit(solution)/shard_map/reduce_scatter | solution.py:54
  153.9 18.3 %while.14 = (s32[]{:T(128)}, f32[256,8,16]{0,2,1:T(8,128)S(1)}, f32[2560,128]{1,0:T(8,128)}, bf16[2560,8,256]{2,0,1:T(8,128)(2,1)}, s32[]{:T(128)}, /*index=5*/s32[]{:T(128)}, s32[]{:T(128)}, s32[]{:T(128)}) while((s32[]{:T(128)}, f32[256,8,16]{0,2,1:T(8,128)S(1)}, f32[2560,128]{1,0:T(8,128)}, bf16[2560,8,256]{2,0,1:T(8,128)(2,1)}, ...), condition=%wide.region_2.0_spmd.clone, body=%wide.region_1.0_spmd.clone.sunk | while | flops 201392128 | bytes 3670173 | solution.py:42
  153.9 1.0 constant_dynamic-slice_fusion.2
  155.1 2.5 fusion.32
  157.6 1.0 constant_dynamic-slice_fusion.2
  158.7 2.5 fusion.32
  161.3 1.0 constant_dynamic-slice_fusion.2
  162.4 2.5 fusion.32
  164.9 1.0 constant_dynamic-slice_fusion.2
  166.1 2.5 fusion.32
  168.6 1.0 constant_dynamic-slice_fusion.2
  169.7 2.5 fusion.32
  173.0 4.6 convert_reduce_fusion
  178.9 57.8 %all-reduce.1 = f32[256,8]{0,1:T(8,128)S(1)} all-reduce(f32[256,8]{0,1:T(8,128)S(1)} %bitcast.37), channel_id=4, replica_groups=mesh['row'=32,'feat'=8] {'row'}, use_global_device_ids=true, to_apply=%region_5.0.clone | all-reduce | flops 2048 | bytes 16384
  236.8 138.9 %all-reduce.4.cloned.1.call-done = f32[256,128]{0,1:T(8,128)} async-done(((f32[256,128]{0,1:T(8,128)}), f32[256,128]{0,1:T(8,128)}) %all-reduce.4.cloned.1.call-update) | async-done | bytes 131088
  375.6 0.9 fusion.19
  376.6 30.6 %all_gather.6 = bf16[256,128]{1,0:T(8,128)(2,1)S(1)} all-gather(bf16[8,128]{1,0:T(8,128)(2,1)S(1)} %copy.12), channel_id=1, replica_groups=mesh['row'=32,'feat'=8] {'row'}, dimensions={0}, use_global_device_ids=true | all-gather | bytes 67584 | tf_op jit(solution)/shard_map/all_gather | solution.py:61
  407.3 6.3 %fusion.14 = bf16[8,16,2560]{2,1,0:T(8,128)(2,1)} fusion(bf16[256,8,16]{0,2,1:T(8,128)(2,1)S(1)} %bitcast.36, s32[2560,8]{0,1:T(8,128)S(1)} %copy-done.2, bf16[2560]{0:T(1024)(128)(2,1)S(1)} %fusion.17), kind=kOutput, calls=%fused_computation.12 | convolution fusion | flops 178585600 | bytes 807936 | tf_op jit(solution)/shard_map/nmk,kmd->nmd/dot_general | solution.py:21
  413.7 84.3 %all-gather.2.cloned.1.call-done = bf16[2560,1024]{0,1:T(8,128)(2,1)} async-done(((bf16[2560,128]{0,1:T(8,128)(2,1)}), bf16[2560,1024]{0,1:T(8,128)(2,1)}) %all-gather.2.cloned.1.call-update) | async-done | bytes 5242896 | tf_op jit(solution)/shard_map/all_gather | solution.py:63
  497.9 4.8 convolution_multiply_fusion
  503.4 115.5 %reduce-scatter.7.cloned.1.call-done = f32[32,128]{1,0:T(8,128)} async-done(((f32[1024,128]{1,0:T(8,128)}), f32[32,128]{1,0:T(8,128)}) %reduce-scatter.7.cloned.1.call-update) | async-done | bytes 16400 | tf_op jit(solution)/shard_map/reduce_scatter | solution.py:68
  (27 shorter events, 3.0 us)
Async XLA Ops:
  7.2 1.1 copy-start
  7.2 8.3 %copy-start.2 = (s32[2560,8]{0,1:T(8,128)S(1)}, s32[2560,8]{0,1:T(8,128)}, u32[]{:S(2)}) copy-start(s32[2560,8]{0,1:T(8,128)} %param.8) | copy-start | bytes 245764
  7.2 146.8 %reduce-scatter.5.cloned.1.call-start = ((), (), s32[]{:S(2)}) async-start(), calls=%async_computation.2 | async-start | bytes 11796480 | tf_op jit(solution)/shard_map/reduce_scatter | solution.py:54
  14.7 360.9 %all-reduce.4.cloned.1.call-start = ((), (), s32[]{:S(2)}) async-start(), calls=%async_computation.5 | async-start | bytes 262144
  20.9 156.7 %copy-start.3 = (u32[256]{0:T(256)S(1)}, u32[256]{0:T(256)}, u32[]{:S(2)}) copy-start(u32[256]{0:T(256)} %constant.42) | copy-start | bytes 3076
  172.3 0.6 copy-start.1
  172.9 325.0 %all-gather.2.cloned.1.call-start = ((), (), s32[]{:S(2)}) async-start(), calls=%async_computation.3 | async-start | bytes 5898240 | tf_op jit(solution)/shard_map/all_gather | solution.py:63
  413.6 205.3 %reduce-scatter.7.cloned.1.call-start = ((), (), s32[]{:S(2)}) async-start(), calls=%async_computation.4 | async-start | bytes 540672 | tf_op jit(solution)/shard_map/reduce_scatter | solution.py:68
Sparse Core Ops, SparseCore 0:
  14.8 139.0 reduce-scatter.4
  173.1 202.5 all-reduce.3
  413.7 84.1 all-gather.1
  502.9 115.9 reduce-scatter.6
where the time goes:
time: 626 us; the launch traced here: 625 us
  waiting for transfers between devices  472 us (75%)
  blocking collectives  88.4 us (14%)
  matrix products  30.3 us (5%)
  between operations  15.1 us (2%)
  other arithmetic  11.1 us (2%)
  local copies, waits for them, and re-layouts  8.63 us (1%)
    unnamed x5, waiting for transfers between devices  139 us
    reduce_scatter x1, waiting for transfers between devices, shards(): lax.psum_scatter(partial_value, 'feat', scatter_dimension=1, tiled=True)  133 us
    reduce_scatter x1, waiting for transfers between devices, shards(): lax.psum_scatter(product * inverse, 'row', scatter_dimension=0, tiled=True)  115 us
    all_gather x1, waiting for transfers between devices, shards(): recon = lax.all_gather(local_recon, 'feat', axis=1, tiled=True)  84.3 us
    unnamed x1, blocking collectives  57.8 us
    all_gather x1, blocking collectives, shards(): lax.all_gather(centroids.astype(jnp.bfloat16), 'row', axis=0, tiled=True)  30.6 us
    dot_general x5, matrix products, add_block(): jnp.einsum('nmk,nmd->kmd', hot_block, rot_block, precision=lax.Precision....  12.7 us
  transfers between devices with their start and end apart: 4, of which 4 were waited for; matrix products, arithmetic and copies ran while one was open for 2% of the time, Pallas kernels for 0%

commit v1 on v0

v1 whole, which is shorter than its diff:
```python
import jax
import jax.numpy as jnp
import numpy as np
from jax import lax
from jax.sharding import Mesh
from jax.sharding import PartitionSpec as P

K = 256
DS = 16

ROW_PARTS = (("z", 8), ("xl", 2), ("c", 2))
FEAT_PARTS = (("y", 4), ("xh", 2))
REDUCE_ORDER = ("c", "xl", "z")
FLAT_ROW_SUMS = False


def split_hi_lo(x):
    hi = x.astype(jnp.bfloat16)
    lo = (x - hi.astype(jnp.float32)).astype(jnp.bfloat16)
    return hi, lo


def row_psum(x, row_names, order):
    if FLAT_ROW_SUMS:
        return lax.psum(x, row_names)
    for name in order:
        x = lax.psum(x, name)
    return x


def shards(vectors, rotation, codes, live_rows, *, row_names, feat_names, row_sizes, order):
    rows = vectors.shape[0]
    local = vectors.shape[1]
    groups = codes.shape[1]
    n_feat = rotation.shape[1] // local
    n_row = int(np.prod(row_sizes))

    full = lax.all_gather(vectors, feat_names, axis=1, tiled=True)
    columns = lax.all_to_all(rotation, feat_names, split_axis=1, concat_axis=0, tiled=True)
    rotated = jnp.dot(full, columns, preferred_element_type=jnp.float32)

    keep = (jnp.arange(rows, dtype=jnp.int32) < live_rows[0]).astype(jnp.bfloat16)
    kinds = jnp.arange(K, dtype=jnp.int32)
    hot = (codes[:, :, None] == kinds[None, None, :]).astype(jnp.bfloat16) * keep[:, None, None]
    hot = hot.reshape(rows, groups * K)

    hi, lo = split_hi_lo(rotated)
    rhs = jnp.concatenate([hi, lo, keep[:, None]], axis=1)
    both = lax.dot_general(hot, rhs, (((0,), (0,)), ((), ())), preferred_element_type=jnp.float32)
    blocks = (both[:, :local] + both[:, local : 2 * local]).reshape(groups, K, groups, DS)
    picks = jnp.arange(groups)
    sums = blocks[picks, :, picks, :]
    counts = both[:, 2 * local].reshape(groups, K)
    packed = jnp.concatenate([sums.reshape(groups, K * DS), counts], axis=1)

    packed = row_psum(packed, row_names, order)
    total_sums = packed[:, : K * DS].reshape(groups, K, DS)
    total_counts = packed[:, K * DS :]
    cents = total_sums / (total_counts[:, :, None] + 1.0)
    centroids_all = cents.transpose(1, 0, 2).reshape(K, groups * DS)

    row_index = lax.axis_index(row_names)
    share = K // n_row
    centroids = lax.dynamic_slice_in_dim(centroids_all, row_index * share, share, 0)

    table = cents.astype(jnp.bfloat16)
    eye = jnp.eye(groups, dtype=jnp.bfloat16)
    diag = (table[:, :, None, :] * eye[:, None, :, None]).reshape(groups * K, groups * DS)
    recon = jnp.dot(hot, diag, preferred_element_type=jnp.float32).astype(jnp.bfloat16)

    inverse = 1.0 / (rows * n_row)
    product = lax.dot_general(
        recon, full, (((0,), (0,)), ((), ())), preferred_element_type=jnp.float32
    )
    product = product * inverse

    grad_rows = (groups * DS * n_feat) // n_row
    parts = local // grad_rows
    pieces = product.reshape(parts, grad_rows, n_feat, local).transpose(0, 2, 1, 3)
    pieces = pieces.reshape(parts * n_feat, grad_rows, local)
    for name in order:
        pieces = lax.psum_scatter(pieces, name, scatter_dimension=0, tiled=True)
    piece = pieces[0]

    perm = []
    sizes = dict(zip(row_names, row_sizes))
    for r in range(n_row):
        coords = {}
        rest = r
        for name, size in reversed(list(zip(row_names, row_sizes))):
            coords[name] = rest % size
            rest //= size
        p = 0
        for name in order:
            p = p * sizes[name] + coords[name]
        a, f = divmod(p, n_feat)
        for src_feat in range(n_feat):
            dst_row = src_feat * parts + a
            perm.append((r * n_feat + src_feat, dst_row * n_feat + f))
    grad_t = lax.ppermute(piece, row_names + feat_names, perm)
    return centroids, grad_t


def solution(mesh):
    row_size = mesh.shape["row"]
    feat_size = mesh.shape["feat"]
    row_sizes = tuple(s for _, s in ROW_PARTS)
    feat_sizes = tuple(s for _, s in FEAT_PARTS)
    if int(np.prod(row_sizes)) != row_size or int(np.prod(feat_sizes)) != feat_size:
        row_parts, feat_parts = (("row", row_size),), (("feat", feat_size),)
    else:
        row_parts, feat_parts = ROW_PARTS, FEAT_PARTS
    names = tuple(n for n, _ in row_parts + feat_parts)
    shape = tuple(s for _, s in row_parts + feat_parts)
    fine = Mesh(np.asarray(mesh.devices).reshape(shape), names)
    row_names = tuple(n for n, _ in row_parts)
    feat_names = tuple(n for n, _ in feat_parts)

    def body(vectors, rotation, codes, live_rows):
        return shards(
            vectors,
            rotation,
            codes,
            live_rows,
            row_names=row_names,
            feat_names=feat_names,
            row_sizes=tuple(s for _, s in row_parts),
            order=REDUCE_ORDER if row_parts is ROW_PARTS else row_names,
        )

    return jax.shard_map(
        body,
        mesh=fine,
        in_specs=(P(row_names, feat_names), P(feat_names, None), P(row_names, feat_names), P(row_names)),
        out_specs=(P(row_names, feat_names), P(row_names, feat_names)),
        check_vma=False,
    )
```

time: 626 us -> 365 us (0.58)
  waiting for transfers between devices: 472 us -> 259 us
  blocking collectives: 88.4 us -> 0 us
  local copies, waits for them, and re-layouts: 8.63 us -> 39 us
  starting transfers between devices: 0.16 us -> 10.7 us
  matrix products: 30.3 us -> 23.1 us
    reduce_scatter x2 -> x3, waiting for transfers between devices: 249 us -> 71.5 us  [shards(): pieces = lax.psum_scatter(pieces, name, scatter_dimension=0, tiled=True)]
    unnamed x5 -> x7, waiting for transfers between devices: 139 us -> 0.78 us
    psum x0 -> x3, waiting for transfers between devices: none -> 118 us  [row_psum(): x = lax.psum(x, name)]
    unnamed x1 -> x0, blocking collectives: 57.8 us -> none
    all_gather x1 -> x0, blocking collectives: 30.6 us -> none  [shards(): lax.all_gather(centroids.astype(jnp.bfloat16), 'row', axis=0, tiled=True)]
    unnamed x10 -> x11, local copies, waits for them, and re-layouts: 2.93 us -> 31.1 us
    all_gather x1, waiting for transfers between devices: 84.3 us -> 63.6 us  [shards(): full = lax.all_gather(vectors, feat_names, axis=1, tiled=True)]
    all_to_all x0 -> x1, starting transfers between devices: none -> 7.43 us  [shards(): lax.all_to_all(rotation, feat_names, split_axis=1, concat_axis=0, tiled=T...]
  transfers between devices with their start and end apart: 4 -> 9, of which waited for: 4 -> 8; matrix products, arithmetic and copies ran while one was open for 2% -> 12% of each run, Pallas kernels for 0% -> 0%
where the time goes in v1:
time: 365 us; the launch traced here: 359 us
  waiting for transfers between devices  259 us (71%)
  local copies, waits for them, and re-layouts  39 us (11%)
  matrix products  23.1 us (6%)
  between operations  15 us (4%)
  other arithmetic  12.6 us (3%)
  starting transfers between devices  10.7 us (3%)
    psum x3, waiting for transfers between devices, row_psum(): x = lax.psum(x, name)  118 us
    reduce_scatter x3, waiting for transfers between devices, shards(): pieces = lax.psum_scatter(pieces, name, scatter_dimension=0, tiled=True)  71.5 us
    all_gather x1, waiting for transfers between devices, shards(): full = lax.all_gather(vectors, feat_names, axis=1, tiled=True)  63.6 us
    unnamed x11, local copies, waits for them, and re-layouts  31.1 us
    mul x1, other arithmetic, shards(): (codes[:, :, None] == kinds[None, None, :]).astype(jnp.bfloat16)  10.6 us
    dot_general x1, matrix products, shards(): lax.dot_general(recon, full, (((0,), (0,)), ((), ())), preferred_element_...  10 us
    dot_general x1, matrix products, shards(): lax.dot_general(hot, rhs, (((0,), (0,)), ((), ())), preferred_element_typ...  8.8 us
    all_to_all x1, starting transfers between devices, shards(): lax.all_to_all(rotation, feat_names, split_axis=1, concat_axis=0, tiled=T...  7.43 us
  transfers between devices with their start and end apart: 9, of which 8 were waited for; matrix products, arithmetic and copies ran while one was open for 12% of the time, Pallas kernels for 0%

profile of v1, /device:TPU:4, one launch (start us, length us, event | category | flops | bytes accessed | tf_op | source)
XLA Modules:
  0.0 359.2 jit_solution(17026292747904781332)
XLA Ops:
  7.2 0.7 all-gather.2.cloned.1.call-update
  7.9 1.8 copy.18
  9.7 7.4 %all-to-all-start = ((bf16[128,8,128]{0,2,1:T(8,128)(2,1)}), bf16[128,8,128]{0,2,1:T(8,128)(2,1)S(1)}, u32[]{:S(2)}, u32[]{:S(2)}) async-start(bf16[128,8,128]{0,2,1:T(8,128)(2,1)} %bitcast.1), calls=%async_computation | async-start | bytes 524288 | tf_op jit(solution)/shard_map/all_to_all | solution.py:39
  17.1 1.3 copy.17
  18.4 3.1 eq.38
  21.5 13.6 %copy.26 = s32[320,8,8,256]{3,1,2,0:T(8,128)} copy(s32[320,8,8,256]{3,2,1,0:T(8,128)S(1)} %bitcast.43) | data formatting | bytes 41943040
  36.0 63.6 %all-gather.2.cloned.1.call-done = bf16[2560,1024]{1,0:T(8,128)(2,1)} async-done(((bf16[2560,128]{1,0:T(8,128)(2,1)}), bf16[2560,1024]{1,0:T(8,128)(2,1)}) %all-gather.2.cloned.1.call-update) | async-done | bytes 5242896 | tf_op jit(solution)/shard_map/all_gather | solution.py:38
  99.6 4.3 %subtract_convert_fusion = (bf16[2560,128]{0,1:T(8,128)(2,1)S(1)}, bf16[2560,128]{0,1:T(8,128)(2,1)S(1)}) fusion(bf16[2560,1024]{1,0:T(8,128)(2,1)} %all-gather.2.cloned.1.call-done, bf16[1024,128]{1,0:T(8,128)(2,1)S(1)} %bitcast.53), kind=kOutput, calls=%fused_computation.14 | convolution fusion | flops 672399360 | bytes 6815744 | tf_op jit(solution)/shard_map/dot_general | solution.py:40
  103.9 8.8 %fusion.1 = f32[2048,257]{0,1:T(8,128)S(1)} fusion(s32[2560,2048]{1,0:T(8,128)} %bitcast.46, s32[2048]{0:T(1024)S(1)} %bitcast.56, bf16[2560]{0:T(1024)(128)(2,1)S(1)} %fusion.13, bf16[2560,1]{0,1:T(2,128)(2,1)S(1)} %compare_convert_fusion, bf16[2560,128]{0,1:T(8,128)(2,1)S(1)} %get-tuple-element.6, bf16[2560,128]{0,1:T(8,128)(2,1)S(1)} %get-tuple-element.7), kind=kOutput, calls=%fused_computation.4 | convolution fusion | flops 2709273600 | bytes 24406016 | tf_op jit(solution)/shard_map/dot_general | solution.py:49
  115.2 0.7 pad_maximum_fusion
  115.9 29.3 %all-reduce.4.cloned.1.call-done = f32[8,4352]{1,0:T(8,128)} async-done(((f32[8,4352]{1,0:T(8,128)}), f32[8,4352]{1,0:T(8,128)}) %all-reduce.4.cloned.1.call-update) | async-done | bytes 139280 | tf_op jit(solution)/shard_map/psum | solution.py:27
  145.3 36.8 %all-reduce.6.cloned.1.call-done = f32[8,4352]{1,0:T(8,128)} async-done(((f32[8,4352]{1,0:T(8,128)}), f32[8,4352]{1,0:T(8,128)}) %all-reduce.6.cloned.1.call-update) | async-done | bytes 139280 | tf_op jit(solution)/shard_map/psum | solution.py:27
  182.3 10.6 %fusion = bf16[2560,8,256]{2,1,0:T(8,128)(2,1)} fusion(s32[2560,8]{1,0:T(8,128)S(1)} %copy.17, bf16[2560]{0:T(1024)(128)(2,1)S(1)} %fusion.13), kind=kLoop, calls=%fused_computation.2 | loop fusion | flops 10485760 | bytes 10572800 | tf_op jit(solution)/shard_map/mul | solution.py:44
  192.9 12.6 %copy.29 = bf16[320,8,8,256]{3,1,2,0:T(8,128)(2,1)} copy(bf16[320,8,8,256]{3,2,1,0:T(8,128)(2,1)} %bitcast.45) | data formatting | bytes 20971520
  205.5 52.2 %all-reduce.8.cloned.1.call-done = f32[8,4352]{1,0:T(8,128)} async-done(((f32[8,4352]{1,0:T(8,128)}), f32[8,4352]{1,0:T(8,128)}) %all-reduce.8.cloned.1.call-update) | async-done | bytes 139280 | tf_op jit(solution)/shard_map/psum | solution.py:27
  257.7 0.9 slice.25
  259.0 0.7 slice_add_fusion.1
  260.5 10.0 %fusion.10 = f32[16,8,8,128]{3,1,2,0:T(8,128)S(1)} fusion(bf16[2560,1024]{1,0:T(8,128)(2,1)} %all-gather.2.cloned.1.call-done, bf16[2560,2048]{1,0:T(8,128)(2,1)} %bitcast.44, bf16[2048,128]{0,1:T(8,128)(2,1)S(1)} %bitcast.49), kind=kOutput, calls=%fused_computation.16 | convolution fusion | flops 2013724672 | bytes 16777216 | tf_op jit(solution)/shard_map/dot_general | solution.py:72
  270.6 0.9 copy.24
  271.6 11.4 %reduce-scatter.4.cloned.1.call-done = f32[16,32,128]{2,1,0:T(8,128)} async-done(((f32[32,32,128]{2,1,0:T(8,128)}), f32[16,32,128]{2,1,0:T(8,128)}) %reduce-scatter.4.cloned.1.call-update) | async-done | bytes 262160 | tf_op jit(solution)/shard_map/reduce_scatter | solution.py:82
  283.1 20.0 %reduce-scatter.6.cloned.1.call-done = f32[8,32,128]{2,1,0:T(8,128)} async-done(((f32[16,32,128]{2,1,0:T(8,128)}), f32[8,32,128]{2,1,0:T(8,128)}) %reduce-scatter.6.cloned.1.call-update) | async-done | bytes 131088 | tf_op jit(solution)/shard_map/reduce_scatter | solution.py:82
  303.4 40.1 %reduce-scatter.8.cloned.1.call-done = f32[1,32,128]{2,1,0:T(8,128)} async-done(((f32[8,32,128]{2,1,0:T(8,128)}), f32[1,32,128]{2,1,0:T(8,128)}) %reduce-scatter.8.cloned.1.call-update) | async-done | bytes 16400 | tf_op jit(solution)/shard_map/reduce_scatter | solution.py:82
  343.5 2.8 collective-permute-start
  347.1 4.6 %collective-permute-done = f32[32,128]{1,0:T(8,128)S(1)} collective-permute-done((f32[32,128]{1,0:T(8,128)}, f32[32,128]{1,0:T(8,128)S(1)}, u32[]{:S(2)}, u32[]{:S(2)}) %collective-permute-start) | collective-permute-done | bytes 16416 | tf_op jit(solution)/shard_map/ppermute | solution.py:100
  (40 shorter events, 6.0 us)
Async XLA Ops:
  7.2 92.4 %all-gather.2.cloned.1.call-start = ((), (), s32[]{:S(2)}) async-start(), calls=%async_computation.4 | async-start | bytes 5898240 | tf_op jit(solution)/shard_map/all_gather | solution.py:38
  9.7 26.1 %all-to-all-start = ((bf16[128,8,128]{0,2,1:T(8,128)(2,1)}), bf16[128,8,128]{0,2,1:T(8,128)(2,1)S(1)}, u32[]{:S(2)}, u32[]{:S(2)}) async-start(bf16[128,8,128]{0,2,1:T(8,128)(2,1)} %bitcast.1), calls=%async_computation | async-start | bytes 524288 | tf_op jit(solution)/shard_map/all_to_all | solution.py:39
  17.1 128.1 %all-reduce.4.cloned.1.call-start = ((), (), s32[]{:S(2)}) async-start(), calls=%async_computation.5 | async-start | bytes 278528 | tf_op jit(solution)/shard_map/psum | solution.py:27
  115.9 66.2 %all-reduce.6.cloned.1.call-start = ((), (), s32[]{:S(2)}) async-start(), calls=%async_computation.6 | async-start | bytes 278528 | tf_op jit(solution)/shard_map/psum | solution.py:27
  145.2 112.5 %all-reduce.8.cloned.1.call-start = ((), (), s32[]{:S(2)}) async-start(), calls=%async_computation.7 | async-start | bytes 278528 | tf_op jit(solution)/shard_map/psum | solution.py:27
  182.1 100.9 %reduce-scatter.4.cloned.1.call-start = ((), (), s32[]{:S(2)}) async-start(), calls=%async_computation.8 | async-start | bytes 786432 | tf_op jit(solution)/shard_map/reduce_scatter | solution.py:82
  271.5 31.6 %reduce-scatter.6.cloned.1.call-start = ((), (), s32[]{:S(2)}) async-start(), calls=%async_computation.9 | async-start | bytes 393216 | tf_op jit(solution)/shard_map/reduce_scatter | solution.py:82
  283.0 60.5 %reduce-scatter.8.cloned.1.call-start = ((), (), s32[]{:S(2)}) async-start(), calls=%async_computation.10 | async-start | bytes 147456 | tf_op jit(solution)/shard_map/reduce_scatter | solution.py:82
  343.5 8.2 %collective-permute-start = (f32[32,128]{1,0:T(8,128)}, f32[32,128]{1,0:T(8,128)S(1)}, u32[]{:S(2)}, u32[]{:S(2)}) collective-permute-start(f32[32,128]{1,0:T(8,128)} %bitcast.57), channel_id=1, source_target_pairs={{0,0},{1,32},{2,64},{3,96},{4,128},{5,160},{6,192},{7,224},{8,16},... | collective-permute-start | bytes 49160 | tf_op jit(solution)/shard_map/ppermute | solution.py:100
Sparse Core Ops, SparseCore 0:
  10.5 89.0 all-gather.1
  116.0 29.1 all-reduce.3
  147.8 34.2 all-reduce.5
  184.3 73.3 all-reduce.7
  271.7 11.2 reduce-scatter.3
  285.3 17.7 reduce-scatter.5
  305.7 37.7 reduce-scatter.7

commit v2 on v1

--- a/solution.py
+++ b/solution.py
@@ -11,20 +11,39 @@
 ROW_PARTS = (("z", 8), ("xl", 2), ("c", 2))
 FEAT_PARTS = (("y", 4), ("xh", 2))
 REDUCE_ORDER = ("c", "xl", "z")
-FLAT_ROW_SUMS = False
 
 
-def split_hi_lo(x):
-    hi = x.astype(jnp.bfloat16)
-    lo = (x - hi.astype(jnp.float32)).astype(jnp.bfloat16)
-    return hi, lo
+def axis_bit(name, bit):
+    return (lax.axis_index(name) >> bit) & 1
 
 
-def row_psum(x, row_names, order):
-    if FLAT_ROW_SUMS:
-        return lax.psum(x, row_names)
+def steps_of(row_names, row_sizes, order):
+    sizes = dict(zip(row_names, row_sizes))
+    out = []
     for name in order:
-        x = lax.psum(x, name)
+        for bit in range(int(sizes[name]).bit_length() - 1):
+            out.append((name, bit, sizes[name]))
+    return out
+
+
+def exchange(x, name, bit, size):
+    pairs = [(i, i ^ (1 << bit)) for i in range(size)]
+    return lax.ppermute(x, name, pairs)
+
+
+def row_psum(x, steps):
+    for name, bit, size in steps:
+        x = x + exchange(x, name, bit, size)
+    return x
+
+
+def row_psum_scatter(x, steps):
+    for name, bit, size in steps:
+        halves = x.reshape((2, x.shape[0] // 2) + x.shape[1:])
+        mine = axis_bit(name, bit)
+        keep = lax.dynamic_index_in_dim(halves, mine, 0, keepdims=False)
+        send = lax.dynamic_index_in_dim(halves, 1 - mine, 0, keepdims=False)
+        x = keep + exchange(send, name, bit, size)
     return x
 
 
@@ -34,6 +53,7 @@
     groups = codes.shape[1]
     n_feat = rotation.shape[1] // local
     n_row = int(np.prod(row_sizes))
+    steps = steps_of(row_names, row_sizes, order)
 
     full = lax.all_gather(vectors, feat_names, axis=1, tiled=True)
     columns = lax.all_to_all(rotation, feat_names, split_axis=1, concat_axis=0, tiled=True)
@@ -41,19 +61,20 @@
 
     keep = (jnp.arange(rows, dtype=jnp.int32) < live_rows[0]).astype(jnp.bfloat16)
     kinds = jnp.arange(K, dtype=jnp.int32)
-    hot = (codes[:, :, None] == kinds[None, None, :]).astype(jnp.bfloat16) * keep[:, None, None]
-    hot = hot.reshape(rows, groups * K)
+    hot = (codes.T[:, None, :] == kinds[None, :, None]).astype(jnp.bfloat16) * keep[None, None, :]
+    hot = hot.reshape(groups * K, rows)
 
-    hi, lo = split_hi_lo(rotated)
-    rhs = jnp.concatenate([hi, lo, keep[:, None]], axis=1)
-    both = lax.dot_general(hot, rhs, (((0,), (0,)), ((), ())), preferred_element_type=jnp.float32)
+    hi = lax.reduce_precision(rotated, exponent_bits=8, mantissa_bits=7)
+    lo = (rotated - hi).astype(jnp.bfloat16)
+    rhs = jnp.concatenate([hi.astype(jnp.bfloat16), lo, keep[:, None]], axis=1)
+    both = jnp.dot(hot, rhs, preferred_element_type=jnp.float32)
     blocks = (both[:, :local] + both[:, local : 2 * local]).reshape(groups, K, groups, DS)
     picks = jnp.arange(groups)
     sums = blocks[picks, :, picks, :]
     counts = both[:, 2 * local].reshape(groups, K)
     packed = jnp.concatenate([sums.reshape(groups, K * DS), counts], axis=1)
 
-    packed = row_psum(packed, row_names, order)
+    packed = row_psum(packed, steps)
     total_sums = packed[:, : K * DS].reshape(groups, K, DS)
     total_counts = packed[:, K * DS :]
     cents = total_sums / (total_counts[:, :, None] + 1.0)
@@ -65,35 +86,32 @@
 
     table = cents.astype(jnp.bfloat16)
     eye = jnp.eye(groups, dtype=jnp.bfloat16)
-    diag = (table[:, :, None, :] * eye[:, None, :, None]).reshape(groups * K, groups * DS)
-    recon = jnp.dot(hot, diag, preferred_element_type=jnp.float32).astype(jnp.bfloat16)
+    diag_t = (table.transpose(0, 2, 1)[:, :, None, :] * eye[:, None, :, None]).reshape(
+        groups * DS, groups * K
+    )
+    recon_t = jnp.dot(diag_t, hot, preferred_element_type=jnp.float32).astype(jnp.bfloat16)
 
     inverse = 1.0 / (rows * n_row)
-    product = lax.dot_general(
-        recon, full, (((0,), (0,)), ((), ())), preferred_element_type=jnp.float32
-    )
+    product = jnp.dot(recon_t, full, preferred_element_type=jnp.float32)
     product = product * inverse
 
     grad_rows = (groups * DS * n_feat) // n_row
     parts = local // grad_rows
     pieces = product.reshape(parts, grad_rows, n_feat, local).transpose(0, 2, 1, 3)
     pieces = pieces.reshape(parts * n_feat, grad_rows, local)
-    for name in order:
-        pieces = lax.psum_scatter(pieces, name, scatter_dimension=0, tiled=True)
-    piece = pieces[0]
+    piece = row_psum_scatter(pieces, steps)[0]
 
     perm = []
-    sizes = dict(zip(row_names, row_sizes))
     for r in range(n_row):
         coords = {}
         rest = r
         for name, size in reversed(list(zip(row_names, row_sizes))):
             coords[name] = rest % size
             rest //= size
-        p = 0
-        for name in order:
-            p = p * sizes[name] + coords[name]
-        a, f = divmod(p, n_feat)
+        q = 0
+        for name, bit, size in steps:
+            q = q * 2 + ((coords[name] >> bit) & 1)
+        a, f = divmod(q, n_feat)
         for src_feat in range(n_feat):
             dst_row = src_feat * parts + a
             perm.append((r * n_feat + src_feat, dst_row * n_feat + f))

time: 365 us -> 199 us (0.55); the launches traced: 359 us -> 199 us
  waiting for transfers between devices: 259 us -> 118 us
  local copies, waits for them, and re-layouts: 39 us -> 7.84 us
  starting transfers between devices: 10.7 us -> 27.1 us
  matrix products: 23.1 us -> 15.2 us
    psum x3 -> x0, waiting for transfers between devices: 118 us -> none  [row_psum(): x = lax.psum(x, name)]
    reduce_scatter x3 -> x0, waiting for transfers between devices: 71.5 us -> none  [shards(): pieces = lax.psum_scatter(pieces, name, scatter_dimension=0, tiled=True)]
    ppermute x0 -> x10, waiting for transfers between devices: none -> 34.8 us  [exchange(): return lax.ppermute(x, name, pairs)]
    unnamed x11 -> x13, local copies, waits for them, and re-layouts: 31.1 us -> 4.66 us
    ppermute x0 -> x10, starting transfers between devices: none -> 16.3 us  [exchange(): return lax.ppermute(x, name, pairs)]
    all_gather x1, waiting for transfers between devices: 63.6 us -> 74.3 us  [shards(): full = lax.all_gather(vectors, feat_names, axis=1, tiled=True)]
    dot_general x2, matrix products: 18.8 us -> 10.7 us  [the longest x1 7.7 us: shards(): product = jnp.dot(recon_t, full, preferred_element_type=jnp.float32)]
    mul x2 -> x3, other arithmetic: 10.7 us -> 15.2 us  [the longest x2 15 us: shards(): (codes.T[:, None, :] == kinds[None, :, None]).astype(jnp.bfloat16)]
  transfers between devices with their start and end apart: 9 -> 13, of which waited for: 8 -> 11; matrix products, arithmetic and copies ran while one was open for 12% -> 9% of each run, Pallas kernels for 0% -> 0%
where the time goes in v2:
time: 199 us
  waiting for transfers between devices  118 us (59%)
  starting transfers between devices  27.1 us (14%)
  other arithmetic  15.8 us (8%)
  matrix products  15.2 us (8%)
  between operations  15 us (8%)
  local copies, waits for them, and re-layouts  7.84 us (4%)
    all_gather x1, waiting for transfers between devices, shards(): full = lax.all_gather(vectors, feat_names, axis=1, tiled=True)  74.3 us
    ppermute x10, waiting for transfers between devices, exchange(): return lax.ppermute(x, name, pairs)  34.8 us
    ppermute x10, starting transfers between devices, exchange(): return lax.ppermute(x, name, pairs)  16.3 us
    mul x2, other arithmetic, shards(): (codes.T[:, None, :] == kinds[None, :, None]).astype(jnp.bfloat16)  15 us
    ppermute x1, waiting for transfers between devices, shards(): grad_t = lax.ppermute(piece, row_names + feat_names, perm)  7.85 us
    dot_general x1, matrix products, shards(): product = jnp.dot(recon_t, full, preferred_element_type=jnp.float32)  7.7 us
    all_to_all x1, starting transfers between devices, shards(): lax.all_to_all(rotation, feat_names, split_axis=1, concat_axis=0, tiled=T...  7.43 us
    unnamed x13, local copies, waits for them, and re-layouts  4.66 us
  transfers between devices with their start and end apart: 13, of which 11 were waited for; matrix products, arithmetic and copies ran while one was open for 9% of the time, Pallas kernels for 0%

profile of v2, /device:TPU:4, one launch (start us, length us, event | category | flops | bytes accessed | tf_op | source)
XLA Modules:
  0.0 198.6 jit_solution(13419684051986915436)
XLA Ops:
  7.9 1.8 copy.14
  9.7 7.4 %all-to-all-start = ((bf16[128,8,128]{0,2,1:T(8,128)(2,1)}), bf16[128,8,128]{0,2,1:T(8,128)(2,1)S(1)}, u32[]{:S(2)}, u32[]{:S(2)}) async-start(bf16[128,8,128]{0,2,1:T(8,128)(2,1)} %bitcast.3), calls=%async_computation | async-start | bytes 524288 | tf_op jit(solution)/shard_map/all_to_all | solution.py:59
  17.8 7.3 %fusion.1 = bf16[2048,2560]{1,0:T(8,128)(2,1)} fusion(s32[2048]{0:T(1024)S(1)} %bitcast.83, s32[8,2560]{1,0:T(8,128)} %bitcast.78, bf16[2560]{0:T(1024)(128)(2,1)S(1)} %fusion.11), kind=kLoop, calls=%fused_computation.4 | loop fusion | flops 10485760 | bytes 10580992 | tf_op jit(solution)/shard_map/mul | solution.py:64
  25.3 74.3 %all-gather.2.cloned.1.call-done = bf16[2560,1024]{1,0:T(8,128)(2,1)} async-done(((bf16[2560,128]{1,0:T(8,128)(2,1)}), bf16[2560,1024]{1,0:T(8,128)(2,1)}) %all-gather.2.cloned.1.call-update) | async-done | bytes 5242896 | tf_op jit(solution)/shard_map/all_gather | solution.py:58
  99.6 4.5 %reduce-precision_convert_fusion = (bf16[2560,128]{0,1:T(8,128)(2,1)S(1)}, bf16[2560,128]{0,1:T(8,128)(2,1)S(1)}) fusion(bf16[2560,1024]{1,0:T(8,128)(2,1)} %all-gather.2.cloned.1.call-done, bf16[1024,128]{1,0:T(8,128)(2,1)S(1)} %bitcast.72), kind=kOutput, calls=%fused_computation.7 | convolution fusion | flops 672399360 | bytes 6815744 | tf_op jit(solution)/shard_map/dot_general | solution.py:60
  105.1 3.0 %fusion.2 = f32[2048,257]{0,1:T(8,128)S(1)} fusion(bf16[2048,2560]{1,0:T(8,128)(2,1)S(1)} %copy-done, bf16[2560,1]{0,1:T(2,128)(2,1)S(1)} %compare_convert_fusion, bf16[2560,128]{0,1:T(8,128)(2,1)S(1)} %get-tuple-element.7, bf16[2560,128]{0,1:T(8,128)(2,1)S(1)} %get-tuple-element.6), kind=kOutput, calls=%fused_computation.8 | convolution fusion | flops 2698787840 | bytes 13906944 | tf_op jit(solution)/shard_map/dot_general | solution.py:70
  110.7 1.3 collective-permute-done
  112.1 2.2 %collective-permute-start.1 = (f32[8,4352]{1,0:T(8,128)S(1)}, f32[8,4352]{1,0:T(8,128)S(1)}, u32[]{:S(2)}, u32[]{:S(2)}) collective-permute-start(f32[8,4352]{1,0:T(8,128)S(1)} %add.92), channel_id=1, source_target_pairs={{0,16},{16,0},{1,17},{17,1},{2,18},{18,2},{3,19},{19,3},{4,20},{20... | collective-permute-start | bytes 417800 | tf_op jit(solution)/shard_map/ppermute | solution.py:31
  114.3 4.0 %collective-permute-done.1 = f32[8,4352]{1,0:T(8,128)S(1)} collective-permute-done((f32[8,4352]{1,0:T(8,128)S(1)}, f32[8,4352]{1,0:T(8,128)S(1)}, u32[]{:S(2)}, u32[]{:S(2)}) %collective-permute-start.1) | collective-permute-done | bytes 139296 | tf_op jit(solution)/shard_map/ppermute | solution.py:31
  118.3 1.6 collective-permute-start.2
  119.9 3.7 %collective-permute-done.2 = f32[8,4352]{1,0:T(8,128)S(1)} collective-permute-done((f32[8,4352]{1,0:T(8,128)S(1)}, f32[8,4352]{1,0:T(8,128)S(1)}, u32[]{:S(2)}, u32[]{:S(2)}) %collective-permute-start.2) | collective-permute-done | bytes 139296 | tf_op jit(solution)/shard_map/ppermute | solution.py:31
  123.6 2.6 %collective-permute-start.3 = (f32[8,4352]{1,0:T(8,128)S(1)}, f32[8,4352]{1,0:T(8,128)S(1)}, u32[]{:S(2)}, u32[]{:S(2)}) collective-permute-start(f32[8,4352]{1,0:T(8,128)S(1)} %add.94), channel_id=1, source_target_pairs={{0,64},{32,96},{64,0},{96,32},{128,192},{160,224},{192,128},{224,1... | collective-permute-start | bytes 417800 | tf_op jit(solution)/shard_map/ppermute | solution.py:31
  126.2 5.6 %collective-permute-done.3 = f32[8,4352]{1,0:T(8,128)S(1)} collective-permute-done((f32[8,4352]{1,0:T(8,128)S(1)}, f32[8,4352]{1,0:T(8,128)S(1)}, u32[]{:S(2)}, u32[]{:S(2)}) %collective-permute-start.3) | collective-permute-done | bytes 139296 | tf_op jit(solution)/shard_map/ppermute | solution.py:31
  131.9 6.0 %collective-permute-start.4 = (f32[8,4352]{1,0:T(8,128)S(1)}, f32[8,4352]{1,0:T(8,128)S(1)}, u32[]{:S(2)}, u32[]{:S(2)}) collective-permute-start(f32[8,4352]{1,0:T(8,128)S(1)} %add.95), channel_id=1, source_target_pairs={{0,128},{32,160},{64,192},{96,224},{128,0},{160,32},{192,64},{224,... | collective-permute-start | bytes 417800 | tf_op jit(solution)/shard_map/ppermute | solution.py:31
  137.9 7.7 %fusion = bf16[8,256,2560]{2,1,0:T(8,128)(2,1)} fusion(s32[8,2560]{1,0:T(8,128)S(1)} %bitcast.79, bf16[2560]{0:T(1024)(128)(2,1)S(1)} %fusion.11), kind=kLoop, calls=%fused_computation.3 | loop fusion | flops 10485760 | bytes 10572800 | tf_op jit(solution)/shard_map/mul | solution.py:64
  146.8 7.7 %fusion.9 = f32[16,8,8,128]{3,1,2,0:T(8,128)S(1)} fusion(bf16[2560,1024]{1,0:T(8,128)(2,1)} %all-gather.2.cloned.1.call-done, bf16[128,2048]{1,0:T(8,128)(2,1)S(1)} %bitcast.67, bf16[2048,2560]{1,0:T(8,128)(2,1)} %bitcast.64), kind=kOutput, calls=%fused_computation.16 | convolution fusion | flops 2013724672 | bytes 16777216 | tf_op jit(solution)/shard_map/dot_general | solution.py:95
  154.9 1.5 collective-permute-done.5
  157.7 4.4 %collective-permute-done.6 = f32[8,32,128]{2,1,0:T(8,128)S(1)} collective-permute-done((f32[8,32,128]{2,1,0:T(8,128)S(1)}, f32[8,32,128]{2,1,0:T(8,128)S(1)}, u32[]{:S(2)}, u32[]{:S(2)}) %collective-permute-start.6) | collective-permute-done | bytes 131104 | tf_op jit(solution)/shard_map/ppermute | solution.py:31
  162.2 4.2 %collective-permute-done.7 = f32[4,32,128]{2,1,0:T(8,128)S(1)} collective-permute-done((f32[4,32,128]{2,1,0:T(8,128)S(1)}, f32[4,32,128]{2,1,0:T(8,128)S(1)}, u32[]{:S(2)}, u32[]{:S(2)}) %collective-permute-start.7) | collective-permute-done | bytes 65568 | tf_op jit(solution)/shard_map/ppermute | solution.py:31
  166.6 4.8 %collective-permute-done.8 = f32[2,32,128]{2,1,0:T(8,128)S(1)} collective-permute-done((f32[2,32,128]{2,1,0:T(8,128)S(1)}, f32[2,32,128]{2,1,0:T(8,128)S(1)}, u32[]{:S(2)}, u32[]{:S(2)}) %collective-permute-start.8) | collective-permute-done | bytes 32800 | tf_op jit(solution)/shard_map/ppermute | solution.py:31
  171.4 2.3 %collective-permute-start.9 = (f32[1,32,128]{2,1,0:T(8,128)S(1)}, f32[1,32,128]{2,1,0:T(8,128)S(1)}, u32[]{:S(2)}, u32[]{:S(2)}) collective-permute-start(f32[1,32,128]{2,1,0:T(8,128)S(1)} %constant_dynamic-slice_fusion), channel_id=1, source_target_pairs={{0,128},{32,160},{64,192},{96,224},{128,0},{160,32},{192,64},{224,... | collective-permute-start | bytes 49160 | tf_op jit(solution)/shard_map/ppermute | solution.py:31
  174.0 5.2 %collective-permute-done.9 = f32[1,32,128]{2,1,0:T(8,128)S(1)} collective-permute-done((f32[1,32,128]{2,1,0:T(8,128)S(1)}, f32[1,32,128]{2,1,0:T(8,128)S(1)}, u32[]{:S(2)}, u32[]{:S(2)}) %collective-permute-start.9) | collective-permute-done | bytes 16416 | tf_op jit(solution)/shard_map/ppermute | solution.py:31
  179.2 3.3 %collective-permute-start.10 = (f32[32,128]{1,0:T(8,128)S(1)}, f32[32,128]{1,0:T(8,128)S(1)}, u32[]{:S(2)}, u32[]{:S(2)}) collective-permute-start(f32[32,128]{1,0:T(8,128)S(1)} %add_bitcast_fusion), channel_id=1, source_target_pairs={{0,0},{1,32},{2,64},{3,96},{4,128},{5,160},{6,192},{7,224},{8,16},... | collective-permute-start | bytes 49160 | tf_op jit(solution)/shard_map/ppermute | solution.py:118
  183.3 7.8 %collective-permute-done.10 = f32[32,128]{1,0:T(8,128)S(1)} collective-permute-done((f32[32,128]{1,0:T(8,128)S(1)}, f32[32,128]{1,0:T(8,128)S(1)}, u32[]{:S(2)}, u32[]{:S(2)}) %collective-permute-start.10) | collective-permute-done | bytes 16416 | tf_op jit(solution)/shard_map/ppermute | solution.py:118
  (58 shorter events, 9.1 us)
Async XLA Ops:
  7.2 92.4 %all-gather.2.cloned.1.call-start = ((), (), s32[]{:S(2)}) async-start(), calls=%async_computation.1 | async-start | bytes 5898240 | tf_op jit(solution)/shard_map/all_gather | solution.py:58
  9.7 15.5 %all-to-all-start = ((bf16[128,8,128]{0,2,1:T(8,128)(2,1)}), bf16[128,8,128]{0,2,1:T(8,128)(2,1)S(1)}, u32[]{:S(2)}, u32[]{:S(2)}) async-start(bf16[128,8,128]{0,2,1:T(8,128)(2,1)} %bitcast.3), calls=%async_computation | async-start | bytes 524288 | tf_op jit(solution)/shard_map/all_to_all | solution.py:59
  99.6 5.5 %copy-start = (bf16[2048,2560]{1,0:T(8,128)(2,1)S(1)}, bf16[2048,2560]{1,0:T(8,128)(2,1)}, u32[]{:S(2)}) copy-start(bf16[2048,2560]{1,0:T(8,128)(2,1)} %fusion.1) | copy-start | bytes 31457284
  108.3 29.6 %copy-start.1 = (s32[2560,8]{0,1:T(8,128)S(1)}, s32[2560,8]{0,1:T(8,128)}, u32[]{:S(2)}) copy-start(s32[2560,8]{0,1:T(8,128)} %param.6) | copy-start | bytes 245764
  110.6 1.4 collective-permute-start
  112.1 6.1 %collective-permute-start.1 = (f32[8,4352]{1,0:T(8,128)S(1)}, f32[8,4352]{1,0:T(8,128)S(1)}, u32[]{:S(2)}, u32[]{:S(2)}) collective-permute-start(f32[8,4352]{1,0:T(8,128)S(1)} %add.92), channel_id=1, source_target_pairs={{0,16},{16,0},{1,17},{17,1},{2,18},{18,2},{3,19},{19,3},{4,20},{20... | collective-permute-start | bytes 417800 | tf_op jit(solution)/shard_map/ppermute | solution.py:31
  118.3 5.3 %collective-permute-start.2 = (f32[8,4352]{1,0:T(8,128)S(1)}, f32[8,4352]{1,0:T(8,128)S(1)}, u32[]{:S(2)}, u32[]{:S(2)}) collective-permute-start(f32[8,4352]{1,0:T(8,128)S(1)} %add.93), channel_id=1, source_target_pairs={{0,32},{32,0},{64,96},{96,64},{128,160},{160,128},{192,224},{224,1... | collective-permute-start | bytes 417800 | tf_op jit(solution)/shard_map/ppermute | solution.py:31
  123.6 8.3 %collective-permute-start.3 = (f32[8,4352]{1,0:T(8,128)S(1)}, f32[8,4352]{1,0:T(8,128)S(1)}, u32[]{:S(2)}, u32[]{:S(2)}) collective-permute-start(f32[8,4352]{1,0:T(8,128)S(1)} %add.94), channel_id=1, source_target_pairs={{0,64},{32,96},{64,0},{96,32},{128,192},{160,224},{192,128},{224,1... | collective-permute-start | bytes 417800 | tf_op jit(solution)/shard_map/ppermute | solution.py:31
  131.9 13.8 %collective-permute-start.4 = (f32[8,4352]{1,0:T(8,128)S(1)}, f32[8,4352]{1,0:T(8,128)S(1)}, u32[]{:S(2)}, u32[]{:S(2)}) collective-permute-start(f32[8,4352]{1,0:T(8,128)S(1)} %add.95), channel_id=1, source_target_pairs={{0,128},{32,160},{64,192},{96,224},{128,0},{160,32},{192,64},{224,... | collective-permute-start | bytes 417800 | tf_op jit(solution)/shard_map/ppermute | solution.py:31
  154.8 1.6 collective-permute-start.5
  156.5 5.6 %collective-permute-start.6 = (f32[8,32,128]{2,1,0:T(8,128)S(1)}, f32[8,32,128]{2,1,0:T(8,128)S(1)}, u32[]{:S(2)}, u32[]{:S(2)}) collective-permute-start(f32[8,32,128]{2,1,0:T(8,128)S(1)} %dynamic-slice_bitcast_fusion.1), channel_id=1, source_target_pairs={{0,16},{16,0},{1,17},{17,1},{2,18},{18,2},{3,19},{19,3},{4,20},{20... | collective-permute-start | bytes 393224 | tf_op jit(solution)/shard_map/ppermute | solution.py:31
  162.1 4.4 %collective-permute-start.7 = (f32[4,32,128]{2,1,0:T(8,128)S(1)}, f32[4,32,128]{2,1,0:T(8,128)S(1)}, u32[]{:S(2)}, u32[]{:S(2)}) collective-permute-start(f32[4,32,128]{2,1,0:T(8,128)S(1)} %dynamic-slice_bitcast_fusion.2), channel_id=1, source_target_pairs={{0,32},{32,0},{64,96},{96,64},{128,160},{160,128},{192,224},{224,1... | collective-permute-start | bytes 196616 | tf_op jit(solution)/shard_map/ppermute | solution.py:31
  166.5 4.9 %collective-permute-start.8 = (f32[2,32,128]{2,1,0:T(8,128)S(1)}, f32[2,32,128]{2,1,0:T(8,128)S(1)}, u32[]{:S(2)}, u32[]{:S(2)}) collective-permute-start(f32[2,32,128]{2,1,0:T(8,128)S(1)} %dynamic-slice_bitcast_fusion.3), channel_id=1, source_target_pairs={{0,64},{32,96},{64,0},{96,32},{128,192},{160,224},{192,128},{224,1... | collective-permute-start | bytes 98312 | tf_op jit(solution)/shard_map/ppermute | solution.py:31
  171.4 7.8 %collective-permute-start.9 = (f32[1,32,128]{2,1,0:T(8,128)S(1)}, f32[1,32,128]{2,1,0:T(8,128)S(1)}, u32[]{:S(2)}, u32[]{:S(2)}) collective-permute-start(f32[1,32,128]{2,1,0:T(8,128)S(1)} %constant_dynamic-slice_fusion), channel_id=1, source_target_pairs={{0,128},{32,160},{64,192},{96,224},{128,0},{160,32},{192,64},{224,... | collective-permute-start | bytes 49160 | tf_op jit(solution)/shard_map/ppermute | solution.py:31
  179.2 11.9 %collective-permute-start.10 = (f32[32,128]{1,0:T(8,128)S(1)}, f32[32,128]{1,0:T(8,128)S(1)}, u32[]{:S(2)}, u32[]{:S(2)}) collective-permute-start(f32[32,128]{1,0:T(8,128)S(1)} %add_bitcast_fusion), channel_id=1, source_target_pairs={{0,0},{1,32},{2,64},{3,96},{4,128},{5,160},{6,192},{7,224},{8,16},... | collective-permute-start | bytes 49160 | tf_op jit(solution)/shard_map/ppermute | solution.py:118
Sparse Core Ops, SparseCore 0:
  10.5 89.0 all-gather.1

commit v3 on v2

--- a/solution.py
+++ b/solution.py
@@ -11,6 +11,7 @@
 ROW_PARTS = (("z", 8), ("xl", 2), ("c", 2))
 FEAT_PARTS = (("y", 4), ("xh", 2))
 REDUCE_ORDER = ("c", "xl", "z")
+GATHER_BY_ALL_TO_ALL = True
 
 
 def axis_bit(name, bit):
@@ -55,9 +56,17 @@
     n_row = int(np.prod(row_sizes))
     steps = steps_of(row_names, row_sizes, order)
 
-    full = lax.all_gather(vectors, feat_names, axis=1, tiled=True)
+    if GATHER_BY_ALL_TO_ALL:
+        copies = jnp.broadcast_to(vectors[None], (n_feat,) + vectors.shape)
+        blocks_in = lax.all_to_all(copies, feat_names, split_axis=0, concat_axis=0, tiled=True)
+    else:
+        full = lax.all_gather(vectors, feat_names, axis=1, tiled=True)
+        blocks_in = full.reshape(rows, n_feat, local).transpose(1, 0, 2)
     columns = lax.all_to_all(rotation, feat_names, split_axis=1, concat_axis=0, tiled=True)
-    rotated = jnp.dot(full, columns, preferred_element_type=jnp.float32)
+    columns = columns.reshape(n_feat, local, local)
+    rotated = lax.dot_general(
+        blocks_in, columns, (((0, 2), (0, 1)), ((), ())), preferred_element_type=jnp.float32
+    )
 
     keep = (jnp.arange(rows, dtype=jnp.int32) < live_rows[0]).astype(jnp.bfloat16)
     kinds = jnp.arange(K, dtype=jnp.int32)
@@ -92,7 +101,9 @@
     recon_t = jnp.dot(diag_t, hot, preferred_element_type=jnp.float32).astype(jnp.bfloat16)
 
     inverse = 1.0 / (rows * n_row)
-    product = jnp.dot(recon_t, full, preferred_element_type=jnp.float32)
+    product = lax.dot_general(
+        recon_t, blocks_in, (((1,), (1,)), ((), ())), preferred_element_type=jnp.float32
+    )
     product = product * inverse
 
     grad_rows = (groups * DS * n_feat) // n_row

time: 199 us -> 179 us (0.90)
  waiting for transfers between devices: 118 us -> 93.1 us
  between operations: 15 us -> 1.58 us
  blocking collectives: 0 us -> 13.3 us
  matrix products: 15.2 us -> 17.7 us
    all_gather x1 -> x0, waiting for transfers between devices: 74.3 us -> none  [shards(): full = lax.all_gather(vectors, feat_names, axis=1, tiled=True)]
    all_to_all x1, waiting for transfers between devices: 0.01 us -> 51.3 us  [shards(): lax.all_to_all(copies, feat_names, split_axis=0, concat_axis=0, tiled=True)]
    all_to_all x0 -> x1, blocking collectives: none -> 13.3 us  [shards(): lax.all_to_all(rotation, feat_names, split_axis=1, concat_axis=0, tiled=T...]
    broadcast_in_dim x0 -> x1, local copies, waits for them, and re-layouts: none -> 4.01 us  [shards(): copies = jnp.broadcast_to(vectors[None], (n_feat,) + vectors.shape)]
    dot_general x1, matrix products: 3.03 us -> 5.71 us  [shards(): both = jnp.dot(hot, rhs, preferred_element_type=jnp.float32)]
    unnamed x13 -> x10, local copies, waits for them, and re-layouts: 4.66 us -> 2.86 us
  transfers between devices with their start and end apart: 13 -> 12, of which waited for: 11 -> 11; matrix products, arithmetic and copies ran while one was open for 9% -> 9% of each run, Pallas kernels for 0% -> 0%
where the time goes in v3:
time: 179 us
  waiting for transfers between devices  93.1 us (52%)
  starting transfers between devices  28.2 us (16%)
  matrix products  17.7 us (10%)
  other arithmetic  14.9 us (8%)
  blocking collectives  13.3 us (7%)
  local copies, waits for them, and re-layouts  9.82 us (5%)
    all_to_all x1, waiting for transfers between devices, shards(): lax.all_to_all(copies, feat_names, split_axis=0, concat_axis=0, tiled=True)  51.3 us
    ppermute x10, waiting for transfers between devices, exchange(): return lax.ppermute(x, name, pairs)  34.7 us
    ppermute x10, starting transfers between devices, exchange(): return lax.ppermute(x, name, pairs)  16.8 us
    mul x2, other arithmetic, shards(): (codes.T[:, None, :] == kinds[None, :, None]).astype(jnp.bfloat16)  14.1 us
    all_to_all x1, blocking collectives, shards(): lax.all_to_all(rotation, feat_names, split_axis=1, concat_axis=0, tiled=T...  13.3 us
    dot_general x1, matrix products, shards(): lax.dot_general(recon_t, blocks_in, (((1,), (1,)), ((), ())), preferred_e...  7.69 us
    all_to_all x1, starting transfers between devices, shards(): lax.all_to_all(copies, feat_names, split_axis=0, concat_axis=0, tiled=True)  7.32 us
    ppermute x1, waiting for transfers between devices, shards(): grad_t = lax.ppermute(piece, row_names + feat_names, perm)  7.09 us
  transfers between devices with their start and end apart: 12, of which 11 were waited for; matrix products, arithmetic and copies ran while one was open for 9% of the time, Pallas kernels for 0%

profile of v3, /device:TPU:4, one launch (start us, length us, event | category | flops | bytes accessed | tf_op | source)
XLA Modules:
  0.0 178.7 jit_solution(12330762174001875745)
XLA Ops:
  1.8 13.3 %all_to_all.21 = bf16[128,8,128]{0,2,1:T(8,128)(2,1)S(1)} all-to-all(bf16[128,8,128]{0,2,1:T(8,128)(2,1)S(1)} %bitcast.77), channel_id=1, replica_groups=mesh['z'=8,'xl'=2,'c'=2,'y'=4,'xh'=2] {'y','xh'}, dimensions={1} | all-to-all | bytes 524288 | tf_op jit(solution)/shard_map/all_to_all | solution.py:65
  15.1 4.0 %broadcast_in_dim.2 = bf16[8,2560,128]{2,1,0:T(8,128)(2,1)} broadcast(bf16[2560,128]{1,0:T(8,128)(2,1)} %param.4), dimensions={1,2} | broadcast | bytes 5898240 | tf_op jit(solution)/shard_map/broadcast_in_dim | solution.py:60
  19.1 7.3 %all-to-all-start = ((bf16[8,2560,128]{2,1,0:T(8,128)(2,1)}), bf16[8,2560,128]{2,1,0:T(8,128)(2,1)}, u32[]{:S(2)}, u32[]{:S(2)}) async-start(bf16[8,2560,128]{2,1,0:T(8,128)(2,1)} %broadcast_in_dim.2), calls=%async_computation | async-start | bytes 10485760 | tf_op jit(solution)/shard_map/all_to_all | solution.py:61
  27.1 6.4 %fusion.1 = bf16[2048,2560]{1,0:T(8,128)(2,1)} fusion(s32[2048]{0:T(1024)S(1)} %bitcast.87, s32[8,2560]{1,0:T(8,128)S(1)} %bitcast.82, bf16[2560]{0:T(1024)(128)(2,1)S(1)} %fusion.12), kind=kLoop, calls=%fused_computation.4 | loop fusion | flops 10485760 | bytes 10580992 | tf_op jit(solution)/shard_map/mul | solution.py:73
  33.6 51.3 %all-to-all-done = bf16[8,2560,128]{2,1,0:T(8,128)(2,1)} async-done(((bf16[8,2560,128]{2,1,0:T(8,128)(2,1)}), bf16[8,2560,128]{2,1,0:T(8,128)(2,1)}, u32[]{:S(2)}, u32[]{:S(2)}) %all-to-all-start) | async-done | bytes 5242912 | tf_op jit(solution)/shard_map/all_to_all | solution.py:61
  84.9 4.3 %reduce-precision_convert_fusion = (bf16[2560,128]{0,1:T(8,128)(2,1)S(1)}, bf16[2560,128]{0,1:T(8,128)(2,1)S(1)}) fusion(bf16[8,2560,128]{2,1,0:T(8,128)(2,1)} %all-to-all-done, bf16[128,8,128]{0,2,1:T(8,128)(2,1)S(1)} %all_to_all.21), kind=kOutput, calls=%fused_computation.9 | convolution fusion | flops 672399360 | bytes 6815744 | tf_op jit(solution)/shard_map/dot_general | solution.py:67
  89.2 5.7 %fusion.3 = f32[2048,257]{0,1:T(8,128)S(1)} fusion(bf16[2048,2560]{1,0:T(8,128)(2,1)} %fusion.1, bf16[2560,1]{0,1:T(2,128)(2,1)S(1)} %compare_convert_fusion, bf16[2560,128]{0,1:T(8,128)(2,1)S(1)} %get-tuple-element.5, bf16[2560,128]{0,1:T(8,128)(2,1)S(1)} %get-tuple-element.4), kind=kOutput, calls=%fused_computation.10 | convolution fusion | flops 2698787840 | bytes 13906944 | tf_op jit(solution)/shard_map/dot_general | solution.py:79
  97.5 1.3 collective-permute-done
  100.1 4.5 %collective-permute-done.1 = f32[8,4352]{1,0:T(8,128)S(1)} collective-permute-done((f32[8,4352]{1,0:T(8,128)S(1)}, f32[8,4352]{1,0:T(8,128)S(1)}, u32[]{:S(2)}, u32[]{:S(2)}) %collective-permute-start.1) | collective-permute-done | bytes 139296 | tf_op jit(solution)/shard_map/ppermute | solution.py:32
  104.7 2.0 %collective-permute-start.2 = (f32[8,4352]{1,0:T(8,128)S(1)}, f32[8,4352]{1,0:T(8,128)S(1)}, u32[]{:S(2)}, u32[]{:S(2)}) collective-permute-start(f32[8,4352]{1,0:T(8,128)S(1)} %add.93), channel_id=1, source_target_pairs={{0,32},{32,0},{64,96},{96,64},{128,160},{160,128},{192,224},{224,1... | collective-permute-start | bytes 417800 | tf_op jit(solution)/shard_map/ppermute | solution.py:32
  106.7 3.2 %collective-permute-done.2 = f32[8,4352]{1,0:T(8,128)S(1)} collective-permute-done((f32[8,4352]{1,0:T(8,128)S(1)}, f32[8,4352]{1,0:T(8,128)S(1)}, u32[]{:S(2)}, u32[]{:S(2)}) %collective-permute-start.2) | collective-permute-done | bytes 139296 | tf_op jit(solution)/shard_map/ppermute | solution.py:32
  109.9 3.4 %collective-permute-start.3 = (f32[8,4352]{1,0:T(8,128)S(1)}, f32[8,4352]{1,0:T(8,128)S(1)}, u32[]{:S(2)}, u32[]{:S(2)}) collective-permute-start(f32[8,4352]{1,0:T(8,128)S(1)} %add.94), channel_id=1, source_target_pairs={{0,64},{32,96},{64,0},{96,32},{128,192},{160,224},{192,128},{224,1... | collective-permute-start | bytes 417800 | tf_op jit(solution)/shard_map/ppermute | solution.py:32
  113.2 5.2 %collective-permute-done.3 = f32[8,4352]{1,0:T(8,128)S(1)} collective-permute-done((f32[8,4352]{1,0:T(8,128)S(1)}, f32[8,4352]{1,0:T(8,128)S(1)}, u32[]{:S(2)}, u32[]{:S(2)}) %collective-permute-start.3) | collective-permute-done | bytes 139296 | tf_op jit(solution)/shard_map/ppermute | solution.py:32
  118.4 6.7 %collective-permute-start.4 = (f32[8,4352]{1,0:T(8,128)S(1)}, f32[8,4352]{1,0:T(8,128)S(1)}, u32[]{:S(2)}, u32[]{:S(2)}) collective-permute-start(f32[8,4352]{1,0:T(8,128)S(1)} %add.95), channel_id=1, source_target_pairs={{0,128},{32,160},{64,192},{96,224},{128,0},{160,32},{192,64},{224,... | collective-permute-start | bytes 417800 | tf_op jit(solution)/shard_map/ppermute | solution.py:32
  125.1 7.7 %fusion = bf16[8,256,2560]{2,1,0:T(8,128)(2,1)} fusion(s32[8,2560]{1,0:T(8,128)S(1)} %bitcast.83, bf16[2560]{0:T(1024)(128)(2,1)S(1)} %fusion.12), kind=kLoop, calls=%fused_computation.3 | loop fusion | flops 10485760 | bytes 10572800 | tf_op jit(solution)/shard_map/mul | solution.py:73
  134.0 7.7 %convolution_multiply_fusion = f32[128,8,128]{2,0,1:T(8,128)S(1)} fusion(bf16[8,2560,128]{2,1,0:T(8,128)(2,1)} %all-to-all-done, bf16[128,2048]{1,0:T(8,128)(2,1)S(1)} %bitcast.73, bf16[2048,2560]{1,0:T(8,128)(2,1)} %bitcast.70), kind=kOutput, calls=%fused_computation.17 | convolution fusion | flops 2013724672 | bytes 16777216 | tf_op jit(solution)/shard_map/dot_general | solution.py:104
  141.9 1.5 collective-permute-done.5
  144.7 4.3 %collective-permute-done.6 = f32[8,32,128]{2,1,0:T(8,128)S(1)} collective-permute-done((f32[8,32,128]{2,1,0:T(8,128)S(1)}, f32[8,32,128]{2,1,0:T(8,128)S(1)}, u32[]{:S(2)}, u32[]{:S(2)}) %collective-permute-start.6) | collective-permute-done | bytes 131104 | tf_op jit(solution)/shard_map/ppermute | solution.py:32
  149.2 4.2 %collective-permute-done.7 = f32[4,32,128]{2,1,0:T(8,128)S(1)} collective-permute-done((f32[4,32,128]{2,1,0:T(8,128)S(1)}, f32[4,32,128]{2,1,0:T(8,128)S(1)}, u32[]{:S(2)}, u32[]{:S(2)}) %collective-permute-start.7) | collective-permute-done | bytes 65568 | tf_op jit(solution)/shard_map/ppermute | solution.py:32
  154.1 4.3 %collective-permute-done.8 = f32[2,32,128]{2,1,0:T(8,128)S(1)} collective-permute-done((f32[2,32,128]{2,1,0:T(8,128)S(1)}, f32[2,32,128]{2,1,0:T(8,128)S(1)}, u32[]{:S(2)}, u32[]{:S(2)}) %collective-permute-start.8) | collective-permute-done | bytes 32800 | tf_op jit(solution)/shard_map/ppermute | solution.py:32
  158.4 1.3 collective-permute-start.9
  160.0 6.1 %collective-permute-done.9 = f32[1,32,128]{2,1,0:T(8,128)S(1)} collective-permute-done((f32[1,32,128]{2,1,0:T(8,128)S(1)}, f32[1,32,128]{2,1,0:T(8,128)S(1)}, u32[]{:S(2)}, u32[]{:S(2)}) %collective-permute-start.9) | collective-permute-done | bytes 16416 | tf_op jit(solution)/shard_map/ppermute | solution.py:32
  166.2 4.1 %collective-permute-start.10 = (f32[32,128]{1,0:T(8,128)S(1)}, f32[32,128]{1,0:T(8,128)S(1)}, u32[]{:S(2)}, u32[]{:S(2)}) collective-permute-start(f32[32,128]{1,0:T(8,128)S(1)} %add_bitcast_fusion), channel_id=1, source_target_pairs={{0,0},{1,32},{2,64},{3,96},{4,128},{5,160},{6,192},{7,224},{8,16},... | collective-permute-start | bytes 49160 | tf_op jit(solution)/shard_map/ppermute | solution.py:129
  171.0 7.1 %collective-permute-done.10 = f32[32,128]{1,0:T(8,128)S(1)} collective-permute-done((f32[32,128]{1,0:T(8,128)S(1)}, f32[32,128]{1,0:T(8,128)S(1)}, u32[]{:S(2)}, u32[]{:S(2)}) %collective-permute-start.10) | collective-permute-done | bytes 16416 | tf_op jit(solution)/shard_map/ppermute | solution.py:129
  (53 shorter events, 10.1 us)
Async XLA Ops:
  19.1 8.0 %copy-start = (s32[2560,8]{0,1:T(8,128)S(1)}, s32[2560,8]{0,1:T(8,128)}, u32[]{:S(2)}) copy-start(s32[2560,8]{0,1:T(8,128)} %param.6) | copy-start | bytes 245764
  19.1 65.8 %all-to-all-start = ((bf16[8,2560,128]{2,1,0:T(8,128)(2,1)}), bf16[8,2560,128]{2,1,0:T(8,128)(2,1)}, u32[]{:S(2)}, u32[]{:S(2)}) async-start(bf16[8,2560,128]{2,1,0:T(8,128)(2,1)} %broadcast_in_dim.2), calls=%async_computation | async-start | bytes 10485760 | tf_op jit(solution)/shard_map/all_to_all | solution.py:61
  97.4 1.4 collective-permute-start
  98.9 5.8 %collective-permute-start.1 = (f32[8,4352]{1,0:T(8,128)S(1)}, f32[8,4352]{1,0:T(8,128)S(1)}, u32[]{:S(2)}, u32[]{:S(2)}) collective-permute-start(f32[8,4352]{1,0:T(8,128)S(1)} %add.92), channel_id=1, source_target_pairs={{0,16},{16,0},{1,17},{17,1},{2,18},{18,2},{3,19},{19,3},{4,20},{20... | collective-permute-start | bytes 417800 | tf_op jit(solution)/shard_map/ppermute | solution.py:32
  104.7 5.2 %collective-permute-start.2 = (f32[8,4352]{1,0:T(8,128)S(1)}, f32[8,4352]{1,0:T(8,128)S(1)}, u32[]{:S(2)}, u32[]{:S(2)}) collective-permute-start(f32[8,4352]{1,0:T(8,128)S(1)} %add.93), channel_id=1, source_target_pairs={{0,32},{32,0},{64,96},{96,64},{128,160},{160,128},{192,224},{224,1... | collective-permute-start | bytes 417800 | tf_op jit(solution)/shard_map/ppermute | solution.py:32
  109.9 8.5 %collective-permute-start.3 = (f32[8,4352]{1,0:T(8,128)S(1)}, f32[8,4352]{1,0:T(8,128)S(1)}, u32[]{:S(2)}, u32[]{:S(2)}) collective-permute-start(f32[8,4352]{1,0:T(8,128)S(1)} %add.94), channel_id=1, source_target_pairs={{0,64},{32,96},{64,0},{96,32},{128,192},{160,224},{192,128},{224,1... | collective-permute-start | bytes 417800 | tf_op jit(solution)/shard_map/ppermute | solution.py:32
  118.4 14.4 %collective-permute-start.4 = (f32[8,4352]{1,0:T(8,128)S(1)}, f32[8,4352]{1,0:T(8,128)S(1)}, u32[]{:S(2)}, u32[]{:S(2)}) collective-permute-start(f32[8,4352]{1,0:T(8,128)S(1)} %add.95), channel_id=1, source_target_pairs={{0,128},{32,160},{64,192},{96,224},{128,0},{160,32},{192,64},{224,... | collective-permute-start | bytes 417800 | tf_op jit(solution)/shard_map/ppermute | solution.py:32
  141.8 1.6 collective-permute-start.5
  143.4 5.6 %collective-permute-start.6 = (f32[8,32,128]{2,1,0:T(8,128)S(1)}, f32[8,32,128]{2,1,0:T(8,128)S(1)}, u32[]{:S(2)}, u32[]{:S(2)}) collective-permute-start(f32[8,32,128]{2,1,0:T(8,128)S(1)} %dynamic-slice_bitcast_fusion.1), channel_id=1, source_target_pairs={{0,16},{16,0},{1,17},{17,1},{2,18},{18,2},{3,19},{19,3},{4,20},{20... | collective-permute-start | bytes 393224 | tf_op jit(solution)/shard_map/ppermute | solution.py:32
  149.1 4.4 %collective-permute-start.7 = (f32[4,32,128]{2,1,0:T(8,128)S(1)}, f32[4,32,128]{2,1,0:T(8,128)S(1)}, u32[]{:S(2)}, u32[]{:S(2)}) collective-permute-start(f32[4,32,128]{2,1,0:T(8,128)S(1)} %dynamic-slice_bitcast_fusion.2), channel_id=1, source_target_pairs={{0,32},{32,0},{64,96},{96,64},{128,160},{160,128},{192,224},{224,1... | collective-permute-start | bytes 196616 | tf_op jit(solution)/shard_map/ppermute | solution.py:32
  153.5 4.9 %collective-permute-start.8 = (f32[2,32,128]{2,1,0:T(8,128)S(1)}, f32[2,32,128]{2,1,0:T(8,128)S(1)}, u32[]{:S(2)}, u32[]{:S(2)}) collective-permute-start(f32[2,32,128]{2,1,0:T(8,128)S(1)} %dynamic-slice_bitcast_fusion.3), channel_id=1, source_target_pairs={{0,64},{32,96},{64,0},{96,32},{128,192},{160,224},{192,128},{224,1... | collective-permute-start | bytes 98312 | tf_op jit(solution)/shard_map/ppermute | solution.py:32
  158.4 7.7 %collective-permute-start.9 = (f32[1,32,128]{2,1,0:T(8,128)S(1)}, f32[1,32,128]{2,1,0:T(8,128)S(1)}, u32[]{:S(2)}, u32[]{:S(2)}) collective-permute-start(f32[1,32,128]{2,1,0:T(8,128)S(1)} %constant_dynamic-slice_fusion), channel_id=1, source_target_pairs={{0,128},{32,160},{64,192},{96,224},{128,0},{160,32},{192,64},{224,... | collective-permute-start | bytes 49160 | tf_op jit(solution)/shard_map/ppermute | solution.py:32
  166.2 11.9 %collective-permute-start.10 = (f32[32,128]{1,0:T(8,128)S(1)}, f32[32,128]{1,0:T(8,128)S(1)}, u32[]{:S(2)}, u32[]{:S(2)}) collective-permute-start(f32[32,128]{1,0:T(8,128)S(1)} %add_bitcast_fusion), channel_id=1, source_target_pairs={{0,0},{1,32},{2,64},{3,96},{4,128},{5,160},{6,192},{7,224},{8,16},... | collective-permute-start | bytes 49160 | tf_op jit(solution)/shard_map/ppermute | solution.py:129

commit v4 on v3

--- a/solution.py
+++ b/solution.py
@@ -11,7 +11,6 @@
 ROW_PARTS = (("z", 8), ("xl", 2), ("c", 2))
 FEAT_PARTS = (("y", 4), ("xh", 2))
 REDUCE_ORDER = ("c", "xl", "z")
-GATHER_BY_ALL_TO_ALL = True
 
 
 def axis_bit(name, bit):
@@ -56,14 +55,12 @@
     n_row = int(np.prod(row_sizes))
     steps = steps_of(row_names, row_sizes, order)
 
-    if GATHER_BY_ALL_TO_ALL:
-        copies = jnp.broadcast_to(vectors[None], (n_feat,) + vectors.shape)
-        blocks_in = lax.all_to_all(copies, feat_names, split_axis=0, concat_axis=0, tiled=True)
-    else:
-        full = lax.all_gather(vectors, feat_names, axis=1, tiled=True)
-        blocks_in = full.reshape(rows, n_feat, local).transpose(1, 0, 2)
-    columns = lax.all_to_all(rotation, feat_names, split_axis=1, concat_axis=0, tiled=True)
-    columns = columns.reshape(n_feat, local, local)
+    copies = jnp.broadcast_to(vectors[None], (n_feat,) + vectors.shape)
+    rotation_blocks = rotation.reshape(local, n_feat, local).transpose(1, 0, 2)
+    outgoing = jnp.concatenate([copies, rotation_blocks], axis=1)
+    incoming = lax.all_to_all(outgoing, feat_names, split_axis=0, concat_axis=0, tiled=True)
+    blocks_in = incoming[:, :rows]
+    columns = incoming[:, rows:]
     rotated = lax.dot_general(
         blocks_in, columns, (((0, 2), (0, 1)), ((), ())), preferred_element_type=jnp.float32
     )

time: 179 us -> 171 us (0.955)
  blocking collectives: 13.3 us -> 0 us
  waiting for transfers between devices: 93.1 us -> 97 us
  other arithmetic: 14.9 us -> 17.7 us
  local copies, waits for them, and re-layouts: 9.82 us -> 7.57 us
    all_to_all x1 -> x0, blocking collectives: 13.3 us -> none  [shards(): lax.all_to_all(rotation, feat_names, split_axis=1, concat_axis=0, tiled=T...]
    all_to_all x1, waiting for transfers between devices: 51.3 us -> 55.3 us  [shards(): lax.all_to_all(outgoing, feat_names, split_axis=0, concat_axis=0, tiled=T...]
    broadcast_in_dim x1, local copies, waits for them, and re-layouts: 4.01 us -> 0.44 us  [shards(): copies = jnp.broadcast_to(vectors[None], (n_feat,) + vectors.shape)]
    concatenate x0 -> x1, other arithmetic: none -> 2.81 us  [shards(): outgoing = jnp.concatenate([copies, rotation_blocks], axis=1)]
    unnamed x10 -> x11, local copies, waits for them, and re-layouts: 2.86 us -> 4.19 us
where the time goes in v4:
time: 171 us; the launch traced here: 170 us
  waiting for transfers between devices  97 us (57%)
  starting transfers between devices  28.5 us (17%)
  matrix products  17.9 us (10%)
  other arithmetic  17.7 us (10%)
  local copies, waits for them, and re-layouts  7.57 us (4%)
    all_to_all x1, waiting for transfers between devices, shards(): lax.all_to_all(outgoing, feat_names, split_axis=0, concat_axis=0, tiled=T...  55.3 us
    ppermute x10, waiting for transfers between devices, exchange(): return lax.ppermute(x, name, pairs)  34.6 us
    ppermute x10, starting transfers between devices, exchange(): return lax.ppermute(x, name, pairs)  16.9 us
    mul x2, other arithmetic, shards(): (codes.T[:, None, :] == kinds[None, :, None]).astype(jnp.bfloat16)  14.1 us
    dot_general x1, matrix products, shards(): lax.dot_general(recon_t, blocks_in, (((1,), (1,)), ((), ())), preferred_e...  8.68 us
    all_to_all x1, starting transfers between devices, shards(): lax.all_to_all(outgoing, feat_names, split_axis=0, concat_axis=0, tiled=T...  7.56 us
    ppermute x1, waiting for transfers between devices, shards(): grad_t = lax.ppermute(piece, row_names + feat_names, perm)  7.12 us
    dot_general x1, matrix products, shards(): both = jnp.dot(hot, rhs, preferred_element_type=jnp.float32)  5.74 us
  transfers between devices with their start and end apart: 12, of which 11 were waited for; matrix products, arithmetic and copies ran while one was open for 9% of the time, Pallas kernels for 0%

profile of v4, /device:TPU:4, one launch (start us, length us, event | category | flops | bytes accessed | tf_op | source)
XLA Modules:
  0.0 170.3 jit_solution(6498354996560499657)
XLA Ops:
  1.8 1.3 copy.12
  3.5 2.8 %pad_maximum_fusion = bf16[8,2688,128]{1,2,0:T(8,128)(2,1)} fusion(bf16[8,128,128]{1,2,0:T(8,128)(2,1)S(1)} %bitcast.72, bf16[8,2560,128]{1,2,0:T(8,128)(2,1)S(1)} %broadcast_in_dim.2), kind=kLoop, calls=%fused_computation.5 | loop fusion | flops 11010048 | bytes 11010048 | tf_op jit(solution)/shard_map/concatenate | solution.py:60
  6.3 7.6 %all-to-all-start = ((bf16[8,2688,128]{1,2,0:T(8,128)(2,1)}), bf16[8,2688,128]{1,2,0:T(8,128)(2,1)}, u32[]{:S(2)}, u32[]{:S(2)}) async-start(bf16[8,2688,128]{1,2,0:T(8,128)(2,1)} %pad_maximum_fusion), calls=%async_computation | async-start | bytes 11010048 | tf_op jit(solution)/shard_map/all_to_all | solution.py:61
  14.6 6.4 %fusion.1 = bf16[2048,2560]{1,0:T(8,128)(2,1)} fusion(s32[2048]{0:T(1024)S(1)} %bitcast.82, s32[8,2560]{1,0:T(8,128)S(1)} %bitcast.77, bf16[2560]{0:T(1024)(128)(2,1)S(1)} %fusion.22), kind=kLoop, calls=%fused_computation.4 | loop fusion | flops 10485760 | bytes 10580992 | tf_op jit(solution)/shard_map/mul | solution.py:70
  21.0 55.3 %all-to-all-done = bf16[8,2688,128]{1,2,0:T(8,128)(2,1)} async-done(((bf16[8,2688,128]{1,2,0:T(8,128)(2,1)}), bf16[8,2688,128]{1,2,0:T(8,128)(2,1)}, u32[]{:S(2)}, u32[]{:S(2)}) %all-to-all-start) | async-done | bytes 5505056 | tf_op jit(solution)/shard_map/all_to_all | solution.py:61
  76.3 3.5 %reduce-precision_convert_fusion = (bf16[2560,128]{0,1:T(8,128)(2,1)S(1)}, bf16[2560,128]{0,1:T(8,128)(2,1)S(1)}) fusion(bf16[8,2688,128]{1,2,0:T(8,128)(2,1)} %all-to-all-done), kind=kOutput, calls=%fused_computation.14 | convolution fusion | flops 672399360 | bytes 6815744 | tf_op jit(solution)/shard_map/dot_general | solution.py:64
  79.8 5.7 %fusion.10 = f32[2048,257]{0,1:T(8,128)S(1)} fusion(bf16[2048,2560]{1,0:T(8,128)(2,1)} %fusion.1, bf16[2560,1]{0,1:T(2,128)(2,1)S(1)} %compare_convert_fusion, bf16[2560,128]{0,1:T(8,128)(2,1)S(1)} %get-tuple-element.5, bf16[2560,128]{0,1:T(8,128)(2,1)S(1)} %get-tuple-element.4), kind=kOutput, calls=%fused_computation.15 | convolution fusion | flops 2698787840 | bytes 13906944 | tf_op jit(solution)/shard_map/dot_general | solution.py:76
  88.1 1.3 collective-permute-done
  90.7 4.5 %collective-permute-done.1 = f32[8,4352]{1,0:T(8,128)S(1)} collective-permute-done((f32[8,4352]{1,0:T(8,128)S(1)}, f32[8,4352]{1,0:T(8,128)S(1)}, u32[]{:S(2)}, u32[]{:S(2)}) %collective-permute-start.1) | collective-permute-done | bytes 139296 | tf_op jit(solution)/shard_map/ppermute | solution.py:31
  95.3 2.0 %collective-permute-start.2 = (f32[8,4352]{1,0:T(8,128)S(1)}, f32[8,4352]{1,0:T(8,128)S(1)}, u32[]{:S(2)}, u32[]{:S(2)}) collective-permute-start(f32[8,4352]{1,0:T(8,128)S(1)} %add.93), channel_id=1, source_target_pairs={{0,32},{32,0},{64,96},{96,64},{128,160},{160,128},{192,224},{224,1... | collective-permute-start | bytes 417800 | tf_op jit(solution)/shard_map/ppermute | solution.py:31
  97.3 3.2 %collective-permute-done.2 = f32[8,4352]{1,0:T(8,128)S(1)} collective-permute-done((f32[8,4352]{1,0:T(8,128)S(1)}, f32[8,4352]{1,0:T(8,128)S(1)}, u32[]{:S(2)}, u32[]{:S(2)}) %collective-permute-start.2) | collective-permute-done | bytes 139296 | tf_op jit(solution)/shard_map/ppermute | solution.py:31
  100.5 3.4 %collective-permute-start.3 = (f32[8,4352]{1,0:T(8,128)S(1)}, f32[8,4352]{1,0:T(8,128)S(1)}, u32[]{:S(2)}, u32[]{:S(2)}) collective-permute-start(f32[8,4352]{1,0:T(8,128)S(1)} %add.94), channel_id=1, source_target_pairs={{0,64},{32,96},{64,0},{96,32},{128,192},{160,224},{192,128},{224,1... | collective-permute-start | bytes 417800 | tf_op jit(solution)/shard_map/ppermute | solution.py:31
  103.8 5.2 %collective-permute-done.3 = f32[8,4352]{1,0:T(8,128)S(1)} collective-permute-done((f32[8,4352]{1,0:T(8,128)S(1)}, f32[8,4352]{1,0:T(8,128)S(1)}, u32[]{:S(2)}, u32[]{:S(2)}) %collective-permute-start.3) | collective-permute-done | bytes 139296 | tf_op jit(solution)/shard_map/ppermute | solution.py:31
  109.0 6.7 %collective-permute-start.4 = (f32[8,4352]{1,0:T(8,128)S(1)}, f32[8,4352]{1,0:T(8,128)S(1)}, u32[]{:S(2)}, u32[]{:S(2)}) collective-permute-start(f32[8,4352]{1,0:T(8,128)S(1)} %add.95), channel_id=1, source_target_pairs={{0,128},{32,160},{64,192},{96,224},{128,0},{160,32},{192,64},{224,... | collective-permute-start | bytes 417800 | tf_op jit(solution)/shard_map/ppermute | solution.py:31
  115.7 7.7 %fusion = bf16[8,256,2560]{2,1,0:T(8,128)(2,1)} fusion(s32[8,2560]{1,0:T(8,128)S(1)} %bitcast.78, bf16[2560]{0:T(1024)(128)(2,1)S(1)} %fusion.22), kind=kLoop, calls=%fused_computation.3 | loop fusion | flops 10485760 | bytes 10572800 | tf_op jit(solution)/shard_map/mul | solution.py:70
  124.6 8.7 %fusion.17 = f32[128,8,128]{2,0,1:T(8,128)S(1)} fusion(bf16[8,2688,128]{1,2,0:T(8,128)(2,1)} %all-to-all-done, bf16[128,2048]{1,0:T(8,128)(2,1)S(1)} %bitcast.68, bf16[2048,2560]{1,0:T(8,128)(2,1)} %bitcast.65), kind=kOutput, calls=%fused_computation.22 | convolution fusion | flops 2013724672 | bytes 16777216 | tf_op jit(solution)/shard_map/dot_general | solution.py:101
  133.4 1.5 collective-permute-done.5
  136.3 4.3 %collective-permute-done.6 = f32[8,32,128]{2,1,0:T(8,128)S(1)} collective-permute-done((f32[8,32,128]{2,1,0:T(8,128)S(1)}, f32[8,32,128]{2,1,0:T(8,128)S(1)}, u32[]{:S(2)}, u32[]{:S(2)}) %collective-permute-start.6) | collective-permute-done | bytes 131104 | tf_op jit(solution)/shard_map/ppermute | solution.py:31
  140.8 4.2 %collective-permute-done.7 = f32[4,32,128]{2,1,0:T(8,128)S(1)} collective-permute-done((f32[4,32,128]{2,1,0:T(8,128)S(1)}, f32[4,32,128]{2,1,0:T(8,128)S(1)}, u32[]{:S(2)}, u32[]{:S(2)}) %collective-permute-start.7) | collective-permute-done | bytes 65568 | tf_op jit(solution)/shard_map/ppermute | solution.py:31
  145.7 4.3 %collective-permute-done.8 = f32[2,32,128]{2,1,0:T(8,128)S(1)} collective-permute-done((f32[2,32,128]{2,1,0:T(8,128)S(1)}, f32[2,32,128]{2,1,0:T(8,128)S(1)}, u32[]{:S(2)}, u32[]{:S(2)}) %collective-permute-start.8) | collective-permute-done | bytes 32800 | tf_op jit(solution)/shard_map/ppermute | solution.py:31
  150.0 1.3 collective-permute-start.9
  151.6 6.1 %collective-permute-done.9 = f32[1,32,128]{2,1,0:T(8,128)S(1)} collective-permute-done((f32[1,32,128]{2,1,0:T(8,128)S(1)}, f32[1,32,128]{2,1,0:T(8,128)S(1)}, u32[]{:S(2)}, u32[]{:S(2)}) %collective-permute-start.9) | collective-permute-done | bytes 16416 | tf_op jit(solution)/shard_map/ppermute | solution.py:31
  157.7 4.0 %collective-permute-start.10 = (f32[32,128]{1,0:T(8,128)S(1)}, f32[32,128]{1,0:T(8,128)S(1)}, u32[]{:S(2)}, u32[]{:S(2)}) collective-permute-start(f32[32,128]{1,0:T(8,128)S(1)} %add_bitcast_fusion), channel_id=1, source_target_pairs={{0,0},{1,32},{2,64},{3,96},{4,128},{5,160},{6,192},{7,224},{8,16},... | collective-permute-start | bytes 49160 | tf_op jit(solution)/shard_map/ppermute | solution.py:126
  162.5 7.1 %collective-permute-done.10 = f32[32,128]{1,0:T(8,128)S(1)} collective-permute-done((f32[32,128]{1,0:T(8,128)S(1)}, f32[32,128]{1,0:T(8,128)S(1)}, u32[]{:S(2)}, u32[]{:S(2)}) %collective-permute-start.10) | collective-permute-done | bytes 16416 | tf_op jit(solution)/shard_map/ppermute | solution.py:126
  (54 shorter events, 10.5 us)
Async XLA Ops:
  6.3 8.3 %copy-start = (s32[2560,8]{0,1:T(8,128)S(1)}, s32[2560,8]{0,1:T(8,128)}, u32[]{:S(2)}) copy-start(s32[2560,8]{0,1:T(8,128)} %param.6) | copy-start | bytes 245764
  6.3 70.0 %all-to-all-start = ((bf16[8,2688,128]{1,2,0:T(8,128)(2,1)}), bf16[8,2688,128]{1,2,0:T(8,128)(2,1)}, u32[]{:S(2)}, u32[]{:S(2)}) async-start(bf16[8,2688,128]{1,2,0:T(8,128)(2,1)} %pad_maximum_fusion), calls=%async_computation | async-start | bytes 11010048 | tf_op jit(solution)/shard_map/all_to_all | solution.py:61
  88.0 1.4 collective-permute-start
  89.4 5.8 %collective-permute-start.1 = (f32[8,4352]{1,0:T(8,128)S(1)}, f32[8,4352]{1,0:T(8,128)S(1)}, u32[]{:S(2)}, u32[]{:S(2)}) collective-permute-start(f32[8,4352]{1,0:T(8,128)S(1)} %add.92), channel_id=1, source_target_pairs={{0,16},{16,0},{1,17},{17,1},{2,18},{18,2},{3,19},{19,3},{4,20},{20... | collective-permute-start | bytes 417800 | tf_op jit(solution)/shard_map/ppermute | solution.py:31
  95.3 5.2 %collective-permute-start.2 = (f32[8,4352]{1,0:T(8,128)S(1)}, f32[8,4352]{1,0:T(8,128)S(1)}, u32[]{:S(2)}, u32[]{:S(2)}) collective-permute-start(f32[8,4352]{1,0:T(8,128)S(1)} %add.93), channel_id=1, source_target_pairs={{0,32},{32,0},{64,96},{96,64},{128,160},{160,128},{192,224},{224,1... | collective-permute-start | bytes 417800 | tf_op jit(solution)/shard_map/ppermute | solution.py:31
  100.5 8.5 %collective-permute-start.3 = (f32[8,4352]{1,0:T(8,128)S(1)}, f32[8,4352]{1,0:T(8,128)S(1)}, u32[]{:S(2)}, u32[]{:S(2)}) collective-permute-start(f32[8,4352]{1,0:T(8,128)S(1)} %add.94), channel_id=1, source_target_pairs={{0,64},{32,96},{64,0},{96,32},{128,192},{160,224},{192,128},{224,1... | collective-permute-start | bytes 417800 | tf_op jit(solution)/shard_map/ppermute | solution.py:31
  109.0 14.4 %collective-permute-start.4 = (f32[8,4352]{1,0:T(8,128)S(1)}, f32[8,4352]{1,0:T(8,128)S(1)}, u32[]{:S(2)}, u32[]{:S(2)}) collective-permute-start(f32[8,4352]{1,0:T(8,128)S(1)} %add.95), channel_id=1, source_target_pairs={{0,128},{32,160},{64,192},{96,224},{128,0},{160,32},{192,64},{224,... | collective-permute-start | bytes 417800 | tf_op jit(solution)/shard_map/ppermute | solution.py:31
  133.3 1.6 collective-permute-start.5
  135.0 5.6 %collective-permute-start.6 = (f32[8,32,128]{2,1,0:T(8,128)S(1)}, f32[8,32,128]{2,1,0:T(8,128)S(1)}, u32[]{:S(2)}, u32[]{:S(2)}) collective-permute-start(f32[8,32,128]{2,1,0:T(8,128)S(1)} %dynamic-slice_bitcast_fusion.1), channel_id=1, source_target_pairs={{0,16},{16,0},{1,17},{17,1},{2,18},{18,2},{3,19},{19,3},{4,20},{20... | collective-permute-start | bytes 393224 | tf_op jit(solution)/shard_map/ppermute | solution.py:31
  140.7 4.4 %collective-permute-start.7 = (f32[4,32,128]{2,1,0:T(8,128)S(1)}, f32[4,32,128]{2,1,0:T(8,128)S(1)}, u32[]{:S(2)}, u32[]{:S(2)}) collective-permute-start(f32[4,32,128]{2,1,0:T(8,128)S(1)} %dynamic-slice_bitcast_fusion.2), channel_id=1, source_target_pairs={{0,32},{32,0},{64,96},{96,64},{128,160},{160,128},{192,224},{224,1... | collective-permute-start | bytes 196616 | tf_op jit(solution)/shard_map/ppermute | solution.py:31
  145.1 4.9 %collective-permute-start.8 = (f32[2,32,128]{2,1,0:T(8,128)S(1)}, f32[2,32,128]{2,1,0:T(8,128)S(1)}, u32[]{:S(2)}, u32[]{:S(2)}) collective-permute-start(f32[2,32,128]{2,1,0:T(8,128)S(1)} %dynamic-slice_bitcast_fusion.3), channel_id=1, source_target_pairs={{0,64},{32,96},{64,0},{96,32},{128,192},{160,224},{192,128},{224,1... | collective-permute-start | bytes 98312 | tf_op jit(solution)/shard_map/ppermute | solution.py:31
  150.0 7.7 %collective-permute-start.9 = (f32[1,32,128]{2,1,0:T(8,128)S(1)}, f32[1,32,128]{2,1,0:T(8,128)S(1)}, u32[]{:S(2)}, u32[]{:S(2)}) collective-permute-start(f32[1,32,128]{2,1,0:T(8,128)S(1)} %constant_dynamic-slice_fusion), channel_id=1, source_target_pairs={{0,128},{32,160},{64,192},{96,224},{128,0},{160,32},{192,64},{224,... | collective-permute-start | bytes 49160 | tf_op jit(solution)/shard_map/ppermute | solution.py:31
  157.7 11.9 %collective-permute-start.10 = (f32[32,128]{1,0:T(8,128)S(1)}, f32[32,128]{1,0:T(8,128)S(1)}, u32[]{:S(2)}, u32[]{:S(2)}) collective-permute-start(f32[32,128]{1,0:T(8,128)S(1)} %add_bitcast_fusion), channel_id=1, source_target_pairs={{0,0},{1,32},{2,64},{3,96},{4,128},{5,160},{6,192},{7,224},{8,16},... | collective-permute-start | bytes 49160 | tf_op jit(solution)/shard_map/ppermute | solution.py:126

commit v5 on v2

v5 whole, which is shorter than its diff:
```python
import functools

import jax
import jax.numpy as jnp
import numpy as np
from jax import lax
from jax.experimental import pallas as pl
from jax.sharding import Mesh
from jax.sharding import PartitionSpec as P

K = 256
DS = 16

ROW_PARTS = (("z", 8), ("xl", 2), ("c", 2))
FEAT_PARTS = (("y", 4), ("xh", 2))
REDUCE_ORDER = ("c", "xl", "z")
GROUP = 8


def axis_bit(name, bit):
    return (lax.axis_index(name) >> bit) & 1


def steps_of(row_names, row_sizes, order):
    sizes = dict(zip(row_names, row_sizes))
    out = []
    for name in order:
        for bit in range(int(sizes[name]).bit_length() - 1):
            out.append((name, bit, sizes[name]))
    return out


def exchange(x, name, bit, size):
    pairs = [(i, i ^ (1 << bit)) for i in range(size)]
    return lax.ppermute(x, name, pairs)


def row_psum(x, steps):
    for name, bit, size in steps:
        x = x + exchange(x, name, bit, size)
    return x


def row_psum_scatter(x, steps):
    for name, bit, size in steps:
        halves = x.reshape((2, x.shape[0] // 2) + x.shape[1:])
        mine = axis_bit(name, bit)
        keep = lax.dynamic_index_in_dim(halves, mine, 0, keepdims=False)
        send = lax.dynamic_index_in_dim(halves, 1 - mine, 0, keepdims=False)
        x = keep + exchange(send, name, bit, size)
    return x


def means_kernel(codes_ref, vec_ref, hi_ref, lo_ref):
    rows = codes_ref.shape[1]
    kinds = lax.broadcasted_iota(jnp.int32, (K, rows), 0)
    one = jnp.ones((K, rows), jnp.bfloat16)
    zero = jnp.zeros((K, rows), jnp.bfloat16)
    for i in range(codes_ref.shape[0]):
        hot = jnp.where(codes_ref[pl.ds(i, 1), :] == kinds, one, zero)
        h = jnp.dot(hot, vec_ref[...], preferred_element_type=jnp.float32)
        hi = h.astype(jnp.bfloat16)
        hi_ref[i] = hi
        lo_ref[i] = (h - hi.astype(jnp.float32)).astype(jnp.bfloat16)


def codeword_means(codes_all, vectors):
    m_all, rows = codes_all.shape
    width = vectors.shape[1]
    out = jax.ShapeDtypeStruct((m_all, K, width), jnp.bfloat16)
    return pl.pallas_call(
        means_kernel,
        grid=(m_all // GROUP,),
        in_specs=[
            pl.BlockSpec((GROUP, rows), lambda g: (g, 0)),
            pl.BlockSpec((rows, width), lambda g: (0, 0)),
        ],
        out_specs=[
            pl.BlockSpec((GROUP, K, width), lambda g: (g, 0, 0)),
            pl.BlockSpec((GROUP, K, width), lambda g: (g, 0, 0)),
        ],
        out_shape=[out, out],
        cost_estimate=pl.CostEstimate(
            flops=2 * m_all * K * rows * width,
            transcendentals=0,
            bytes_accessed=codes_all.size * 4 + vectors.size * 2 + 2 * m_all * K * width * 2,
        ),
    )(codes_all, vectors)


def broadcast_over(x, names, count):
    copies = jnp.broadcast_to(x[None], (count,) + x.shape)
    return lax.all_to_all(copies, names, split_axis=0, concat_axis=0, tiled=True)


def shards(vectors, rotation, codes, live_rows, *, row_names, feat_names, row_sizes, order):
    rows = vectors.shape[0]
    local = vectors.shape[1]
    groups = codes.shape[1]
    n_feat = rotation.shape[1] // local
    m_all = groups * n_feat
    n_row = int(np.prod(row_sizes))
    steps = steps_of(row_names, row_sizes, order)

    keep = jnp.arange(rows, dtype=jnp.int32) < live_rows[0]
    masked = jnp.where(keep[:, None], codes, -1).T
    codes_all = broadcast_over(masked, feat_names, n_feat).reshape(m_all, rows)

    kinds = jnp.arange(K, dtype=jnp.int32)
    counts = jnp.sum(
        (masked[:, None, :] == kinds[None, :, None]).astype(jnp.float32), axis=2
    )

    h_hi, h_lo = codeword_means(codes_all, vectors)

    rot3 = rotation.reshape(local, m_all, DS).transpose(1, 0, 2)
    dims = (((2,), (1,)), ((0,), (0,)))
    partial = lax.dot_general(h_hi, rot3, dims, preferred_element_type=jnp.float32)
    partial = partial + lax.dot_general(h_lo, rot3, dims, preferred_element_type=jnp.float32)

    partial = partial.reshape(n_feat, groups, K, DS)
    sums = jnp.sum(
        lax.all_to_all(partial, feat_names, split_axis=0, concat_axis=0, tiled=True), axis=0
    )
    packed = jnp.concatenate([sums.reshape(groups, K * DS), counts], axis=1)

    packed = row_psum(packed, steps)
    total_sums = packed[:, : K * DS].reshape(groups, K, DS)
    total_counts = packed[:, K * DS :]
    cents = total_sums / (total_counts[:, :, None] + 1.0)
    centroids_all = cents.transpose(1, 0, 2).reshape(K, groups * DS)

    row_index = lax.axis_index(row_names)
    share = K // n_row
    centroids = lax.dynamic_slice_in_dim(centroids_all, row_index * share, share, 0)

    table = broadcast_over(cents.astype(jnp.bfloat16), feat_names, n_feat)
    table = table.reshape(m_all, K, DS)
    dims = (((1,), (1,)), ((0,), (0,)))
    grad = lax.dot_general(table, h_hi, dims, preferred_element_type=jnp.float32)
    grad = grad + lax.dot_general(table, h_lo, dims, preferred_element_type=jnp.float32)
    inverse = 1.0 / (rows * n_row)
    grad = grad.reshape(m_all * DS, local) * inverse

    grad_rows = (m_all * DS) // n_row
    pieces = grad.reshape(n_row, grad_rows, local)
    position = []
    for r in range(n_row):
        coords = {}
        rest = r
        for name, size in reversed(list(zip(row_names, row_sizes))):
            coords[name] = rest % size
            rest //= size
        q = 0
        for name, bit, size in steps:
            q = q * 2 + ((coords[name] >> bit) & 1)
        position.append((q, r))
    source = np.array([r for _, r in sorted(position)], dtype=np.int32)
    pieces = pieces[source]
    grad_t = row_psum_scatter(pieces, steps)[0]
    return centroids, grad_t


def solution(mesh):
    row_size = mesh.shape["row"]
    feat_size = mesh.shape["feat"]
    row_sizes = tuple(s for _, s in ROW_PARTS)
    feat_sizes = tuple(s for _, s in FEAT_PARTS)
    if int(np.prod(row_sizes)) != row_size or int(np.prod(feat_sizes)) != feat_size:
        row_parts, feat_parts = (("row", row_size),), (("feat", feat_size),)
    else:
        row_parts, feat_parts = ROW_PARTS, FEAT_PARTS
    names = tuple(n for n, _ in row_parts + feat_parts)
    shape = tuple(s for _, s in row_parts + feat_parts)
    fine = Mesh(np.asarray(mesh.devices).reshape(shape), names)
    row_names = tuple(n for n, _ in row_parts)
    feat_names = tuple(n for n, _ in feat_parts)

    body = functools.partial(
        shards,
        row_names=row_names,
        feat_names=feat_names,
        row_sizes=tuple(s for _, s in row_parts),
        order=REDUCE_ORDER if row_parts is ROW_PARTS else row_names,
    )
    return jax.shard_map(
        body,
        mesh=fine,
        in_specs=(P(row_names, feat_names), P(feat_names, None), P(row_names, feat_names), P(row_names)),
        out_specs=(P(row_names, feat_names), P(row_names, feat_names)),
        check_vma=False,
    )
```

time: 199 us -> 153 us (0.77); the launches traced: 199 us -> 151 us
  waiting for transfers between devices: 118 us -> 58.8 us
  Pallas kernels: 0 us -> 25.4 us
  starting transfers between devices: 27.1 us -> 43.5 us
  between operations: 15 us -> 1.49 us
  other arithmetic: 15.8 us -> 4.45 us
  matrix products: 15.2 us -> 9.46 us
    all_gather x1 -> x0, waiting for transfers between devices: 74.3 us -> none  [shards(): full = lax.all_gather(vectors, feat_names, axis=1, tiled=True)]
    all_to_all x1 -> x3, waiting for transfers between devices: 0.01 us -> 27.9 us  [the longest x2 16.7 us: broadcast_over(): lax.all_to_all(copies, names, split_axis=0, concat_axis=0, tiled=True)]
    pallas_call x0 -> x1, Pallas kernels: none -> 25.4 us  [codeword_means(): pl.pallas_call(means_kernel, grid=(m_all // GROUP,), in_specs=[pl.BlockSp...]
    mul x3 -> x0, other arithmetic: 15.2 us -> none  [the longest x2 15 us: shards(): (codes.T[:, None, :] == kinds[None, :, None]).astype(jnp.bfloat16)]
    all_to_all x1 -> x3, starting transfers between devices: 7.43 us -> 19.8 us  [the longest x2 13.7 us: broadcast_over(): lax.all_to_all(copies, names, split_axis=0, concat_axis=0, tiled=True)]
    ppermute x1 -> x0, waiting for transfers between devices: 7.85 us -> none  [shards(): grad_t = lax.ppermute(piece, row_names + feat_names, perm)]
    ppermute x10, starting transfers between devices: 16.3 us -> 23.7 us  [exchange(): return lax.ppermute(x, name, pairs)]
    dot_general x3 -> x4, matrix products: 15.2 us -> 9.46 us  [the longest x1 3.53 us: shards(): lax.dot_general(h_hi, rot3, dims, preferred_element_type=jnp.float32)]
  transfers between devices with their start and end apart: 13 -> 13, of which waited for: 11 -> 13; matrix products, arithmetic and copies ran while one was open for 9% -> 3% of each run, Pallas kernels for 0% -> 0%
where the time goes in v5:
time: 153 us; the launch traced here: 151 us
  waiting for transfers between devices  58.8 us (38%)
  starting transfers between devices  43.5 us (28%)
  Pallas kernels  25.4 us (17%)
  matrix products  9.46 us (6%)
  local copies, waits for them, and re-layouts  7.49 us (5%)
  other arithmetic  4.45 us (3%)
    ppermute x10, waiting for transfers between devices, exchange(): return lax.ppermute(x, name, pairs)  30.9 us
    pallas_call x1, Pallas kernels, codeword_means(): pl.pallas_call(means_kernel, grid=(m_all // GROUP,), in_specs=[pl.BlockSp...  25.4 us
    ppermute x10, starting transfers between devices, exchange(): return lax.ppermute(x, name, pairs)  23.7 us
    all_to_all x2, waiting for transfers between devices, broadcast_over(): lax.all_to_all(copies, names, split_axis=0, concat_axis=0, tiled=True)  16.7 us
    all_to_all x2, starting transfers between devices, broadcast_over(): lax.all_to_all(copies, names, split_axis=0, concat_axis=0, tiled=True)  13.7 us
    all_to_all x1, waiting for transfers between devices, shards(): lax.all_to_all(partial, feat_names, split_axis=0, concat_axis=0, tiled=True)  11.2 us
    all_to_all x1, starting transfers between devices, shards(): lax.all_to_all(partial, feat_names, split_axis=0, concat_axis=0, tiled=True)  6.13 us
    dot_general x1, matrix products, shards(): lax.dot_general(h_hi, rot3, dims, preferred_element_type=jnp.float32)  3.53 us
  transfers between devices with their start and end apart: 13, of which 13 were waited for; matrix products, arithmetic and copies ran while one was open for 3% of the time, Pallas kernels for 0%

profile of v5, /device:TPU:4, one launch (start us, length us, event | category | flops | bytes accessed | tf_op | source)
XLA Modules:
  0.0 150.6 jit_solution(10450047018464691768)
XLA Ops:
  3.1 7.4 %all-to-all-start = ((s32[8,8,2560]{2,1,0:T(8,128)}), s32[8,8,2560]{2,1,0:T(8,128)S(1)}, u32[]{:S(2)}, u32[]{:S(2)}) async-start(s32[8,8,2560]{2,1,0:T(8,128)} %broadcast_in_dim.20), calls=%async_computation | async-start | bytes 1310720 | tf_op jit(solution)/shard_map/all_to_all | solution.py:93
  11.6 9.2 %all-to-all-done = s32[8,8,2560]{2,1,0:T(8,128)S(1)} async-done(((s32[8,8,2560]{2,1,0:T(8,128)}), s32[8,8,2560]{2,1,0:T(8,128)S(1)}, u32[]{:S(2)}, u32[]{:S(2)}) %all-to-all-start) | async-done | bytes 655392 | tf_op jit(solution)/shard_map/all_to_all | solution.py:93
  21.8 25.4 %shard_map.77 = (bf16[64,256,128]{2,1,0:T(8,128)(2,1)}, bf16[64,256,128]{2,1,0:T(8,128)(2,1)}) custom-call(s32[64,2560]{1,0:T(8,128)} %bitcast.53, bf16[2560,128]{1,0:T(8,128)(2,1)} %vec_ref.1), custom_call_target="tpu_custom_call" | custom-call | flops 10737418240 | bytes 9699328 | tf_op jit(solution)/shard_map/pallas_call | solution.py:71
  47.2 3.5 %fusion.4 = f32[64,256,16]{1,2,0:T(8,128)S(1)} fusion(bf16[64,256,128]{2,1,0:T(8,128)(2,1)} %get-tuple-element.4, bf16[64,128,16]{1,2,0:T(8,128)(2,1)S(1)} %bitcast.46), kind=kOutput, calls=%fused_computation.26 | convolution fusion | flops 67108864 | bytes 5505024 | tf_op jit(solution)/shard_map/dot_general | solution.py:118
  50.7 2.3 %convolution_add_fusion = f32[64,256,16]{1,2,0:T(8,128)} fusion(f32[64,256,16]{1,2,0:T(8,128)S(1)} %fusion.4, bf16[64,256,128]{2,1,0:T(8,128)(2,1)S(1)} %copy-done, bf16[64,128,16]{1,2,0:T(8,128)(2,1)S(1)} %bitcast.47), kind=kOutput, calls=%fused_computation.3 | convolution fusion | flops 67371008 | bytes 6553600 | tf_op jit(solution)/shard_map/dot_general | solution.py:119
  53.0 6.1 %all-to-all-start.1 = ((f32[8,8,256,16]{2,3,1,0:T(8,128)}), f32[8,8,256,16]{2,3,1,0:T(8,128)S(1)}, u32[]{:S(2)}, u32[]{:S(2)}) async-start(f32[8,8,256,16]{2,3,1,0:T(8,128)} %bitcast.6), calls=%async_computation.1 | async-start | bytes 2097152 | tf_op jit(solution)/shard_map/all_to_all | solution.py:123
  59.1 2.3 %convert_reduce_fusion = f32[8,256]{1,0:T(8,128)S(1)} fusion(s32[8,2560]{1,0:T(8,128)S(1)} %select_bitcast_fusion), kind=kLoop, calls=%fused_computation.1 | loop fusion | flops 15726592 | bytes 90112 | tf_op jit(solution)/shard_map/reduce_sum | solution.py:110
  61.5 11.2 %all-to-all-done.1 = f32[8,8,256,16]{2,3,1,0:T(8,128)S(1)} async-done(((f32[8,8,256,16]{2,3,1,0:T(8,128)}), f32[8,8,256,16]{2,3,1,0:T(8,128)S(1)}, u32[]{:S(2)}, u32[]{:S(2)}) %all-to-all-start.1) | async-done | bytes 1048608 | tf_op jit(solution)/shard_map/all_to_all | solution.py:123
  76.5 4.5 %collective-permute-done.1 = f32[8,4352]{1,0:T(8,128)S(1)} collective-permute-done((f32[8,4352]{1,0:T(8,128)S(1)}, f32[8,4352]{1,0:T(8,128)S(1)}, u32[]{:S(2)}, u32[]{:S(2)}) %collective-permute-start.1) | collective-permute-done | bytes 139296 | tf_op jit(solution)/shard_map/ppermute | solution.py:35
  81.0 2.0 %collective-permute-start.2 = (f32[8,4352]{1,0:T(8,128)S(1)}, f32[8,4352]{1,0:T(8,128)S(1)}, u32[]{:S(2)}, u32[]{:S(2)}) collective-permute-start(f32[8,4352]{1,0:T(8,128)S(1)} %add.100), channel_id=1, source_target_pairs={{0,32},{32,0},{64,96},{96,64},{128,160},{160,128},{192,224},{224,1... | collective-permute-start | bytes 417800 | tf_op jit(solution)/shard_map/ppermute | solution.py:35
  83.0 3.2 %collective-permute-done.2 = f32[8,4352]{1,0:T(8,128)S(1)} collective-permute-done((f32[8,4352]{1,0:T(8,128)S(1)}, f32[8,4352]{1,0:T(8,128)S(1)}, u32[]{:S(2)}, u32[]{:S(2)}) %collective-permute-start.2) | collective-permute-done | bytes 139296 | tf_op jit(solution)/shard_map/ppermute | solution.py:35
  86.2 3.4 %collective-permute-start.3 = (f32[8,4352]{1,0:T(8,128)S(1)}, f32[8,4352]{1,0:T(8,128)S(1)}, u32[]{:S(2)}, u32[]{:S(2)}) collective-permute-start(f32[8,4352]{1,0:T(8,128)S(1)} %add.101), channel_id=1, source_target_pairs={{0,64},{32,96},{64,0},{96,32},{128,192},{160,224},{192,128},{224,1... | collective-permute-start | bytes 417800 | tf_op jit(solution)/shard_map/ppermute | solution.py:35
  89.5 5.2 %collective-permute-done.3 = f32[8,4352]{1,0:T(8,128)S(1)} collective-permute-done((f32[8,4352]{1,0:T(8,128)S(1)}, f32[8,4352]{1,0:T(8,128)S(1)}, u32[]{:S(2)}, u32[]{:S(2)}) %collective-permute-start.3) | collective-permute-done | bytes 139296 | tf_op jit(solution)/shard_map/ppermute | solution.py:35
  94.7 6.5 %collective-permute-start.4 = (f32[8,4352]{1,0:T(8,128)S(1)}, f32[8,4352]{1,0:T(8,128)S(1)}, u32[]{:S(2)}, u32[]{:S(2)}) collective-permute-start(f32[8,4352]{1,0:T(8,128)S(1)} %add.102), channel_id=1, source_target_pairs={{0,128},{32,160},{64,192},{96,224},{128,0},{160,32},{192,64},{224,... | collective-permute-start | bytes 417800 | tf_op jit(solution)/shard_map/ppermute | solution.py:35
  101.2 3.4 %collective-permute-done.4 = f32[8,4352]{1,0:T(8,128)S(1)} collective-permute-done((f32[8,4352]{1,0:T(8,128)S(1)}, f32[8,4352]{1,0:T(8,128)S(1)}, u32[]{:S(2)}, u32[]{:S(2)}) %collective-permute-start.4) | collective-permute-done | bytes 139296 | tf_op jit(solution)/shard_map/ppermute | solution.py:35
  106.5 6.2 %all-to-all-start.2 = ((bf16[8,8,256,16]{2,3,1,0:T(8,128)(2,1)}), bf16[8,8,256,16]{2,3,1,0:T(8,128)(2,1)S(1)}, u32[]{:S(2)}, u32[]{:S(2)}) async-start(bf16[8,8,256,16]{2,3,1,0:T(8,128)(2,1)} %broadcast_in_dim.34), calls=%async_computation.2 | async-start | bytes 1048576 | tf_op jit(solution)/shard_map/all_to_all | solution.py:93
  112.7 7.5 %all-to-all-done.2 = bf16[8,8,256,16]{2,3,1,0:T(8,128)(2,1)S(1)} async-done(((bf16[8,8,256,16]{2,3,1,0:T(8,128)(2,1)}), bf16[8,8,256,16]{2,3,1,0:T(8,128)(2,1)S(1)}, u32[]{:S(2)}, u32[]{:S(2)}) %all-to-all-start.2) | async-done | bytes 524320 | tf_op jit(solution)/shard_map/all_to_all | solution.py:93
  120.3 3.0 %fusion.5 = f32[64,16,128]{2,1,0:T(8,128)S(1)} fusion(bf16[64,256,16]{1,2,0:T(8,128)(2,1)S(1)} %bitcast.44, bf16[64,256,128]{2,1,0:T(8,128)(2,1)} %get-tuple-element.4), kind=kOutput, calls=%fused_computation.27 | convolution fusion | flops 67108864 | bytes 5242880 | tf_op jit(solution)/shard_map/dot_general | solution.py:140
  128.1 4.3 %collective-permute-done.6 = f32[8,32,128]{2,1,0:T(8,128)S(1)} collective-permute-done((f32[8,32,128]{2,1,0:T(8,128)S(1)}, f32[8,32,128]{2,1,0:T(8,128)S(1)}, u32[]{:S(2)}, u32[]{:S(2)}) %collective-permute-start.6) | collective-permute-done | bytes 131104 | tf_op jit(solution)/shard_map/ppermute | solution.py:35
  132.5 4.2 %collective-permute-done.7 = f32[4,32,128]{2,1,0:T(8,128)S(1)} collective-permute-done((f32[4,32,128]{2,1,0:T(8,128)S(1)}, f32[4,32,128]{2,1,0:T(8,128)S(1)}, u32[]{:S(2)}, u32[]{:S(2)}) %collective-permute-start.7) | collective-permute-done | bytes 65568 | tf_op jit(solution)/shard_map/ppermute | solution.py:35
  136.8 3.5 %collective-permute-start.8 = (f32[2,32,128]{2,1,0:T(8,128)S(1)}, f32[2,32,128]{2,1,0:T(8,128)S(1)}, u32[]{:S(2)}, u32[]{:S(2)}) collective-permute-start(f32[2,32,128]{2,1,0:T(8,128)S(1)} %dynamic-slice_bitcast_fusion.3), channel_id=1, source_target_pairs={{0,64},{32,96},{64,0},{96,32},{128,192},{160,224},{192,128},{224,1... | collective-permute-start | bytes 98312 | tf_op jit(solution)/shard_map/ppermute | solution.py:35
  140.6 1.6 %collective-permute-done.8 = f32[2,32,128]{2,1,0:T(8,128)S(1)} collective-permute-done((f32[2,32,128]{2,1,0:T(8,128)S(1)}, f32[2,32,128]{2,1,0:T(8,128)S(1)}, u32[]{:S(2)}, u32[]{:S(2)}) %collective-permute-start.8) | collective-permute-done | bytes 32800 | tf_op jit(solution)/shard_map/ppermute | solution.py:35
  142.2 5.4 %collective-permute-start.9 = (f32[1,32,128]{2,1,0:T(8,128)S(1)}, f32[1,32,128]{2,1,0:T(8,128)S(1)}, u32[]{:S(2)}, u32[]{:S(2)}) collective-permute-start(f32[1,32,128]{2,1,0:T(8,128)S(1)} %constant_dynamic-slice_fusion), channel_id=1, source_target_pairs={{0,128},{32,160},{64,192},{96,224},{128,0},{160,32},{192,64},{224,... | collective-permute-start | bytes 49160 | tf_op jit(solution)/shard_map/ppermute | solution.py:35
  148.3 1.6 %collective-permute-done.9 = f32[1,32,128]{2,1,0:T(8,128)S(1)} collective-permute-done((f32[1,32,128]{2,1,0:T(8,128)S(1)}, f32[1,32,128]{2,1,0:T(8,128)S(1)}, u32[]{:S(2)}, u32[]{:S(2)}) %collective-permute-start.9) | collective-permute-done | bytes 16416 | tf_op jit(solution)/shard_map/ppermute | solution.py:35
  (50 shorter events, 16.0 us)
Async XLA Ops:
  3.1 17.8 %all-to-all-start = ((s32[8,8,2560]{2,1,0:T(8,128)}), s32[8,8,2560]{2,1,0:T(8,128)S(1)}, u32[]{:S(2)}, u32[]{:S(2)}) async-start(s32[8,8,2560]{2,1,0:T(8,128)} %broadcast_in_dim.20), calls=%async_computation | async-start | bytes 1310720 | tf_op jit(solution)/shard_map/all_to_all | solution.py:93
  20.8 0.9 copy-start.2
  47.2 3.5 %copy-start = (bf16[64,256,128]{2,1,0:T(8,128)(2,1)S(1)}, bf16[64,256,128]{2,1,0:T(8,128)(2,1)}, u32[]{:S(2)}) copy-start(bf16[64,256,128]{2,1,0:T(8,128)(2,1)} %get-tuple-element.5) | copy-start | bytes 12582916
  53.0 19.6 %all-to-all-start.1 = ((f32[8,8,256,16]{2,3,1,0:T(8,128)}), f32[8,8,256,16]{2,3,1,0:T(8,128)S(1)}, u32[]{:S(2)}, u32[]{:S(2)}) async-start(f32[8,8,256,16]{2,3,1,0:T(8,128)} %bitcast.6), calls=%async_computation.1 | async-start | bytes 2097152 | tf_op jit(solution)/shard_map/all_to_all | solution.py:123
  73.7 39.0 %copy-start.3 = (s32[32]{0:T(128)S(1)}, s32[32]{0:T(128)}, u32[]{:S(2)}) copy-start(s32[32]{0:T(128)} %constant.81) | copy-start | bytes 388
  73.7 1.4 collective-permute-start
  75.2 5.8 %collective-permute-start.1 = (f32[8,4352]{1,0:T(8,128)S(1)}, f32[8,4352]{1,0:T(8,128)S(1)}, u32[]{:S(2)}, u32[]{:S(2)}) collective-permute-start(f32[8,4352]{1,0:T(8,128)S(1)} %fusion.3), channel_id=1, source_target_pairs={{0,16},{16,0},{1,17},{17,1},{2,18},{18,2},{3,19},{19,3},{4,20},{20... | collective-permute-start | bytes 417800 | tf_op jit(solution)/shard_map/ppermute | solution.py:35
  81.0 5.2 %collective-permute-start.2 = (f32[8,4352]{1,0:T(8,128)S(1)}, f32[8,4352]{1,0:T(8,128)S(1)}, u32[]{:S(2)}, u32[]{:S(2)}) collective-permute-start(f32[8,4352]{1,0:T(8,128)S(1)} %add.100), channel_id=1, source_target_pairs={{0,32},{32,0},{64,96},{96,64},{128,160},{160,128},{192,224},{224,1... | collective-permute-start | bytes 417800 | tf_op jit(solution)/shard_map/ppermute | solution.py:35
  86.2 8.5 %collective-permute-start.3 = (f32[8,4352]{1,0:T(8,128)S(1)}, f32[8,4352]{1,0:T(8,128)S(1)}, u32[]{:S(2)}, u32[]{:S(2)}) collective-permute-start(f32[8,4352]{1,0:T(8,128)S(1)} %add.101), channel_id=1, source_target_pairs={{0,64},{32,96},{64,0},{96,32},{128,192},{160,224},{192,128},{224,1... | collective-permute-start | bytes 417800 | tf_op jit(solution)/shard_map/ppermute | solution.py:35
  94.7 9.9 %collective-permute-start.4 = (f32[8,4352]{1,0:T(8,128)S(1)}, f32[8,4352]{1,0:T(8,128)S(1)}, u32[]{:S(2)}, u32[]{:S(2)}) collective-permute-start(f32[8,4352]{1,0:T(8,128)S(1)} %add.102), channel_id=1, source_target_pairs={{0,128},{32,160},{64,192},{96,224},{128,0},{160,32},{192,64},{224,... | collective-permute-start | bytes 417800 | tf_op jit(solution)/shard_map/ppermute | solution.py:35
  106.5 13.8 %all-to-all-start.2 = ((bf16[8,8,256,16]{2,3,1,0:T(8,128)(2,1)}), bf16[8,8,256,16]{2,3,1,0:T(8,128)(2,1)S(1)}, u32[]{:S(2)}, u32[]{:S(2)}) async-start(bf16[8,8,256,16]{2,3,1,0:T(8,128)(2,1)} %broadcast_in_dim.34), calls=%async_computation.2 | async-start | bytes 1048576 | tf_op jit(solution)/shard_map/all_to_all | solution.py:93
  120.3 3.4 %copy-start.1 = (bf16[64,256,128]{2,1,0:T(8,128)(2,1)S(1)}, bf16[64,256,128]{2,1,0:T(8,128)(2,1)}, u32[]{:S(2)}) copy-start(bf16[64,256,128]{2,1,0:T(8,128)(2,1)} %get-tuple-element.5) | copy-start | bytes 12582916
  125.0 1.6 %collective-permute-start.5 = (f32[16,32,128]{2,1,0:T(8,128)S(1)}, f32[16,32,128]{2,1,0:T(8,128)S(1)}, u32[]{:S(2)}, u32[]{:S(2)}) collective-permute-start(f32[16,32,128]{2,1,0:T(8,128)S(1)} %dynamic-slice_bitcast_fusion), channel_id=1, source_target_pairs={{0,8},{8,0},{1,9},{9,1},{2,10},{10,2},{3,11},{11,3},{4,12},{12,4},... | collective-permute-start | bytes 786440 | tf_op jit(solution)/shard_map/ppermute | solution.py:35
  126.7 5.6 %collective-permute-start.6 = (f32[8,32,128]{2,1,0:T(8,128)S(1)}, f32[8,32,128]{2,1,0:T(8,128)S(1)}, u32[]{:S(2)}, u32[]{:S(2)}) collective-permute-start(f32[8,32,128]{2,1,0:T(8,128)S(1)} %dynamic-slice_bitcast_fusion.1), channel_id=1, source_target_pairs={{0,16},{16,0},{1,17},{17,1},{2,18},{18,2},{3,19},{19,3},{4,20},{20... | collective-permute-start | bytes 393224 | tf_op jit(solution)/shard_map/ppermute | solution.py:35
  132.4 4.4 %collective-permute-start.7 = (f32[4,32,128]{2,1,0:T(8,128)S(1)}, f32[4,32,128]{2,1,0:T(8,128)S(1)}, u32[]{:S(2)}, u32[]{:S(2)}) collective-permute-start(f32[4,32,128]{2,1,0:T(8,128)S(1)} %dynamic-slice_bitcast_fusion.2), channel_id=1, source_target_pairs={{0,32},{32,0},{64,96},{96,64},{128,160},{160,128},{192,224},{224,1... | collective-permute-start | bytes 196616 | tf_op jit(solution)/shard_map/ppermute | solution.py:35
  136.8 5.4 %collective-permute-start.8 = (f32[2,32,128]{2,1,0:T(8,128)S(1)}, f32[2,32,128]{2,1,0:T(8,128)S(1)}, u32[]{:S(2)}, u32[]{:S(2)}) collective-permute-start(f32[2,32,128]{2,1,0:T(8,128)S(1)} %dynamic-slice_bitcast_fusion.3), channel_id=1, source_target_pairs={{0,64},{32,96},{64,0},{96,32},{128,192},{160,224},{192,128},{224,1... | collective-permute-start | bytes 98312 | tf_op jit(solution)/shard_map/ppermute | solution.py:35
  142.2 7.7 %collective-permute-start.9 = (f32[1,32,128]{2,1,0:T(8,128)S(1)}, f32[1,32,128]{2,1,0:T(8,128)S(1)}, u32[]{:S(2)}, u32[]{:S(2)}) collective-permute-start(f32[1,32,128]{2,1,0:T(8,128)S(1)} %constant_dynamic-slice_fusion), channel_id=1, source_target_pairs={{0,128},{32,160},{64,192},{96,224},{128,0},{160,32},{192,64},{224,... | collective-permute-start | bytes 49160 | tf_op jit(solution)/shard_map/ppermute | solution.py:35

commit v6 on v5

--- a/solution.py
+++ b/solution.py
@@ -53,7 +53,7 @@
 
 def means_kernel(codes_ref, vec_ref, hi_ref, lo_ref):
     rows = codes_ref.shape[1]
-    kinds = lax.broadcasted_iota(jnp.int32, (K, rows), 0)
+    kinds = lax.broadcasted_iota(jnp.int32, (K, rows), 0).astype(codes_ref.dtype)
     one = jnp.ones((K, rows), jnp.bfloat16)
     zero = jnp.zeros((K, rows), jnp.bfloat16)
     for i in range(codes_ref.shape[0]):
@@ -83,7 +83,7 @@
         cost_estimate=pl.CostEstimate(
             flops=2 * m_all * K * rows * width,
             transcendentals=0,
-            bytes_accessed=codes_all.size * 4 + vectors.size * 2 + 2 * m_all * K * width * 2,
+            bytes_accessed=codes_all.size * 2 + vectors.size * 2 + 2 * m_all * K * width * 2,
         ),
     )(codes_all, vectors)
 
@@ -104,7 +104,8 @@
 
     keep = jnp.arange(rows, dtype=jnp.int32) < live_rows[0]
     masked = jnp.where(keep[:, None], codes, -1).T
-    codes_all = broadcast_over(masked, feat_names, n_feat).reshape(m_all, rows)
+    codes_all = broadcast_over(masked.astype(jnp.bfloat16), feat_names, n_feat)
+    codes_all = codes_all.reshape(m_all, rows)
 
     kinds = jnp.arange(K, dtype=jnp.int32)
     counts = jnp.sum(

time: 153 us -> 149 us (0.974)
  waiting for transfers between devices: 58.8 us -> 55.1 us
    all_to_all x2, waiting for transfers between devices: 16.7 us -> 13.2 us  [broadcast_over(): lax.all_to_all(copies, names, split_axis=0, concat_axis=0, tiled=True)]
where the time goes in v6:
time: 149 us; the launch traced here: 146 us
  waiting for transfers between devices  55.1 us (37%)
  starting transfers between devices  43.3 us (29%)
  Pallas kernels  25.4 us (17%)
  matrix products  9.45 us (6%)
  local copies, waits for them, and re-layouts  7.17 us (5%)
  other arithmetic  4.46 us (3%)
  between operations  1.49 us (1%)
    ppermute x10, waiting for transfers between devices, exchange(): return lax.ppermute(x, name, pairs)  30.9 us
    pallas_call x1, Pallas kernels, codeword_means(): pl.pallas_call(means_kernel, grid=(m_all // GROUP,), in_specs=[pl.BlockSp...  25.4 us
    ppermute x10, starting transfers between devices, exchange(): return lax.ppermute(x, name, pairs)  23.7 us
    all_to_all x2, starting transfers between devices, broadcast_over(): lax.all_to_all(copies, names, split_axis=0, concat_axis=0, tiled=True)  13.5 us
    all_to_all x2, waiting for transfers between devices, broadcast_over(): lax.all_to_all(copies, names, split_axis=0, concat_axis=0, tiled=True)  13.2 us
    all_to_all x1, waiting for transfers between devices, shards(): lax.all_to_all(partial, feat_names, split_axis=0, concat_axis=0, tiled=True)  11 us
    all_to_all x1, starting transfers between devices, shards(): lax.all_to_all(partial, feat_names, split_axis=0, concat_axis=0, tiled=True)  6.12 us
    dot_general x1, matrix products, shards(): lax.dot_general(h_hi, rot3, dims, preferred_element_type=jnp.float32)  3.53 us
  transfers between devices with their start and end apart: 13, of which 13 were waited for; matrix products, arithmetic and copies ran while one was open for 3% of the time, Pallas kernels for 0%

profile of v6, /device:TPU:4, one launch (start us, length us, event | category | flops | bytes accessed | tf_op | source)
XLA Modules:
  0.0 146.3 jit_solution(14507135382620224528)
XLA Ops:
  2.9 7.4 %all-to-all-start = ((bf16[8,8,2560]{2,1,0:T(8,128)(2,1)}), bf16[8,8,2560]{2,1,0:T(8,128)(2,1)S(1)}, u32[]{:S(2)}, u32[]{:S(2)}) async-start(bf16[8,8,2560]{2,1,0:T(8,128)(2,1)} %broadcast_in_dim.20), calls=%async_computation | async-start | bytes 655360 | tf_op jit(solution)/shard_map/all_to_all | solution.py:93
  11.5 5.7 %all-to-all-done = bf16[8,8,2560]{2,1,0:T(8,128)(2,1)S(1)} async-done(((bf16[8,8,2560]{2,1,0:T(8,128)(2,1)}), bf16[8,8,2560]{2,1,0:T(8,128)(2,1)S(1)}, u32[]{:S(2)}, u32[]{:S(2)}) %all-to-all-start) | async-done | bytes 327712 | tf_op jit(solution)/shard_map/all_to_all | solution.py:93
  17.9 25.4 %shard_map.77 = (bf16[64,256,128]{2,1,0:T(8,128)(2,1)}, bf16[64,256,128]{2,1,0:T(8,128)(2,1)}) custom-call(bf16[64,2560]{1,0:T(8,128)(2,1)} %bitcast.56, bf16[2560,128]{1,0:T(8,128)(2,1)} %vec_ref.1), custom_call_target="tpu_custom_call" | custom-call | flops 10737418240 | bytes 9371648 | tf_op jit(solution)/shard_map/pallas_call | solution.py:71
  43.3 3.5 %fusion.5 = f32[64,256,16]{1,2,0:T(8,128)S(1)} fusion(bf16[64,256,128]{2,1,0:T(8,128)(2,1)} %get-tuple-element.4, bf16[64,128,16]{1,2,0:T(8,128)(2,1)S(1)} %bitcast.47), kind=kOutput, calls=%fused_computation.27 | convolution fusion | flops 67108864 | bytes 5505024 | tf_op jit(solution)/shard_map/dot_general | solution.py:119
  46.8 2.3 %convolution_add_fusion = f32[64,256,16]{1,2,0:T(8,128)} fusion(f32[64,256,16]{1,2,0:T(8,128)S(1)} %fusion.5, bf16[64,256,128]{2,1,0:T(8,128)(2,1)S(1)} %copy-done, bf16[64,128,16]{1,2,0:T(8,128)(2,1)S(1)} %bitcast.48), kind=kOutput, calls=%fused_computation.3 | convolution fusion | flops 67371008 | bytes 6553600 | tf_op jit(solution)/shard_map/dot_general | solution.py:120
  49.1 6.1 %all-to-all-start.1 = ((f32[8,8,256,16]{2,3,1,0:T(8,128)}), f32[8,8,256,16]{2,3,1,0:T(8,128)S(1)}, u32[]{:S(2)}, u32[]{:S(2)}) async-start(f32[8,8,256,16]{2,3,1,0:T(8,128)} %bitcast.6), calls=%async_computation.1 | async-start | bytes 2097152 | tf_op jit(solution)/shard_map/all_to_all | solution.py:124
  55.2 2.3 %convert_reduce_fusion = f32[8,256]{1,0:T(8,128)S(1)} fusion(s32[8,2560]{1,0:T(8,128)S(1)} %get-tuple-element.15), kind=kLoop, calls=%fused_computation.1 | loop fusion | flops 15726592 | bytes 90112 | tf_op jit(solution)/shard_map/reduce_sum | solution.py:111
  57.5 11.0 %all-to-all-done.1 = f32[8,8,256,16]{2,3,1,0:T(8,128)S(1)} async-done(((f32[8,8,256,16]{2,3,1,0:T(8,128)}), f32[8,8,256,16]{2,3,1,0:T(8,128)S(1)}, u32[]{:S(2)}, u32[]{:S(2)}) %all-to-all-start.1) | async-done | bytes 1048608 | tf_op jit(solution)/shard_map/all_to_all | solution.py:124
  72.4 4.5 %collective-permute-done.1 = f32[8,4352]{1,0:T(8,128)S(1)} collective-permute-done((f32[8,4352]{1,0:T(8,128)S(1)}, f32[8,4352]{1,0:T(8,128)S(1)}, u32[]{:S(2)}, u32[]{:S(2)}) %collective-permute-start.1) | collective-permute-done | bytes 139296 | tf_op jit(solution)/shard_map/ppermute | solution.py:35
  76.9 2.0 %collective-permute-start.2 = (f32[8,4352]{1,0:T(8,128)S(1)}, f32[8,4352]{1,0:T(8,128)S(1)}, u32[]{:S(2)}, u32[]{:S(2)}) collective-permute-start(f32[8,4352]{1,0:T(8,128)S(1)} %add.100), channel_id=1, source_target_pairs={{0,32},{32,0},{64,96},{96,64},{128,160},{160,128},{192,224},{224,1... | collective-permute-start | bytes 417800 | tf_op jit(solution)/shard_map/ppermute | solution.py:35
  78.9 3.2 %collective-permute-done.2 = f32[8,4352]{1,0:T(8,128)S(1)} collective-permute-done((f32[8,4352]{1,0:T(8,128)S(1)}, f32[8,4352]{1,0:T(8,128)S(1)}, u32[]{:S(2)}, u32[]{:S(2)}) %collective-permute-start.2) | collective-permute-done | bytes 139296 | tf_op jit(solution)/shard_map/ppermute | solution.py:35
  82.1 3.4 %collective-permute-start.3 = (f32[8,4352]{1,0:T(8,128)S(1)}, f32[8,4352]{1,0:T(8,128)S(1)}, u32[]{:S(2)}, u32[]{:S(2)}) collective-permute-start(f32[8,4352]{1,0:T(8,128)S(1)} %add.101), channel_id=1, source_target_pairs={{0,64},{32,96},{64,0},{96,32},{128,192},{160,224},{192,128},{224,1... | collective-permute-start | bytes 417800 | tf_op jit(solution)/shard_map/ppermute | solution.py:35
  85.5 5.2 %collective-permute-done.3 = f32[8,4352]{1,0:T(8,128)S(1)} collective-permute-done((f32[8,4352]{1,0:T(8,128)S(1)}, f32[8,4352]{1,0:T(8,128)S(1)}, u32[]{:S(2)}, u32[]{:S(2)}) %collective-permute-start.3) | collective-permute-done | bytes 139296 | tf_op jit(solution)/shard_map/ppermute | solution.py:35
  90.7 6.5 %collective-permute-start.4 = (f32[8,4352]{1,0:T(8,128)S(1)}, f32[8,4352]{1,0:T(8,128)S(1)}, u32[]{:S(2)}, u32[]{:S(2)}) collective-permute-start(f32[8,4352]{1,0:T(8,128)S(1)} %add.102), channel_id=1, source_target_pairs={{0,128},{32,160},{64,192},{96,224},{128,0},{160,32},{192,64},{224,... | collective-permute-start | bytes 417800 | tf_op jit(solution)/shard_map/ppermute | solution.py:35
  97.2 3.4 %collective-permute-done.4 = f32[8,4352]{1,0:T(8,128)S(1)} collective-permute-done((f32[8,4352]{1,0:T(8,128)S(1)}, f32[8,4352]{1,0:T(8,128)S(1)}, u32[]{:S(2)}, u32[]{:S(2)}) %collective-permute-start.4) | collective-permute-done | bytes 139296 | tf_op jit(solution)/shard_map/ppermute | solution.py:35
  102.4 6.1 %all-to-all-start.2 = ((bf16[8,8,256,16]{2,3,1,0:T(8,128)(2,1)}), bf16[8,8,256,16]{2,3,1,0:T(8,128)(2,1)S(1)}, u32[]{:S(2)}, u32[]{:S(2)}) async-start(bf16[8,8,256,16]{2,3,1,0:T(8,128)(2,1)} %broadcast_in_dim.34), calls=%async_computation.2 | async-start | bytes 1048576 | tf_op jit(solution)/shard_map/all_to_all | solution.py:93
  108.5 7.5 %all-to-all-done.2 = bf16[8,8,256,16]{2,3,1,0:T(8,128)(2,1)S(1)} async-done(((bf16[8,8,256,16]{2,3,1,0:T(8,128)(2,1)}), bf16[8,8,256,16]{2,3,1,0:T(8,128)(2,1)S(1)}, u32[]{:S(2)}, u32[]{:S(2)}) %all-to-all-start.2) | async-done | bytes 524320 | tf_op jit(solution)/shard_map/all_to_all | solution.py:93
  116.1 3.0 %fusion.6 = f32[64,16,128]{2,1,0:T(8,128)S(1)} fusion(bf16[64,256,16]{1,2,0:T(8,128)(2,1)S(1)} %bitcast.45, bf16[64,256,128]{2,1,0:T(8,128)(2,1)} %get-tuple-element.4), kind=kOutput, calls=%fused_computation.28 | convolution fusion | flops 67108864 | bytes 5242880 | tf_op jit(solution)/shard_map/dot_general | solution.py:141
  123.8 4.3 %collective-permute-done.6 = f32[8,32,128]{2,1,0:T(8,128)S(1)} collective-permute-done((f32[8,32,128]{2,1,0:T(8,128)S(1)}, f32[8,32,128]{2,1,0:T(8,128)S(1)}, u32[]{:S(2)}, u32[]{:S(2)}) %collective-permute-start.6) | collective-permute-done | bytes 131104 | tf_op jit(solution)/shard_map/ppermute | solution.py:35
  128.3 4.2 %collective-permute-done.7 = f32[4,32,128]{2,1,0:T(8,128)S(1)} collective-permute-done((f32[4,32,128]{2,1,0:T(8,128)S(1)}, f32[4,32,128]{2,1,0:T(8,128)S(1)}, u32[]{:S(2)}, u32[]{:S(2)}) %collective-permute-start.7) | collective-permute-done | bytes 65568 | tf_op jit(solution)/shard_map/ppermute | solution.py:35
  132.6 3.5 %collective-permute-start.8 = (f32[2,32,128]{2,1,0:T(8,128)S(1)}, f32[2,32,128]{2,1,0:T(8,128)S(1)}, u32[]{:S(2)}, u32[]{:S(2)}) collective-permute-start(f32[2,32,128]{2,1,0:T(8,128)S(1)} %dynamic-slice_bitcast_fusion.3), channel_id=1, source_target_pairs={{0,64},{32,96},{64,0},{96,32},{128,192},{160,224},{192,128},{224,1... | collective-permute-start | bytes 98312 | tf_op jit(solution)/shard_map/ppermute | solution.py:35
  136.4 1.6 %collective-permute-done.8 = f32[2,32,128]{2,1,0:T(8,128)S(1)} collective-permute-done((f32[2,32,128]{2,1,0:T(8,128)S(1)}, f32[2,32,128]{2,1,0:T(8,128)S(1)}, u32[]{:S(2)}, u32[]{:S(2)}) %collective-permute-start.8) | collective-permute-done | bytes 32800 | tf_op jit(solution)/shard_map/ppermute | solution.py:35
  138.0 5.4 %collective-permute-start.9 = (f32[1,32,128]{2,1,0:T(8,128)S(1)}, f32[1,32,128]{2,1,0:T(8,128)S(1)}, u32[]{:S(2)}, u32[]{:S(2)}) collective-permute-start(f32[1,32,128]{2,1,0:T(8,128)S(1)} %constant_dynamic-slice_fusion), channel_id=1, source_target_pairs={{0,128},{32,160},{64,192},{96,224},{128,0},{160,32},{192,64},{224,... | collective-permute-start | bytes 49160 | tf_op jit(solution)/shard_map/ppermute | solution.py:35
  144.1 1.6 %collective-permute-done.9 = f32[1,32,128]{2,1,0:T(8,128)S(1)} collective-permute-done((f32[1,32,128]{2,1,0:T(8,128)S(1)}, f32[1,32,128]{2,1,0:T(8,128)S(1)}, u32[]{:S(2)}, u32[]{:S(2)}) %collective-permute-start.9) | collective-permute-done | bytes 16416 | tf_op jit(solution)/shard_map/ppermute | solution.py:35
  (50 shorter events, 15.7 us)
Async XLA Ops:
  2.9 14.2 %all-to-all-start = ((bf16[8,8,2560]{2,1,0:T(8,128)(2,1)}), bf16[8,8,2560]{2,1,0:T(8,128)(2,1)S(1)}, u32[]{:S(2)}, u32[]{:S(2)}) async-start(bf16[8,8,2560]{2,1,0:T(8,128)(2,1)} %broadcast_in_dim.20), calls=%async_computation | async-start | bytes 655360 | tf_op jit(solution)/shard_map/all_to_all | solution.py:93
  17.2 0.7 copy-start.2
  43.3 3.5 %copy-start = (bf16[64,256,128]{2,1,0:T(8,128)(2,1)S(1)}, bf16[64,256,128]{2,1,0:T(8,128)(2,1)}, u32[]{:S(2)}) copy-start(bf16[64,256,128]{2,1,0:T(8,128)(2,1)} %get-tuple-element.5) | copy-start | bytes 12582916
  49.1 19.5 %all-to-all-start.1 = ((f32[8,8,256,16]{2,3,1,0:T(8,128)}), f32[8,8,256,16]{2,3,1,0:T(8,128)S(1)}, u32[]{:S(2)}, u32[]{:S(2)}) async-start(f32[8,8,256,16]{2,3,1,0:T(8,128)} %bitcast.6), calls=%async_computation.1 | async-start | bytes 2097152 | tf_op jit(solution)/shard_map/all_to_all | solution.py:124
  69.6 38.9 %copy-start.3 = (s32[32]{0:T(128)S(1)}, s32[32]{0:T(128)}, u32[]{:S(2)}) copy-start(s32[32]{0:T(128)} %constant.81) | copy-start | bytes 388
  69.6 1.4 collective-permute-start
  71.1 5.8 %collective-permute-start.1 = (f32[8,4352]{1,0:T(8,128)S(1)}, f32[8,4352]{1,0:T(8,128)S(1)}, u32[]{:S(2)}, u32[]{:S(2)}) collective-permute-start(f32[8,4352]{1,0:T(8,128)S(1)} %fusion.3), channel_id=1, source_target_pairs={{0,16},{16,0},{1,17},{17,1},{2,18},{18,2},{3,19},{19,3},{4,20},{20... | collective-permute-start | bytes 417800 | tf_op jit(solution)/shard_map/ppermute | solution.py:35
  76.9 5.2 %collective-permute-start.2 = (f32[8,4352]{1,0:T(8,128)S(1)}, f32[8,4352]{1,0:T(8,128)S(1)}, u32[]{:S(2)}, u32[]{:S(2)}) collective-permute-start(f32[8,4352]{1,0:T(8,128)S(1)} %add.100), channel_id=1, source_target_pairs={{0,32},{32,0},{64,96},{96,64},{128,160},{160,128},{192,224},{224,1... | collective-permute-start | bytes 417800 | tf_op jit(solution)/shard_map/ppermute | solution.py:35
  82.1 8.5 %collective-permute-start.3 = (f32[8,4352]{1,0:T(8,128)S(1)}, f32[8,4352]{1,0:T(8,128)S(1)}, u32[]{:S(2)}, u32[]{:S(2)}) collective-permute-start(f32[8,4352]{1,0:T(8,128)S(1)} %add.101), channel_id=1, source_target_pairs={{0,64},{32,96},{64,0},{96,32},{128,192},{160,224},{192,128},{224,1... | collective-permute-start | bytes 417800 | tf_op jit(solution)/shard_map/ppermute | solution.py:35
  90.7 9.9 %collective-permute-start.4 = (f32[8,4352]{1,0:T(8,128)S(1)}, f32[8,4352]{1,0:T(8,128)S(1)}, u32[]{:S(2)}, u32[]{:S(2)}) collective-permute-start(f32[8,4352]{1,0:T(8,128)S(1)} %add.102), channel_id=1, source_target_pairs={{0,128},{32,160},{64,192},{96,224},{128,0},{160,32},{192,64},{224,... | collective-permute-start | bytes 417800 | tf_op jit(solution)/shard_map/ppermute | solution.py:35
  102.4 13.6 %all-to-all-start.2 = ((bf16[8,8,256,16]{2,3,1,0:T(8,128)(2,1)}), bf16[8,8,256,16]{2,3,1,0:T(8,128)(2,1)S(1)}, u32[]{:S(2)}, u32[]{:S(2)}) async-start(bf16[8,8,256,16]{2,3,1,0:T(8,128)(2,1)} %broadcast_in_dim.34), calls=%async_computation.2 | async-start | bytes 1048576 | tf_op jit(solution)/shard_map/all_to_all | solution.py:93
  116.1 3.4 %copy-start.1 = (bf16[64,256,128]{2,1,0:T(8,128)(2,1)S(1)}, bf16[64,256,128]{2,1,0:T(8,128)(2,1)}, u32[]{:S(2)}) copy-start(bf16[64,256,128]{2,1,0:T(8,128)(2,1)} %get-tuple-element.5) | copy-start | bytes 12582916
  120.8 1.6 %collective-permute-start.5 = (f32[16,32,128]{2,1,0:T(8,128)S(1)}, f32[16,32,128]{2,1,0:T(8,128)S(1)}, u32[]{:S(2)}, u32[]{:S(2)}) collective-permute-start(f32[16,32,128]{2,1,0:T(8,128)S(1)} %dynamic-slice_bitcast_fusion), channel_id=1, source_target_pairs={{0,8},{8,0},{1,9},{9,1},{2,10},{10,2},{3,11},{11,3},{4,12},{12,4},... | collective-permute-start | bytes 786440 | tf_op jit(solution)/shard_map/ppermute | solution.py:35
  122.5 5.6 %collective-permute-start.6 = (f32[8,32,128]{2,1,0:T(8,128)S(1)}, f32[8,32,128]{2,1,0:T(8,128)S(1)}, u32[]{:S(2)}, u32[]{:S(2)}) collective-permute-start(f32[8,32,128]{2,1,0:T(8,128)S(1)} %dynamic-slice_bitcast_fusion.1), channel_id=1, source_target_pairs={{0,16},{16,0},{1,17},{17,1},{2,18},{18,2},{3,19},{19,3},{4,20},{20... | collective-permute-start | bytes 393224 | tf_op jit(solution)/shard_map/ppermute | solution.py:35
  128.2 4.4 %collective-permute-start.7 = (f32[4,32,128]{2,1,0:T(8,128)S(1)}, f32[4,32,128]{2,1,0:T(8,128)S(1)}, u32[]{:S(2)}, u32[]{:S(2)}) collective-permute-start(f32[4,32,128]{2,1,0:T(8,128)S(1)} %dynamic-slice_bitcast_fusion.2), channel_id=1, source_target_pairs={{0,32},{32,0},{64,96},{96,64},{128,160},{160,128},{192,224},{224,1... | collective-permute-start | bytes 196616 | tf_op jit(solution)/shard_map/ppermute | solution.py:35
  132.6 5.4 %collective-permute-start.8 = (f32[2,32,128]{2,1,0:T(8,128)S(1)}, f32[2,32,128]{2,1,0:T(8,128)S(1)}, u32[]{:S(2)}, u32[]{:S(2)}) collective-permute-start(f32[2,32,128]{2,1,0:T(8,128)S(1)} %dynamic-slice_bitcast_fusion.3), channel_id=1, source_target_pairs={{0,64},{32,96},{64,0},{96,32},{128,192},{160,224},{192,128},{224,1... | collective-permute-start | bytes 98312 | tf_op jit(solution)/shard_map/ppermute | solution.py:35
  138.0 7.7 %collective-permute-start.9 = (f32[1,32,128]{2,1,0:T(8,128)S(1)}, f32[1,32,128]{2,1,0:T(8,128)S(1)}, u32[]{:S(2)}, u32[]{:S(2)}) collective-permute-start(f32[1,32,128]{2,1,0:T(8,128)S(1)} %constant_dynamic-slice_fusion), channel_id=1, source_target_pairs={{0,128},{32,160},{64,192},{96,224},{128,0},{160,32},{192,64},{224,... | collective-permute-start | bytes 49160 | tf_op jit(solution)/shard_map/ppermute | solution.py:35

commit v7 on v6

--- a/solution.py
+++ b/solution.py
@@ -14,6 +14,7 @@
 ROW_PARTS = (("z", 8), ("xl", 2), ("c", 2))
 FEAT_PARTS = (("y", 4), ("xh", 2))
 REDUCE_ORDER = ("c", "xl", "z")
+RING = ("z", 8)
 GROUP = 8
 
 
@@ -49,6 +50,25 @@
         send = lax.dynamic_index_in_dim(halves, 1 - mine, 0, keepdims=False)
         x = keep + exchange(send, name, bit, size)
     return x
+
+
+def ring_scatter(x, name, size):
+    me = lax.axis_index(name)
+    total = lax.dynamic_index_in_dim(x, me, 0, keepdims=False)
+    for shift in range(1, size):
+        part = lax.dynamic_index_in_dim(x, (me + shift) % size, 0, keepdims=False)
+        total = total + lax.ppermute(part, name, [(i, (i + shift) % size) for i in range(size)])
+    return total
+
+
+def ring_gather(y, name, size):
+    me = lax.axis_index(name)
+    out = jnp.zeros((size,) + y.shape, y.dtype)
+    out = lax.dynamic_update_index_in_dim(out, y, me, 0)
+    for shift in range(1, size):
+        got = lax.ppermute(y, name, [(i, (i + shift) % size) for i in range(size)])
+        out = lax.dynamic_update_index_in_dim(out, got, (me - shift) % size, 0)
+    return out
 
 
 def means_kernel(codes_ref, vec_ref, hi_ref, lo_ref):
@@ -93,7 +113,7 @@
     return lax.all_to_all(copies, names, split_axis=0, concat_axis=0, tiled=True)
 
 
-def shards(vectors, rotation, codes, live_rows, *, row_names, feat_names, row_sizes, order):
+def shards(vectors, rotation, codes, live_rows, *, row_names, feat_names, row_sizes, order, ring):
     rows = vectors.shape[0]
     local = vectors.shape[1]
     groups = codes.shape[1]
@@ -123,11 +143,22 @@
     sums = jnp.sum(
         lax.all_to_all(partial, feat_names, split_axis=0, concat_axis=0, tiled=True), axis=0
     )
-    packed = jnp.concatenate([sums.reshape(groups, K * DS), counts], axis=1)
-
-    packed = row_psum(packed, steps)
-    total_sums = packed[:, : K * DS].reshape(groups, K, DS)
-    total_counts = packed[:, K * DS :]
+    width = groups * DS
+    packed = jnp.concatenate(
+        [sums.transpose(1, 0, 2).reshape(K, width), counts.T], axis=1
+    )
+
+    if ring is None:
+        packed = row_psum(packed, steps)
+    else:
+        ring_name, ring_size = ring
+        pair_steps = [st for st in steps if st[0] != ring_name]
+        packed = row_psum(packed[None], pair_steps[:1])[0]
+        part = ring_scatter(packed.reshape((ring_size, K // ring_size) + packed.shape[1:]), ring_name, ring_size)
+        part = row_psum(part, pair_steps[1:])
+        packed = ring_gather(part, ring_name, ring_size).reshape(packed.shape)
+    total_sums = packed[:, :width].reshape(K, groups, DS).transpose(1, 0, 2)
+    total_counts = packed[:, width:].T
     cents = total_sums / (total_counts[:, :, None] + 1.0)
     centroids_all = cents.transpose(1, 0, 2).reshape(K, groups * DS)
 
@@ -145,6 +176,18 @@
 
     grad_rows = (m_all * DS) // n_row
     pieces = grad.reshape(n_row, grad_rows, local)
+    if ring is not None:
+        ring_name, ring_size = ring
+        pair_steps = [st for st in steps if st[0] != ring_name]
+        names_sizes = list(zip(row_names, row_sizes))
+        axes_order = [i for i, (n, _) in enumerate(names_sizes) if n != ring_name]
+        axes_order = axes_order[::-1] + [i for i, (n, _) in enumerate(names_sizes) if n == ring_name]
+        grid = pieces.reshape(tuple(sz for _, sz in names_sizes) + (grad_rows, local))
+        grid = grid.transpose(tuple(axes_order) + (len(names_sizes), len(names_sizes) + 1))
+        pieces = grid.reshape(n_row, grad_rows, local)
+        part = row_psum_scatter(pieces, pair_steps)
+        grad_t = ring_scatter(part, ring_name, ring_size)
+        return centroids, grad_t
     position = []
     for r in range(n_row):
         coords = {}
@@ -183,6 +226,7 @@
         feat_names=feat_names,
         row_sizes=tuple(s for _, s in row_parts),
         order=REDUCE_ORDER if row_parts is ROW_PARTS else row_names,
+        ring=RING if row_parts is ROW_PARTS else None,
     )
     return jax.shard_map(
         body,

time: 149 us -> 158 us (1.060)
  starting transfers between devices: 43.3 us -> 68.1 us
  waiting for transfers between devices: 55.1 us -> 42.3 us
  local copies, waits for them, and re-layouts: 7.17 us -> 4.7 us
    ppermute x0 -> x21, starting transfers between devices: none -> 45.6 us  [the longest x14 32.8 us: ring_scatter(): lax.ppermute(part, name, [(i, (i + shift) % size) for i in range(size)])]
    ppermute x10 -> x4, waiting for transfers between devices: 30.9 us -> 9.71 us  [exchange(): return lax.ppermute(x, name, pairs)]
    ppermute x10 -> x4, starting transfers between devices: 23.7 us -> 2.8 us  [exchange(): return lax.ppermute(x, name, pairs)]
    ppermute x0 -> x21, waiting for transfers between devices: none -> 8.3 us  [the longest x14 4.96 us: ring_scatter(): lax.ppermute(part, name, [(i, (i + shift) % size) for i in range(size)])]
  transfers between devices with their start and end apart: 13 -> 28, of which waited for: 13 -> 13; matrix products, arithmetic and copies ran while one was open for 3% -> 3% of each run, Pallas kernels for 0% -> 0%
where the time goes in v7:
time: 158 us; the launch traced here: 156 us
  starting transfers between devices  68.1 us (43%)
  waiting for transfers between devices  42.3 us (27%)
  Pallas kernels  25.4 us (16%)
  matrix products  9.43 us (6%)
  local copies, waits for them, and re-layouts  4.7 us (3%)
  other arithmetic  4.69 us (3%)
  between operations  1.77 us (1%)
    ppermute x14, starting transfers between devices, ring_scatter(): lax.ppermute(part, name, [(i, (i + shift) % size) for i in range(size)])  32.8 us
    pallas_call x1, Pallas kernels, codeword_means(): pl.pallas_call(means_kernel, grid=(m_all // GROUP,), in_specs=[pl.BlockSp...  25.4 us
    all_to_all x2, starting transfers between devices, broadcast_over(): lax.all_to_all(copies, names, split_axis=0, concat_axis=0, tiled=True)  13.5 us
    all_to_all x2, waiting for transfers between devices, broadcast_over(): lax.all_to_all(copies, names, split_axis=0, concat_axis=0, tiled=True)  13.2 us
    ppermute x7, starting transfers between devices, ring_gather(): got = lax.ppermute(y, name, [(i, (i + shift) % size) for i in range(size)])  12.9 us
    all_to_all x1, waiting for transfers between devices, shards(): lax.all_to_all(partial, feat_names, split_axis=0, concat_axis=0, tiled=True)  11 us
    ppermute x4, waiting for transfers between devices, exchange(): return lax.ppermute(x, name, pairs)  9.71 us
    all_to_all x1, starting transfers between devices, shards(): lax.all_to_all(partial, feat_names, split_axis=0, concat_axis=0, tiled=True)  6.13 us
  transfers between devices with their start and end apart: 28, of which 13 were waited for; matrix products, arithmetic and copies ran while one was open for 3% of the time, Pallas kernels for 0%

profile of v7, /device:TPU:4, one launch (start us, length us, event | category | flops | bytes accessed | tf_op | source)
XLA Modules:
  0.0 156.3 jit_solution(3103589114428862345)
XLA Ops:
  3.0 7.4 %all-to-all-start = ((bf16[8,8,2560]{2,1,0:T(8,128)(2,1)}), bf16[8,8,2560]{2,1,0:T(8,128)(2,1)S(1)}, u32[]{:S(2)}, u32[]{:S(2)}) async-start(bf16[8,8,2560]{2,1,0:T(8,128)(2,1)} %broadcast_in_dim.62), calls=%async_computation | async-start | bytes 655360 | tf_op jit(solution)/shard_map/all_to_all | solution.py:113
  11.5 5.7 %all-to-all-done = bf16[8,8,2560]{2,1,0:T(8,128)(2,1)S(1)} async-done(((bf16[8,8,2560]{2,1,0:T(8,128)(2,1)}), bf16[8,8,2560]{2,1,0:T(8,128)(2,1)S(1)}, u32[]{:S(2)}, u32[]{:S(2)}) %all-to-all-start) | async-done | bytes 327712 | tf_op jit(solution)/shard_map/all_to_all | solution.py:113
  18.0 25.4 %shard_map.59 = (bf16[64,256,128]{2,1,0:T(8,128)(2,1)}, bf16[64,256,128]{2,1,0:T(8,128)(2,1)}) custom-call(bf16[64,2560]{1,0:T(8,128)(2,1)} %bitcast.136, bf16[2560,128]{1,0:T(8,128)(2,1)} %vec_ref.1), custom_call_target="tpu_custom_call" | custom-call | flops 10737418240 | bytes 9371648 | tf_op jit(solution)/shard_map/pallas_call | solution.py:91
  43.4 3.5 %fusion.17 = f32[64,256,16]{1,2,0:T(8,128)S(1)} fusion(bf16[64,256,128]{2,1,0:T(8,128)(2,1)} %get-tuple-element.4, bf16[64,128,16]{1,2,0:T(8,128)(2,1)S(1)} %bitcast.122), kind=kOutput, calls=%fused_computation.56 | convolution fusion | flops 67108864 | bytes 5505024 | tf_op jit(solution)/shard_map/dot_general | solution.py:139
  46.9 2.3 %convolution_add_fusion = f32[64,256,16]{1,2,0:T(8,128)} fusion(f32[64,256,16]{1,2,0:T(8,128)S(1)} %fusion.17, bf16[64,256,128]{2,1,0:T(8,128)(2,1)S(1)} %copy-done, bf16[64,128,16]{1,2,0:T(8,128)(2,1)S(1)} %bitcast.123), kind=kOutput, calls=%fused_computation.2 | convolution fusion | flops 67371008 | bytes 6553600 | tf_op jit(solution)/shard_map/dot_general | solution.py:140
  49.2 6.1 %all-to-all-start.1 = ((f32[8,8,256,16]{2,3,1,0:T(8,128)}), f32[8,8,256,16]{2,3,1,0:T(8,128)S(1)}, u32[]{:S(2)}, u32[]{:S(2)}) async-start(f32[8,8,256,16]{2,3,1,0:T(8,128)} %bitcast.6), calls=%async_computation.1 | async-start | bytes 2097152 | tf_op jit(solution)/shard_map/all_to_all | solution.py:144
  55.3 2.3 %convert_reduce_fusion = f32[8,256]{1,0:T(8,128)S(1)} fusion(s32[8,2560]{1,0:T(8,128)S(1)} %get-tuple-element.11), kind=kLoop, calls=%fused_computation | loop fusion | flops 15726592 | bytes 90112 | tf_op jit(solution)/shard_map/reduce_sum | solution.py:131
  57.6 11.0 %all-to-all-done.1 = f32[8,8,256,16]{2,3,1,0:T(8,128)S(1)} async-done(((f32[8,8,256,16]{2,3,1,0:T(8,128)}), f32[8,8,256,16]{2,3,1,0:T(8,128)S(1)}, u32[]{:S(2)}, u32[]{:S(2)}) %all-to-all-start.1) | async-done | bytes 1048608 | tf_op jit(solution)/shard_map/all_to_all | solution.py:144
  72.4 3.3 %collective-permute-start.2 = (f32[32,136]{1,0:T(8,128)S(1)}, f32[32,136]{1,0:T(8,128)S(1)}, u32[]{:S(2)}, u32[]{:S(2)}) collective-permute-start(f32[32,136]{1,0:T(8,128)S(1)} %get-tuple-element.20), channel_id=1, source_target_pairs={{0,64},{32,96},{64,128},{96,160},{128,192},{160,224},{192,0},{224,... | collective-permute-start | bytes 52232 | tf_op jit(solution)/shard_map/ppermute | solution.py:60
  75.7 4.0 %collective-permute-start.3 = (f32[32,136]{1,0:T(8,128)S(1)}, f32[32,136]{1,0:T(8,128)S(1)}, u32[]{:S(2)}, u32[]{:S(2)}) collective-permute-start(f32[32,136]{1,0:T(8,128)S(1)} %get-tuple-element.19), channel_id=1, source_target_pairs={{0,96},{32,128},{64,160},{96,192},{128,224},{160,0},{192,32},{224,... | collective-permute-start | bytes 52232 | tf_op jit(solution)/shard_map/ppermute | solution.py:60
  80.2 4.9 %collective-permute-start.5 = (f32[32,136]{1,0:T(8,128)S(1)}, f32[32,136]{1,0:T(8,128)S(1)}, u32[]{:S(2)}, u32[]{:S(2)}) collective-permute-start(f32[32,136]{1,0:T(8,128)S(1)} %get-tuple-element.17), channel_id=1, source_target_pairs={{0,160},{32,192},{64,224},{96,0},{128,32},{160,64},{192,96},{224,1... | collective-permute-start | bytes 52232 | tf_op jit(solution)/shard_map/ppermute | solution.py:60
  85.2 2.7 %collective-permute-start.6 = (f32[32,136]{1,0:T(8,128)S(1)}, f32[32,136]{1,0:T(8,128)S(1)}, u32[]{:S(2)}, u32[]{:S(2)}) collective-permute-start(f32[32,136]{1,0:T(8,128)S(1)} %get-tuple-element.16), channel_id=1, source_target_pairs={{0,192},{32,224},{64,0},{96,32},{128,64},{160,96},{192,128},{224,1... | collective-permute-start | bytes 52232 | tf_op jit(solution)/shard_map/ppermute | solution.py:60
  93.1 2.7 %collective-permute-done.8 = f32[32,136]{1,0:T(8,128)S(1)} collective-permute-done((f32[32,136]{1,0:T(8,128)S(1)}, f32[32,136]{1,0:T(8,128)S(1)}, u32[]{:S(2)}, u32[]{:S(2)}) %collective-permute-start.8) | collective-permute-done | bytes 17440 | tf_op jit(solution)/shard_map/ppermute | solution.py:36
  97.8 3.2 %collective-permute-start.11 = (f32[32,136]{1,0:T(8,128)S(1)}, f32[32,136]{1,0:T(8,128)S(1)}, u32[]{:S(2)}, u32[]{:S(2)}) collective-permute-start(f32[32,136]{1,0:T(8,128)S(1)} %get-tuple-element.9), channel_id=1, source_target_pairs={{0,96},{32,128},{64,160},{96,192},{128,224},{160,0},{192,32},{224,... | collective-permute-start | bytes 52232 | tf_op jit(solution)/shard_map/ppermute | solution.py:69
  102.9 4.1 %collective-permute-start.13 = (f32[32,136]{1,0:T(8,128)S(1)}, f32[32,136]{1,0:T(8,128)S(1)}, u32[]{:S(2)}, u32[]{:S(2)}) collective-permute-start(f32[32,136]{1,0:T(8,128)S(1)} %get-tuple-element.9), channel_id=1, source_target_pairs={{0,160},{32,192},{64,224},{96,0},{128,32},{160,64},{192,96},{224,1... | collective-permute-start | bytes 52232 | tf_op jit(solution)/shard_map/ppermute | solution.py:69
  108.9 2.9 %collective-permute-done.14 = f32[32,136]{1,0:T(8,128)S(1)} collective-permute-done((f32[32,136]{1,0:T(8,128)S(1)}, f32[32,136]{1,0:T(8,128)S(1)}, u32[]{:S(2)}, u32[]{:S(2)}) %collective-permute-start.14) | collective-permute-done | bytes 17440 | tf_op jit(solution)/shard_map/ppermute | solution.py:69
  113.4 6.1 %all-to-all-start.2 = ((bf16[8,8,256,16]{2,3,1,0:T(8,128)(2,1)}), bf16[8,8,256,16]{2,3,1,0:T(8,128)(2,1)S(1)}, u32[]{:S(2)}, u32[]{:S(2)}) async-start(bf16[8,8,256,16]{2,3,1,0:T(8,128)(2,1)} %broadcast_in_dim.72), calls=%async_computation.2 | async-start | bytes 1048576 | tf_op jit(solution)/shard_map/all_to_all | solution.py:113
  119.5 7.5 %all-to-all-done.2 = bf16[8,8,256,16]{2,3,1,0:T(8,128)(2,1)S(1)} async-done(((bf16[8,8,256,16]{2,3,1,0:T(8,128)(2,1)}), bf16[8,8,256,16]{2,3,1,0:T(8,128)(2,1)S(1)}, u32[]{:S(2)}, u32[]{:S(2)}) %all-to-all-start.2) | async-done | bytes 524320 | tf_op jit(solution)/shard_map/all_to_all | solution.py:113
  127.0 3.0 %fusion.18 = f32[64,16,128]{2,1,0:T(8,128)S(1)} fusion(bf16[64,256,16]{1,2,0:T(8,128)(2,1)S(1)} %bitcast.120, bf16[64,256,128]{2,1,0:T(8,128)(2,1)} %get-tuple-element.4), kind=kOutput, calls=%fused_computation.57 | convolution fusion | flops 67108864 | bytes 5242880 | tf_op jit(solution)/shard_map/dot_general | solution.py:172
  134.3 4.2 %collective-permute-done.17 = f32[8,32,128]{2,1,0:T(8,128)S(1)} collective-permute-done((f32[8,32,128]{2,1,0:T(8,128)S(1)}, f32[8,32,128]{2,1,0:T(8,128)S(1)}, u32[]{:S(2)}, u32[]{:S(2)}) %collective-permute-start.17) | collective-permute-done | bytes 131104 | tf_op jit(solution)/shard_map/ppermute | solution.py:36
  139.6 3.0 %collective-permute-start.19 = (f32[32,128]{1,0:T(8,128)S(1)}, f32[32,128]{1,0:T(8,128)S(1)}, u32[]{:S(2)}, u32[]{:S(2)}) collective-permute-start(f32[32,128]{1,0:T(8,128)S(1)} %get-tuple-element.27), channel_id=1, source_target_pairs={{0,64},{32,96},{64,128},{96,160},{128,192},{160,224},{192,0},{224,... | collective-permute-start | bytes 49160 | tf_op jit(solution)/shard_map/ppermute | solution.py:60
  144.2 2.9 %collective-permute-start.21 = (f32[32,128]{1,0:T(8,128)S(1)}, f32[32,128]{1,0:T(8,128)S(1)}, u32[]{:S(2)}, u32[]{:S(2)}) collective-permute-start(f32[32,128]{1,0:T(8,128)S(1)} %get-tuple-element.25), channel_id=1, source_target_pairs={{0,128},{32,160},{64,192},{96,224},{128,0},{160,32},{192,64},{224,... | collective-permute-start | bytes 49160 | tf_op jit(solution)/shard_map/ppermute | solution.py:60
  147.2 2.4 %collective-permute-start.22 = (f32[32,128]{1,0:T(8,128)S(1)}, f32[32,128]{1,0:T(8,128)S(1)}, u32[]{:S(2)}, u32[]{:S(2)}) collective-permute-start(f32[32,128]{1,0:T(8,128)S(1)} %get-tuple-element.24), channel_id=1, source_target_pairs={{0,160},{32,192},{64,224},{96,0},{128,32},{160,64},{192,96},{224,1... | collective-permute-start | bytes 49160 | tf_op jit(solution)/shard_map/ppermute | solution.py:60
  149.6 2.4 %collective-permute-start.23 = (f32[32,128]{1,0:T(8,128)S(1)}, f32[32,128]{1,0:T(8,128)S(1)}, u32[]{:S(2)}, u32[]{:S(2)}) collective-permute-start(f32[32,128]{1,0:T(8,128)S(1)} %get-tuple-element.23), channel_id=1, source_target_pairs={{0,192},{32,224},{64,0},{96,32},{128,64},{160,96},{192,128},{224,1... | collective-permute-start | bytes 49160 | tf_op jit(solution)/shard_map/ppermute | solution.py:60
  (81 shorter events, 31.4 us)
Async XLA Ops:
  3.0 14.2 %all-to-all-start = ((bf16[8,8,2560]{2,1,0:T(8,128)(2,1)}), bf16[8,8,2560]{2,1,0:T(8,128)(2,1)S(1)}, u32[]{:S(2)}, u32[]{:S(2)}) async-start(bf16[8,8,2560]{2,1,0:T(8,128)(2,1)} %broadcast_in_dim.62), calls=%async_computation | async-start | bytes 655360 | tf_op jit(solution)/shard_map/all_to_all | solution.py:113
  49.2 19.5 %all-to-all-start.1 = ((f32[8,8,256,16]{2,3,1,0:T(8,128)}), f32[8,8,256,16]{2,3,1,0:T(8,128)S(1)}, u32[]{:S(2)}, u32[]{:S(2)}) async-start(f32[8,8,256,16]{2,3,1,0:T(8,128)} %bitcast.6), calls=%async_computation.1 | async-start | bytes 2097152 | tf_op jit(solution)/shard_map/all_to_all | solution.py:144
  70.4 14.8 %collective-permute-start.1 = (f32[32,136]{1,0:T(8,128)S(1)}, f32[32,136]{1,0:T(8,128)S(1)}, u32[]{:S(2)}, u32[]{:S(2)}) collective-permute-start(f32[32,136]{1,0:T(8,128)S(1)} %get-tuple-element.14), channel_id=1, source_target_pairs={{0,32},{32,64},{64,96},{96,128},{128,160},{160,192},{192,224},{224... | collective-permute-start | bytes 52232 | tf_op jit(solution)/shard_map/ppermute | solution.py:60
  72.4 15.5 %collective-permute-start.2 = (f32[32,136]{1,0:T(8,128)S(1)}, f32[32,136]{1,0:T(8,128)S(1)}, u32[]{:S(2)}, u32[]{:S(2)}) collective-permute-start(f32[32,136]{1,0:T(8,128)S(1)} %get-tuple-element.20), channel_id=1, source_target_pairs={{0,64},{32,96},{64,128},{96,160},{128,192},{160,224},{192,0},{224,... | collective-permute-start | bytes 52232 | tf_op jit(solution)/shard_map/ppermute | solution.py:60
  75.7 13.2 %collective-permute-start.3 = (f32[32,136]{1,0:T(8,128)S(1)}, f32[32,136]{1,0:T(8,128)S(1)}, u32[]{:S(2)}, u32[]{:S(2)}) collective-permute-start(f32[32,136]{1,0:T(8,128)S(1)} %get-tuple-element.19), channel_id=1, source_target_pairs={{0,96},{32,128},{64,160},{96,192},{128,224},{160,0},{192,32},{224,... | collective-permute-start | bytes 52232 | tf_op jit(solution)/shard_map/ppermute | solution.py:60
  79.7 9.2 %collective-permute-start.4 = (f32[32,136]{1,0:T(8,128)S(1)}, f32[32,136]{1,0:T(8,128)S(1)}, u32[]{:S(2)}, u32[]{:S(2)}) collective-permute-start(f32[32,136]{1,0:T(8,128)S(1)} %get-tuple-element.18), channel_id=1, source_target_pairs={{0,128},{32,160},{64,192},{96,224},{128,0},{160,32},{192,64},{224,... | collective-permute-start | bytes 52232 | tf_op jit(solution)/shard_map/ppermute | solution.py:60
  80.2 8.6 %collective-permute-start.5 = (f32[32,136]{1,0:T(8,128)S(1)}, f32[32,136]{1,0:T(8,128)S(1)}, u32[]{:S(2)}, u32[]{:S(2)}) collective-permute-start(f32[32,136]{1,0:T(8,128)S(1)} %get-tuple-element.17), channel_id=1, source_target_pairs={{0,160},{32,192},{64,224},{96,0},{128,32},{160,64},{192,96},{224,1... | collective-permute-start | bytes 52232 | tf_op jit(solution)/shard_map/ppermute | solution.py:60
  85.2 5.1 %collective-permute-start.6 = (f32[32,136]{1,0:T(8,128)S(1)}, f32[32,136]{1,0:T(8,128)S(1)}, u32[]{:S(2)}, u32[]{:S(2)}) collective-permute-start(f32[32,136]{1,0:T(8,128)S(1)} %get-tuple-element.16), channel_id=1, source_target_pairs={{0,192},{32,224},{64,0},{96,32},{128,64},{160,96},{192,128},{224,1... | collective-permute-start | bytes 52232 | tf_op jit(solution)/shard_map/ppermute | solution.py:60
  91.8 4.0 %collective-permute-start.8 = (f32[32,136]{1,0:T(8,128)S(1)}, f32[32,136]{1,0:T(8,128)S(1)}, u32[]{:S(2)}, u32[]{:S(2)}) collective-permute-start(f32[32,136]{1,0:T(8,128)S(1)} %fusion.6), channel_id=1, source_target_pairs={{0,16},{16,0},{1,17},{17,1},{2,18},{18,2},{3,19},{19,3},{4,20},{20... | collective-permute-start | bytes 52232 | tf_op jit(solution)/shard_map/ppermute | solution.py:36
  95.8 11.2 %collective-permute-start.9 = (f32[32,136]{1,0:T(8,128)S(1)}, f32[32,136]{1,0:T(8,128)S(1)}, u32[]{:S(2)}, u32[]{:S(2)}) collective-permute-start(f32[32,136]{1,0:T(8,128)S(1)} %get-tuple-element.9), channel_id=1, source_target_pairs={{0,32},{32,64},{64,96},{96,128},{128,160},{160,192},{192,224},{224... | collective-permute-start | bytes 52232 | tf_op jit(solution)/shard_map/ppermute | solution.py:69
  96.1 12.2 %collective-permute-start.10 = (f32[32,136]{1,0:T(8,128)S(1)}, f32[32,136]{1,0:T(8,128)S(1)}, u32[]{:S(2)}, u32[]{:S(2)}) collective-permute-start(f32[32,136]{1,0:T(8,128)S(1)} %get-tuple-element.9), channel_id=1, source_target_pairs={{0,64},{32,96},{64,128},{96,160},{128,192},{160,224},{192,0},{224,... | collective-permute-start | bytes 52232 | tf_op jit(solution)/shard_map/ppermute | solution.py:69
  97.8 11.1 %collective-permute-start.11 = (f32[32,136]{1,0:T(8,128)S(1)}, f32[32,136]{1,0:T(8,128)S(1)}, u32[]{:S(2)}, u32[]{:S(2)}) collective-permute-start(f32[32,136]{1,0:T(8,128)S(1)} %get-tuple-element.9), channel_id=1, source_target_pairs={{0,96},{32,128},{64,160},{96,192},{128,224},{160,0},{192,32},{224,... | collective-permute-start | bytes 52232 | tf_op jit(solution)/shard_map/ppermute | solution.py:69
  101.0 7.9 %collective-permute-start.12 = (f32[32,136]{1,0:T(8,128)S(1)}, f32[32,136]{1,0:T(8,128)S(1)}, u32[]{:S(2)}, u32[]{:S(2)}) collective-permute-start(f32[32,136]{1,0:T(8,128)S(1)} %get-tuple-element.9), channel_id=1, source_target_pairs={{0,128},{32,160},{64,192},{96,224},{128,0},{160,32},{192,64},{224,... | collective-permute-start | bytes 52232 | tf_op jit(solution)/shard_map/ppermute | solution.py:69
  102.9 6.0 %collective-permute-start.13 = (f32[32,136]{1,0:T(8,128)S(1)}, f32[32,136]{1,0:T(8,128)S(1)}, u32[]{:S(2)}, u32[]{:S(2)}) collective-permute-start(f32[32,136]{1,0:T(8,128)S(1)} %get-tuple-element.9), channel_id=1, source_target_pairs={{0,160},{32,192},{64,224},{96,0},{128,32},{160,64},{192,96},{224,1... | collective-permute-start | bytes 52232 | tf_op jit(solution)/shard_map/ppermute | solution.py:69
  107.0 4.8 %collective-permute-start.14 = (f32[32,136]{1,0:T(8,128)S(1)}, f32[32,136]{1,0:T(8,128)S(1)}, u32[]{:S(2)}, u32[]{:S(2)}) collective-permute-start(f32[32,136]{1,0:T(8,128)S(1)} %get-tuple-element.9), channel_id=1, source_target_pairs={{0,192},{32,224},{64,0},{96,32},{128,64},{160,96},{192,128},{224,1... | collective-permute-start | bytes 52232 | tf_op jit(solution)/shard_map/ppermute | solution.py:69
  108.3 4.0 %collective-permute-start.15 = (f32[32,136]{1,0:T(8,128)S(1)}, f32[32,136]{1,0:T(8,128)S(1)}, u32[]{:S(2)}, u32[]{:S(2)}) collective-permute-start(f32[32,136]{1,0:T(8,128)S(1)} %get-tuple-element.9), channel_id=1, source_target_pairs={{0,224},{32,0},{64,32},{96,64},{128,96},{160,128},{192,160},{224,1... | collective-permute-start | bytes 52232 | tf_op jit(solution)/shard_map/ppermute | solution.py:69
  113.4 13.6 %all-to-all-start.2 = ((bf16[8,8,256,16]{2,3,1,0:T(8,128)(2,1)}), bf16[8,8,256,16]{2,3,1,0:T(8,128)(2,1)S(1)}, u32[]{:S(2)}, u32[]{:S(2)}) async-start(bf16[8,8,256,16]{2,3,1,0:T(8,128)(2,1)} %broadcast_in_dim.72), calls=%async_computation.2 | async-start | bytes 1048576 | tf_op jit(solution)/shard_map/all_to_all | solution.py:113
  132.9 5.6 %collective-permute-start.17 = (f32[8,32,128]{2,1,0:T(8,128)S(1)}, f32[8,32,128]{2,1,0:T(8,128)S(1)}, u32[]{:S(2)}, u32[]{:S(2)}) collective-permute-start(f32[8,32,128]{2,1,0:T(8,128)S(1)} %dynamic-slice_bitcast_fusion.1), channel_id=1, source_target_pairs={{0,16},{16,0},{1,17},{17,1},{2,18},{18,2},{3,19},{19,3},{4,20},{20... | collective-permute-start | bytes 393224 | tf_op jit(solution)/shard_map/ppermute | solution.py:36
  138.6 11.0 %collective-permute-start.18 = (f32[32,128]{1,0:T(8,128)S(1)}, f32[32,128]{1,0:T(8,128)S(1)}, u32[]{:S(2)}, u32[]{:S(2)}) collective-permute-start(f32[32,128]{1,0:T(8,128)S(1)} %get-tuple-element.21), channel_id=1, source_target_pairs={{0,32},{32,64},{64,96},{96,128},{128,160},{160,192},{192,224},{224... | collective-permute-start | bytes 49160 | tf_op jit(solution)/shard_map/ppermute | solution.py:60
  139.6 12.4 %collective-permute-start.19 = (f32[32,128]{1,0:T(8,128)S(1)}, f32[32,128]{1,0:T(8,128)S(1)}, u32[]{:S(2)}, u32[]{:S(2)}) collective-permute-start(f32[32,128]{1,0:T(8,128)S(1)} %get-tuple-element.27), channel_id=1, source_target_pairs={{0,64},{32,96},{64,128},{96,160},{128,192},{160,224},{192,0},{224,... | collective-permute-start | bytes 49160 | tf_op jit(solution)/shard_map/ppermute | solution.py:60
  142.7 11.0 %collective-permute-start.20 = (f32[32,128]{1,0:T(8,128)S(1)}, f32[32,128]{1,0:T(8,128)S(1)}, u32[]{:S(2)}, u32[]{:S(2)}) collective-permute-start(f32[32,128]{1,0:T(8,128)S(1)} %get-tuple-element.26), channel_id=1, source_target_pairs={{0,96},{32,128},{64,160},{96,192},{128,224},{160,0},{192,32},{224,... | collective-permute-start | bytes 49160 | tf_op jit(solution)/shard_map/ppermute | solution.py:60
  144.2 9.5 %collective-permute-start.21 = (f32[32,128]{1,0:T(8,128)S(1)}, f32[32,128]{1,0:T(8,128)S(1)}, u32[]{:S(2)}, u32[]{:S(2)}) collective-permute-start(f32[32,128]{1,0:T(8,128)S(1)} %get-tuple-element.25), channel_id=1, source_target_pairs={{0,128},{32,160},{64,192},{96,224},{128,0},{160,32},{192,64},{224,... | collective-permute-start | bytes 49160 | tf_op jit(solution)/shard_map/ppermute | solution.py:60
  147.2 6.5 %collective-permute-start.22 = (f32[32,128]{1,0:T(8,128)S(1)}, f32[32,128]{1,0:T(8,128)S(1)}, u32[]{:S(2)}, u32[]{:S(2)}) collective-permute-start(f32[32,128]{1,0:T(8,128)S(1)} %get-tuple-element.24), channel_id=1, source_target_pairs={{0,160},{32,192},{64,224},{96,0},{128,32},{160,64},{192,96},{224,1... | collective-permute-start | bytes 49160 | tf_op jit(solution)/shard_map/ppermute | solution.py:60
  149.6 4.6 %collective-permute-start.23 = (f32[32,128]{1,0:T(8,128)S(1)}, f32[32,128]{1,0:T(8,128)S(1)}, u32[]{:S(2)}, u32[]{:S(2)}) collective-permute-start(f32[32,128]{1,0:T(8,128)S(1)} %get-tuple-element.23), channel_id=1, source_target_pairs={{0,192},{32,224},{64,0},{96,32},{128,64},{160,96},{192,128},{224,1... | collective-permute-start | bytes 49160 | tf_op jit(solution)/shard_map/ppermute | solution.py:60
  (7 other events, 18.5 us)

commit v8 on v6

--- a/solution.py
+++ b/solution.py
@@ -51,41 +51,57 @@
     return x
 
 
-def means_kernel(codes_ref, vec_ref, hi_ref, lo_ref):
+def means_kernel(codes_ref, vec_ref, rot_ref, hi_ref, lo_ref, sums_ref):
     rows = codes_ref.shape[1]
+    group = codes_ref.shape[0]
     kinds = lax.broadcasted_iota(jnp.int32, (K, rows), 0).astype(codes_ref.dtype)
     one = jnp.ones((K, rows), jnp.bfloat16)
     zero = jnp.zeros((K, rows), jnp.bfloat16)
-    for i in range(codes_ref.shape[0]):
+    lanes = lax.broadcasted_iota(jnp.int32, (K, group * DS), 1) // DS
+    total = jnp.zeros((K, group * DS), jnp.float32)
+    for i in range(group):
         hot = jnp.where(codes_ref[pl.ds(i, 1), :] == kinds, one, zero)
         h = jnp.dot(hot, vec_ref[...], preferred_element_type=jnp.float32)
         hi = h.astype(jnp.bfloat16)
+        lo = (h - hi.astype(jnp.float32)).astype(jnp.bfloat16)
         hi_ref[i] = hi
-        lo_ref[i] = (h - hi.astype(jnp.float32)).astype(jnp.bfloat16)
-
-
-def codeword_means(codes_all, vectors):
+        lo_ref[i] = lo
+        rot = rot_ref[...]
+        part = jnp.dot(hi, rot, preferred_element_type=jnp.float32)
+        part = part + jnp.dot(lo, rot, preferred_element_type=jnp.float32)
+        total = jnp.where(lanes == i, part, total)
+    sums_ref[...] = total
+
+
+def codeword_means(codes_all, vectors, rotation):
     m_all, rows = codes_all.shape
     width = vectors.shape[1]
     out = jax.ShapeDtypeStruct((m_all, K, width), jnp.bfloat16)
+    sums = jax.ShapeDtypeStruct((K, m_all * DS), jnp.float32)
     return pl.pallas_call(
         means_kernel,
         grid=(m_all // GROUP,),
         in_specs=[
             pl.BlockSpec((GROUP, rows), lambda g: (g, 0)),
             pl.BlockSpec((rows, width), lambda g: (0, 0)),
+            pl.BlockSpec((width, GROUP * DS), lambda g: (0, g)),
         ],
         out_specs=[
             pl.BlockSpec((GROUP, K, width), lambda g: (g, 0, 0)),
             pl.BlockSpec((GROUP, K, width), lambda g: (g, 0, 0)),
+            pl.BlockSpec((K, GROUP * DS), lambda g: (0, g)),
         ],
-        out_shape=[out, out],
+        out_shape=[out, out, sums],
         cost_estimate=pl.CostEstimate(
-            flops=2 * m_all * K * rows * width,
+            flops=2 * m_all * K * width * (rows + 2 * GROUP * DS),
             transcendentals=0,
-            bytes_accessed=codes_all.size * 2 + vectors.size * 2 + 2 * m_all * K * width * 2,
+            bytes_accessed=codes_all.size * 2
+            + vectors.size * 2
+            + rotation.size * 2
+            + 2 * m_all * K * width * 2
+            + K * m_all * DS * 4,
         ),
-    )(codes_all, vectors)
+    )(codes_all, vectors, rotation)
 
 
 def broadcast_over(x, names, count):
@@ -112,31 +128,27 @@
         (masked[:, None, :] == kinds[None, :, None]).astype(jnp.float32), axis=2
     )
 
-    h_hi, h_lo = codeword_means(codes_all, vectors)
-
-    rot3 = rotation.reshape(local, m_all, DS).transpose(1, 0, 2)
-    dims = (((2,), (1,)), ((0,), (0,)))
-    partial = lax.dot_general(h_hi, rot3, dims, preferred_element_type=jnp.float32)
-    partial = partial + lax.dot_general(h_lo, rot3, dims, preferred_element_type=jnp.float32)
-
-    partial = partial.reshape(n_feat, groups, K, DS)
+    h_hi, h_lo, partial = codeword_means(codes_all, vectors, rotation)
+
+    width = groups * DS
+    partial = partial.reshape(K, n_feat, width)
     sums = jnp.sum(
-        lax.all_to_all(partial, feat_names, split_axis=0, concat_axis=0, tiled=True), axis=0
-    )
-    packed = jnp.concatenate([sums.reshape(groups, K * DS), counts], axis=1)
+        lax.all_to_all(partial, feat_names, split_axis=1, concat_axis=1, tiled=True), axis=1
+    )
+    packed = jnp.concatenate([sums, counts.T], axis=1)
 
     packed = row_psum(packed, steps)
-    total_sums = packed[:, : K * DS].reshape(groups, K, DS)
-    total_counts = packed[:, K * DS :]
+    total_sums = packed[:, :width].reshape(K, groups, DS)
+    total_counts = packed[:, width:]
     cents = total_sums / (total_counts[:, :, None] + 1.0)
-    centroids_all = cents.transpose(1, 0, 2).reshape(K, groups * DS)
+    centroids_all = cents.reshape(K, width)
 
     row_index = lax.axis_index(row_names)
     share = K // n_row
     centroids = lax.dynamic_slice_in_dim(centroids_all, row_index * share, share, 0)
 
-    table = broadcast_over(cents.astype(jnp.bfloat16), feat_names, n_feat)
-    table = table.reshape(m_all, K, DS)
+    table = broadcast_over(centroids_all.astype(jnp.bfloat16), feat_names, n_feat)
+    table = table.reshape(n_feat, K, groups, DS).transpose(0, 2, 1, 3).reshape(m_all, K, DS)
     dims = (((1,), (1,)), ((0,), (0,)))
     grad = lax.dot_general(table, h_hi, dims, preferred_element_type=jnp.float32)
     grad = grad + lax.dot_general(table, h_lo, dims, preferred_element_type=jnp.float32)

time: 149 us -> 152 us (1.020)
  blocking collectives: 0 us -> 14.1 us
  Pallas kernels: 25.4 us -> 35.4 us
  starting transfers between devices: 43.3 us -> 36.1 us
  matrix products: 9.45 us -> 3.64 us
  waiting for transfers between devices: 55.1 us -> 49.6 us
  local copies, waits for them, and re-layouts: 7.17 us -> 5.12 us
    all_to_all x0 -> x1, blocking collectives: none -> 14.1 us  [broadcast_over(): lax.all_to_all(copies, names, split_axis=0, concat_axis=0, tiled=True)]
    pallas_call x1, Pallas kernels: 25.4 us -> 35.4 us  [codeword_means(): pl.pallas_call(means_kernel, grid=(m_all // GROUP,), in_specs=[pl.BlockSp...]
    all_to_all x2 -> x1, starting transfers between devices: 13.5 us -> 6.08 us  [broadcast_over(): lax.all_to_all(copies, names, split_axis=0, concat_axis=0, tiled=True)]
    dot_general x2 -> x0, matrix products: 5.8 us -> none  [the longest x1 3.53 us: shards(): lax.dot_general(h_hi, rot3, dims, preferred_element_type=jnp.float32)]
    all_to_all x2 -> x1, waiting for transfers between devices: 13.2 us -> 7.54 us  [broadcast_over(): lax.all_to_all(copies, names, split_axis=0, concat_axis=0, tiled=True)]
    unnamed x10 -> x5, local copies, waits for them, and re-layouts: 2.98 us -> 1.13 us
  transfers between devices with their start and end apart: 13 -> 12, of which waited for: 13 -> 12; matrix products, arithmetic and copies ran while one was open for 3% -> 2% of each run, Pallas kernels for 0% -> 0%
where the time goes in v8:
time: 152 us; the launch traced here: 150 us
  waiting for transfers between devices  49.6 us (33%)
  starting transfers between devices  36.1 us (24%)
  Pallas kernels  35.4 us (23%)
  blocking collectives  14.1 us (9%)
  local copies, waits for them, and re-layouts  5.12 us (3%)
  other arithmetic  4.13 us (3%)
  matrix products  3.64 us (2%)
    pallas_call x1, Pallas kernels, codeword_means(): pl.pallas_call(means_kernel, grid=(m_all // GROUP,), in_specs=[pl.BlockSp...  35.4 us
    ppermute x10, waiting for transfers between devices, exchange(): return lax.ppermute(x, name, pairs)  31.2 us
    ppermute x10, starting transfers between devices, exchange(): return lax.ppermute(x, name, pairs)  23.7 us
    all_to_all x1, blocking collectives, broadcast_over(): lax.all_to_all(copies, names, split_axis=0, concat_axis=0, tiled=True)  14.1 us
    all_to_all x1, waiting for transfers between devices, shards(): lax.all_to_all(partial, feat_names, split_axis=1, concat_axis=1, tiled=True)  10.9 us
    all_to_all x1, waiting for transfers between devices, broadcast_over(): lax.all_to_all(copies, names, split_axis=0, concat_axis=0, tiled=True)  7.54 us
    all_to_all x1, starting transfers between devices, shards(): lax.all_to_all(partial, feat_names, split_axis=1, concat_axis=1, tiled=True)  6.38 us
    all_to_all x1, starting transfers between devices, broadcast_over(): lax.all_to_all(copies, names, split_axis=0, concat_axis=0, tiled=True)  6.08 us
  transfers between devices with their start and end apart: 12, of which 12 were waited for; matrix products, arithmetic and copies ran while one was open for 2% of the time, Pallas kernels for 0%

profile of v8, /device:TPU:4, one launch (start us, length us, event | category | flops | bytes accessed | tf_op | source)
XLA Modules:
  0.0 149.6 jit_solution(13915606085446163708)
XLA Ops:
  2.2 14.1 %all_to_all.15 = bf16[8,8,2560]{2,1,0:T(8,128)(2,1)} all-to-all(bf16[8,8,2560]{2,1,0:T(8,128)(2,1)S(1)} %broadcast_in_dim.20), channel_id=1, replica_groups=mesh['z'=8,'xl'=2,'c'=2,'y'=4,'xh'=2] {'y','xh'}, dimensions={0} | all-to-all | bytes 655360 | tf_op jit(solution)/shard_map/all_to_all | solution.py:109
  16.4 35.4 %shard_map.77 = (bf16[64,256,128]{2,1,0:T(8,128)(2,1)}, bf16[64,256,128]{2,1,0:T(8,128)(2,1)}, f32[256,1024]{1,0:T(8,128)}) custom-call(bf16[64,2560]{1,0:T(8,128)(2,1)} %bitcast.56, bf16[2560,128]{1,0:T(8,128)(2,1)} %vec_ref.1, bf16[128,1024]{1,0:T(8,128)(2,1)} %rot_ref.1), custom_call_target="tpu_custom_call" | custom-call | flops 11811160064 | bytes 10682368 | tf_op jit(solution)/shard_map/pallas_call | solution.py:81
  51.8 2.2 %copy_bitcast_fusion = f32[256,8,128]{2,0,1:T(8,128)} fusion(f32[256,1024]{1,0:T(8,128)} %get-tuple-element.5), kind=kLoop, calls=%fused_computation.5 | loop fusion | bytes 2097152 | tf_op jit(solution)/shard_map/reshape | solution.py:134
  54.0 6.4 %all-to-all-start.1 = ((f32[256,8,128]{2,0,1:T(8,128)}), f32[256,8,128]{2,0,1:T(8,128)S(1)}, u32[]{:S(2)}, u32[]{:S(2)}) async-start(f32[256,8,128]{2,0,1:T(8,128)} %copy_bitcast_fusion), calls=%async_computation.1 | async-start | bytes 2097152 | tf_op jit(solution)/shard_map/all_to_all | solution.py:136
  60.4 2.3 %convert_reduce_fusion = f32[8,256]{1,0:T(8,128)S(1)} fusion(s32[8,2560]{1,0:T(8,128)S(1)} %get-tuple-element.15), kind=kLoop, calls=%fused_computation.1 | loop fusion | flops 15726592 | bytes 90112 | tf_op jit(solution)/shard_map/reduce_sum | solution.py:127
  62.7 10.9 %all-to-all-done.1 = f32[256,8,128]{2,0,1:T(8,128)S(1)} async-done(((f32[256,8,128]{2,0,1:T(8,128)}), f32[256,8,128]{2,0,1:T(8,128)S(1)}, u32[]{:S(2)}, u32[]{:S(2)}) %all-to-all-start.1) | async-done | bytes 1048608 | tf_op jit(solution)/shard_map/all_to_all | solution.py:136
  73.9 1.3 collective-permute-done
  76.6 4.5 %collective-permute-done.1 = f32[256,136]{0,1:T(8,128)S(1)} collective-permute-done((f32[256,136]{0,1:T(8,128)S(1)}, f32[256,136]{0,1:T(8,128)S(1)}, u32[]{:S(2)}, u32[]{:S(2)}) %collective-permute-start.1) | collective-permute-done | bytes 139296 | tf_op jit(solution)/shard_map/ppermute | solution.py:35
  81.1 2.0 %collective-permute-start.2 = (f32[256,136]{0,1:T(8,128)S(1)}, f32[256,136]{0,1:T(8,128)S(1)}, u32[]{:S(2)}, u32[]{:S(2)}) collective-permute-start(f32[256,136]{0,1:T(8,128)S(1)} %add.96), channel_id=1, source_target_pairs={{0,32},{32,0},{64,96},{96,64},{128,160},{160,128},{192,224},{224,1... | collective-permute-start | bytes 417800 | tf_op jit(solution)/shard_map/ppermute | solution.py:35
  83.1 3.2 %collective-permute-done.2 = f32[256,136]{0,1:T(8,128)S(1)} collective-permute-done((f32[256,136]{0,1:T(8,128)S(1)}, f32[256,136]{0,1:T(8,128)S(1)}, u32[]{:S(2)}, u32[]{:S(2)}) %collective-permute-start.2) | collective-permute-done | bytes 139296 | tf_op jit(solution)/shard_map/ppermute | solution.py:35
  86.3 3.4 %collective-permute-start.3 = (f32[256,136]{0,1:T(8,128)S(1)}, f32[256,136]{0,1:T(8,128)S(1)}, u32[]{:S(2)}, u32[]{:S(2)}) collective-permute-start(f32[256,136]{0,1:T(8,128)S(1)} %add.97), channel_id=1, source_target_pairs={{0,64},{32,96},{64,0},{96,32},{128,192},{160,224},{192,128},{224,1... | collective-permute-start | bytes 417800 | tf_op jit(solution)/shard_map/ppermute | solution.py:35
  89.7 5.2 %collective-permute-done.3 = f32[256,136]{0,1:T(8,128)S(1)} collective-permute-done((f32[256,136]{0,1:T(8,128)S(1)}, f32[256,136]{0,1:T(8,128)S(1)}, u32[]{:S(2)}, u32[]{:S(2)}) %collective-permute-start.3) | collective-permute-done | bytes 139296 | tf_op jit(solution)/shard_map/ppermute | solution.py:35
  94.8 6.5 %collective-permute-start.4 = (f32[256,136]{0,1:T(8,128)S(1)}, f32[256,136]{0,1:T(8,128)S(1)}, u32[]{:S(2)}, u32[]{:S(2)}) collective-permute-start(f32[256,136]{0,1:T(8,128)S(1)} %add.98), channel_id=1, source_target_pairs={{0,128},{32,160},{64,192},{96,224},{128,0},{160,32},{192,64},{224,... | collective-permute-start | bytes 417800 | tf_op jit(solution)/shard_map/ppermute | solution.py:35
  101.3 3.4 %collective-permute-done.4 = f32[256,136]{0,1:T(8,128)S(1)} collective-permute-done((f32[256,136]{0,1:T(8,128)S(1)}, f32[256,136]{0,1:T(8,128)S(1)}, u32[]{:S(2)}, u32[]{:S(2)}) %collective-permute-start.4) | collective-permute-done | bytes 139296 | tf_op jit(solution)/shard_map/ppermute | solution.py:35
  105.7 6.1 %all-to-all-start.2 = ((bf16[8,256,128]{1,2,0:T(8,128)(2,1)}), bf16[8,256,128]{1,2,0:T(8,128)(2,1)S(1)}, u32[]{:S(2)}, u32[]{:S(2)}) async-start(bf16[8,256,128]{1,2,0:T(8,128)(2,1)} %broadcast_in_dim.34), calls=%async_computation.2 | async-start | bytes 1048576 | tf_op jit(solution)/shard_map/all_to_all | solution.py:109
  111.8 7.5 %all-to-all-done.2 = bf16[8,256,128]{1,2,0:T(8,128)(2,1)S(1)} async-done(((bf16[8,256,128]{1,2,0:T(8,128)(2,1)}), bf16[8,256,128]{1,2,0:T(8,128)(2,1)S(1)}, u32[]{:S(2)}, u32[]{:S(2)}) %all-to-all-start.2) | async-done | bytes 524320 | tf_op jit(solution)/shard_map/all_to_all | solution.py:109
  119.3 3.0 %fusion.4 = f32[64,16,128]{2,1,0:T(8,128)S(1)} fusion(bf16[64,256,16]{1,2,0:T(8,128)(2,1)S(1)} %bitcast.47, bf16[64,256,128]{2,1,0:T(8,128)(2,1)} %get-tuple-element.6), kind=kOutput, calls=%fused_computation.26 | convolution fusion | flops 67108864 | bytes 5242880 | tf_op jit(solution)/shard_map/dot_general | solution.py:153
  124.2 1.5 %collective-permute-done.5 = f32[16,32,128]{2,1,0:T(8,128)S(1)} collective-permute-done((f32[16,32,128]{2,1,0:T(8,128)S(1)}, f32[16,32,128]{2,1,0:T(8,128)S(1)}, u32[]{:S(2)}, u32[]{:S(2)}) %collective-permute-start.5) | collective-permute-done | bytes 262176 | tf_op jit(solution)/shard_map/ppermute | solution.py:35
  127.1 4.3 %collective-permute-done.6 = f32[8,32,128]{2,1,0:T(8,128)S(1)} collective-permute-done((f32[8,32,128]{2,1,0:T(8,128)S(1)}, f32[8,32,128]{2,1,0:T(8,128)S(1)}, u32[]{:S(2)}, u32[]{:S(2)}) %collective-permute-start.6) | collective-permute-done | bytes 131104 | tf_op jit(solution)/shard_map/ppermute | solution.py:35
  131.5 4.2 %collective-permute-done.7 = f32[4,32,128]{2,1,0:T(8,128)S(1)} collective-permute-done((f32[4,32,128]{2,1,0:T(8,128)S(1)}, f32[4,32,128]{2,1,0:T(8,128)S(1)}, u32[]{:S(2)}, u32[]{:S(2)}) %collective-permute-start.7) | collective-permute-done | bytes 65568 | tf_op jit(solution)/shard_map/ppermute | solution.py:35
  135.8 3.5 %collective-permute-start.8 = (f32[2,32,128]{2,1,0:T(8,128)S(1)}, f32[2,32,128]{2,1,0:T(8,128)S(1)}, u32[]{:S(2)}, u32[]{:S(2)}) collective-permute-start(f32[2,32,128]{2,1,0:T(8,128)S(1)} %dynamic-slice_bitcast_fusion.3), channel_id=1, source_target_pairs={{0,64},{32,96},{64,0},{96,32},{128,192},{160,224},{192,128},{224,1... | collective-permute-start | bytes 98312 | tf_op jit(solution)/shard_map/ppermute | solution.py:35
  139.4 1.9 %collective-permute-done.8 = f32[2,32,128]{2,1,0:T(8,128)S(1)} collective-permute-done((f32[2,32,128]{2,1,0:T(8,128)S(1)}, f32[2,32,128]{2,1,0:T(8,128)S(1)}, u32[]{:S(2)}, u32[]{:S(2)}) %collective-permute-start.8) | collective-permute-done | bytes 32800 | tf_op jit(solution)/shard_map/ppermute | solution.py:35
  141.3 5.4 %collective-permute-start.9 = (f32[1,32,128]{2,1,0:T(8,128)S(1)}, f32[1,32,128]{2,1,0:T(8,128)S(1)}, u32[]{:S(2)}, u32[]{:S(2)}) collective-permute-start(f32[1,32,128]{2,1,0:T(8,128)S(1)} %constant_dynamic-slice_fusion), channel_id=1, source_target_pairs={{0,128},{32,160},{64,192},{96,224},{128,0},{160,32},{192,64},{224,... | collective-permute-start | bytes 49160 | tf_op jit(solution)/shard_map/ppermute | solution.py:35
  147.4 1.6 %collective-permute-done.9 = f32[1,32,128]{2,1,0:T(8,128)S(1)} collective-permute-done((f32[1,32,128]{2,1,0:T(8,128)S(1)}, f32[1,32,128]{2,1,0:T(8,128)S(1)}, u32[]{:S(2)}, u32[]{:S(2)}) %collective-permute-start.9) | collective-permute-done | bytes 16416 | tf_op jit(solution)/shard_map/ppermute | solution.py:35
  (38 shorter events, 8.2 us)
Async XLA Ops:
  54.0 57.8 %copy-start.1 = (s32[32]{0:T(128)S(1)}, s32[32]{0:T(128)}, u32[]{:S(2)}) copy-start(s32[32]{0:T(128)} %constant.81) | copy-start | bytes 388
  54.0 19.6 %all-to-all-start.1 = ((f32[256,8,128]{2,0,1:T(8,128)}), f32[256,8,128]{2,0,1:T(8,128)S(1)}, u32[]{:S(2)}, u32[]{:S(2)}) async-start(f32[256,8,128]{2,0,1:T(8,128)} %copy_bitcast_fusion), calls=%async_computation.1 | async-start | bytes 2097152 | tf_op jit(solution)/shard_map/all_to_all | solution.py:136
  73.8 1.4 collective-permute-start
  75.3 5.8 %collective-permute-start.1 = (f32[256,136]{0,1:T(8,128)S(1)}, f32[256,136]{0,1:T(8,128)S(1)}, u32[]{:S(2)}, u32[]{:S(2)}) collective-permute-start(f32[256,136]{0,1:T(8,128)S(1)} %fusion.1), channel_id=1, source_target_pairs={{0,16},{16,0},{1,17},{17,1},{2,18},{18,2},{3,19},{19,3},{4,20},{20... | collective-permute-start | bytes 417800 | tf_op jit(solution)/shard_map/ppermute | solution.py:35
  81.1 5.2 %collective-permute-start.2 = (f32[256,136]{0,1:T(8,128)S(1)}, f32[256,136]{0,1:T(8,128)S(1)}, u32[]{:S(2)}, u32[]{:S(2)}) collective-permute-start(f32[256,136]{0,1:T(8,128)S(1)} %add.96), channel_id=1, source_target_pairs={{0,32},{32,0},{64,96},{96,64},{128,160},{160,128},{192,224},{224,1... | collective-permute-start | bytes 417800 | tf_op jit(solution)/shard_map/ppermute | solution.py:35
  86.3 8.5 %collective-permute-start.3 = (f32[256,136]{0,1:T(8,128)S(1)}, f32[256,136]{0,1:T(8,128)S(1)}, u32[]{:S(2)}, u32[]{:S(2)}) collective-permute-start(f32[256,136]{0,1:T(8,128)S(1)} %add.97), channel_id=1, source_target_pairs={{0,64},{32,96},{64,0},{96,32},{128,192},{160,224},{192,128},{224,1... | collective-permute-start | bytes 417800 | tf_op jit(solution)/shard_map/ppermute | solution.py:35
  94.8 9.9 %collective-permute-start.4 = (f32[256,136]{0,1:T(8,128)S(1)}, f32[256,136]{0,1:T(8,128)S(1)}, u32[]{:S(2)}, u32[]{:S(2)}) collective-permute-start(f32[256,136]{0,1:T(8,128)S(1)} %add.98), channel_id=1, source_target_pairs={{0,128},{32,160},{64,192},{96,224},{128,0},{160,32},{192,64},{224,... | collective-permute-start | bytes 417800 | tf_op jit(solution)/shard_map/ppermute | solution.py:35
  105.7 13.6 %all-to-all-start.2 = ((bf16[8,256,128]{1,2,0:T(8,128)(2,1)}), bf16[8,256,128]{1,2,0:T(8,128)(2,1)S(1)}, u32[]{:S(2)}, u32[]{:S(2)}) async-start(bf16[8,256,128]{1,2,0:T(8,128)(2,1)} %broadcast_in_dim.34), calls=%async_computation.2 | async-start | bytes 1048576 | tf_op jit(solution)/shard_map/all_to_all | solution.py:109
  119.3 3.4 %copy-start = (bf16[64,256,128]{2,1,0:T(8,128)(2,1)S(1)}, bf16[64,256,128]{2,1,0:T(8,128)(2,1)}, u32[]{:S(2)}) copy-start(bf16[64,256,128]{2,1,0:T(8,128)(2,1)} %get-tuple-element.7) | copy-start | bytes 12582916
  124.1 1.6 %collective-permute-start.5 = (f32[16,32,128]{2,1,0:T(8,128)S(1)}, f32[16,32,128]{2,1,0:T(8,128)S(1)}, u32[]{:S(2)}, u32[]{:S(2)}) collective-permute-start(f32[16,32,128]{2,1,0:T(8,128)S(1)} %dynamic-slice_bitcast_fusion), channel_id=1, source_target_pairs={{0,8},{8,0},{1,9},{9,1},{2,10},{10,2},{3,11},{11,3},{4,12},{12,4},... | collective-permute-start | bytes 786440 | tf_op jit(solution)/shard_map/ppermute | solution.py:35
  125.8 5.6 %collective-permute-start.6 = (f32[8,32,128]{2,1,0:T(8,128)S(1)}, f32[8,32,128]{2,1,0:T(8,128)S(1)}, u32[]{:S(2)}, u32[]{:S(2)}) collective-permute-start(f32[8,32,128]{2,1,0:T(8,128)S(1)} %dynamic-slice_bitcast_fusion.1), channel_id=1, source_target_pairs={{0,16},{16,0},{1,17},{17,1},{2,18},{18,2},{3,19},{19,3},{4,20},{20... | collective-permute-start | bytes 393224 | tf_op jit(solution)/shard_map/ppermute | solution.py:35
  131.4 4.4 %collective-permute-start.7 = (f32[4,32,128]{2,1,0:T(8,128)S(1)}, f32[4,32,128]{2,1,0:T(8,128)S(1)}, u32[]{:S(2)}, u32[]{:S(2)}) collective-permute-start(f32[4,32,128]{2,1,0:T(8,128)S(1)} %dynamic-slice_bitcast_fusion.2), channel_id=1, source_target_pairs={{0,32},{32,0},{64,96},{96,64},{128,160},{160,128},{192,224},{224,1... | collective-permute-start | bytes 196616 | tf_op jit(solution)/shard_map/ppermute | solution.py:35
  135.8 5.4 %collective-permute-start.8 = (f32[2,32,128]{2,1,0:T(8,128)S(1)}, f32[2,32,128]{2,1,0:T(8,128)S(1)}, u32[]{:S(2)}, u32[]{:S(2)}) collective-permute-start(f32[2,32,128]{2,1,0:T(8,128)S(1)} %dynamic-slice_bitcast_fusion.3), channel_id=1, source_target_pairs={{0,64},{32,96},{64,0},{96,32},{128,192},{160,224},{192,128},{224,1... | collective-permute-start | bytes 98312 | tf_op jit(solution)/shard_map/ppermute | solution.py:35
  141.3 7.7 %collective-permute-start.9 = (f32[1,32,128]{2,1,0:T(8,128)S(1)}, f32[1,32,128]{2,1,0:T(8,128)S(1)}, u32[]{:S(2)}, u32[]{:S(2)}) collective-permute-start(f32[1,32,128]{2,1,0:T(8,128)S(1)} %constant_dynamic-slice_fusion), channel_id=1, source_target_pairs={{0,128},{32,160},{64,192},{96,224},{128,0},{160,32},{192,64},{224,... | collective-permute-start | bytes 49160 | tf_op jit(solution)/shard_map/ppermute | solution.py:35

commit v9 on v6

--- a/solution.py
+++ b/solution.py
@@ -51,7 +51,7 @@
     return x
 
 
-def means_kernel(codes_ref, vec_ref, hi_ref, lo_ref):
+def means_kernel(codes_ref, vec_ref, hi_ref, mid_ref, lo_ref):
     rows = codes_ref.shape[1]
     kinds = lax.broadcasted_iota(jnp.int32, (K, rows), 0).astype(codes_ref.dtype)
     one = jnp.ones((K, rows), jnp.bfloat16)
@@ -60,8 +60,11 @@
         hot = jnp.where(codes_ref[pl.ds(i, 1), :] == kinds, one, zero)
         h = jnp.dot(hot, vec_ref[...], preferred_element_type=jnp.float32)
         hi = h.astype(jnp.bfloat16)
+        rest = h - hi.astype(jnp.float32)
+        mid = rest.astype(jnp.bfloat16)
         hi_ref[i] = hi
-        lo_ref[i] = (h - hi.astype(jnp.float32)).astype(jnp.bfloat16)
+        mid_ref[i] = mid
+        lo_ref[i] = (rest - mid.astype(jnp.float32)).astype(jnp.bfloat16)
 
 
 def codeword_means(codes_all, vectors):
@@ -75,15 +78,12 @@
             pl.BlockSpec((GROUP, rows), lambda g: (g, 0)),
             pl.BlockSpec((rows, width), lambda g: (0, 0)),
         ],
-        out_specs=[
-            pl.BlockSpec((GROUP, K, width), lambda g: (g, 0, 0)),
-            pl.BlockSpec((GROUP, K, width), lambda g: (g, 0, 0)),
-        ],
-        out_shape=[out, out],
+        out_specs=[pl.BlockSpec((GROUP, K, width), lambda g: (g, 0, 0))] * 3,
+        out_shape=[out] * 3,
         cost_estimate=pl.CostEstimate(
             flops=2 * m_all * K * rows * width,
             transcendentals=0,
-            bytes_accessed=codes_all.size * 2 + vectors.size * 2 + 2 * m_all * K * width * 2,
+            bytes_accessed=codes_all.size * 2 + vectors.size * 2 + 3 * m_all * K * width * 2,
         ),
     )(codes_all, vectors)
 
@@ -112,12 +112,13 @@
         (masked[:, None, :] == kinds[None, :, None]).astype(jnp.float32), axis=2
     )
 
-    h_hi, h_lo = codeword_means(codes_all, vectors)
+    h_parts = codeword_means(codes_all, vectors)
 
     rot3 = rotation.reshape(local, m_all, DS).transpose(1, 0, 2)
     dims = (((2,), (1,)), ((0,), (0,)))
-    partial = lax.dot_general(h_hi, rot3, dims, preferred_element_type=jnp.float32)
-    partial = partial + lax.dot_general(h_lo, rot3, dims, preferred_element_type=jnp.float32)
+    partial = sum(
+        lax.dot_general(part, rot3, dims, preferred_element_type=jnp.float32) for part in h_parts
+    )
 
     partial = partial.reshape(n_feat, groups, K, DS)
     sums = jnp.sum(
@@ -138,8 +139,9 @@
     table = broadcast_over(cents.astype(jnp.bfloat16), feat_names, n_feat)
     table = table.reshape(m_all, K, DS)
     dims = (((1,), (1,)), ((0,), (0,)))
-    grad = lax.dot_general(table, h_hi, dims, preferred_element_type=jnp.float32)
-    grad = grad + lax.dot_general(table, h_lo, dims, preferred_element_type=jnp.float32)
+    grad = sum(
+        lax.dot_general(table, part, dims, preferred_element_type=jnp.float32) for part in h_parts
+    )
     inverse = 1.0 / (rows * n_row)
     grad = grad.reshape(m_all * DS, local) * inverse
 

time: 149 us -> 154 us (1.034)
  local copies, waits for them, and re-layouts: 7.17 us -> 9.71 us
  matrix products: 9.45 us -> 11.3 us
    unnamed x10 -> x14, local copies, waits for them, and re-layouts: 2.98 us -> 5.52 us
    dot_general x4 -> x6, matrix products: 9.45 us -> 11.3 us  [the longest x3 6.97 us: shards(): lax.dot_general(part, rot3, dims, preferred_element_type=jnp.float32)]
where the time goes in v9:
time: 154 us; the launch traced here: 151 us
  waiting for transfers between devices  55.4 us (36%)
  starting transfers between devices  43.2 us (28%)
  Pallas kernels  25.5 us (17%)
  matrix products  11.3 us (7%)
  local copies, waits for them, and re-layouts  9.71 us (6%)
  other arithmetic  4.46 us (3%)
    ppermute x10, waiting for transfers between devices, exchange(): return lax.ppermute(x, name, pairs)  31.2 us
    pallas_call x1, Pallas kernels, codeword_means(): pl.pallas_call(means_kernel, grid=(m_all // GROUP,), in_specs=[pl.BlockSp...  25.5 us
    ppermute x10, starting transfers between devices, exchange(): return lax.ppermute(x, name, pairs)  23.5 us
    all_to_all x2, starting transfers between devices, broadcast_over(): lax.all_to_all(copies, names, split_axis=0, concat_axis=0, tiled=True)  13.5 us
    all_to_all x2, waiting for transfers between devices, broadcast_over(): lax.all_to_all(copies, names, split_axis=0, concat_axis=0, tiled=True)  13.2 us
    all_to_all x1, waiting for transfers between devices, shards(): lax.all_to_all(partial, feat_names, split_axis=0, concat_axis=0, tiled=True)  11 us
    dot_general x3, matrix products, shards(): lax.dot_general(part, rot3, dims, preferred_element_type=jnp.float32)  6.97 us
    all_to_all x1, starting transfers between devices, shards(): lax.all_to_all(partial, feat_names, split_axis=0, concat_axis=0, tiled=True)  6.13 us
  transfers between devices with their start and end apart: 13, of which 13 were waited for; matrix products, arithmetic and copies ran while one was open for 3% of the time, Pallas kernels for 0%

profile of v9, /device:TPU:4, one launch (start us, length us, event | category | flops | bytes accessed | tf_op | source)
XLA Modules:
  0.0 151.1 jit_solution(14054449787691140693)
XLA Ops:
  2.9 7.4 %all-to-all-start = ((bf16[8,8,2560]{2,1,0:T(8,128)(2,1)}), bf16[8,8,2560]{2,1,0:T(8,128)(2,1)S(1)}, u32[]{:S(2)}, u32[]{:S(2)}) async-start(bf16[8,8,2560]{2,1,0:T(8,128)(2,1)} %broadcast_in_dim.20), calls=%async_computation | async-start | bytes 655360 | tf_op jit(solution)/shard_map/all_to_all | solution.py:93
  11.5 5.7 %all-to-all-done = bf16[8,8,2560]{2,1,0:T(8,128)(2,1)S(1)} async-done(((bf16[8,8,2560]{2,1,0:T(8,128)(2,1)}), bf16[8,8,2560]{2,1,0:T(8,128)(2,1)S(1)}, u32[]{:S(2)}, u32[]{:S(2)}) %all-to-all-start) | async-done | bytes 327712 | tf_op jit(solution)/shard_map/all_to_all | solution.py:93
  18.0 25.5 %shard_map.77 = (bf16[64,256,128]{2,1,0:T(8,128)(2,1)}, bf16[64,256,128]{2,1,0:T(8,128)(2,1)}, bf16[64,256,128]{2,1,0:T(8,128)(2,1)}) custom-call(bf16[64,2560]{1,0:T(8,128)(2,1)} %bitcast.62, bf16[2560,128]{1,0:T(8,128)(2,1)} %vec_ref.1), custom_call_target="tpu_custom_call" | custom-call | flops 10737418240 | bytes 13565952 | tf_op jit(solution)/shard_map/pallas_call | solution.py:74
  43.5 3.5 %fusion.5 = f32[64,256,16]{1,2,0:T(8,128)S(1)} fusion(bf16[64,256,128]{2,1,0:T(8,128)(2,1)} %get-tuple-element.5, bf16[64,128,16]{1,2,0:T(8,128)(2,1)S(1)} %bitcast.52), kind=kOutput, calls=%fused_computation.29 | convolution fusion | flops 67108864 | bytes 5505024 | tf_op jit(solution)/shard_map/dot_general | solution.py:120
  49.2 2.2 %convolution_add_fusion = f32[64,256,16]{1,2,0:T(8,128)} fusion(f32[64,256,16]{1,2,0:T(8,128)S(1)} %convolution_add_fusion.1, bf16[64,256,128]{2,1,0:T(8,128)(2,1)S(1)} %copy-done, bf16[64,128,16]{1,2,0:T(8,128)(2,1)S(1)} %bitcast.54), kind=kOutput, calls=%fused_computation.3 | convolution fusion | flops 67371008 | bytes 6553600 | tf_op jit(solution)/shard_map/dot_general | solution.py:120
  51.5 6.1 %all-to-all-start.1 = ((f32[8,8,256,16]{2,3,1,0:T(8,128)}), f32[8,8,256,16]{2,3,1,0:T(8,128)S(1)}, u32[]{:S(2)}, u32[]{:S(2)}) async-start(f32[8,8,256,16]{2,3,1,0:T(8,128)} %bitcast.6), calls=%async_computation.1 | async-start | bytes 2097152 | tf_op jit(solution)/shard_map/all_to_all | solution.py:125
  57.6 2.3 %convert_reduce_fusion = f32[8,256]{1,0:T(8,128)S(1)} fusion(s32[8,2560]{1,0:T(8,128)S(1)} %get-tuple-element.17), kind=kLoop, calls=%fused_computation.1 | loop fusion | flops 15726592 | bytes 90112 | tf_op jit(solution)/shard_map/reduce_sum | solution.py:111
  59.9 11.0 %all-to-all-done.1 = f32[8,8,256,16]{2,3,1,0:T(8,128)S(1)} async-done(((f32[8,8,256,16]{2,3,1,0:T(8,128)}), f32[8,8,256,16]{2,3,1,0:T(8,128)S(1)}, u32[]{:S(2)}, u32[]{:S(2)}) %all-to-all-start.1) | async-done | bytes 1048608 | tf_op jit(solution)/shard_map/all_to_all | solution.py:125
  74.8 4.5 %collective-permute-done.1 = f32[8,4352]{1,0:T(8,128)S(1)} collective-permute-done((f32[8,4352]{1,0:T(8,128)S(1)}, f32[8,4352]{1,0:T(8,128)S(1)}, u32[]{:S(2)}, u32[]{:S(2)}) %collective-permute-start.1) | collective-permute-done | bytes 139296 | tf_op jit(solution)/shard_map/ppermute | solution.py:35
  79.3 2.0 %collective-permute-start.2 = (f32[8,4352]{1,0:T(8,128)S(1)}, f32[8,4352]{1,0:T(8,128)S(1)}, u32[]{:S(2)}, u32[]{:S(2)}) collective-permute-start(f32[8,4352]{1,0:T(8,128)S(1)} %add.107), channel_id=1, source_target_pairs={{0,32},{32,0},{64,96},{96,64},{128,160},{160,128},{192,224},{224,1... | collective-permute-start | bytes 417800 | tf_op jit(solution)/shard_map/ppermute | solution.py:35
  81.3 3.2 %collective-permute-done.2 = f32[8,4352]{1,0:T(8,128)S(1)} collective-permute-done((f32[8,4352]{1,0:T(8,128)S(1)}, f32[8,4352]{1,0:T(8,128)S(1)}, u32[]{:S(2)}, u32[]{:S(2)}) %collective-permute-start.2) | collective-permute-done | bytes 139296 | tf_op jit(solution)/shard_map/ppermute | solution.py:35
  84.5 3.4 %collective-permute-start.3 = (f32[8,4352]{1,0:T(8,128)S(1)}, f32[8,4352]{1,0:T(8,128)S(1)}, u32[]{:S(2)}, u32[]{:S(2)}) collective-permute-start(f32[8,4352]{1,0:T(8,128)S(1)} %add.108), channel_id=1, source_target_pairs={{0,64},{32,96},{64,0},{96,32},{128,192},{160,224},{192,128},{224,1... | collective-permute-start | bytes 417800 | tf_op jit(solution)/shard_map/ppermute | solution.py:35
  87.9 5.2 %collective-permute-done.3 = f32[8,4352]{1,0:T(8,128)S(1)} collective-permute-done((f32[8,4352]{1,0:T(8,128)S(1)}, f32[8,4352]{1,0:T(8,128)S(1)}, u32[]{:S(2)}, u32[]{:S(2)}) %collective-permute-start.3) | collective-permute-done | bytes 139296 | tf_op jit(solution)/shard_map/ppermute | solution.py:35
  93.0 6.7 %collective-permute-start.4 = (f32[8,4352]{1,0:T(8,128)S(1)}, f32[8,4352]{1,0:T(8,128)S(1)}, u32[]{:S(2)}, u32[]{:S(2)}) collective-permute-start(f32[8,4352]{1,0:T(8,128)S(1)} %add.109), channel_id=1, source_target_pairs={{0,128},{32,160},{64,192},{96,224},{128,0},{160,32},{192,64},{224,... | collective-permute-start | bytes 417800 | tf_op jit(solution)/shard_map/ppermute | solution.py:35
  99.7 3.5 %collective-permute-done.4 = f32[8,4352]{1,0:T(8,128)S(1)} collective-permute-done((f32[8,4352]{1,0:T(8,128)S(1)}, f32[8,4352]{1,0:T(8,128)S(1)}, u32[]{:S(2)}, u32[]{:S(2)}) %collective-permute-start.4) | collective-permute-done | bytes 139296 | tf_op jit(solution)/shard_map/ppermute | solution.py:35
  105.0 6.1 %all-to-all-start.2 = ((bf16[8,8,256,16]{2,3,1,0:T(8,128)(2,1)}), bf16[8,8,256,16]{2,3,1,0:T(8,128)(2,1)S(1)}, u32[]{:S(2)}, u32[]{:S(2)}) async-start(bf16[8,8,256,16]{2,3,1,0:T(8,128)(2,1)} %broadcast_in_dim.34), calls=%async_computation.2 | async-start | bytes 1048576 | tf_op jit(solution)/shard_map/all_to_all | solution.py:93
  111.1 7.5 %all-to-all-done.2 = bf16[8,8,256,16]{2,3,1,0:T(8,128)(2,1)S(1)} async-done(((bf16[8,8,256,16]{2,3,1,0:T(8,128)(2,1)}), bf16[8,8,256,16]{2,3,1,0:T(8,128)(2,1)S(1)}, u32[]{:S(2)}, u32[]{:S(2)}) %all-to-all-start.2) | async-done | bytes 524320 | tf_op jit(solution)/shard_map/all_to_all | solution.py:93
  118.6 3.0 %fusion.6 = f32[64,16,128]{2,1,0:T(8,128)S(1)} fusion(bf16[64,256,16]{1,2,0:T(8,128)(2,1)S(1)} %bitcast.49, bf16[64,256,128]{2,1,0:T(8,128)(2,1)} %get-tuple-element.5), kind=kOutput, calls=%fused_computation.30 | convolution fusion | flops 67108864 | bytes 5242880 | tf_op jit(solution)/shard_map/dot_general | solution.py:143
  128.6 4.3 %collective-permute-done.6 = f32[8,32,128]{2,1,0:T(8,128)S(1)} collective-permute-done((f32[8,32,128]{2,1,0:T(8,128)S(1)}, f32[8,32,128]{2,1,0:T(8,128)S(1)}, u32[]{:S(2)}, u32[]{:S(2)}) %collective-permute-start.6) | collective-permute-done | bytes 131104 | tf_op jit(solution)/shard_map/ppermute | solution.py:35
  133.0 4.2 %collective-permute-done.7 = f32[4,32,128]{2,1,0:T(8,128)S(1)} collective-permute-done((f32[4,32,128]{2,1,0:T(8,128)S(1)}, f32[4,32,128]{2,1,0:T(8,128)S(1)}, u32[]{:S(2)}, u32[]{:S(2)}) %collective-permute-start.7) | collective-permute-done | bytes 65568 | tf_op jit(solution)/shard_map/ppermute | solution.py:35
  137.3 3.5 %collective-permute-start.8 = (f32[2,32,128]{2,1,0:T(8,128)S(1)}, f32[2,32,128]{2,1,0:T(8,128)S(1)}, u32[]{:S(2)}, u32[]{:S(2)}) collective-permute-start(f32[2,32,128]{2,1,0:T(8,128)S(1)} %dynamic-slice_bitcast_fusion.3), channel_id=1, source_target_pairs={{0,64},{32,96},{64,0},{96,32},{128,192},{160,224},{192,128},{224,1... | collective-permute-start | bytes 98312 | tf_op jit(solution)/shard_map/ppermute | solution.py:35
  141.1 1.6 %collective-permute-done.8 = f32[2,32,128]{2,1,0:T(8,128)S(1)} collective-permute-done((f32[2,32,128]{2,1,0:T(8,128)S(1)}, f32[2,32,128]{2,1,0:T(8,128)S(1)}, u32[]{:S(2)}, u32[]{:S(2)}) %collective-permute-start.8) | collective-permute-done | bytes 32800 | tf_op jit(solution)/shard_map/ppermute | solution.py:35
  142.8 5.1 %collective-permute-start.9 = (f32[1,32,128]{2,1,0:T(8,128)S(1)}, f32[1,32,128]{2,1,0:T(8,128)S(1)}, u32[]{:S(2)}, u32[]{:S(2)}) collective-permute-start(f32[1,32,128]{2,1,0:T(8,128)S(1)} %constant_dynamic-slice_fusion), channel_id=1, source_target_pairs={{0,128},{32,160},{64,192},{96,224},{128,0},{160,32},{192,64},{224,... | collective-permute-start | bytes 49160 | tf_op jit(solution)/shard_map/ppermute | solution.py:35
  148.6 1.9 %collective-permute-done.9 = f32[1,32,128]{2,1,0:T(8,128)S(1)} collective-permute-done((f32[1,32,128]{2,1,0:T(8,128)S(1)}, f32[1,32,128]{2,1,0:T(8,128)S(1)}, u32[]{:S(2)}, u32[]{:S(2)}) %collective-permute-start.9) | collective-permute-done | bytes 16416 | tf_op jit(solution)/shard_map/ppermute | solution.py:35
  (56 shorter events, 20.1 us)
Async XLA Ops:
  2.9 14.2 %all-to-all-start = ((bf16[8,8,2560]{2,1,0:T(8,128)(2,1)}), bf16[8,8,2560]{2,1,0:T(8,128)(2,1)S(1)}, u32[]{:S(2)}, u32[]{:S(2)}) async-start(bf16[8,8,2560]{2,1,0:T(8,128)(2,1)} %broadcast_in_dim.20), calls=%async_computation | async-start | bytes 655360 | tf_op jit(solution)/shard_map/all_to_all | solution.py:93
  17.2 0.8 copy-start.4
  43.5 3.5 %copy-start.2 = (bf16[64,256,128]{2,1,0:T(8,128)(2,1)S(1)}, bf16[64,256,128]{2,1,0:T(8,128)(2,1)}, u32[]{:S(2)}) copy-start(bf16[64,256,128]{2,1,0:T(8,128)(2,1)} %get-tuple-element.6) | copy-start | bytes 12582916
  47.0 2.2 %copy-start = (bf16[64,256,128]{2,1,0:T(8,128)(2,1)S(1)}, bf16[64,256,128]{2,1,0:T(8,128)(2,1)}, u32[]{:S(2)}) copy-start(bf16[64,256,128]{2,1,0:T(8,128)(2,1)} %get-tuple-element.7) | copy-start | bytes 12582916
  51.5 19.5 %all-to-all-start.1 = ((f32[8,8,256,16]{2,3,1,0:T(8,128)}), f32[8,8,256,16]{2,3,1,0:T(8,128)S(1)}, u32[]{:S(2)}, u32[]{:S(2)}) async-start(f32[8,8,256,16]{2,3,1,0:T(8,128)} %bitcast.6), calls=%async_computation.1 | async-start | bytes 2097152 | tf_op jit(solution)/shard_map/all_to_all | solution.py:125
  72.0 39.1 %copy-start.5 = (s32[32]{0:T(128)S(1)}, s32[32]{0:T(128)}, u32[]{:S(2)}) copy-start(s32[32]{0:T(128)} %constant.81) | copy-start | bytes 388
  72.0 1.4 collective-permute-start
  73.5 5.8 %collective-permute-start.1 = (f32[8,4352]{1,0:T(8,128)S(1)}, f32[8,4352]{1,0:T(8,128)S(1)}, u32[]{:S(2)}, u32[]{:S(2)}) collective-permute-start(f32[8,4352]{1,0:T(8,128)S(1)} %fusion.3), channel_id=1, source_target_pairs={{0,16},{16,0},{1,17},{17,1},{2,18},{18,2},{3,19},{19,3},{4,20},{20... | collective-permute-start | bytes 417800 | tf_op jit(solution)/shard_map/ppermute | solution.py:35
  79.3 5.2 %collective-permute-start.2 = (f32[8,4352]{1,0:T(8,128)S(1)}, f32[8,4352]{1,0:T(8,128)S(1)}, u32[]{:S(2)}, u32[]{:S(2)}) collective-permute-start(f32[8,4352]{1,0:T(8,128)S(1)} %add.107), channel_id=1, source_target_pairs={{0,32},{32,0},{64,96},{96,64},{128,160},{160,128},{192,224},{224,1... | collective-permute-start | bytes 417800 | tf_op jit(solution)/shard_map/ppermute | solution.py:35
  84.5 8.5 %collective-permute-start.3 = (f32[8,4352]{1,0:T(8,128)S(1)}, f32[8,4352]{1,0:T(8,128)S(1)}, u32[]{:S(2)}, u32[]{:S(2)}) collective-permute-start(f32[8,4352]{1,0:T(8,128)S(1)} %add.108), channel_id=1, source_target_pairs={{0,64},{32,96},{64,0},{96,32},{128,192},{160,224},{192,128},{224,1... | collective-permute-start | bytes 417800 | tf_op jit(solution)/shard_map/ppermute | solution.py:35
  93.0 10.1 %collective-permute-start.4 = (f32[8,4352]{1,0:T(8,128)S(1)}, f32[8,4352]{1,0:T(8,128)S(1)}, u32[]{:S(2)}, u32[]{:S(2)}) collective-permute-start(f32[8,4352]{1,0:T(8,128)S(1)} %add.109), channel_id=1, source_target_pairs={{0,128},{32,160},{64,192},{96,224},{128,0},{160,32},{192,64},{224,... | collective-permute-start | bytes 417800 | tf_op jit(solution)/shard_map/ppermute | solution.py:35
  105.0 13.6 %all-to-all-start.2 = ((bf16[8,8,256,16]{2,3,1,0:T(8,128)(2,1)}), bf16[8,8,256,16]{2,3,1,0:T(8,128)(2,1)S(1)}, u32[]{:S(2)}, u32[]{:S(2)}) async-start(bf16[8,8,256,16]{2,3,1,0:T(8,128)(2,1)} %broadcast_in_dim.34), calls=%async_computation.2 | async-start | bytes 1048576 | tf_op jit(solution)/shard_map/all_to_all | solution.py:93
  118.6 3.4 %copy-start.3 = (bf16[64,256,128]{2,1,0:T(8,128)(2,1)S(1)}, bf16[64,256,128]{2,1,0:T(8,128)(2,1)}, u32[]{:S(2)}) copy-start(bf16[64,256,128]{2,1,0:T(8,128)(2,1)} %get-tuple-element.6) | copy-start | bytes 12582916
  122.1 2.2 %copy-start.1 = (bf16[64,256,128]{2,1,0:T(8,128)(2,1)S(1)}, bf16[64,256,128]{2,1,0:T(8,128)(2,1)}, u32[]{:S(2)}) copy-start(bf16[64,256,128]{2,1,0:T(8,128)(2,1)} %get-tuple-element.7) | copy-start | bytes 12582916
  125.6 1.6 %collective-permute-start.5 = (f32[16,32,128]{2,1,0:T(8,128)S(1)}, f32[16,32,128]{2,1,0:T(8,128)S(1)}, u32[]{:S(2)}, u32[]{:S(2)}) collective-permute-start(f32[16,32,128]{2,1,0:T(8,128)S(1)} %dynamic-slice_bitcast_fusion), channel_id=1, source_target_pairs={{0,8},{8,0},{1,9},{9,1},{2,10},{10,2},{3,11},{11,3},{4,12},{12,4},... | collective-permute-start | bytes 786440 | tf_op jit(solution)/shard_map/ppermute | solution.py:35
  127.3 5.6 %collective-permute-start.6 = (f32[8,32,128]{2,1,0:T(8,128)S(1)}, f32[8,32,128]{2,1,0:T(8,128)S(1)}, u32[]{:S(2)}, u32[]{:S(2)}) collective-permute-start(f32[8,32,128]{2,1,0:T(8,128)S(1)} %dynamic-slice_bitcast_fusion.1), channel_id=1, source_target_pairs={{0,16},{16,0},{1,17},{17,1},{2,18},{18,2},{3,19},{19,3},{4,20},{20... | collective-permute-start | bytes 393224 | tf_op jit(solution)/shard_map/ppermute | solution.py:35
  132.9 4.4 %collective-permute-start.7 = (f32[4,32,128]{2,1,0:T(8,128)S(1)}, f32[4,32,128]{2,1,0:T(8,128)S(1)}, u32[]{:S(2)}, u32[]{:S(2)}) collective-permute-start(f32[4,32,128]{2,1,0:T(8,128)S(1)} %dynamic-slice_bitcast_fusion.2), channel_id=1, source_target_pairs={{0,32},{32,0},{64,96},{96,64},{128,160},{160,128},{192,224},{224,1... | collective-permute-start | bytes 196616 | tf_op jit(solution)/shard_map/ppermute | solution.py:35
  137.3 5.4 %collective-permute-start.8 = (f32[2,32,128]{2,1,0:T(8,128)S(1)}, f32[2,32,128]{2,1,0:T(8,128)S(1)}, u32[]{:S(2)}, u32[]{:S(2)}) collective-permute-start(f32[2,32,128]{2,1,0:T(8,128)S(1)} %dynamic-slice_bitcast_fusion.3), channel_id=1, source_target_pairs={{0,64},{32,96},{64,0},{96,32},{128,192},{160,224},{192,128},{224,1... | collective-permute-start | bytes 98312 | tf_op jit(solution)/shard_map/ppermute | solution.py:35
  142.8 7.7 %collective-permute-start.9 = (f32[1,32,128]{2,1,0:T(8,128)S(1)}, f32[1,32,128]{2,1,0:T(8,128)S(1)}, u32[]{:S(2)}, u32[]{:S(2)}) collective-permute-start(f32[1,32,128]{2,1,0:T(8,128)S(1)} %constant_dynamic-slice_fusion), channel_id=1, source_target_pairs={{0,128},{32,160},{64,192},{96,224},{128,0},{160,32},{192,64},{224,... | collective-permute-start | bytes 49160 | tf_op jit(solution)/shard_map/ppermute | solution.py:35

commit v10 on v9

--- a/solution.py
+++ b/solution.py
@@ -51,8 +51,9 @@
     return x
 
 
-def means_kernel(codes_ref, vec_ref, hi_ref, mid_ref, lo_ref):
+def means_kernel(codes_ref, vec_ref, out_ref):
     rows = codes_ref.shape[1]
+    width = vec_ref.shape[1]
     kinds = lax.broadcasted_iota(jnp.int32, (K, rows), 0).astype(codes_ref.dtype)
     one = jnp.ones((K, rows), jnp.bfloat16)
     zero = jnp.zeros((K, rows), jnp.bfloat16)
@@ -62,15 +63,14 @@
         hi = h.astype(jnp.bfloat16)
         rest = h - hi.astype(jnp.float32)
         mid = rest.astype(jnp.bfloat16)
-        hi_ref[i] = hi
-        mid_ref[i] = mid
-        lo_ref[i] = (rest - mid.astype(jnp.float32)).astype(jnp.bfloat16)
+        out_ref[i, :, pl.ds(0, width)] = hi
+        out_ref[i, :, pl.ds(width, width)] = mid
+        out_ref[i, :, pl.ds(2 * width, width)] = (rest - mid.astype(jnp.float32)).astype(jnp.bfloat16)
 
 
 def codeword_means(codes_all, vectors):
     m_all, rows = codes_all.shape
     width = vectors.shape[1]
-    out = jax.ShapeDtypeStruct((m_all, K, width), jnp.bfloat16)
     return pl.pallas_call(
         means_kernel,
         grid=(m_all // GROUP,),
@@ -78,8 +78,8 @@
             pl.BlockSpec((GROUP, rows), lambda g: (g, 0)),
             pl.BlockSpec((rows, width), lambda g: (0, 0)),
         ],
-        out_specs=[pl.BlockSpec((GROUP, K, width), lambda g: (g, 0, 0))] * 3,
-        out_shape=[out] * 3,
+        out_specs=pl.BlockSpec((GROUP, K, 3 * width), lambda g: (g, 0, 0)),
+        out_shape=jax.ShapeDtypeStruct((m_all, K, 3 * width), jnp.bfloat16),
         cost_estimate=pl.CostEstimate(
             flops=2 * m_all * K * rows * width,
             transcendentals=0,
@@ -116,9 +116,8 @@
 
     rot3 = rotation.reshape(local, m_all, DS).transpose(1, 0, 2)
     dims = (((2,), (1,)), ((0,), (0,)))
-    partial = sum(
-        lax.dot_general(part, rot3, dims, preferred_element_type=jnp.float32) for part in h_parts
-    )
+    rot3 = jnp.concatenate([rot3] * 3, axis=1)
+    partial = lax.dot_general(h_parts, rot3, dims, preferred_element_type=jnp.float32)
 
     partial = partial.reshape(n_feat, groups, K, DS)
     sums = jnp.sum(
@@ -139,9 +138,8 @@
     table = broadcast_over(cents.astype(jnp.bfloat16), feat_names, n_feat)
     table = table.reshape(m_all, K, DS)
     dims = (((1,), (1,)), ((0,), (0,)))
-    grad = sum(
-        lax.dot_general(table, part, dims, preferred_element_type=jnp.float32) for part in h_parts
-    )
+    grad = lax.dot_general(table, h_parts, dims, preferred_element_type=jnp.float32)
+    grad = grad[..., :local] + grad[..., local : 2 * local] + grad[..., 2 * local :]
     inverse = 1.0 / (rows * n_row)
     grad = grad.reshape(m_all * DS, local) * inverse
 

time: 154 us -> 155 us (level)
  matrix products: 11.3 us -> 15.3 us
  local copies, waits for them, and re-layouts: 9.71 us -> 6.68 us
    dot_general x6 -> x2, matrix products: 11.3 us -> 15.3 us  [the longest x1 9.01 us: shards(): lax.dot_general(h_parts, rot3, dims, preferred_element_type=jnp.float32)]
    unnamed x14 -> x6, local copies, waits for them, and re-layouts: 5.52 us -> 2.52 us
where the time goes in v10:
time: 155 us; the launch traced here: 152 us
  waiting for transfers between devices  55.4 us (36%)
  starting transfers between devices  43.2 us (28%)
  Pallas kernels  25.5 us (16%)
  matrix products  15.3 us (10%)
  local copies, waits for them, and re-layouts  6.68 us (4%)
  other arithmetic  4.54 us (3%)
    ppermute x10, waiting for transfers between devices, exchange(): return lax.ppermute(x, name, pairs)  31.2 us
    pallas_call x1, Pallas kernels, codeword_means(): pl.pallas_call(means_kernel, grid=(m_all // GROUP,), in_specs=[pl.BlockSp...  25.5 us
    ppermute x10, starting transfers between devices, exchange(): return lax.ppermute(x, name, pairs)  23.5 us
    all_to_all x2, starting transfers between devices, broadcast_over(): lax.all_to_all(copies, names, split_axis=0, concat_axis=0, tiled=True)  13.5 us
    all_to_all x2, waiting for transfers between devices, broadcast_over(): lax.all_to_all(copies, names, split_axis=0, concat_axis=0, tiled=True)  13.2 us
    all_to_all x1, waiting for transfers between devices, shards(): lax.all_to_all(partial, feat_names, split_axis=0, concat_axis=0, tiled=True)  11 us
    dot_general x1, matrix products, shards(): lax.dot_general(h_parts, rot3, dims, preferred_element_type=jnp.float32)  9.01 us
    dot_general x1, matrix products, shards(): lax.dot_general(table, h_parts, dims, preferred_element_type=jnp.float32)  6.32 us
  transfers between devices with their start and end apart: 13, of which 13 were waited for; matrix products, arithmetic and copies ran while one was open for 3% of the time, Pallas kernels for 0%

profile of v10, /device:TPU:4, one launch (start us, length us, event | category | flops | bytes accessed | tf_op | source)
XLA Modules:
  0.0 152.2 jit_solution(13981833582406771518)
XLA Ops:
  2.9 7.4 %all-to-all-start = ((bf16[8,8,2560]{2,1,0:T(8,128)(2,1)}), bf16[8,8,2560]{2,1,0:T(8,128)(2,1)S(1)}, u32[]{:S(2)}, u32[]{:S(2)}) async-start(bf16[8,8,2560]{2,1,0:T(8,128)(2,1)} %broadcast_in_dim.20), calls=%async_computation | async-start | bytes 655360 | tf_op jit(solution)/shard_map/all_to_all | solution.py:93
  11.5 5.7 %all-to-all-done = bf16[8,8,2560]{2,1,0:T(8,128)(2,1)S(1)} async-done(((bf16[8,8,2560]{2,1,0:T(8,128)(2,1)}), bf16[8,8,2560]{2,1,0:T(8,128)(2,1)S(1)}, u32[]{:S(2)}, u32[]{:S(2)}) %all-to-all-start) | async-done | bytes 327712 | tf_op jit(solution)/shard_map/all_to_all | solution.py:93
  17.9 25.5 %shard_map.77 = bf16[64,256,384]{2,1,0:T(8,128)(2,1)} custom-call(bf16[64,2560]{1,0:T(8,128)(2,1)} %bitcast.48, bf16[2560,128]{1,0:T(8,128)(2,1)} %vec_ref.1), custom_call_target="tpu_custom_call" | custom-call | flops 10737418240 | bytes 13565952 | tf_op jit(solution)/shard_map/pallas_call | solution.py:74
  43.5 9.0 %fusion = f32[64,256,16]{1,2,0:T(8,128)} fusion(bf16[64,256,384]{2,1,0:T(8,128)(2,1)} %shard_map.77, bf16[64,128,16]{1,2,0:T(8,128)(2,1)S(1)} %bitcast.52), kind=kOutput, calls=%fused_computation.3 | convolution fusion | flops 203685888 | bytes 13893632 | tf_op jit(solution)/shard_map/dot_general | solution.py:120
  52.5 6.1 %all-to-all-start.1 = ((f32[8,8,256,16]{2,3,1,0:T(8,128)}), f32[8,8,256,16]{2,3,1,0:T(8,128)S(1)}, u32[]{:S(2)}, u32[]{:S(2)}) async-start(f32[8,8,256,16]{2,3,1,0:T(8,128)} %bitcast.5), calls=%async_computation.1 | async-start | bytes 2097152 | tf_op jit(solution)/shard_map/all_to_all | solution.py:124
  58.6 2.3 %convert_reduce_fusion = f32[8,256]{1,0:T(8,128)S(1)} fusion(s32[8,2560]{1,0:T(8,128)S(1)} %get-tuple-element.11), kind=kLoop, calls=%fused_computation.1 | loop fusion | flops 15726592 | bytes 90112 | tf_op jit(solution)/shard_map/reduce_sum | solution.py:111
  61.0 11.0 %all-to-all-done.1 = f32[8,8,256,16]{2,3,1,0:T(8,128)S(1)} async-done(((f32[8,8,256,16]{2,3,1,0:T(8,128)}), f32[8,8,256,16]{2,3,1,0:T(8,128)S(1)}, u32[]{:S(2)}, u32[]{:S(2)}) %all-to-all-start.1) | async-done | bytes 1048608 | tf_op jit(solution)/shard_map/all_to_all | solution.py:124
  75.8 4.5 %collective-permute-done.1 = f32[8,4352]{1,0:T(8,128)S(1)} collective-permute-done((f32[8,4352]{1,0:T(8,128)S(1)}, f32[8,4352]{1,0:T(8,128)S(1)}, u32[]{:S(2)}, u32[]{:S(2)}) %collective-permute-start.1) | collective-permute-done | bytes 139296 | tf_op jit(solution)/shard_map/ppermute | solution.py:35
  80.3 2.0 %collective-permute-start.2 = (f32[8,4352]{1,0:T(8,128)S(1)}, f32[8,4352]{1,0:T(8,128)S(1)}, u32[]{:S(2)}, u32[]{:S(2)}) collective-permute-start(f32[8,4352]{1,0:T(8,128)S(1)} %add.99), channel_id=1, source_target_pairs={{0,32},{32,0},{64,96},{96,64},{128,160},{160,128},{192,224},{224,1... | collective-permute-start | bytes 417800 | tf_op jit(solution)/shard_map/ppermute | solution.py:35
  82.3 3.2 %collective-permute-done.2 = f32[8,4352]{1,0:T(8,128)S(1)} collective-permute-done((f32[8,4352]{1,0:T(8,128)S(1)}, f32[8,4352]{1,0:T(8,128)S(1)}, u32[]{:S(2)}, u32[]{:S(2)}) %collective-permute-start.2) | collective-permute-done | bytes 139296 | tf_op jit(solution)/shard_map/ppermute | solution.py:35
  85.5 3.4 %collective-permute-start.3 = (f32[8,4352]{1,0:T(8,128)S(1)}, f32[8,4352]{1,0:T(8,128)S(1)}, u32[]{:S(2)}, u32[]{:S(2)}) collective-permute-start(f32[8,4352]{1,0:T(8,128)S(1)} %add.100), channel_id=1, source_target_pairs={{0,64},{32,96},{64,0},{96,32},{128,192},{160,224},{192,128},{224,1... | collective-permute-start | bytes 417800 | tf_op jit(solution)/shard_map/ppermute | solution.py:35
  88.9 5.2 %collective-permute-done.3 = f32[8,4352]{1,0:T(8,128)S(1)} collective-permute-done((f32[8,4352]{1,0:T(8,128)S(1)}, f32[8,4352]{1,0:T(8,128)S(1)}, u32[]{:S(2)}, u32[]{:S(2)}) %collective-permute-start.3) | collective-permute-done | bytes 139296 | tf_op jit(solution)/shard_map/ppermute | solution.py:35
  94.0 6.7 %collective-permute-start.4 = (f32[8,4352]{1,0:T(8,128)S(1)}, f32[8,4352]{1,0:T(8,128)S(1)}, u32[]{:S(2)}, u32[]{:S(2)}) collective-permute-start(f32[8,4352]{1,0:T(8,128)S(1)} %add.101), channel_id=1, source_target_pairs={{0,128},{32,160},{64,192},{96,224},{128,0},{160,32},{192,64},{224,... | collective-permute-start | bytes 417800 | tf_op jit(solution)/shard_map/ppermute | solution.py:35
  100.7 3.5 %collective-permute-done.4 = f32[8,4352]{1,0:T(8,128)S(1)} collective-permute-done((f32[8,4352]{1,0:T(8,128)S(1)}, f32[8,4352]{1,0:T(8,128)S(1)}, u32[]{:S(2)}, u32[]{:S(2)}) %collective-permute-start.4) | collective-permute-done | bytes 139296 | tf_op jit(solution)/shard_map/ppermute | solution.py:35
  106.0 6.1 %all-to-all-start.2 = ((bf16[8,8,256,16]{2,3,1,0:T(8,128)(2,1)}), bf16[8,8,256,16]{2,3,1,0:T(8,128)(2,1)S(1)}, u32[]{:S(2)}, u32[]{:S(2)}) async-start(bf16[8,8,256,16]{2,3,1,0:T(8,128)(2,1)} %broadcast_in_dim.34), calls=%async_computation.2 | async-start | bytes 1048576 | tf_op jit(solution)/shard_map/all_to_all | solution.py:93
  112.1 7.5 %all-to-all-done.2 = bf16[8,8,256,16]{2,3,1,0:T(8,128)(2,1)S(1)} async-done(((bf16[8,8,256,16]{2,3,1,0:T(8,128)(2,1)}), bf16[8,8,256,16]{2,3,1,0:T(8,128)(2,1)S(1)}, u32[]{:S(2)}, u32[]{:S(2)}) %all-to-all-start.2) | async-done | bytes 524320 | tf_op jit(solution)/shard_map/all_to_all | solution.py:93
  119.6 6.3 %fusion.12 = f32[64,16,384]{2,1,0:T(8,128)S(1)} fusion(bf16[64,256,16]{1,2,0:T(8,128)(2,1)S(1)} %bitcast.40, bf16[64,256,384]{2,1,0:T(8,128)(2,1)} %shard_map.77), kind=kOutput, calls=%fused_computation.34 | convolution fusion | flops 201326592 | bytes 14680064 | tf_op jit(solution)/shard_map/dot_general | solution.py:141
  126.8 1.5 collective-permute-done.5
  129.7 4.3 %collective-permute-done.6 = f32[8,32,128]{2,1,0:T(8,128)S(1)} collective-permute-done((f32[8,32,128]{2,1,0:T(8,128)S(1)}, f32[8,32,128]{2,1,0:T(8,128)S(1)}, u32[]{:S(2)}, u32[]{:S(2)}) %collective-permute-start.6) | collective-permute-done | bytes 131104 | tf_op jit(solution)/shard_map/ppermute | solution.py:35
  134.1 4.2 %collective-permute-done.7 = f32[4,32,128]{2,1,0:T(8,128)S(1)} collective-permute-done((f32[4,32,128]{2,1,0:T(8,128)S(1)}, f32[4,32,128]{2,1,0:T(8,128)S(1)}, u32[]{:S(2)}, u32[]{:S(2)}) %collective-permute-start.7) | collective-permute-done | bytes 65568 | tf_op jit(solution)/shard_map/ppermute | solution.py:35
  138.4 3.5 %collective-permute-start.8 = (f32[2,32,128]{2,1,0:T(8,128)S(1)}, f32[2,32,128]{2,1,0:T(8,128)S(1)}, u32[]{:S(2)}, u32[]{:S(2)}) collective-permute-start(f32[2,32,128]{2,1,0:T(8,128)S(1)} %dynamic-slice_bitcast_fusion.3), channel_id=1, source_target_pairs={{0,64},{32,96},{64,0},{96,32},{128,192},{160,224},{192,128},{224,1... | collective-permute-start | bytes 98312 | tf_op jit(solution)/shard_map/ppermute | solution.py:35
  142.2 1.6 %collective-permute-done.8 = f32[2,32,128]{2,1,0:T(8,128)S(1)} collective-permute-done((f32[2,32,128]{2,1,0:T(8,128)S(1)}, f32[2,32,128]{2,1,0:T(8,128)S(1)}, u32[]{:S(2)}, u32[]{:S(2)}) %collective-permute-start.8) | collective-permute-done | bytes 32800 | tf_op jit(solution)/shard_map/ppermute | solution.py:35
  143.8 5.1 %collective-permute-start.9 = (f32[1,32,128]{2,1,0:T(8,128)S(1)}, f32[1,32,128]{2,1,0:T(8,128)S(1)}, u32[]{:S(2)}, u32[]{:S(2)}) collective-permute-start(f32[1,32,128]{2,1,0:T(8,128)S(1)} %constant_dynamic-slice_fusion), channel_id=1, source_target_pairs={{0,128},{32,160},{64,192},{96,224},{128,0},{160,32},{192,64},{224,... | collective-permute-start | bytes 49160 | tf_op jit(solution)/shard_map/ppermute | solution.py:35
  149.7 1.9 %collective-permute-done.9 = f32[1,32,128]{2,1,0:T(8,128)S(1)} collective-permute-done((f32[1,32,128]{2,1,0:T(8,128)S(1)}, f32[1,32,128]{2,1,0:T(8,128)S(1)}, u32[]{:S(2)}, u32[]{:S(2)}) %collective-permute-start.9) | collective-permute-done | bytes 16416 | tf_op jit(solution)/shard_map/ppermute | solution.py:35
  (45 shorter events, 13.1 us)
Async XLA Ops:
  2.9 14.2 %all-to-all-start = ((bf16[8,8,2560]{2,1,0:T(8,128)(2,1)}), bf16[8,8,2560]{2,1,0:T(8,128)(2,1)S(1)}, u32[]{:S(2)}, u32[]{:S(2)}) async-start(bf16[8,8,2560]{2,1,0:T(8,128)(2,1)} %broadcast_in_dim.20), calls=%async_computation | async-start | bytes 655360 | tf_op jit(solution)/shard_map/all_to_all | solution.py:93
  17.2 0.7 copy-start
  43.5 68.6 %copy-start.1 = (s32[32]{0:T(128)S(1)}, s32[32]{0:T(128)}, u32[]{:S(2)}) copy-start(s32[32]{0:T(128)} %constant.81) | copy-start | bytes 388
  52.5 19.5 %all-to-all-start.1 = ((f32[8,8,256,16]{2,3,1,0:T(8,128)}), f32[8,8,256,16]{2,3,1,0:T(8,128)S(1)}, u32[]{:S(2)}, u32[]{:S(2)}) async-start(f32[8,8,256,16]{2,3,1,0:T(8,128)} %bitcast.5), calls=%async_computation.1 | async-start | bytes 2097152 | tf_op jit(solution)/shard_map/all_to_all | solution.py:124
  73.0 1.4 collective-permute-start
  74.5 5.8 %collective-permute-start.1 = (f32[8,4352]{1,0:T(8,128)S(1)}, f32[8,4352]{1,0:T(8,128)S(1)}, u32[]{:S(2)}, u32[]{:S(2)}) collective-permute-start(f32[8,4352]{1,0:T(8,128)S(1)} %fusion.10), channel_id=1, source_target_pairs={{0,16},{16,0},{1,17},{17,1},{2,18},{18,2},{3,19},{19,3},{4,20},{20... | collective-permute-start | bytes 417800 | tf_op jit(solution)/shard_map/ppermute | solution.py:35
  80.3 5.2 %collective-permute-start.2 = (f32[8,4352]{1,0:T(8,128)S(1)}, f32[8,4352]{1,0:T(8,128)S(1)}, u32[]{:S(2)}, u32[]{:S(2)}) collective-permute-start(f32[8,4352]{1,0:T(8,128)S(1)} %add.99), channel_id=1, source_target_pairs={{0,32},{32,0},{64,96},{96,64},{128,160},{160,128},{192,224},{224,1... | collective-permute-start | bytes 417800 | tf_op jit(solution)/shard_map/ppermute | solution.py:35
  85.5 8.5 %collective-permute-start.3 = (f32[8,4352]{1,0:T(8,128)S(1)}, f32[8,4352]{1,0:T(8,128)S(1)}, u32[]{:S(2)}, u32[]{:S(2)}) collective-permute-start(f32[8,4352]{1,0:T(8,128)S(1)} %add.100), channel_id=1, source_target_pairs={{0,64},{32,96},{64,0},{96,32},{128,192},{160,224},{192,128},{224,1... | collective-permute-start | bytes 417800 | tf_op jit(solution)/shard_map/ppermute | solution.py:35
  94.0 10.1 %collective-permute-start.4 = (f32[8,4352]{1,0:T(8,128)S(1)}, f32[8,4352]{1,0:T(8,128)S(1)}, u32[]{:S(2)}, u32[]{:S(2)}) collective-permute-start(f32[8,4352]{1,0:T(8,128)S(1)} %add.101), channel_id=1, source_target_pairs={{0,128},{32,160},{64,192},{96,224},{128,0},{160,32},{192,64},{224,... | collective-permute-start | bytes 417800 | tf_op jit(solution)/shard_map/ppermute | solution.py:35
  106.0 13.6 %all-to-all-start.2 = ((bf16[8,8,256,16]{2,3,1,0:T(8,128)(2,1)}), bf16[8,8,256,16]{2,3,1,0:T(8,128)(2,1)S(1)}, u32[]{:S(2)}, u32[]{:S(2)}) async-start(bf16[8,8,256,16]{2,3,1,0:T(8,128)(2,1)} %broadcast_in_dim.34), calls=%async_computation.2 | async-start | bytes 1048576 | tf_op jit(solution)/shard_map/all_to_all | solution.py:93
  126.7 1.6 %collective-permute-start.5 = (f32[16,32,128]{2,1,0:T(8,128)S(1)}, f32[16,32,128]{2,1,0:T(8,128)S(1)}, u32[]{:S(2)}, u32[]{:S(2)}) collective-permute-start(f32[16,32,128]{2,1,0:T(8,128)S(1)} %dynamic-slice_bitcast_fusion), channel_id=1, source_target_pairs={{0,8},{8,0},{1,9},{9,1},{2,10},{10,2},{3,11},{11,3},{4,12},{12,4},... | collective-permute-start | bytes 786440 | tf_op jit(solution)/shard_map/ppermute | solution.py:35
  128.3 5.6 %collective-permute-start.6 = (f32[8,32,128]{2,1,0:T(8,128)S(1)}, f32[8,32,128]{2,1,0:T(8,128)S(1)}, u32[]{:S(2)}, u32[]{:S(2)}) collective-permute-start(f32[8,32,128]{2,1,0:T(8,128)S(1)} %dynamic-slice_bitcast_fusion.1), channel_id=1, source_target_pairs={{0,16},{16,0},{1,17},{17,1},{2,18},{18,2},{3,19},{19,3},{4,20},{20... | collective-permute-start | bytes 393224 | tf_op jit(solution)/shard_map/ppermute | solution.py:35
  134.0 4.4 %collective-permute-start.7 = (f32[4,32,128]{2,1,0:T(8,128)S(1)}, f32[4,32,128]{2,1,0:T(8,128)S(1)}, u32[]{:S(2)}, u32[]{:S(2)}) collective-permute-start(f32[4,32,128]{2,1,0:T(8,128)S(1)} %dynamic-slice_bitcast_fusion.2), channel_id=1, source_target_pairs={{0,32},{32,0},{64,96},{96,64},{128,160},{160,128},{192,224},{224,1... | collective-permute-start | bytes 196616 | tf_op jit(solution)/shard_map/ppermute | solution.py:35
  138.4 5.4 %collective-permute-start.8 = (f32[2,32,128]{2,1,0:T(8,128)S(1)}, f32[2,32,128]{2,1,0:T(8,128)S(1)}, u32[]{:S(2)}, u32[]{:S(2)}) collective-permute-start(f32[2,32,128]{2,1,0:T(8,128)S(1)} %dynamic-slice_bitcast_fusion.3), channel_id=1, source_target_pairs={{0,64},{32,96},{64,0},{96,32},{128,192},{160,224},{192,128},{224,1... | collective-permute-start | bytes 98312 | tf_op jit(solution)/shard_map/ppermute | solution.py:35
  143.8 7.7 %collective-permute-start.9 = (f32[1,32,128]{2,1,0:T(8,128)S(1)}, f32[1,32,128]{2,1,0:T(8,128)S(1)}, u32[]{:S(2)}, u32[]{:S(2)}) collective-permute-start(f32[1,32,128]{2,1,0:T(8,128)S(1)} %constant_dynamic-slice_fusion), channel_id=1, source_target_pairs={{0,128},{32,160},{64,192},{96,224},{128,0},{160,32},{192,64},{224,... | collective-permute-start | bytes 49160 | tf_op jit(solution)/shard_map/ppermute | solution.py:35

commit v11 on v10

--- a/solution.py
+++ b/solution.py
@@ -114,10 +114,16 @@
 
     h_parts = codeword_means(codes_all, vectors)
 
-    rot3 = rotation.reshape(local, m_all, DS).transpose(1, 0, 2)
+    n_grp = m_all // groups
+    h_grp = h_parts.reshape(n_grp, groups * K, 3 * local)
+    rot_grp = rotation.reshape(local, n_grp, groups * DS).transpose(1, 0, 2)
+    rot_grp = jnp.concatenate([rot_grp] * 3, axis=1)
     dims = (((2,), (1,)), ((0,), (0,)))
-    rot3 = jnp.concatenate([rot3] * 3, axis=1)
-    partial = lax.dot_general(h_parts, rot3, dims, preferred_element_type=jnp.float32)
+    blocks = lax.dot_general(h_grp, rot_grp, dims, preferred_element_type=jnp.float32)
+    blocks = blocks.reshape(n_grp, groups, K, groups, DS)
+    picks = jnp.arange(groups)
+    partial = blocks[:, picks, :, picks, :]
+    partial = partial.transpose(1, 0, 2, 3).reshape(m_all, K, DS)
 
     partial = partial.reshape(n_feat, groups, K, DS)
     sums = jnp.sum(
@@ -136,9 +142,12 @@
     centroids = lax.dynamic_slice_in_dim(centroids_all, row_index * share, share, 0)
 
     table = broadcast_over(cents.astype(jnp.bfloat16), feat_names, n_feat)
-    table = table.reshape(m_all, K, DS)
-    dims = (((1,), (1,)), ((0,), (0,)))
-    grad = lax.dot_general(table, h_parts, dims, preferred_element_type=jnp.float32)
+    table = table.reshape(n_grp, groups, K, DS)
+    eye = jnp.eye(groups, dtype=jnp.bfloat16)
+    table_bd = table.transpose(0, 1, 3, 2)[:, :, :, None, :] * eye[None, :, None, :, None]
+    table_bd = table_bd.reshape(n_grp, groups * DS, groups * K)
+    dims = (((2,), (1,)), ((0,), (0,)))
+    grad = lax.dot_general(table_bd, h_grp, dims, preferred_element_type=jnp.float32)
     grad = grad[..., :local] + grad[..., local : 2 * local] + grad[..., 2 * local :]
     inverse = 1.0 / (rows * n_row)
     grad = grad.reshape(m_all * DS, local) * inverse

time: 155 us -> 188 us (1.21)
  local copies, waits for them, and re-layouts: 6.68 us -> 35.6 us
  matrix products: 15.3 us -> 20.1 us
    mul x0 -> x3, local copies, waits for them, and re-layouts: none -> 10.3 us  [shards(): table.transpose(0, 1, 3, 2)[:, :, :, None, :] * eye[None, :, None, :, None]]
    unnamed x6 -> x8, local copies, waits for them, and re-layouts: 2.52 us -> 10.1 us
    reshape x0 -> x2, local copies, waits for them, and re-layouts: none -> 5.88 us  [the longest x1 5.7 us: shards(): blocks = blocks.reshape(n_grp, groups, K, groups, DS)]
    dot_general x2, matrix products: 15.3 us -> 20.1 us  [the longest x1 11.8 us: shards(): lax.dot_general(h_grp, rot_grp, dims, preferred_element_type=jnp.float32)]
    gather x0 -> x1, local copies, waits for them, and re-layouts: none -> 4 us  [shards(): partial = blocks[:, picks, :, picks, :]]
where the time goes in v11:
time: 188 us; the launch traced here: 185 us
  waiting for transfers between devices  54.7 us (29%)
  starting transfers between devices  43.5 us (23%)
  local copies, waits for them, and re-layouts  35.6 us (19%)
  Pallas kernels  25.5 us (14%)
  matrix products  20.1 us (11%)
  other arithmetic  4.54 us (2%)
    ppermute x10, waiting for transfers between devices, exchange(): return lax.ppermute(x, name, pairs)  30.9 us
    pallas_call x1, Pallas kernels, codeword_means(): pl.pallas_call(means_kernel, grid=(m_all // GROUP,), in_specs=[pl.BlockSp...  25.5 us
    ppermute x10, starting transfers between devices, exchange(): return lax.ppermute(x, name, pairs)  23.7 us
    all_to_all x2, starting transfers between devices, broadcast_over(): lax.all_to_all(copies, names, split_axis=0, concat_axis=0, tiled=True)  13.5 us
    all_to_all x2, waiting for transfers between devices, broadcast_over(): lax.all_to_all(copies, names, split_axis=0, concat_axis=0, tiled=True)  12.8 us
    dot_general x1, matrix products, shards(): lax.dot_general(h_grp, rot_grp, dims, preferred_element_type=jnp.float32)  11.8 us
    all_to_all x1, waiting for transfers between devices, shards(): lax.all_to_all(partial, feat_names, split_axis=0, concat_axis=0, tiled=True)  11 us
    mul x3, local copies, waits for them, and re-layouts, shards(): table.transpose(0, 1, 3, 2)[:, :, :, None, :] * eye[None, :, None, :, None]  10.3 us
  transfers between devices with their start and end apart: 13, of which 13 were waited for; matrix products, arithmetic and copies ran while one was open for 3% of the time, Pallas kernels for 0%

profile of v11, /device:TPU:4, one launch (start us, length us, event | category | flops | bytes accessed | tf_op | source)
XLA Modules:
  0.0 185.4 jit_solution(14562538933597347951)
XLA Ops:
  2.9 7.4 %all-to-all-start = ((bf16[8,8,2560]{2,1,0:T(8,128)(2,1)}), bf16[8,8,2560]{2,1,0:T(8,128)(2,1)S(1)}, u32[]{:S(2)}, u32[]{:S(2)}) async-start(bf16[8,8,2560]{2,1,0:T(8,128)(2,1)} %broadcast_in_dim.20), calls=%async_computation | async-start | bytes 655360 | tf_op jit(solution)/shard_map/all_to_all | solution.py:93
  11.7 5.5 %all-to-all-done = bf16[8,8,2560]{2,1,0:T(8,128)(2,1)S(1)} async-done(((bf16[8,8,2560]{2,1,0:T(8,128)(2,1)}), bf16[8,8,2560]{2,1,0:T(8,128)(2,1)S(1)}, u32[]{:S(2)}, u32[]{:S(2)}) %all-to-all-start) | async-done | bytes 327712 | tf_op jit(solution)/shard_map/all_to_all | solution.py:93
  17.9 25.5 %shard_map.77 = bf16[64,256,384]{2,1,0:T(8,128)(2,1)} custom-call(bf16[64,2560]{1,0:T(8,128)(2,1)} %bitcast.69, bf16[2560,128]{1,0:T(8,128)(2,1)} %vec_ref.1), custom_call_target="tpu_custom_call" | custom-call | flops 10737418240 | bytes 13565952 | tf_op jit(solution)/shard_map/pallas_call | solution.py:74
  43.5 11.8 %fusion.3 = f32[8,2048,128]{1,2,0:T(8,128)} fusion(bf16[8,2048,384]{2,1,0:T(8,128)(2,1)} %bitcast.53, bf16[8,128,128]{2,1,0:T(8,128)(2,1)S(1)} %bitcast.66), kind=kOutput, calls=%fused_computation.7 | convolution fusion | flops 1612972032 | bytes 21233664 | tf_op jit(solution)/shard_map/dot_general | solution.py:122
  55.3 7.5 %copy.45 = f32[128,8,8,256]{3,2,1,0:T(8,128)S(1)} copy(f32[128,8,8,256]{3,1,2,0:T(8,128)} %bitcast.56) | data formatting | bytes 16777216
  62.8 5.7 %copy.36 = f32[8,8,256,8,16]{2,4,3,1,0:T(8,128)} copy(f32[8,8,256,8,16]{2,1,4,3,0:T(8,128)S(1)} %bitcast.55) | data formatting | bytes 16777216 | tf_op jit(solution)/shard_map/reshape | solution.py:123
  68.5 4.0 %gather_fusion = f32[8,8,256,16]{2,3,1,0:T(8,128)S(1)} fusion(f32[8,8,256,8,16]{2,4,3,1,0:T(8,128)} %copy.36, s32[8]{0:T(128)S(1)} %or_bitcast_fusion), kind=kCustom, calls=%fused_computation | custom fusion | bytes 2097216 | tf_op jit(solution)/shard_map/gather | solution.py:125
  73.6 6.3 %all-to-all-start.1 = ((f32[8,8,256,16]{2,3,1,0:T(8,128)}), f32[8,8,256,16]{2,3,1,0:T(8,128)S(1)}, u32[]{:S(2)}, u32[]{:S(2)}) async-start(f32[8,8,256,16]{2,3,1,0:T(8,128)} %copy.37), calls=%async_computation.1 | async-start | bytes 2097152 | tf_op jit(solution)/shard_map/all_to_all | solution.py:130
  82.2 11.0 %all-to-all-done.1 = f32[8,8,256,16]{2,3,1,0:T(8,128)S(1)} async-done(((f32[8,8,256,16]{2,3,1,0:T(8,128)}), f32[8,8,256,16]{2,3,1,0:T(8,128)S(1)}, u32[]{:S(2)}, u32[]{:S(2)}) %all-to-all-start.1) | async-done | bytes 1048608 | tf_op jit(solution)/shard_map/all_to_all | solution.py:130
  97.1 4.5 %collective-permute-done.1 = f32[8,4352]{1,0:T(8,128)S(1)} collective-permute-done((f32[8,4352]{1,0:T(8,128)S(1)}, f32[8,4352]{1,0:T(8,128)S(1)}, u32[]{:S(2)}, u32[]{:S(2)}) %collective-permute-start.1) | collective-permute-done | bytes 139296 | tf_op jit(solution)/shard_map/ppermute | solution.py:35
  103.6 3.2 %collective-permute-done.2 = f32[8,4352]{1,0:T(8,128)S(1)} collective-permute-done((f32[8,4352]{1,0:T(8,128)S(1)}, f32[8,4352]{1,0:T(8,128)S(1)}, u32[]{:S(2)}, u32[]{:S(2)}) %collective-permute-start.2) | collective-permute-done | bytes 139296 | tf_op jit(solution)/shard_map/ppermute | solution.py:35
  106.8 3.4 %collective-permute-start.3 = (f32[8,4352]{1,0:T(8,128)S(1)}, f32[8,4352]{1,0:T(8,128)S(1)}, u32[]{:S(2)}, u32[]{:S(2)}) collective-permute-start(f32[8,4352]{1,0:T(8,128)S(1)} %add.102), channel_id=1, source_target_pairs={{0,64},{32,96},{64,0},{96,32},{128,192},{160,224},{192,128},{224,1... | collective-permute-start | bytes 417800 | tf_op jit(solution)/shard_map/ppermute | solution.py:35
  110.2 5.2 %collective-permute-done.3 = f32[8,4352]{1,0:T(8,128)S(1)} collective-permute-done((f32[8,4352]{1,0:T(8,128)S(1)}, f32[8,4352]{1,0:T(8,128)S(1)}, u32[]{:S(2)}, u32[]{:S(2)}) %collective-permute-start.3) | collective-permute-done | bytes 139296 | tf_op jit(solution)/shard_map/ppermute | solution.py:35
  115.3 6.5 %collective-permute-start.4 = (f32[8,4352]{1,0:T(8,128)S(1)}, f32[8,4352]{1,0:T(8,128)S(1)}, u32[]{:S(2)}, u32[]{:S(2)}) collective-permute-start(f32[8,4352]{1,0:T(8,128)S(1)} %add.103), channel_id=1, source_target_pairs={{0,128},{32,160},{64,192},{96,224},{128,0},{160,32},{192,64},{224,... | collective-permute-start | bytes 417800 | tf_op jit(solution)/shard_map/ppermute | solution.py:35
  121.8 3.4 %collective-permute-done.4 = f32[8,4352]{1,0:T(8,128)S(1)} collective-permute-done((f32[8,4352]{1,0:T(8,128)S(1)}, f32[8,4352]{1,0:T(8,128)S(1)}, u32[]{:S(2)}, u32[]{:S(2)}) %collective-permute-start.4) | collective-permute-done | bytes 139296 | tf_op jit(solution)/shard_map/ppermute | solution.py:35
  127.1 6.1 %all-to-all-start.2 = ((bf16[8,8,256,16]{2,3,1,0:T(8,128)(2,1)}), bf16[8,8,256,16]{2,3,1,0:T(8,128)(2,1)S(1)}, u32[]{:S(2)}, u32[]{:S(2)}) async-start(bf16[8,8,256,16]{2,3,1,0:T(8,128)(2,1)} %broadcast_in_dim.21), calls=%async_computation.2 | async-start | bytes 1048576 | tf_op jit(solution)/shard_map/all_to_all | solution.py:93
  133.4 7.3 %all-to-all-done.2 = bf16[8,8,256,16]{2,3,1,0:T(8,128)(2,1)S(1)} async-done(((bf16[8,8,256,16]{2,3,1,0:T(8,128)(2,1)}), bf16[8,8,256,16]{2,3,1,0:T(8,128)(2,1)S(1)}, u32[]{:S(2)}, u32[]{:S(2)}) %all-to-all-start.2) | async-done | bytes 524320 | tf_op jit(solution)/shard_map/all_to_all | solution.py:93
  140.7 2.8 %mul.42 = bf16[8,8,16,8,256]{4,3,2,1,0:T(8,128)(2,1)} broadcast(bf16[8,8,16,256]{3,2,1,0:T(8,128)(2,1)S(1)} %bitcast.58), dimensions={0,1,2,4} | broadcast | bytes 4718592 | tf_op jit(solution)/shard_map/mul | solution.py:147
  143.5 7.4 %mul.43 = bf16[8,128,2048]{2,1,0:T(8,128)(2,1)} reshape(bf16[8,8,16,8,256]{4,3,2,1,0:T(8,128)(2,1)} %mul.42) | data formatting | bytes 8388608 | tf_op jit(solution)/shard_map/mul | solution.py:147
  150.9 8.2 %fusion = f32[8,128,384]{2,1,0:T(8,128)S(1)} fusion(bf16[8,2048,384]{2,1,0:T(8,128)(2,1)} %bitcast.54, bf16[8,128,2048]{2,1,0:T(8,128)(2,1)} %mul.43, bf16[128,2048]{1,0:T(8,128)(2,1)S(1)} %bitcast.57), kind=kOutput, calls=%fused_computation.4 | convolution fusion | flops 1612709888 | bytes 18874368 | tf_op jit(solution)/shard_map/dot_general | solution.py:150
  162.9 4.3 %collective-permute-done.6 = f32[8,32,128]{2,1,0:T(8,128)S(1)} collective-permute-done((f32[8,32,128]{2,1,0:T(8,128)S(1)}, f32[8,32,128]{2,1,0:T(8,128)S(1)}, u32[]{:S(2)}, u32[]{:S(2)}) %collective-permute-start.6) | collective-permute-done | bytes 131104 | tf_op jit(solution)/shard_map/ppermute | solution.py:35
  167.3 4.2 %collective-permute-done.7 = f32[4,32,128]{2,1,0:T(8,128)S(1)} collective-permute-done((f32[4,32,128]{2,1,0:T(8,128)S(1)}, f32[4,32,128]{2,1,0:T(8,128)S(1)}, u32[]{:S(2)}, u32[]{:S(2)}) %collective-permute-start.7) | collective-permute-done | bytes 65568 | tf_op jit(solution)/shard_map/ppermute | solution.py:35
  171.6 3.5 %collective-permute-start.8 = (f32[2,32,128]{2,1,0:T(8,128)S(1)}, f32[2,32,128]{2,1,0:T(8,128)S(1)}, u32[]{:S(2)}, u32[]{:S(2)}) collective-permute-start(f32[2,32,128]{2,1,0:T(8,128)S(1)} %dynamic-slice_bitcast_fusion.3), channel_id=1, source_target_pairs={{0,64},{32,96},{64,0},{96,32},{128,192},{160,224},{192,128},{224,1... | collective-permute-start | bytes 98312 | tf_op jit(solution)/shard_map/ppermute | solution.py:35
  177.0 5.4 %collective-permute-start.9 = (f32[1,32,128]{2,1,0:T(8,128)S(1)}, f32[1,32,128]{2,1,0:T(8,128)S(1)}, u32[]{:S(2)}, u32[]{:S(2)}) collective-permute-start(f32[1,32,128]{2,1,0:T(8,128)S(1)} %constant_dynamic-slice_fusion), channel_id=1, source_target_pairs={{0,128},{32,160},{64,192},{96,224},{128,0},{160,32},{192,64},{224,... | collective-permute-start | bytes 49160 | tf_op jit(solution)/shard_map/ppermute | solution.py:35
  (56 shorter events, 23.7 us)
Async XLA Ops:
  2.9 14.2 %all-to-all-start = ((bf16[8,8,2560]{2,1,0:T(8,128)(2,1)}), bf16[8,8,2560]{2,1,0:T(8,128)(2,1)S(1)}, u32[]{:S(2)}, u32[]{:S(2)}) async-start(bf16[8,8,2560]{2,1,0:T(8,128)(2,1)} %broadcast_in_dim.20), calls=%async_computation | async-start | bytes 655360 | tf_op jit(solution)/shard_map/all_to_all | solution.py:93
  17.2 0.7 copy-start
  73.6 59.8 %copy-start.1 = (s32[32]{0:T(128)S(1)}, s32[32]{0:T(128)}, u32[]{:S(2)}) copy-start(s32[32]{0:T(128)} %constant.97) | copy-start | bytes 388
  73.6 19.6 %all-to-all-start.1 = ((f32[8,8,256,16]{2,3,1,0:T(8,128)}), f32[8,8,256,16]{2,3,1,0:T(8,128)S(1)}, u32[]{:S(2)}, u32[]{:S(2)}) async-start(f32[8,8,256,16]{2,3,1,0:T(8,128)} %copy.37), calls=%async_computation.1 | async-start | bytes 2097152 | tf_op jit(solution)/shard_map/all_to_all | solution.py:130
  94.3 1.4 collective-permute-start
  95.8 5.8 %collective-permute-start.1 = (f32[8,4352]{1,0:T(8,128)S(1)}, f32[8,4352]{1,0:T(8,128)S(1)}, u32[]{:S(2)}, u32[]{:S(2)}) collective-permute-start(f32[8,4352]{1,0:T(8,128)S(1)} %fusion.14), channel_id=1, source_target_pairs={{0,16},{16,0},{1,17},{17,1},{2,18},{18,2},{3,19},{19,3},{4,20},{20... | collective-permute-start | bytes 417800 | tf_op jit(solution)/shard_map/ppermute | solution.py:35
  101.6 5.2 %collective-permute-start.2 = (f32[8,4352]{1,0:T(8,128)S(1)}, f32[8,4352]{1,0:T(8,128)S(1)}, u32[]{:S(2)}, u32[]{:S(2)}) collective-permute-start(f32[8,4352]{1,0:T(8,128)S(1)} %add.101), channel_id=1, source_target_pairs={{0,32},{32,0},{64,96},{96,64},{128,160},{160,128},{192,224},{224,1... | collective-permute-start | bytes 417800 | tf_op jit(solution)/shard_map/ppermute | solution.py:35
  106.8 8.5 %collective-permute-start.3 = (f32[8,4352]{1,0:T(8,128)S(1)}, f32[8,4352]{1,0:T(8,128)S(1)}, u32[]{:S(2)}, u32[]{:S(2)}) collective-permute-start(f32[8,4352]{1,0:T(8,128)S(1)} %add.102), channel_id=1, source_target_pairs={{0,64},{32,96},{64,0},{96,32},{128,192},{160,224},{192,128},{224,1... | collective-permute-start | bytes 417800 | tf_op jit(solution)/shard_map/ppermute | solution.py:35
  115.3 9.9 %collective-permute-start.4 = (f32[8,4352]{1,0:T(8,128)S(1)}, f32[8,4352]{1,0:T(8,128)S(1)}, u32[]{:S(2)}, u32[]{:S(2)}) collective-permute-start(f32[8,4352]{1,0:T(8,128)S(1)} %add.103), channel_id=1, source_target_pairs={{0,128},{32,160},{64,192},{96,224},{128,0},{160,32},{192,64},{224,... | collective-permute-start | bytes 417800 | tf_op jit(solution)/shard_map/ppermute | solution.py:35
  127.1 13.6 %all-to-all-start.2 = ((bf16[8,8,256,16]{2,3,1,0:T(8,128)(2,1)}), bf16[8,8,256,16]{2,3,1,0:T(8,128)(2,1)S(1)}, u32[]{:S(2)}, u32[]{:S(2)}) async-start(bf16[8,8,256,16]{2,3,1,0:T(8,128)(2,1)} %broadcast_in_dim.21), calls=%async_computation.2 | async-start | bytes 1048576 | tf_op jit(solution)/shard_map/all_to_all | solution.py:93
  159.8 1.6 collective-permute-start.5
  161.5 5.6 %collective-permute-start.6 = (f32[8,32,128]{2,1,0:T(8,128)S(1)}, f32[8,32,128]{2,1,0:T(8,128)S(1)}, u32[]{:S(2)}, u32[]{:S(2)}) collective-permute-start(f32[8,32,128]{2,1,0:T(8,128)S(1)} %dynamic-slice_bitcast_fusion.1), channel_id=1, source_target_pairs={{0,16},{16,0},{1,17},{17,1},{2,18},{18,2},{3,19},{19,3},{4,20},{20... | collective-permute-start | bytes 393224 | tf_op jit(solution)/shard_map/ppermute | solution.py:35
  167.2 4.4 %collective-permute-start.7 = (f32[4,32,128]{2,1,0:T(8,128)S(1)}, f32[4,32,128]{2,1,0:T(8,128)S(1)}, u32[]{:S(2)}, u32[]{:S(2)}) collective-permute-start(f32[4,32,128]{2,1,0:T(8,128)S(1)} %dynamic-slice_bitcast_fusion.2), channel_id=1, source_target_pairs={{0,32},{32,0},{64,96},{96,64},{128,160},{160,128},{192,224},{224,1... | collective-permute-start | bytes 196616 | tf_op jit(solution)/shard_map/ppermute | solution.py:35
  171.6 5.4 %collective-permute-start.8 = (f32[2,32,128]{2,1,0:T(8,128)S(1)}, f32[2,32,128]{2,1,0:T(8,128)S(1)}, u32[]{:S(2)}, u32[]{:S(2)}) collective-permute-start(f32[2,32,128]{2,1,0:T(8,128)S(1)} %dynamic-slice_bitcast_fusion.3), channel_id=1, source_target_pairs={{0,64},{32,96},{64,0},{96,32},{128,192},{160,224},{192,128},{224,1... | collective-permute-start | bytes 98312 | tf_op jit(solution)/shard_map/ppermute | solution.py:35
  177.0 7.7 %collective-permute-start.9 = (f32[1,32,128]{2,1,0:T(8,128)S(1)}, f32[1,32,128]{2,1,0:T(8,128)S(1)}, u32[]{:S(2)}, u32[]{:S(2)}) collective-permute-start(f32[1,32,128]{2,1,0:T(8,128)S(1)} %constant_dynamic-slice_fusion), channel_id=1, source_target_pairs={{0,128},{32,160},{64,192},{96,224},{128,0},{160,32},{192,64},{224,... | collective-permute-start | bytes 49160 | tf_op jit(solution)/shard_map/ppermute | solution.py:35

commit v12 on v9

--- a/solution.py
+++ b/solution.py
@@ -35,13 +35,40 @@
     return lax.ppermute(x, name, pairs)
 
 
+def pair_quad(steps):
+    if len(steps) >= 2 and steps[0][2] == 2 and steps[1][2] == 2:
+        return (steps[1][0], steps[0][0]), steps[2:]
+    return None, steps
+
+
+def quad_perm(flip):
+    return [(i, i ^ flip) for i in range(4)]
+
+
 def row_psum(x, steps):
+    quad, steps = pair_quad(steps)
+    if quad is not None:
+        inner = lax.ppermute(x, quad, quad_perm(1))
+        outer = lax.ppermute(x, quad, quad_perm(2))
+        both = lax.ppermute(x, quad, quad_perm(3))
+        x = (x + inner) + (outer + both)
     for name, bit, size in steps:
         x = x + exchange(x, name, bit, size)
     return x
 
 
 def row_psum_scatter(x, steps):
+    quad, steps = pair_quad(steps)
+    if quad is not None:
+        quarters = x.reshape((4, x.shape[0] // 4) + x.shape[1:])
+        inner_bit = lax.axis_index(quad[1]) & 1
+        outer_bit = lax.axis_index(quad[0]) & 1
+        def quarter(i, o):
+            return lax.dynamic_index_in_dim(quarters, i * 2 + o, 0, keepdims=False)
+        x = quarter(inner_bit, outer_bit)
+        x = x + lax.ppermute(quarter(1 - inner_bit, outer_bit), quad, quad_perm(1))
+        x = x + lax.ppermute(quarter(inner_bit, 1 - outer_bit), quad, quad_perm(2))
+        x = x + lax.ppermute(quarter(1 - inner_bit, 1 - outer_bit), quad, quad_perm(3))
     for name, bit, size in steps:
         halves = x.reshape((2, x.shape[0] // 2) + x.shape[1:])
         mine = axis_bit(name, bit)

time: 154 us -> 159 us (1.032)
  waiting for transfers between devices: 55.4 us -> 63.7 us
  starting transfers between devices: 43.2 us -> 41.2 us
    ppermute x0 -> x6, waiting for transfers between devices: none -> 11.6 us  [the longest x1 3.93 us: row_psum_scatter(): lax.ppermute(quarter(1 - inner_bit, 1 - outer_bit), quad, quad_perm(3))]
    ppermute x10 -> x6, starting transfers between devices: 23.5 us -> 17.8 us  [exchange(): return lax.ppermute(x, name, pairs)]
    ppermute x0 -> x6, starting transfers between devices: none -> 4.17 us  [the longest x1 1.49 us: row_psum_scatter(): x = x + lax.ppermute(quarter(inner_bit, 1 - outer_bit), quad, quad_perm(2))]
    ppermute x10 -> x6, waiting for transfers between devices: 31.2 us -> 27.8 us  [exchange(): return lax.ppermute(x, name, pairs)]
  transfers between devices with their start and end apart: 13 -> 15, of which waited for: 13 -> 13; matrix products, arithmetic and copies ran while one was open for 3% -> 3% of each run, Pallas kernels for 0% -> 0%
where the time goes in v12:
time: 159 us; the launch traced here: 157 us
  waiting for transfers between devices  63.7 us (40%)
  starting transfers between devices  41.2 us (26%)
  Pallas kernels  25.5 us (16%)
  matrix products  11.3 us (7%)
  local copies, waits for them, and re-layouts  9.7 us (6%)
  other arithmetic  4.44 us (3%)
    ppermute x6, waiting for transfers between devices, exchange(): return lax.ppermute(x, name, pairs)  27.8 us
    pallas_call x1, Pallas kernels, codeword_means(): pl.pallas_call(means_kernel, grid=(m_all // GROUP,), in_specs=[pl.BlockSp...  25.5 us
    ppermute x6, starting transfers between devices, exchange(): return lax.ppermute(x, name, pairs)  17.8 us
    all_to_all x2, waiting for transfers between devices, broadcast_over(): lax.all_to_all(copies, names, split_axis=0, concat_axis=0, tiled=True)  13.2 us
    all_to_all x2, starting transfers between devices, broadcast_over(): lax.all_to_all(copies, names, split_axis=0, concat_axis=0, tiled=True)  13.2 us
    all_to_all x1, waiting for transfers between devices, shards(): lax.all_to_all(partial, feat_names, split_axis=0, concat_axis=0, tiled=True)  11 us
    dot_general x3, matrix products, shards(): lax.dot_general(part, rot3, dims, preferred_element_type=jnp.float32)  6.98 us
    all_to_all x1, starting transfers between devices, shards(): lax.all_to_all(partial, feat_names, split_axis=0, concat_axis=0, tiled=True)  6.13 us
  transfers between devices with their start and end apart: 15, of which 13 were waited for; matrix products, arithmetic and copies ran while one was open for 3% of the time, Pallas kernels for 0%

profile of v12, /device:TPU:4, one launch (start us, length us, event | category | flops | bytes accessed | tf_op | source)
XLA Modules:
  0.0 157.4 jit_solution(17654417272109572915)
XLA Ops:
  2.9 7.4 %all-to-all-start = ((bf16[8,8,2560]{2,1,0:T(8,128)(2,1)}), bf16[8,8,2560]{2,1,0:T(8,128)(2,1)S(1)}, u32[]{:S(2)}, u32[]{:S(2)}) async-start(bf16[8,8,2560]{2,1,0:T(8,128)(2,1)} %broadcast_in_dim.20), calls=%async_computation | async-start | bytes 655360 | tf_op jit(solution)/shard_map/all_to_all | solution.py:120
  11.5 5.7 %all-to-all-done = bf16[8,8,2560]{2,1,0:T(8,128)(2,1)S(1)} async-done(((bf16[8,8,2560]{2,1,0:T(8,128)(2,1)}), bf16[8,8,2560]{2,1,0:T(8,128)(2,1)S(1)}, u32[]{:S(2)}, u32[]{:S(2)}) %all-to-all-start) | async-done | bytes 327712 | tf_op jit(solution)/shard_map/all_to_all | solution.py:120
  17.9 25.5 %shard_map.77 = (bf16[64,256,128]{2,1,0:T(8,128)(2,1)}, bf16[64,256,128]{2,1,0:T(8,128)(2,1)}, bf16[64,256,128]{2,1,0:T(8,128)(2,1)}) custom-call(bf16[64,2560]{1,0:T(8,128)(2,1)} %bitcast.63, bf16[2560,128]{1,0:T(8,128)(2,1)} %vec_ref.1), custom_call_target="tpu_custom_call" | custom-call | flops 10737418240 | bytes 13565952 | tf_op jit(solution)/shard_map/pallas_call | solution.py:101
  43.5 3.5 %fusion.6 = f32[64,256,16]{1,2,0:T(8,128)S(1)} fusion(bf16[64,256,128]{2,1,0:T(8,128)(2,1)} %get-tuple-element.5, bf16[64,128,16]{1,2,0:T(8,128)(2,1)S(1)} %bitcast.55), kind=kOutput, calls=%fused_computation.31 | convolution fusion | flops 67108864 | bytes 5505024 | tf_op jit(solution)/shard_map/dot_general | solution.py:147
  49.2 2.2 %convolution_add_fusion = f32[64,256,16]{1,2,0:T(8,128)} fusion(f32[64,256,16]{1,2,0:T(8,128)S(1)} %convolution_add_fusion.1, bf16[64,256,128]{2,1,0:T(8,128)(2,1)S(1)} %copy-done, bf16[64,128,16]{1,2,0:T(8,128)(2,1)S(1)} %bitcast.57), kind=kOutput, calls=%fused_computation.3 | convolution fusion | flops 67371008 | bytes 6553600 | tf_op jit(solution)/shard_map/dot_general | solution.py:147
  51.5 6.1 %all-to-all-start.1 = ((f32[8,8,256,16]{2,3,1,0:T(8,128)}), f32[8,8,256,16]{2,3,1,0:T(8,128)S(1)}, u32[]{:S(2)}, u32[]{:S(2)}) async-start(f32[8,8,256,16]{2,3,1,0:T(8,128)} %bitcast.6), calls=%async_computation.1 | async-start | bytes 2097152 | tf_op jit(solution)/shard_map/all_to_all | solution.py:152
  57.6 2.3 %convert_reduce_fusion = f32[8,256]{1,0:T(8,128)S(1)} fusion(s32[8,2560]{1,0:T(8,128)S(1)} %get-tuple-element.17), kind=kLoop, calls=%fused_computation.1 | loop fusion | flops 15726592 | bytes 90112 | tf_op jit(solution)/shard_map/reduce_sum | solution.py:138
  59.9 11.0 %all-to-all-done.1 = f32[8,8,256,16]{2,3,1,0:T(8,128)S(1)} async-done(((f32[8,8,256,16]{2,3,1,0:T(8,128)}), f32[8,8,256,16]{2,3,1,0:T(8,128)S(1)}, u32[]{:S(2)}, u32[]{:S(2)}) %all-to-all-start.1) | async-done | bytes 1048608 | tf_op jit(solution)/shard_map/all_to_all | solution.py:152
  74.2 3.8 %collective-permute-done.1 = f32[8,4352]{1,0:T(8,128)S(1)} collective-permute-done((f32[8,4352]{1,0:T(8,128)S(1)}, f32[8,4352]{1,0:T(8,128)S(1)}, u32[]{:S(2)}, u32[]{:S(2)}) %collective-permute-start.1) | collective-permute-done | bytes 139296 | tf_op jit(solution)/shard_map/ppermute | solution.py:52
  79.3 2.0 %collective-permute-start.3 = (f32[8,4352]{1,0:T(8,128)S(1)}, f32[8,4352]{1,0:T(8,128)S(1)}, u32[]{:S(2)}, u32[]{:S(2)}) collective-permute-start(f32[8,4352]{1,0:T(8,128)S(1)} %add_add_fusion), channel_id=1, source_target_pairs={{0,32},{32,0},{64,96},{96,64},{128,160},{160,128},{192,224},{224,1... | collective-permute-start | bytes 417800 | tf_op jit(solution)/shard_map/ppermute | solution.py:35
  81.3 4.6 %collective-permute-done.3 = f32[8,4352]{1,0:T(8,128)S(1)} collective-permute-done((f32[8,4352]{1,0:T(8,128)S(1)}, f32[8,4352]{1,0:T(8,128)S(1)}, u32[]{:S(2)}, u32[]{:S(2)}) %collective-permute-start.3) | collective-permute-done | bytes 139296 | tf_op jit(solution)/shard_map/ppermute | solution.py:35
  85.9 3.4 %collective-permute-start.4 = (f32[8,4352]{1,0:T(8,128)S(1)}, f32[8,4352]{1,0:T(8,128)S(1)}, u32[]{:S(2)}, u32[]{:S(2)}) collective-permute-start(f32[8,4352]{1,0:T(8,128)S(1)} %add.124), channel_id=1, source_target_pairs={{0,64},{32,96},{64,0},{96,32},{128,192},{160,224},{192,128},{224,1... | collective-permute-start | bytes 417800 | tf_op jit(solution)/shard_map/ppermute | solution.py:35
  89.2 6.9 %collective-permute-done.4 = f32[8,4352]{1,0:T(8,128)S(1)} collective-permute-done((f32[8,4352]{1,0:T(8,128)S(1)}, f32[8,4352]{1,0:T(8,128)S(1)}, u32[]{:S(2)}, u32[]{:S(2)}) %collective-permute-start.4) | collective-permute-done | bytes 139296 | tf_op jit(solution)/shard_map/ppermute | solution.py:35
  96.1 6.5 %collective-permute-start.5 = (f32[8,4352]{1,0:T(8,128)S(1)}, f32[8,4352]{1,0:T(8,128)S(1)}, u32[]{:S(2)}, u32[]{:S(2)}) collective-permute-start(f32[8,4352]{1,0:T(8,128)S(1)} %add.125), channel_id=1, source_target_pairs={{0,128},{32,160},{64,192},{96,224},{128,0},{160,32},{192,64},{224,... | collective-permute-start | bytes 417800 | tf_op jit(solution)/shard_map/ppermute | solution.py:35
  102.6 6.4 %collective-permute-done.5 = f32[8,4352]{1,0:T(8,128)S(1)} collective-permute-done((f32[8,4352]{1,0:T(8,128)S(1)}, f32[8,4352]{1,0:T(8,128)S(1)}, u32[]{:S(2)}, u32[]{:S(2)}) %collective-permute-start.5) | collective-permute-done | bytes 139296 | tf_op jit(solution)/shard_map/ppermute | solution.py:35
  110.8 5.8 %all-to-all-start.2 = ((bf16[8,8,256,16]{2,3,1,0:T(8,128)(2,1)}), bf16[8,8,256,16]{2,3,1,0:T(8,128)(2,1)S(1)}, u32[]{:S(2)}, u32[]{:S(2)}) async-start(bf16[8,8,256,16]{2,3,1,0:T(8,128)(2,1)} %broadcast_in_dim.34), calls=%async_computation.2 | async-start | bytes 1048576 | tf_op jit(solution)/shard_map/all_to_all | solution.py:120
  116.6 7.5 %all-to-all-done.2 = bf16[8,8,256,16]{2,3,1,0:T(8,128)(2,1)S(1)} async-done(((bf16[8,8,256,16]{2,3,1,0:T(8,128)(2,1)}), bf16[8,8,256,16]{2,3,1,0:T(8,128)(2,1)S(1)}, u32[]{:S(2)}, u32[]{:S(2)}) %all-to-all-start.2) | async-done | bytes 524320 | tf_op jit(solution)/shard_map/all_to_all | solution.py:120
  124.1 3.0 %fusion.7 = f32[64,16,128]{2,1,0:T(8,128)S(1)} fusion(bf16[64,256,16]{1,2,0:T(8,128)(2,1)S(1)} %bitcast.52, bf16[64,256,128]{2,1,0:T(8,128)(2,1)} %get-tuple-element.5), kind=kOutput, calls=%fused_computation.32 | convolution fusion | flops 67108864 | bytes 5242880 | tf_op jit(solution)/shard_map/dot_general | solution.py:170
  133.0 3.9 %collective-permute-done.8 = f32[8,32,128]{2,1,0:T(8,128)S(1)} collective-permute-done((f32[8,32,128]{2,1,0:T(8,128)S(1)}, f32[8,32,128]{2,1,0:T(8,128)S(1)}, u32[]{:S(2)}, u32[]{:S(2)}) %collective-permute-start.8) | collective-permute-done | bytes 131104 | tf_op jit(solution)/shard_map/ppermute | solution.py:71
  137.0 2.7 %collective-permute-done.7 = f32[8,32,128]{2,1,0:T(8,128)S(1)} collective-permute-done((f32[8,32,128]{2,1,0:T(8,128)S(1)}, f32[8,32,128]{2,1,0:T(8,128)S(1)}, u32[]{:S(2)}, u32[]{:S(2)}) %collective-permute-start.7) | collective-permute-done | bytes 131104 | tf_op jit(solution)/shard_map/ppermute | solution.py:70
  139.9 4.2 %collective-permute-done.9 = f32[4,32,128]{2,1,0:T(8,128)S(1)} collective-permute-done((f32[4,32,128]{2,1,0:T(8,128)S(1)}, f32[4,32,128]{2,1,0:T(8,128)S(1)}, u32[]{:S(2)}, u32[]{:S(2)}) %collective-permute-start.9) | collective-permute-done | bytes 65568 | tf_op jit(solution)/shard_map/ppermute | solution.py:35
  144.1 2.8 %collective-permute-start.10 = (f32[2,32,128]{2,1,0:T(8,128)S(1)}, f32[2,32,128]{2,1,0:T(8,128)S(1)}, u32[]{:S(2)}, u32[]{:S(2)}) collective-permute-start(f32[2,32,128]{2,1,0:T(8,128)S(1)} %dynamic-slice_bitcast_fusion.4), channel_id=1, source_target_pairs={{0,64},{32,96},{64,0},{96,32},{128,192},{160,224},{192,128},{224,1... | collective-permute-start | bytes 98312 | tf_op jit(solution)/shard_map/ppermute | solution.py:35
  149.0 3.0 %collective-permute-start.11 = (f32[1,32,128]{2,1,0:T(8,128)S(1)}, f32[1,32,128]{2,1,0:T(8,128)S(1)}, u32[]{:S(2)}, u32[]{:S(2)}) collective-permute-start(f32[1,32,128]{2,1,0:T(8,128)S(1)} %constant_dynamic-slice_fusion), channel_id=1, source_target_pairs={{0,128},{32,160},{64,192},{96,224},{128,0},{160,32},{192,64},{224,... | collective-permute-start | bytes 49160 | tf_op jit(solution)/shard_map/ppermute | solution.py:35
  152.8 4.0 %collective-permute-done.11 = f32[1,32,128]{2,1,0:T(8,128)S(1)} collective-permute-done((f32[1,32,128]{2,1,0:T(8,128)S(1)}, f32[1,32,128]{2,1,0:T(8,128)S(1)}, u32[]{:S(2)}, u32[]{:S(2)}) %collective-permute-start.11) | collective-permute-done | bytes 16416 | tf_op jit(solution)/shard_map/ppermute | solution.py:35
  (57 shorter events, 21.5 us)
Async XLA Ops:
  2.9 14.2 %all-to-all-start = ((bf16[8,8,2560]{2,1,0:T(8,128)(2,1)}), bf16[8,8,2560]{2,1,0:T(8,128)(2,1)S(1)}, u32[]{:S(2)}, u32[]{:S(2)}) async-start(bf16[8,8,2560]{2,1,0:T(8,128)(2,1)} %broadcast_in_dim.20), calls=%async_computation | async-start | bytes 655360 | tf_op jit(solution)/shard_map/all_to_all | solution.py:120
  17.2 0.7 copy-start.4
  43.5 3.5 %copy-start.2 = (bf16[64,256,128]{2,1,0:T(8,128)(2,1)S(1)}, bf16[64,256,128]{2,1,0:T(8,128)(2,1)}, u32[]{:S(2)}) copy-start(bf16[64,256,128]{2,1,0:T(8,128)(2,1)} %get-tuple-element.6) | copy-start | bytes 12582916
  47.0 2.2 %copy-start = (bf16[64,256,128]{2,1,0:T(8,128)(2,1)S(1)}, bf16[64,256,128]{2,1,0:T(8,128)(2,1)}, u32[]{:S(2)}) copy-start(bf16[64,256,128]{2,1,0:T(8,128)(2,1)} %get-tuple-element.7) | copy-start | bytes 12582916
  51.5 19.5 %all-to-all-start.1 = ((f32[8,8,256,16]{2,3,1,0:T(8,128)}), f32[8,8,256,16]{2,3,1,0:T(8,128)S(1)}, u32[]{:S(2)}, u32[]{:S(2)}) async-start(f32[8,8,256,16]{2,3,1,0:T(8,128)} %bitcast.6), calls=%async_computation.1 | async-start | bytes 2097152 | tf_op jit(solution)/shard_map/all_to_all | solution.py:152
  72.0 44.6 %copy-start.5 = (s32[32]{0:T(128)S(1)}, s32[32]{0:T(128)}, u32[]{:S(2)}) copy-start(s32[32]{0:T(128)} %constant.77) | copy-start | bytes 388
  72.0 6.1 %collective-permute-start.1 = (f32[8,4352]{1,0:T(8,128)S(1)}, f32[8,4352]{1,0:T(8,128)S(1)}, u32[]{:S(2)}, u32[]{:S(2)}) collective-permute-start(f32[8,4352]{1,0:T(8,128)S(1)} %pad_maximum_fusion), channel_id=1, source_target_pairs={{0,16},{8,24},{16,0},{24,8},{1,17},{9,25},{17,1},{25,9},{2,18},{10... | collective-permute-start | bytes 417800 | tf_op jit(solution)/shard_map/ppermute | solution.py:52
  73.3 5.9 %collective-permute-start.2 = (f32[8,4352]{1,0:T(8,128)S(1)}, f32[8,4352]{1,0:T(8,128)S(1)}, u32[]{:S(2)}, u32[]{:S(2)}) collective-permute-start(f32[8,4352]{1,0:T(8,128)S(1)} %pad_maximum_fusion), channel_id=1, source_target_pairs={{0,24},{8,16},{16,8},{24,0},{1,25},{9,17},{17,9},{25,1},{2,26},{10... | collective-permute-start | bytes 417800 | tf_op jit(solution)/shard_map/ppermute | solution.py:53
  73.3 5.9 %collective-permute-start = (f32[8,4352]{1,0:T(8,128)S(1)}, f32[8,4352]{1,0:T(8,128)S(1)}, u32[]{:S(2)}, u32[]{:S(2)}) collective-permute-start(f32[8,4352]{1,0:T(8,128)S(1)} %pad_maximum_fusion), channel_id=1, source_target_pairs={{0,8},{8,0},{16,24},{24,16},{1,9},{9,1},{17,25},{25,17},{2,10},{10... | collective-permute-start | bytes 417800 | tf_op jit(solution)/shard_map/ppermute | solution.py:51
  79.3 6.6 %collective-permute-start.3 = (f32[8,4352]{1,0:T(8,128)S(1)}, f32[8,4352]{1,0:T(8,128)S(1)}, u32[]{:S(2)}, u32[]{:S(2)}) collective-permute-start(f32[8,4352]{1,0:T(8,128)S(1)} %add_add_fusion), channel_id=1, source_target_pairs={{0,32},{32,0},{64,96},{96,64},{128,160},{160,128},{192,224},{224,1... | collective-permute-start | bytes 417800 | tf_op jit(solution)/shard_map/ppermute | solution.py:35
  85.9 10.2 %collective-permute-start.4 = (f32[8,4352]{1,0:T(8,128)S(1)}, f32[8,4352]{1,0:T(8,128)S(1)}, u32[]{:S(2)}, u32[]{:S(2)}) collective-permute-start(f32[8,4352]{1,0:T(8,128)S(1)} %add.124), channel_id=1, source_target_pairs={{0,64},{32,96},{64,0},{96,32},{128,192},{160,224},{192,128},{224,1... | collective-permute-start | bytes 417800 | tf_op jit(solution)/shard_map/ppermute | solution.py:35
  96.1 12.8 %collective-permute-start.5 = (f32[8,4352]{1,0:T(8,128)S(1)}, f32[8,4352]{1,0:T(8,128)S(1)}, u32[]{:S(2)}, u32[]{:S(2)}) collective-permute-start(f32[8,4352]{1,0:T(8,128)S(1)} %add.125), channel_id=1, source_target_pairs={{0,128},{32,160},{64,192},{96,224},{128,0},{160,32},{192,64},{224,... | collective-permute-start | bytes 417800 | tf_op jit(solution)/shard_map/ppermute | solution.py:35
  110.8 13.3 %all-to-all-start.2 = ((bf16[8,8,256,16]{2,3,1,0:T(8,128)(2,1)}), bf16[8,8,256,16]{2,3,1,0:T(8,128)(2,1)S(1)}, u32[]{:S(2)}, u32[]{:S(2)}) async-start(bf16[8,8,256,16]{2,3,1,0:T(8,128)(2,1)} %broadcast_in_dim.34), calls=%async_computation.2 | async-start | bytes 1048576 | tf_op jit(solution)/shard_map/all_to_all | solution.py:120
  124.1 3.4 %copy-start.3 = (bf16[64,256,128]{2,1,0:T(8,128)(2,1)S(1)}, bf16[64,256,128]{2,1,0:T(8,128)(2,1)}, u32[]{:S(2)}) copy-start(bf16[64,256,128]{2,1,0:T(8,128)(2,1)} %get-tuple-element.6) | copy-start | bytes 12582916
  127.6 2.2 %copy-start.1 = (bf16[64,256,128]{2,1,0:T(8,128)(2,1)S(1)}, bf16[64,256,128]{2,1,0:T(8,128)(2,1)}, u32[]{:S(2)}) copy-start(bf16[64,256,128]{2,1,0:T(8,128)(2,1)} %get-tuple-element.7) | copy-start | bytes 12582916
  131.1 5.9 %collective-permute-start.8 = (f32[8,32,128]{2,1,0:T(8,128)S(1)}, f32[8,32,128]{2,1,0:T(8,128)S(1)}, u32[]{:S(2)}, u32[]{:S(2)}) collective-permute-start(f32[8,32,128]{2,1,0:T(8,128)S(1)} %get-tuple-element.21), channel_id=1, source_target_pairs={{0,24},{8,16},{16,8},{24,0},{1,25},{9,17},{17,9},{25,1},{2,26},{10... | collective-permute-start | bytes 393224 | tf_op jit(solution)/shard_map/ppermute | solution.py:71
  131.2 8.5 %collective-permute-start.7 = (f32[8,32,128]{2,1,0:T(8,128)S(1)}, f32[8,32,128]{2,1,0:T(8,128)S(1)}, u32[]{:S(2)}, u32[]{:S(2)}) collective-permute-start(f32[8,32,128]{2,1,0:T(8,128)S(1)} %get-tuple-element.22), channel_id=1, source_target_pairs={{0,16},{8,24},{16,0},{24,8},{1,17},{9,25},{17,1},{25,9},{2,18},{10... | collective-permute-start | bytes 393224 | tf_op jit(solution)/shard_map/ppermute | solution.py:70
  132.7 7.0 %collective-permute-start.6 = (f32[8,32,128]{2,1,0:T(8,128)S(1)}, f32[8,32,128]{2,1,0:T(8,128)S(1)}, u32[]{:S(2)}, u32[]{:S(2)}) collective-permute-start(f32[8,32,128]{2,1,0:T(8,128)S(1)} %get-tuple-element.20), channel_id=1, source_target_pairs={{0,8},{8,0},{16,24},{24,16},{1,9},{9,1},{17,25},{25,17},{2,10},{10... | collective-permute-start | bytes 393224 | tf_op jit(solution)/shard_map/ppermute | solution.py:69
  139.7 4.4 %collective-permute-start.9 = (f32[4,32,128]{2,1,0:T(8,128)S(1)}, f32[4,32,128]{2,1,0:T(8,128)S(1)}, u32[]{:S(2)}, u32[]{:S(2)}) collective-permute-start(f32[4,32,128]{2,1,0:T(8,128)S(1)} %dynamic-slice_bitcast_fusion.3), channel_id=1, source_target_pairs={{0,32},{32,0},{64,96},{96,64},{128,160},{160,128},{192,224},{224,1... | collective-permute-start | bytes 196616 | tf_op jit(solution)/shard_map/ppermute | solution.py:35
  144.1 4.9 %collective-permute-start.10 = (f32[2,32,128]{2,1,0:T(8,128)S(1)}, f32[2,32,128]{2,1,0:T(8,128)S(1)}, u32[]{:S(2)}, u32[]{:S(2)}) collective-permute-start(f32[2,32,128]{2,1,0:T(8,128)S(1)} %dynamic-slice_bitcast_fusion.4), channel_id=1, source_target_pairs={{0,64},{32,96},{64,0},{96,32},{128,192},{160,224},{192,128},{224,1... | collective-permute-start | bytes 98312 | tf_op jit(solution)/shard_map/ppermute | solution.py:35
  149.0 7.7 %collective-permute-start.11 = (f32[1,32,128]{2,1,0:T(8,128)S(1)}, f32[1,32,128]{2,1,0:T(8,128)S(1)}, u32[]{:S(2)}, u32[]{:S(2)}) collective-permute-start(f32[1,32,128]{2,1,0:T(8,128)S(1)} %constant_dynamic-slice_fusion), channel_id=1, source_target_pairs={{0,128},{32,160},{64,192},{96,224},{128,0},{160,32},{192,64},{224,... | collective-permute-start | bytes 49160 | tf_op jit(solution)/shard_map/ppermute | solution.py:35

commit v13 on v9

--- a/solution.py
+++ b/solution.py
@@ -5,6 +5,7 @@
 import numpy as np
 from jax import lax
 from jax.experimental import pallas as pl
+from jax.experimental.pallas import tpu as pltpu
 from jax.sharding import Mesh
 from jax.sharding import PartitionSpec as P
 
@@ -51,7 +52,8 @@
     return x
 
 
-def means_kernel(codes_ref, vec_ref, hi_ref, mid_ref, lo_ref):
+def means_kernel(block_ref, codes_ref, vec_ref, *refs):
+    hi_ref, mid_ref, lo_ref = refs[-3:]
     rows = codes_ref.shape[1]
     kinds = lax.broadcasted_iota(jnp.int32, (K, rows), 0).astype(codes_ref.dtype)
     one = jnp.ones((K, rows), jnp.bfloat16)
@@ -67,25 +69,57 @@
         lo_ref[i] = (rest - mid.astype(jnp.float32)).astype(jnp.bfloat16)
 
 
-def codeword_means(codes_all, vectors):
+def codeword_means(own, codes_own, codes_all, vectors):
     m_all, rows = codes_all.shape
     width = vectors.shape[1]
+    n_blocks = m_all // GROUP
     out = jax.ShapeDtypeStruct((m_all, K, width), jnp.bfloat16)
+    out_block = pl.BlockSpec((GROUP, K, width), lambda g, b: (b[0], 0, 0))
+    first = pl.pallas_call(
+        means_kernel,
+        grid_spec=pltpu.PrefetchScalarGridSpec(
+            num_scalar_prefetch=1,
+            grid=(1,),
+            in_specs=[
+                pl.BlockSpec((GROUP, rows), lambda g, b: (0, 0)),
+                pl.BlockSpec((rows, width), lambda g, b: (0, 0)),
+            ],
+            out_specs=[out_block] * 3,
+        ),
+        out_shape=[out] * 3,
+        cost_estimate=pl.CostEstimate(
+            flops=2 * GROUP * K * rows * width,
+            transcendentals=0,
+            bytes_accessed=codes_own.size * 2 + vectors.size * 2 + 3 * GROUP * K * width * 2,
+        ),
+    )(own, codes_own, vectors)
+
+    def other(g, b):
+        return g + (g >= b[0]).astype(jnp.int32)
+
+    rest_block = pl.BlockSpec((GROUP, K, width), lambda g, b: (other(g, b), 0, 0))
     return pl.pallas_call(
         means_kernel,
-        grid=(m_all // GROUP,),
-        in_specs=[
-            pl.BlockSpec((GROUP, rows), lambda g: (g, 0)),
-            pl.BlockSpec((rows, width), lambda g: (0, 0)),
-        ],
-        out_specs=[pl.BlockSpec((GROUP, K, width), lambda g: (g, 0, 0))] * 3,
+        grid_spec=pltpu.PrefetchScalarGridSpec(
+            num_scalar_prefetch=1,
+            grid=(n_blocks - 1,),
+            in_specs=[
+                pl.BlockSpec((GROUP, rows), lambda g, b: (other(g, b), 0)),
+                pl.BlockSpec((rows, width), lambda g, b: (0, 0)),
+                pl.BlockSpec(memory_space=pl.ANY),
+                pl.BlockSpec(memory_space=pl.ANY),
+                pl.BlockSpec(memory_space=pl.ANY),
+            ],
+            out_specs=[rest_block] * 3,
+        ),
         out_shape=[out] * 3,
+        input_output_aliases={3: 0, 4: 1, 5: 2},
         cost_estimate=pl.CostEstimate(
-            flops=2 * m_all * K * rows * width,
+            flops=2 * (m_all - GROUP) * K * rows * width,
             transcendentals=0,
-            bytes_accessed=codes_all.size * 2 + vectors.size * 2 + 3 * m_all * K * width * 2,
-        ),
-    )(codes_all, vectors)
+            bytes_accessed=codes_all.size * 2 + vectors.size * 2 + 3 * (m_all - GROUP) * K * width * 2,
+        ),
+    )(own, codes_all, vectors, *first)
 
 
 def broadcast_over(x, names, count):
@@ -112,7 +146,8 @@
         (masked[:, None, :] == kinds[None, :, None]).astype(jnp.float32), axis=2
     )
 
-    h_parts = codeword_means(codes_all, vectors)
+    own = lax.axis_index(feat_names).reshape(1).astype(jnp.int32)
+    h_parts = codeword_means(own, masked.astype(jnp.bfloat16), codes_all, vectors)
 
     rot3 = rotation.reshape(local, m_all, DS).transpose(1, 0, 2)
     dims = (((2,), (1,)), ((0,), (0,)))

time: 154 us -> 152 us (0.987)
  waiting for transfers between devices: 55.4 us -> 50.5 us
  Pallas kernels: 25.5 us -> 28 us
    all_to_all x2, waiting for transfers between devices: 13.2 us -> 8 us  [broadcast_over(): lax.all_to_all(copies, names, split_axis=0, concat_axis=0, tiled=True)]
    pallas_call x1 -> x2, Pallas kernels: 25.5 us -> 28 us  [codeword_means(): pl.pallas_call(means_kernel, grid_spec=pltpu.PrefetchScalarGridSpec(num_s...]
    unnamed x14 -> x16, local copies, waits for them, and re-layouts: 5.52 us -> 5.51 us
  transfers between devices with their start and end apart: 13 -> 13, of which waited for: 13 -> 13; matrix products, arithmetic and copies ran while one was open for 3% -> 3% of each run, Pallas kernels for 0% -> 3%
where the time goes in v13:
time: 152 us; the launch traced here: 149 us
  waiting for transfers between devices  50.5 us (33%)
  starting transfers between devices  44 us (29%)
  Pallas kernels  28 us (18%)
  matrix products  11.3 us (7%)
  local copies, waits for them, and re-layouts  9.74 us (6%)
  other arithmetic  4.46 us (3%)
  between operations  1.52 us (1%)
    ppermute x10, waiting for transfers between devices, exchange(): return lax.ppermute(x, name, pairs)  30.9 us
    pallas_call x2, Pallas kernels, codeword_means(): pl.pallas_call(means_kernel, grid_spec=pltpu.PrefetchScalarGridSpec(num_s...  28 us
    ppermute x10, starting transfers between devices, exchange(): return lax.ppermute(x, name, pairs)  23.8 us
    all_to_all x2, starting transfers between devices, broadcast_over(): lax.all_to_all(copies, names, split_axis=0, concat_axis=0, tiled=True)  13.5 us
    all_to_all x1, waiting for transfers between devices, shards(): lax.all_to_all(partial, feat_names, split_axis=0, concat_axis=0, tiled=True)  11.6 us
    all_to_all x2, waiting for transfers between devices, broadcast_over(): lax.all_to_all(copies, names, split_axis=0, concat_axis=0, tiled=True)  8 us
    dot_general x3, matrix products, shards(): lax.dot_general(part, rot3, dims, preferred_element_type=jnp.float32)  6.97 us
    all_to_all x1, starting transfers between devices, shards(): lax.all_to_all(partial, feat_names, split_axis=0, concat_axis=0, tiled=True)  6.68 us
  transfers between devices with their start and end apart: 13, of which 13 were waited for; matrix products, arithmetic and copies ran while one was open for 3% of the time, Pallas kernels for 3%

profile of v13, /device:TPU:4, one launch (start us, length us, event | category | flops | bytes accessed | tf_op | source)
XLA Modules:
  0.0 149.5 jit_solution(5410183870162757320)
XLA Ops:
  3.0 7.4 %all-to-all-start = ((bf16[8,8,2560]{2,1,0:T(8,128)(2,1)}), bf16[8,8,2560]{2,1,0:T(8,128)(2,1)S(1)}, u32[]{:S(2)}, u32[]{:S(2)}) async-start(bf16[8,8,2560]{2,1,0:T(8,128)(2,1)} %broadcast_in_dim.20), calls=%async_computation | async-start | bytes 655360 | tf_op jit(solution)/shard_map/all_to_all | solution.py:127
  11.6 5.2 %shard_map.77 = (bf16[64,256,128]{2,1,0:T(8,128)(2,1)}, bf16[64,256,128]{2,1,0:T(8,128)(2,1)}, bf16[64,256,128]{2,1,0:T(8,128)(2,1)}) custom-call(s32[1]{0:T(128)} %bitcast.block_ref, bf16[8,2560]{1,0:T(8,128)(2,1)} %copy-done.5, bf16[2560,128]{1,0:T(8,128)(2,1)} %vec_ref.3), custom_call_target="tpu_custom_call" | custom-call | flops 1342177280 | bytes 2269184 | tf_op jit(solution)/shard_map/pallas_call | solution.py:78
  18.0 22.7 %shard_map.78 = (bf16[64,256,128]{2,1,0:T(8,128)(2,1)}, bf16[64,256,128]{2,1,0:T(8,128)(2,1)}, bf16[64,256,128]{2,1,0:T(8,128)(2,1)}) custom-call(s32[1]{0:T(128)} %bitcast.block_ref, bf16[64,2560]{1,0:T(8,128)(2,1)} %bitcast.63, bf16[2560,128]{1,0:T(8,128)(2,1)} %vec_ref.3, ...), custom_call_target="tpu_custom_call", output_to_operand_aliasing={{0}: (3, {}), {1}: (4, {}), {2}: (5, {})} | custom-call | flops 9395240960 | bytes 11993088 | tf_op jit(solution)/shard_map/pallas_call | solution.py:101
  40.7 3.5 %fusion.5 = f32[64,256,16]{1,2,0:T(8,128)S(1)} fusion(bf16[64,256,128]{2,1,0:T(8,128)(2,1)} %get-tuple-element.11, bf16[64,128,16]{1,2,0:T(8,128)(2,1)S(1)} %bitcast.53), kind=kOutput, calls=%fused_computation.29 | convolution fusion | flops 67108864 | bytes 5505024 | tf_op jit(solution)/shard_map/dot_general | solution.py:155
  46.5 2.2 %convolution_add_fusion = f32[64,256,16]{1,2,0:T(8,128)} fusion(f32[64,256,16]{1,2,0:T(8,128)S(1)} %convolution_add_fusion.1, bf16[64,256,128]{2,1,0:T(8,128)(2,1)S(1)} %copy-done.2, bf16[64,128,16]{1,2,0:T(8,128)(2,1)S(1)} %bitcast.55), kind=kOutput, calls=%fused_computation.3 | convolution fusion | flops 67371008 | bytes 6553600 | tf_op jit(solution)/shard_map/dot_general | solution.py:155
  48.7 6.7 %all-to-all-start.1 = ((f32[8,8,256,16]{2,3,1,0:T(8,128)}), f32[8,8,256,16]{2,3,1,0:T(8,128)S(1)}, u32[]{:S(2)}, u32[]{:S(2)}) async-start(f32[8,8,256,16]{2,3,1,0:T(8,128)} %bitcast.7), calls=%async_computation.1 | async-start | bytes 2097152 | tf_op jit(solution)/shard_map/all_to_all | solution.py:160
  55.4 2.3 %convert_reduce_fusion = f32[8,256]{1,0:T(8,128)S(1)} fusion(s32[8,2560]{1,0:T(8,128)S(1)} %get-tuple-element.23), kind=kLoop, calls=%fused_computation.1 | loop fusion | flops 15726592 | bytes 90112 | tf_op jit(solution)/shard_map/reduce_sum | solution.py:145
  57.7 11.6 %all-to-all-done.1 = f32[8,8,256,16]{2,3,1,0:T(8,128)S(1)} async-done(((f32[8,8,256,16]{2,3,1,0:T(8,128)}), f32[8,8,256,16]{2,3,1,0:T(8,128)S(1)}, u32[]{:S(2)}, u32[]{:S(2)}) %all-to-all-start.1) | async-done | bytes 1048608 | tf_op jit(solution)/shard_map/all_to_all | solution.py:160
  73.4 4.5 %collective-permute-done.1 = f32[8,4352]{1,0:T(8,128)S(1)} collective-permute-done((f32[8,4352]{1,0:T(8,128)S(1)}, f32[8,4352]{1,0:T(8,128)S(1)}, u32[]{:S(2)}, u32[]{:S(2)}) %collective-permute-start.1) | collective-permute-done | bytes 139296 | tf_op jit(solution)/shard_map/ppermute | solution.py:36
  77.9 2.0 %collective-permute-start.2 = (f32[8,4352]{1,0:T(8,128)S(1)}, f32[8,4352]{1,0:T(8,128)S(1)}, u32[]{:S(2)}, u32[]{:S(2)}) collective-permute-start(f32[8,4352]{1,0:T(8,128)S(1)} %add.111), channel_id=1, source_target_pairs={{0,32},{32,0},{64,96},{96,64},{128,160},{160,128},{192,224},{224,1... | collective-permute-start | bytes 417800 | tf_op jit(solution)/shard_map/ppermute | solution.py:36
  79.9 3.2 %collective-permute-done.2 = f32[8,4352]{1,0:T(8,128)S(1)} collective-permute-done((f32[8,4352]{1,0:T(8,128)S(1)}, f32[8,4352]{1,0:T(8,128)S(1)}, u32[]{:S(2)}, u32[]{:S(2)}) %collective-permute-start.2) | collective-permute-done | bytes 139296 | tf_op jit(solution)/shard_map/ppermute | solution.py:36
  83.1 3.4 %collective-permute-start.3 = (f32[8,4352]{1,0:T(8,128)S(1)}, f32[8,4352]{1,0:T(8,128)S(1)}, u32[]{:S(2)}, u32[]{:S(2)}) collective-permute-start(f32[8,4352]{1,0:T(8,128)S(1)} %add.112), channel_id=1, source_target_pairs={{0,64},{32,96},{64,0},{96,32},{128,192},{160,224},{192,128},{224,1... | collective-permute-start | bytes 417800 | tf_op jit(solution)/shard_map/ppermute | solution.py:36
  86.4 5.2 %collective-permute-done.3 = f32[8,4352]{1,0:T(8,128)S(1)} collective-permute-done((f32[8,4352]{1,0:T(8,128)S(1)}, f32[8,4352]{1,0:T(8,128)S(1)}, u32[]{:S(2)}, u32[]{:S(2)}) %collective-permute-start.3) | collective-permute-done | bytes 139296 | tf_op jit(solution)/shard_map/ppermute | solution.py:36
  91.6 6.5 %collective-permute-start.4 = (f32[8,4352]{1,0:T(8,128)S(1)}, f32[8,4352]{1,0:T(8,128)S(1)}, u32[]{:S(2)}, u32[]{:S(2)}) collective-permute-start(f32[8,4352]{1,0:T(8,128)S(1)} %add.113), channel_id=1, source_target_pairs={{0,128},{32,160},{64,192},{96,224},{128,0},{160,32},{192,64},{224,... | collective-permute-start | bytes 417800 | tf_op jit(solution)/shard_map/ppermute | solution.py:36
  98.1 3.4 %collective-permute-done.4 = f32[8,4352]{1,0:T(8,128)S(1)} collective-permute-done((f32[8,4352]{1,0:T(8,128)S(1)}, f32[8,4352]{1,0:T(8,128)S(1)}, u32[]{:S(2)}, u32[]{:S(2)}) %collective-permute-start.4) | collective-permute-done | bytes 139296 | tf_op jit(solution)/shard_map/ppermute | solution.py:36
  103.4 6.1 %all-to-all-start.2 = ((bf16[8,8,256,16]{2,3,1,0:T(8,128)(2,1)}), bf16[8,8,256,16]{2,3,1,0:T(8,128)(2,1)S(1)}, u32[]{:S(2)}, u32[]{:S(2)}) async-start(bf16[8,8,256,16]{2,3,1,0:T(8,128)(2,1)} %broadcast_in_dim.34), calls=%async_computation.2 | async-start | bytes 1048576 | tf_op jit(solution)/shard_map/all_to_all | solution.py:127
  109.5 7.5 %all-to-all-done.2 = bf16[8,8,256,16]{2,3,1,0:T(8,128)(2,1)S(1)} async-done(((bf16[8,8,256,16]{2,3,1,0:T(8,128)(2,1)}), bf16[8,8,256,16]{2,3,1,0:T(8,128)(2,1)S(1)}, u32[]{:S(2)}, u32[]{:S(2)}) %all-to-all-start.2) | async-done | bytes 524320 | tf_op jit(solution)/shard_map/all_to_all | solution.py:127
  117.0 3.0 %fusion.6 = f32[64,16,128]{2,1,0:T(8,128)S(1)} fusion(bf16[64,256,16]{1,2,0:T(8,128)(2,1)S(1)} %bitcast.50, bf16[64,256,128]{2,1,0:T(8,128)(2,1)} %get-tuple-element.11), kind=kOutput, calls=%fused_computation.30 | convolution fusion | flops 67108864 | bytes 5242880 | tf_op jit(solution)/shard_map/dot_general | solution.py:178
  126.9 4.3 %collective-permute-done.6 = f32[8,32,128]{2,1,0:T(8,128)S(1)} collective-permute-done((f32[8,32,128]{2,1,0:T(8,128)S(1)}, f32[8,32,128]{2,1,0:T(8,128)S(1)}, u32[]{:S(2)}, u32[]{:S(2)}) %collective-permute-start.6) | collective-permute-done | bytes 131104 | tf_op jit(solution)/shard_map/ppermute | solution.py:36
  131.4 4.2 %collective-permute-done.7 = f32[4,32,128]{2,1,0:T(8,128)S(1)} collective-permute-done((f32[4,32,128]{2,1,0:T(8,128)S(1)}, f32[4,32,128]{2,1,0:T(8,128)S(1)}, u32[]{:S(2)}, u32[]{:S(2)}) %collective-permute-start.7) | collective-permute-done | bytes 65568 | tf_op jit(solution)/shard_map/ppermute | solution.py:36
  135.7 3.5 %collective-permute-start.8 = (f32[2,32,128]{2,1,0:T(8,128)S(1)}, f32[2,32,128]{2,1,0:T(8,128)S(1)}, u32[]{:S(2)}, u32[]{:S(2)}) collective-permute-start(f32[2,32,128]{2,1,0:T(8,128)S(1)} %dynamic-slice_bitcast_fusion.3), channel_id=1, source_target_pairs={{0,64},{32,96},{64,0},{96,32},{128,192},{160,224},{192,128},{224,1... | collective-permute-start | bytes 98312 | tf_op jit(solution)/shard_map/ppermute | solution.py:36
  139.5 1.6 %collective-permute-done.8 = f32[2,32,128]{2,1,0:T(8,128)S(1)} collective-permute-done((f32[2,32,128]{2,1,0:T(8,128)S(1)}, f32[2,32,128]{2,1,0:T(8,128)S(1)}, u32[]{:S(2)}, u32[]{:S(2)}) %collective-permute-start.8) | collective-permute-done | bytes 32800 | tf_op jit(solution)/shard_map/ppermute | solution.py:36
  141.1 5.4 %collective-permute-start.9 = (f32[1,32,128]{2,1,0:T(8,128)S(1)}, f32[1,32,128]{2,1,0:T(8,128)S(1)}, u32[]{:S(2)}, u32[]{:S(2)}) collective-permute-start(f32[1,32,128]{2,1,0:T(8,128)S(1)} %constant_dynamic-slice_fusion), channel_id=1, source_target_pairs={{0,128},{32,160},{64,192},{96,224},{128,0},{160,32},{192,64},{224,... | collective-permute-start | bytes 49160 | tf_op jit(solution)/shard_map/ppermute | solution.py:36
  147.3 1.6 %collective-permute-done.9 = f32[1,32,128]{2,1,0:T(8,128)S(1)} collective-permute-done((f32[1,32,128]{2,1,0:T(8,128)S(1)}, f32[1,32,128]{2,1,0:T(8,128)S(1)}, u32[]{:S(2)}, u32[]{:S(2)}) %collective-permute-start.9) | collective-permute-done | bytes 16416 | tf_op jit(solution)/shard_map/ppermute | solution.py:36
  (59 shorter events, 20.7 us)
Async XLA Ops:
  2.2 9.3 %copy-start.5 = (bf16[8,2560]{1,0:T(8,128)(2,1)}, bf16[8,2560]{1,0:T(8,128)(2,1)S(1)}, u32[]{:S(2)}) copy-start(bf16[8,2560]{1,0:T(8,128)(2,1)S(1)} %get-tuple-element.22.codes_ref) | copy-start | bytes 122884
  3.0 14.2 %all-to-all-start = ((bf16[8,8,2560]{2,1,0:T(8,128)(2,1)}), bf16[8,8,2560]{2,1,0:T(8,128)(2,1)S(1)}, u32[]{:S(2)}, u32[]{:S(2)}) async-start(bf16[8,8,2560]{2,1,0:T(8,128)(2,1)} %broadcast_in_dim.20), calls=%async_computation | async-start | bytes 655360 | tf_op jit(solution)/shard_map/all_to_all | solution.py:127
  17.2 0.8 copy-start.4
  40.7 3.5 %copy-start = (bf16[64,256,128]{2,1,0:T(8,128)(2,1)S(1)}, bf16[64,256,128]{2,1,0:T(8,128)(2,1)}, u32[]{:S(2)}) copy-start(bf16[64,256,128]{2,1,0:T(8,128)(2,1)} %get-tuple-element.12) | copy-start | bytes 12582916
  44.3 2.2 %copy-start.2 = (bf16[64,256,128]{2,1,0:T(8,128)(2,1)S(1)}, bf16[64,256,128]{2,1,0:T(8,128)(2,1)}, u32[]{:S(2)}) copy-start(bf16[64,256,128]{2,1,0:T(8,128)(2,1)} %get-tuple-element.13) | copy-start | bytes 12582916
  48.7 20.7 %all-to-all-start.1 = ((f32[8,8,256,16]{2,3,1,0:T(8,128)}), f32[8,8,256,16]{2,3,1,0:T(8,128)S(1)}, u32[]{:S(2)}, u32[]{:S(2)}) async-start(f32[8,8,256,16]{2,3,1,0:T(8,128)} %bitcast.7), calls=%async_computation.1 | async-start | bytes 2097152 | tf_op jit(solution)/shard_map/all_to_all | solution.py:160
  70.4 39.1 %copy-start.6 = (s32[32]{0:T(128)S(1)}, s32[32]{0:T(128)}, u32[]{:S(2)}) copy-start(s32[32]{0:T(128)} %constant.86) | copy-start | bytes 388
  70.4 1.6 %collective-permute-start = (f32[8,4352]{1,0:T(8,128)S(1)}, f32[8,4352]{1,0:T(8,128)S(1)}, u32[]{:S(2)}, u32[]{:S(2)}) collective-permute-start(f32[8,4352]{1,0:T(8,128)S(1)} %pad_maximum_fusion), channel_id=1, source_target_pairs={{0,8},{8,0},{1,9},{9,1},{2,10},{10,2},{3,11},{11,3},{4,12},{12,4},... | collective-permute-start | bytes 417800 | tf_op jit(solution)/shard_map/ppermute | solution.py:36
  72.1 5.8 %collective-permute-start.1 = (f32[8,4352]{1,0:T(8,128)S(1)}, f32[8,4352]{1,0:T(8,128)S(1)}, u32[]{:S(2)}, u32[]{:S(2)}) collective-permute-start(f32[8,4352]{1,0:T(8,128)S(1)} %fusion.3), channel_id=1, source_target_pairs={{0,16},{16,0},{1,17},{17,1},{2,18},{18,2},{3,19},{19,3},{4,20},{20... | collective-permute-start | bytes 417800 | tf_op jit(solution)/shard_map/ppermute | solution.py:36
  77.9 5.2 %collective-permute-start.2 = (f32[8,4352]{1,0:T(8,128)S(1)}, f32[8,4352]{1,0:T(8,128)S(1)}, u32[]{:S(2)}, u32[]{:S(2)}) collective-permute-start(f32[8,4352]{1,0:T(8,128)S(1)} %add.111), channel_id=1, source_target_pairs={{0,32},{32,0},{64,96},{96,64},{128,160},{160,128},{192,224},{224,1... | collective-permute-start | bytes 417800 | tf_op jit(solution)/shard_map/ppermute | solution.py:36
  83.1 8.5 %collective-permute-start.3 = (f32[8,4352]{1,0:T(8,128)S(1)}, f32[8,4352]{1,0:T(8,128)S(1)}, u32[]{:S(2)}, u32[]{:S(2)}) collective-permute-start(f32[8,4352]{1,0:T(8,128)S(1)} %add.112), channel_id=1, source_target_pairs={{0,64},{32,96},{64,0},{96,32},{128,192},{160,224},{192,128},{224,1... | collective-permute-start | bytes 417800 | tf_op jit(solution)/shard_map/ppermute | solution.py:36
  91.6 9.9 %collective-permute-start.4 = (f32[8,4352]{1,0:T(8,128)S(1)}, f32[8,4352]{1,0:T(8,128)S(1)}, u32[]{:S(2)}, u32[]{:S(2)}) collective-permute-start(f32[8,4352]{1,0:T(8,128)S(1)} %add.113), channel_id=1, source_target_pairs={{0,128},{32,160},{64,192},{96,224},{128,0},{160,32},{192,64},{224,... | collective-permute-start | bytes 417800 | tf_op jit(solution)/shard_map/ppermute | solution.py:36
  103.4 13.6 %all-to-all-start.2 = ((bf16[8,8,256,16]{2,3,1,0:T(8,128)(2,1)}), bf16[8,8,256,16]{2,3,1,0:T(8,128)(2,1)S(1)}, u32[]{:S(2)}, u32[]{:S(2)}) async-start(bf16[8,8,256,16]{2,3,1,0:T(8,128)(2,1)} %broadcast_in_dim.34), calls=%async_computation.2 | async-start | bytes 1048576 | tf_op jit(solution)/shard_map/all_to_all | solution.py:127
  117.0 3.4 %copy-start.1 = (bf16[64,256,128]{2,1,0:T(8,128)(2,1)S(1)}, bf16[64,256,128]{2,1,0:T(8,128)(2,1)}, u32[]{:S(2)}) copy-start(bf16[64,256,128]{2,1,0:T(8,128)(2,1)} %get-tuple-element.12) | copy-start | bytes 12582916
  120.5 2.2 %copy-start.3 = (bf16[64,256,128]{2,1,0:T(8,128)(2,1)S(1)}, bf16[64,256,128]{2,1,0:T(8,128)(2,1)}, u32[]{:S(2)}) copy-start(bf16[64,256,128]{2,1,0:T(8,128)(2,1)} %get-tuple-element.13) | copy-start | bytes 12582916
  124.0 1.6 %collective-permute-start.5 = (f32[16,32,128]{2,1,0:T(8,128)S(1)}, f32[16,32,128]{2,1,0:T(8,128)S(1)}, u32[]{:S(2)}, u32[]{:S(2)}) collective-permute-start(f32[16,32,128]{2,1,0:T(8,128)S(1)} %dynamic-slice_bitcast_fusion), channel_id=1, source_target_pairs={{0,8},{8,0},{1,9},{9,1},{2,10},{10,2},{3,11},{11,3},{4,12},{12,4},... | collective-permute-start | bytes 786440 | tf_op jit(solution)/shard_map/ppermute | solution.py:36
  125.7 5.6 %collective-permute-start.6 = (f32[8,32,128]{2,1,0:T(8,128)S(1)}, f32[8,32,128]{2,1,0:T(8,128)S(1)}, u32[]{:S(2)}, u32[]{:S(2)}) collective-permute-start(f32[8,32,128]{2,1,0:T(8,128)S(1)} %dynamic-slice_bitcast_fusion.1), channel_id=1, source_target_pairs={{0,16},{16,0},{1,17},{17,1},{2,18},{18,2},{3,19},{19,3},{4,20},{20... | collective-permute-start | bytes 393224 | tf_op jit(solution)/shard_map/ppermute | solution.py:36
  131.3 4.4 %collective-permute-start.7 = (f32[4,32,128]{2,1,0:T(8,128)S(1)}, f32[4,32,128]{2,1,0:T(8,128)S(1)}, u32[]{:S(2)}, u32[]{:S(2)}) collective-permute-start(f32[4,32,128]{2,1,0:T(8,128)S(1)} %dynamic-slice_bitcast_fusion.2), channel_id=1, source_target_pairs={{0,32},{32,0},{64,96},{96,64},{128,160},{160,128},{192,224},{224,1... | collective-permute-start | bytes 196616 | tf_op jit(solution)/shard_map/ppermute | solution.py:36
  135.7 5.4 %collective-permute-start.8 = (f32[2,32,128]{2,1,0:T(8,128)S(1)}, f32[2,32,128]{2,1,0:T(8,128)S(1)}, u32[]{:S(2)}, u32[]{:S(2)}) collective-permute-start(f32[2,32,128]{2,1,0:T(8,128)S(1)} %dynamic-slice_bitcast_fusion.3), channel_id=1, source_target_pairs={{0,64},{32,96},{64,0},{96,32},{128,192},{160,224},{192,128},{224,1... | collective-permute-start | bytes 98312 | tf_op jit(solution)/shard_map/ppermute | solution.py:36
  141.1 7.7 %collective-permute-start.9 = (f32[1,32,128]{2,1,0:T(8,128)S(1)}, f32[1,32,128]{2,1,0:T(8,128)S(1)}, u32[]{:S(2)}, u32[]{:S(2)}) collective-permute-start(f32[1,32,128]{2,1,0:T(8,128)S(1)} %constant_dynamic-slice_fusion), channel_id=1, source_target_pairs={{0,128},{32,160},{64,192},{96,224},{128,0},{160,32},{192,64},{224,... | collective-permute-start | bytes 49160 | tf_op jit(solution)/shard_map/ppermute | solution.py:36

commit v14 on v13

--- a/solution.py
+++ b/solution.py
@@ -177,8 +177,7 @@
     grad = sum(
         lax.dot_general(table, part, dims, preferred_element_type=jnp.float32) for part in h_parts
     )
-    inverse = 1.0 / (rows * n_row)
-    grad = grad.reshape(m_all * DS, local) * inverse
+    grad = grad.reshape(m_all * DS, local)
 
     grad_rows = (m_all * DS) // n_row
     pieces = grad.reshape(n_row, grad_rows, local)
@@ -195,7 +194,7 @@
         position.append((q, r))
     source = np.array([r for _, r in sorted(position)], dtype=np.int32)
     pieces = pieces[source]
-    grad_t = row_psum_scatter(pieces, steps)[0]
+    grad_t = row_psum_scatter(pieces, steps)[0] / float(rows * n_row)
     return centroids, grad_t
 
 

time: 152 us -> 152 us (level)
  no operation moved by 1% of the time
where the time goes in v14:
time: 152 us; the launch traced here: 149 us
  waiting for transfers between devices  50.5 us (33%)
  starting transfers between devices  44 us (29%)
  Pallas kernels  28 us (18%)
  matrix products  11.3 us (7%)
  local copies, waits for them, and re-layouts  9.73 us (6%)
  other arithmetic  4.46 us (3%)
  between operations  1.52 us (1%)
    ppermute x10, waiting for transfers between devices, exchange(): return lax.ppermute(x, name, pairs)  30.9 us
    pallas_call x2, Pallas kernels, codeword_means(): pl.pallas_call(means_kernel, grid_spec=pltpu.PrefetchScalarGridSpec(num_s...  28 us
    ppermute x10, starting transfers between devices, exchange(): return lax.ppermute(x, name, pairs)  23.8 us
    all_to_all x2, starting transfers between devices, broadcast_over(): lax.all_to_all(copies, names, split_axis=0, concat_axis=0, tiled=True)  13.5 us
    all_to_all x1, waiting for transfers between devices, shards(): lax.all_to_all(partial, feat_names, split_axis=0, concat_axis=0, tiled=True)  11.6 us
    all_to_all x2, waiting for transfers between devices, broadcast_over(): lax.all_to_all(copies, names, split_axis=0, concat_axis=0, tiled=True)  8 us
    dot_general x3, matrix products, shards(): lax.dot_general(part, rot3, dims, preferred_element_type=jnp.float32)  6.97 us
    all_to_all x1, starting transfers between devices, shards(): lax.all_to_all(partial, feat_names, split_axis=0, concat_axis=0, tiled=True)  6.68 us
  transfers between devices with their start and end apart: 13, of which 13 were waited for; matrix products, arithmetic and copies ran while one was open for 3% of the time, Pallas kernels for 3%

profile of v14, /device:TPU:4, one launch (start us, length us, event | category | flops | bytes accessed | tf_op | source)
XLA Modules:
  0.0 149.5 jit_solution(15122452422358002165)
XLA Ops:
  3.0 7.4 %all-to-all-start = ((bf16[8,8,2560]{2,1,0:T(8,128)(2,1)}), bf16[8,8,2560]{2,1,0:T(8,128)(2,1)S(1)}, u32[]{:S(2)}, u32[]{:S(2)}) async-start(bf16[8,8,2560]{2,1,0:T(8,128)(2,1)} %broadcast_in_dim.20), calls=%async_computation | async-start | bytes 655360 | tf_op jit(solution)/shard_map/all_to_all | solution.py:127
  11.6 5.2 %shard_map.77 = (bf16[64,256,128]{2,1,0:T(8,128)(2,1)}, bf16[64,256,128]{2,1,0:T(8,128)(2,1)}, bf16[64,256,128]{2,1,0:T(8,128)(2,1)}) custom-call(s32[1]{0:T(128)} %bitcast.block_ref, bf16[8,2560]{1,0:T(8,128)(2,1)} %copy-done.5, bf16[2560,128]{1,0:T(8,128)(2,1)} %vec_ref.3), custom_call_target="tpu_custom_call" | custom-call | flops 1342177280 | bytes 2269184 | tf_op jit(solution)/shard_map/pallas_call | solution.py:78
  18.0 22.7 %shard_map.78 = (bf16[64,256,128]{2,1,0:T(8,128)(2,1)}, bf16[64,256,128]{2,1,0:T(8,128)(2,1)}, bf16[64,256,128]{2,1,0:T(8,128)(2,1)}) custom-call(s32[1]{0:T(128)} %bitcast.block_ref, bf16[64,2560]{1,0:T(8,128)(2,1)} %bitcast.63, bf16[2560,128]{1,0:T(8,128)(2,1)} %vec_ref.3, ...), custom_call_target="tpu_custom_call", output_to_operand_aliasing={{0}: (3, {}), {1}: (4, {}), {2}: (5, {})} | custom-call | flops 9395240960 | bytes 11993088 | tf_op jit(solution)/shard_map/pallas_call | solution.py:101
  40.7 3.5 %fusion.4 = f32[64,256,16]{1,2,0:T(8,128)S(1)} fusion(bf16[64,256,128]{2,1,0:T(8,128)(2,1)} %get-tuple-element.11, bf16[64,128,16]{1,2,0:T(8,128)(2,1)S(1)} %bitcast.53), kind=kOutput, calls=%fused_computation.28 | convolution fusion | flops 67108864 | bytes 5505024 | tf_op jit(solution)/shard_map/dot_general | solution.py:155
  46.5 2.2 %convolution_add_fusion = f32[64,256,16]{1,2,0:T(8,128)} fusion(f32[64,256,16]{1,2,0:T(8,128)S(1)} %convolution_add_fusion.1, bf16[64,256,128]{2,1,0:T(8,128)(2,1)S(1)} %copy-done.2, bf16[64,128,16]{1,2,0:T(8,128)(2,1)S(1)} %bitcast.55), kind=kOutput, calls=%fused_computation.3 | convolution fusion | flops 67371008 | bytes 6553600 | tf_op jit(solution)/shard_map/dot_general | solution.py:155
  48.7 6.7 %all-to-all-start.1 = ((f32[8,8,256,16]{2,3,1,0:T(8,128)}), f32[8,8,256,16]{2,3,1,0:T(8,128)S(1)}, u32[]{:S(2)}, u32[]{:S(2)}) async-start(f32[8,8,256,16]{2,3,1,0:T(8,128)} %bitcast.7), calls=%async_computation.1 | async-start | bytes 2097152 | tf_op jit(solution)/shard_map/all_to_all | solution.py:160
  55.4 2.3 %convert_reduce_fusion = f32[8,256]{1,0:T(8,128)S(1)} fusion(s32[8,2560]{1,0:T(8,128)S(1)} %get-tuple-element.23), kind=kLoop, calls=%fused_computation.1 | loop fusion | flops 15726592 | bytes 90112 | tf_op jit(solution)/shard_map/reduce_sum | solution.py:145
  57.7 11.6 %all-to-all-done.1 = f32[8,8,256,16]{2,3,1,0:T(8,128)S(1)} async-done(((f32[8,8,256,16]{2,3,1,0:T(8,128)}), f32[8,8,256,16]{2,3,1,0:T(8,128)S(1)}, u32[]{:S(2)}, u32[]{:S(2)}) %all-to-all-start.1) | async-done | bytes 1048608 | tf_op jit(solution)/shard_map/all_to_all | solution.py:160
  73.4 4.5 %collective-permute-done.1 = f32[8,4352]{1,0:T(8,128)S(1)} collective-permute-done((f32[8,4352]{1,0:T(8,128)S(1)}, f32[8,4352]{1,0:T(8,128)S(1)}, u32[]{:S(2)}, u32[]{:S(2)}) %collective-permute-start.1) | collective-permute-done | bytes 139296 | tf_op jit(solution)/shard_map/ppermute | solution.py:36
  77.9 2.0 %collective-permute-start.2 = (f32[8,4352]{1,0:T(8,128)S(1)}, f32[8,4352]{1,0:T(8,128)S(1)}, u32[]{:S(2)}, u32[]{:S(2)}) collective-permute-start(f32[8,4352]{1,0:T(8,128)S(1)} %add.111), channel_id=1, source_target_pairs={{0,32},{32,0},{64,96},{96,64},{128,160},{160,128},{192,224},{224,1... | collective-permute-start | bytes 417800 | tf_op jit(solution)/shard_map/ppermute | solution.py:36
  79.9 3.2 %collective-permute-done.2 = f32[8,4352]{1,0:T(8,128)S(1)} collective-permute-done((f32[8,4352]{1,0:T(8,128)S(1)}, f32[8,4352]{1,0:T(8,128)S(1)}, u32[]{:S(2)}, u32[]{:S(2)}) %collective-permute-start.2) | collective-permute-done | bytes 139296 | tf_op jit(solution)/shard_map/ppermute | solution.py:36
  83.1 3.4 %collective-permute-start.3 = (f32[8,4352]{1,0:T(8,128)S(1)}, f32[8,4352]{1,0:T(8,128)S(1)}, u32[]{:S(2)}, u32[]{:S(2)}) collective-permute-start(f32[8,4352]{1,0:T(8,128)S(1)} %add.112), channel_id=1, source_target_pairs={{0,64},{32,96},{64,0},{96,32},{128,192},{160,224},{192,128},{224,1... | collective-permute-start | bytes 417800 | tf_op jit(solution)/shard_map/ppermute | solution.py:36
  86.4 5.2 %collective-permute-done.3 = f32[8,4352]{1,0:T(8,128)S(1)} collective-permute-done((f32[8,4352]{1,0:T(8,128)S(1)}, f32[8,4352]{1,0:T(8,128)S(1)}, u32[]{:S(2)}, u32[]{:S(2)}) %collective-permute-start.3) | collective-permute-done | bytes 139296 | tf_op jit(solution)/shard_map/ppermute | solution.py:36
  91.6 6.5 %collective-permute-start.4 = (f32[8,4352]{1,0:T(8,128)S(1)}, f32[8,4352]{1,0:T(8,128)S(1)}, u32[]{:S(2)}, u32[]{:S(2)}) collective-permute-start(f32[8,4352]{1,0:T(8,128)S(1)} %add.113), channel_id=1, source_target_pairs={{0,128},{32,160},{64,192},{96,224},{128,0},{160,32},{192,64},{224,... | collective-permute-start | bytes 417800 | tf_op jit(solution)/shard_map/ppermute | solution.py:36
  98.1 3.4 %collective-permute-done.4 = f32[8,4352]{1,0:T(8,128)S(1)} collective-permute-done((f32[8,4352]{1,0:T(8,128)S(1)}, f32[8,4352]{1,0:T(8,128)S(1)}, u32[]{:S(2)}, u32[]{:S(2)}) %collective-permute-start.4) | collective-permute-done | bytes 139296 | tf_op jit(solution)/shard_map/ppermute | solution.py:36
  103.4 6.1 %all-to-all-start.2 = ((bf16[8,8,256,16]{2,3,1,0:T(8,128)(2,1)}), bf16[8,8,256,16]{2,3,1,0:T(8,128)(2,1)S(1)}, u32[]{:S(2)}, u32[]{:S(2)}) async-start(bf16[8,8,256,16]{2,3,1,0:T(8,128)(2,1)} %broadcast_in_dim.34), calls=%async_computation.2 | async-start | bytes 1048576 | tf_op jit(solution)/shard_map/all_to_all | solution.py:127
  109.5 7.5 %all-to-all-done.2 = bf16[8,8,256,16]{2,3,1,0:T(8,128)(2,1)S(1)} async-done(((bf16[8,8,256,16]{2,3,1,0:T(8,128)(2,1)}), bf16[8,8,256,16]{2,3,1,0:T(8,128)(2,1)S(1)}, u32[]{:S(2)}, u32[]{:S(2)}) %all-to-all-start.2) | async-done | bytes 524320 | tf_op jit(solution)/shard_map/all_to_all | solution.py:127
  117.0 3.0 %fusion.5 = f32[64,16,128]{2,1,0:T(8,128)S(1)} fusion(bf16[64,256,16]{1,2,0:T(8,128)(2,1)S(1)} %bitcast.50, bf16[64,256,128]{2,1,0:T(8,128)(2,1)} %get-tuple-element.11), kind=kOutput, calls=%fused_computation.29 | convolution fusion | flops 67108864 | bytes 5242880 | tf_op jit(solution)/shard_map/dot_general | solution.py:178
  127.0 4.3 %collective-permute-done.6 = f32[8,32,128]{2,1,0:T(8,128)S(1)} collective-permute-done((f32[8,32,128]{2,1,0:T(8,128)S(1)}, f32[8,32,128]{2,1,0:T(8,128)S(1)}, u32[]{:S(2)}, u32[]{:S(2)}) %collective-permute-start.6) | collective-permute-done | bytes 131104 | tf_op jit(solution)/shard_map/ppermute | solution.py:36
  131.4 4.2 %collective-permute-done.7 = f32[4,32,128]{2,1,0:T(8,128)S(1)} collective-permute-done((f32[4,32,128]{2,1,0:T(8,128)S(1)}, f32[4,32,128]{2,1,0:T(8,128)S(1)}, u32[]{:S(2)}, u32[]{:S(2)}) %collective-permute-start.7) | collective-permute-done | bytes 65568 | tf_op jit(solution)/shard_map/ppermute | solution.py:36
  135.7 3.5 %collective-permute-start.8 = (f32[2,32,128]{2,1,0:T(8,128)S(1)}, f32[2,32,128]{2,1,0:T(8,128)S(1)}, u32[]{:S(2)}, u32[]{:S(2)}) collective-permute-start(f32[2,32,128]{2,1,0:T(8,128)S(1)} %dynamic-slice_bitcast_fusion.3), channel_id=1, source_target_pairs={{0,64},{32,96},{64,0},{96,32},{128,192},{160,224},{192,128},{224,1... | collective-permute-start | bytes 98312 | tf_op jit(solution)/shard_map/ppermute | solution.py:36
  139.5 1.6 %collective-permute-done.8 = f32[2,32,128]{2,1,0:T(8,128)S(1)} collective-permute-done((f32[2,32,128]{2,1,0:T(8,128)S(1)}, f32[2,32,128]{2,1,0:T(8,128)S(1)}, u32[]{:S(2)}, u32[]{:S(2)}) %collective-permute-start.8) | collective-permute-done | bytes 32800 | tf_op jit(solution)/shard_map/ppermute | solution.py:36
  141.2 5.4 %collective-permute-start.9 = (f32[1,32,128]{2,1,0:T(8,128)S(1)}, f32[1,32,128]{2,1,0:T(8,128)S(1)}, u32[]{:S(2)}, u32[]{:S(2)}) collective-permute-start(f32[1,32,128]{2,1,0:T(8,128)S(1)} %constant_dynamic-slice_fusion), channel_id=1, source_target_pairs={{0,128},{32,160},{64,192},{96,224},{128,0},{160,32},{192,64},{224,... | collective-permute-start | bytes 49160 | tf_op jit(solution)/shard_map/ppermute | solution.py:36
  147.3 1.6 %collective-permute-done.9 = f32[1,32,128]{2,1,0:T(8,128)S(1)} collective-permute-done((f32[1,32,128]{2,1,0:T(8,128)S(1)}, f32[1,32,128]{2,1,0:T(8,128)S(1)}, u32[]{:S(2)}, u32[]{:S(2)}) %collective-permute-start.9) | collective-permute-done | bytes 16416 | tf_op jit(solution)/shard_map/ppermute | solution.py:36
  (59 shorter events, 20.8 us)
Async XLA Ops:
  2.2 9.3 %copy-start.5 = (bf16[8,2560]{1,0:T(8,128)(2,1)}, bf16[8,2560]{1,0:T(8,128)(2,1)S(1)}, u32[]{:S(2)}) copy-start(bf16[8,2560]{1,0:T(8,128)(2,1)S(1)} %get-tuple-element.22.codes_ref) | copy-start | bytes 122884
  3.0 14.2 %all-to-all-start = ((bf16[8,8,2560]{2,1,0:T(8,128)(2,1)}), bf16[8,8,2560]{2,1,0:T(8,128)(2,1)S(1)}, u32[]{:S(2)}, u32[]{:S(2)}) async-start(bf16[8,8,2560]{2,1,0:T(8,128)(2,1)} %broadcast_in_dim.20), calls=%async_computation | async-start | bytes 655360 | tf_op jit(solution)/shard_map/all_to_all | solution.py:127
  17.2 0.8 copy-start.4
  40.7 3.5 %copy-start = (bf16[64,256,128]{2,1,0:T(8,128)(2,1)S(1)}, bf16[64,256,128]{2,1,0:T(8,128)(2,1)}, u32[]{:S(2)}) copy-start(bf16[64,256,128]{2,1,0:T(8,128)(2,1)} %get-tuple-element.12) | copy-start | bytes 12582916
  44.3 2.2 %copy-start.2 = (bf16[64,256,128]{2,1,0:T(8,128)(2,1)S(1)}, bf16[64,256,128]{2,1,0:T(8,128)(2,1)}, u32[]{:S(2)}) copy-start(bf16[64,256,128]{2,1,0:T(8,128)(2,1)} %get-tuple-element.13) | copy-start | bytes 12582916
  48.7 20.7 %all-to-all-start.1 = ((f32[8,8,256,16]{2,3,1,0:T(8,128)}), f32[8,8,256,16]{2,3,1,0:T(8,128)S(1)}, u32[]{:S(2)}, u32[]{:S(2)}) async-start(f32[8,8,256,16]{2,3,1,0:T(8,128)} %bitcast.7), calls=%async_computation.1 | async-start | bytes 2097152 | tf_op jit(solution)/shard_map/all_to_all | solution.py:160
  70.4 39.1 %copy-start.6 = (s32[32]{0:T(128)S(1)}, s32[32]{0:T(128)}, u32[]{:S(2)}) copy-start(s32[32]{0:T(128)} %constant.87) | copy-start | bytes 388
  70.4 1.6 %collective-permute-start = (f32[8,4352]{1,0:T(8,128)S(1)}, f32[8,4352]{1,0:T(8,128)S(1)}, u32[]{:S(2)}, u32[]{:S(2)}) collective-permute-start(f32[8,4352]{1,0:T(8,128)S(1)} %pad_maximum_fusion), channel_id=1, source_target_pairs={{0,8},{8,0},{1,9},{9,1},{2,10},{10,2},{3,11},{11,3},{4,12},{12,4},... | collective-permute-start | bytes 417800 | tf_op jit(solution)/shard_map/ppermute | solution.py:36
  72.1 5.8 %collective-permute-start.1 = (f32[8,4352]{1,0:T(8,128)S(1)}, f32[8,4352]{1,0:T(8,128)S(1)}, u32[]{:S(2)}, u32[]{:S(2)}) collective-permute-start(f32[8,4352]{1,0:T(8,128)S(1)} %fusion.2), channel_id=1, source_target_pairs={{0,16},{16,0},{1,17},{17,1},{2,18},{18,2},{3,19},{19,3},{4,20},{20... | collective-permute-start | bytes 417800 | tf_op jit(solution)/shard_map/ppermute | solution.py:36
  77.9 5.2 %collective-permute-start.2 = (f32[8,4352]{1,0:T(8,128)S(1)}, f32[8,4352]{1,0:T(8,128)S(1)}, u32[]{:S(2)}, u32[]{:S(2)}) collective-permute-start(f32[8,4352]{1,0:T(8,128)S(1)} %add.111), channel_id=1, source_target_pairs={{0,32},{32,0},{64,96},{96,64},{128,160},{160,128},{192,224},{224,1... | collective-permute-start | bytes 417800 | tf_op jit(solution)/shard_map/ppermute | solution.py:36
  83.1 8.5 %collective-permute-start.3 = (f32[8,4352]{1,0:T(8,128)S(1)}, f32[8,4352]{1,0:T(8,128)S(1)}, u32[]{:S(2)}, u32[]{:S(2)}) collective-permute-start(f32[8,4352]{1,0:T(8,128)S(1)} %add.112), channel_id=1, source_target_pairs={{0,64},{32,96},{64,0},{96,32},{128,192},{160,224},{192,128},{224,1... | collective-permute-start | bytes 417800 | tf_op jit(solution)/shard_map/ppermute | solution.py:36
  91.6 9.9 %collective-permute-start.4 = (f32[8,4352]{1,0:T(8,128)S(1)}, f32[8,4352]{1,0:T(8,128)S(1)}, u32[]{:S(2)}, u32[]{:S(2)}) collective-permute-start(f32[8,4352]{1,0:T(8,128)S(1)} %add.113), channel_id=1, source_target_pairs={{0,128},{32,160},{64,192},{96,224},{128,0},{160,32},{192,64},{224,... | collective-permute-start | bytes 417800 | tf_op jit(solution)/shard_map/ppermute | solution.py:36
  103.4 13.6 %all-to-all-start.2 = ((bf16[8,8,256,16]{2,3,1,0:T(8,128)(2,1)}), bf16[8,8,256,16]{2,3,1,0:T(8,128)(2,1)S(1)}, u32[]{:S(2)}, u32[]{:S(2)}) async-start(bf16[8,8,256,16]{2,3,1,0:T(8,128)(2,1)} %broadcast_in_dim.34), calls=%async_computation.2 | async-start | bytes 1048576 | tf_op jit(solution)/shard_map/all_to_all | solution.py:127
  117.0 3.4 %copy-start.1 = (bf16[64,256,128]{2,1,0:T(8,128)(2,1)S(1)}, bf16[64,256,128]{2,1,0:T(8,128)(2,1)}, u32[]{:S(2)}) copy-start(bf16[64,256,128]{2,1,0:T(8,128)(2,1)} %get-tuple-element.12) | copy-start | bytes 12582916
  120.5 2.2 %copy-start.3 = (bf16[64,256,128]{2,1,0:T(8,128)(2,1)S(1)}, bf16[64,256,128]{2,1,0:T(8,128)(2,1)}, u32[]{:S(2)}) copy-start(bf16[64,256,128]{2,1,0:T(8,128)(2,1)} %get-tuple-element.13) | copy-start | bytes 12582916
  124.0 1.6 %collective-permute-start.5 = (f32[16,32,128]{2,1,0:T(8,128)S(1)}, f32[16,32,128]{2,1,0:T(8,128)S(1)}, u32[]{:S(2)}, u32[]{:S(2)}) collective-permute-start(f32[16,32,128]{2,1,0:T(8,128)S(1)} %dynamic-slice_bitcast_fusion), channel_id=1, source_target_pairs={{0,8},{8,0},{1,9},{9,1},{2,10},{10,2},{3,11},{11,3},{4,12},{12,4},... | collective-permute-start | bytes 786440 | tf_op jit(solution)/shard_map/ppermute | solution.py:36
  125.7 5.6 %collective-permute-start.6 = (f32[8,32,128]{2,1,0:T(8,128)S(1)}, f32[8,32,128]{2,1,0:T(8,128)S(1)}, u32[]{:S(2)}, u32[]{:S(2)}) collective-permute-start(f32[8,32,128]{2,1,0:T(8,128)S(1)} %dynamic-slice_bitcast_fusion.1), channel_id=1, source_target_pairs={{0,16},{16,0},{1,17},{17,1},{2,18},{18,2},{3,19},{19,3},{4,20},{20... | collective-permute-start | bytes 393224 | tf_op jit(solution)/shard_map/ppermute | solution.py:36
  131.3 4.4 %collective-permute-start.7 = (f32[4,32,128]{2,1,0:T(8,128)S(1)}, f32[4,32,128]{2,1,0:T(8,128)S(1)}, u32[]{:S(2)}, u32[]{:S(2)}) collective-permute-start(f32[4,32,128]{2,1,0:T(8,128)S(1)} %dynamic-slice_bitcast_fusion.2), channel_id=1, source_target_pairs={{0,32},{32,0},{64,96},{96,64},{128,160},{160,128},{192,224},{224,1... | collective-permute-start | bytes 196616 | tf_op jit(solution)/shard_map/ppermute | solution.py:36
  135.7 5.4 %collective-permute-start.8 = (f32[2,32,128]{2,1,0:T(8,128)S(1)}, f32[2,32,128]{2,1,0:T(8,128)S(1)}, u32[]{:S(2)}, u32[]{:S(2)}) collective-permute-start(f32[2,32,128]{2,1,0:T(8,128)S(1)} %dynamic-slice_bitcast_fusion.3), channel_id=1, source_target_pairs={{0,64},{32,96},{64,0},{96,32},{128,192},{160,224},{192,128},{224,1... | collective-permute-start | bytes 98312 | tf_op jit(solution)/shard_map/ppermute | solution.py:36
  141.2 7.7 %collective-permute-start.9 = (f32[1,32,128]{2,1,0:T(8,128)S(1)}, f32[1,32,128]{2,1,0:T(8,128)S(1)}, u32[]{:S(2)}, u32[]{:S(2)}) collective-permute-start(f32[1,32,128]{2,1,0:T(8,128)S(1)} %constant_dynamic-slice_fusion), channel_id=1, source_target_pairs={{0,128},{32,160},{64,192},{96,224},{128,0},{160,32},{192,64},{224,... | collective-permute-start | bytes 49160 | tf_op jit(solution)/shard_map/ppermute | solution.py:36

commit v15 on v14

--- a/solution.py
+++ b/solution.py
@@ -155,24 +155,48 @@
         lax.dot_general(part, rot3, dims, preferred_element_type=jnp.float32) for part in h_parts
     )
 
-    partial = partial.reshape(n_feat, groups, K, DS)
-    sums = jnp.sum(
-        lax.all_to_all(partial, feat_names, split_axis=0, concat_axis=0, tiled=True), axis=0
-    )
-    packed = jnp.concatenate([sums.reshape(groups, K * DS), counts], axis=1)
-
-    packed = row_psum(packed, steps)
-    total_sums = packed[:, : K * DS].reshape(groups, K, DS)
-    total_counts = packed[:, K * DS :]
-    cents = total_sums / (total_counts[:, :, None] + 1.0)
-    centroids_all = cents.transpose(1, 0, 2).reshape(K, groups * DS)
-
-    row_index = lax.axis_index(row_names)
-    share = K // n_row
-    centroids = lax.dynamic_slice_in_dim(centroids_all, row_index * share, share, 0)
-
-    table = broadcast_over(cents.astype(jnp.bfloat16), feat_names, n_feat)
-    table = table.reshape(m_all, K, DS)
+    if "c" in row_names:
+        group_names = feat_names + ("c",)
+        half = K // 2
+        counts = counts + lax.ppermute(counts, "c", [(0, 1), (1, 0)])
+        core = lax.axis_index("c")
+        counts = lax.dynamic_index_in_dim(
+            counts.reshape(groups, K // 16, 2, 8), core, 2, keepdims=False
+        ).reshape(groups, half)
+        parts = partial.reshape(n_feat, groups, K // 16, 2, 8, DS).transpose(0, 3, 1, 2, 4, 5)
+        parts = parts.reshape(2 * n_feat, groups, half, DS)
+        sums = jnp.sum(
+            lax.all_to_all(parts, group_names, split_axis=0, concat_axis=0, tiled=True), axis=0
+        )
+        packed = jnp.concatenate([sums.reshape(groups, half * DS), counts], axis=1)
+        packed = row_psum(packed, [st for st in steps if st[0] != "c"])
+        total_sums = packed[:, : half * DS].reshape(groups, half, DS)
+        total_counts = packed[:, half * DS :]
+        cents = total_sums / (total_counts[:, :, None] + 1.0)
+        centroids_all = cents.transpose(1, 0, 2).reshape(half, groups * DS)
+        row_index = lax.axis_index(row_names)
+        share = K // n_row
+        centroids = lax.dynamic_slice_in_dim(centroids_all, (row_index // 2) * share, share, 0)
+        table = broadcast_over(cents.astype(jnp.bfloat16), group_names, 2 * n_feat)
+        table = table.reshape(n_feat, 2, groups, K // 16, 8, DS).transpose(0, 2, 3, 1, 4, 5)
+        table = table.reshape(m_all, K, DS)
+    else:
+        partial = partial.reshape(n_feat, groups, K, DS)
+        sums = jnp.sum(
+            lax.all_to_all(partial, feat_names, split_axis=0, concat_axis=0, tiled=True), axis=0
+        )
+        packed = jnp.concatenate([sums.reshape(groups, K * DS), counts], axis=1)
+        packed = row_psum(packed, steps)
+        total_sums = packed[:, : K * DS].reshape(groups, K, DS)
+        total_counts = packed[:, K * DS :]
+        cents = total_sums / (total_counts[:, :, None] + 1.0)
+        centroids_all = cents.transpose(1, 0, 2).reshape(K, groups * DS)
+        row_index = lax.axis_index(row_names)
+        share = K // n_row
+        centroids = lax.dynamic_slice_in_dim(centroids_all, row_index * share, share, 0)
+        table = broadcast_over(cents.astype(jnp.bfloat16), feat_names, n_feat)
+        table = table.reshape(m_all, K, DS)
+
     dims = (((1,), (1,)), ((0,), (0,)))
     grad = sum(
         lax.dot_general(table, part, dims, preferred_element_type=jnp.float32) for part in h_parts

time: 152 us -> 171 us (1.12)
  local copies, waits for them, and re-layouts: 9.73 us -> 34.2 us
  waiting for transfers between devices: 50.5 us -> 47.6 us
    transpose x1 -> x3, local copies, waits for them, and re-layouts: 0.3 us -> 11.1 us  [the longest x1 7.79 us: shards(): partial.reshape(n_feat, groups, K // 16, 2, 8, DS)]
    reshape x2 -> x5, local copies, waits for them, and re-layouts: 0.98 us -> 6.76 us  [the longest x1 5.97 us: shards(): parts = parts.reshape(2 * n_feat, groups, half, DS)]
    ppermute x10 -> x9, waiting for transfers between devices: 30.9 us -> 25.2 us  [exchange(): return lax.ppermute(x, name, pairs)]
    add x0 -> x1, local copies, waits for them, and re-layouts: none -> 4.61 us  [shards(): sum((lax.dot_general(part, rot3, dims, preferred_element_type=jnp.float32...]
    all_to_all x0 -> x1, local copies, waits for them, and re-layouts: none -> 3.07 us  [broadcast_over(): lax.all_to_all(copies, names, split_axis=0, concat_axis=0, tiled=True)]
    all_to_all x2, waiting for transfers between devices: 8 us -> 10.2 us  [broadcast_over(): lax.all_to_all(copies, names, split_axis=0, concat_axis=0, tiled=True)]
    ppermute x10 -> x9, starting transfers between devices: 23.8 us -> 22.8 us  [exchange(): return lax.ppermute(x, name, pairs)]
    unnamed x16 -> x19, local copies, waits for them, and re-layouts: 5.51 us -> 5.74 us
where the time goes in v15:
time: 171 us; the launch traced here: 169 us
  waiting for transfers between devices  47.6 us (28%)
  starting transfers between devices  43.8 us (26%)
  local copies, waits for them, and re-layouts  34.2 us (20%)
  Pallas kernels  28 us (16%)
  matrix products  9.63 us (6%)
  other arithmetic  4.25 us (2%)
    pallas_call x2, Pallas kernels, codeword_means(): pl.pallas_call(means_kernel, grid_spec=pltpu.PrefetchScalarGridSpec(num_s...  28 us
    ppermute x9, waiting for transfers between devices, exchange(): return lax.ppermute(x, name, pairs)  25.2 us
    ppermute x9, starting transfers between devices, exchange(): return lax.ppermute(x, name, pairs)  22.8 us
    all_to_all x2, starting transfers between devices, broadcast_over(): lax.all_to_all(copies, names, split_axis=0, concat_axis=0, tiled=True)  14 us
    all_to_all x1, waiting for transfers between devices, shards(): lax.all_to_all(parts, group_names, split_axis=0, concat_axis=0, tiled=True)  11.2 us
    all_to_all x2, waiting for transfers between devices, broadcast_over(): lax.all_to_all(copies, names, split_axis=0, concat_axis=0, tiled=True)  10.2 us
    transpose x1, local copies, waits for them, and re-layouts, shards(): partial.reshape(n_feat, groups, K // 16, 2, 8, DS)  7.79 us
    all_to_all x1, starting transfers between devices, shards(): lax.all_to_all(parts, group_names, split_axis=0, concat_axis=0, tiled=True)  6.71 us
  transfers between devices with their start and end apart: 13, of which 13 were waited for; matrix products, arithmetic and copies ran while one was open for 3% of the time, Pallas kernels for 3%

profile of v15, /device:TPU:4, one launch (start us, length us, event | category | flops | bytes accessed | tf_op | source)
XLA Modules:
  0.0 169.0 jit_solution(284710165870149137)
XLA Ops:
  3.0 7.4 %all-to-all-start = ((bf16[8,8,2560]{2,1,0:T(8,128)(2,1)}), bf16[8,8,2560]{2,1,0:T(8,128)(2,1)S(1)}, u32[]{:S(2)}, u32[]{:S(2)}) async-start(bf16[8,8,2560]{2,1,0:T(8,128)(2,1)} %broadcast_in_dim.20), calls=%async_computation | async-start | bytes 655360 | tf_op jit(solution)/shard_map/all_to_all | solution.py:127
  11.5 5.2 %shard_map.77 = (bf16[64,256,128]{2,1,0:T(8,128)(2,1)}, bf16[64,256,128]{2,1,0:T(8,128)(2,1)}, bf16[64,256,128]{2,1,0:T(8,128)(2,1)}) custom-call(s32[1]{0:T(128)} %bitcast.block_ref, bf16[8,2560]{1,0:T(8,128)(2,1)} %copy-done.6, bf16[2560,128]{1,0:T(8,128)(2,1)} %vec_ref.3), custom_call_target="tpu_custom_call" | custom-call | flops 1342177280 | bytes 2269184 | tf_op jit(solution)/shard_map/pallas_call | solution.py:78
  17.9 22.8 %shard_map.78 = (bf16[64,256,128]{2,1,0:T(8,128)(2,1)}, bf16[64,256,128]{2,1,0:T(8,128)(2,1)}, bf16[64,256,128]{2,1,0:T(8,128)(2,1)}) custom-call(s32[1]{0:T(128)} %bitcast.block_ref, bf16[64,2560]{1,0:T(8,128)(2,1)} %bitcast.72, bf16[2560,128]{1,0:T(8,128)(2,1)} %vec_ref.3, ...), custom_call_target="tpu_custom_call", output_to_operand_aliasing={{0}: (3, {}), {1}: (4, {}), {2}: (5, {})} | custom-call | flops 9395240960 | bytes 11993088 | tf_op jit(solution)/shard_map/pallas_call | solution.py:101
  40.7 3.5 %fusion.3 = f32[64,256,16]{1,2,0:T(8,128)S(1)} fusion(bf16[64,256,128]{2,1,0:T(8,128)(2,1)} %get-tuple-element.11, bf16[64,128,16]{1,2,0:T(8,128)(2,1)S(1)} %bitcast.62), kind=kOutput, calls=%fused_computation.29 | convolution fusion | flops 67108864 | bytes 5505024 | tf_op jit(solution)/shard_map/dot_general | solution.py:155
  47.6 4.6 %copy.57 = f32[64,256,16]{2,1,0:T(8,128)} copy(f32[64,256,16]{1,2,0:T(8,128)S(1)} %convolution_add_fusion) | data formatting | bytes 2097152 | tf_op jit(solution)/shard_map/add | solution.py:154
  52.2 7.8 %copy.58 = f32[8,2,8,16,8,16]{5,4,3,2,1,0:T(8,128)} copy(f32[8,2,8,16,8,16]{5,4,1,3,2,0:T(8,128)} %bitcast.59) | data formatting | bytes 2097152 | tf_op jit(solution)/shard_map/transpose | solution.py:166
  60.0 6.0 %copy.59 = f32[16,8,128,16]{2,3,1,0:T(8,128)} copy(f32[16,8,128,16]{3,2,1,0:T(8,128)} %bitcast.60) | data formatting | bytes 2097152 | tf_op jit(solution)/shard_map/reshape | solution.py:167
  66.0 6.7 %all-to-all-start.1 = ((f32[16,8,128,16]{2,3,1,0:T(8,128)}), f32[16,8,128,16]{2,3,1,0:T(8,128)S(1)}, u32[]{:S(2)}, u32[]{:S(2)}) async-start(f32[16,8,128,16]{2,3,1,0:T(8,128)} %copy.59), calls=%async_computation.1 | async-start | bytes 2097152 | tf_op jit(solution)/shard_map/all_to_all | solution.py:169
  72.7 2.3 %convert_reduce_fusion = f32[8,256]{1,0:T(8,128)S(1)} fusion(s32[8,2560]{1,0:T(8,128)S(1)} %get-tuple-element.25), kind=kLoop, calls=%fused_computation.1 | loop fusion | flops 15726592 | bytes 90112 | tf_op jit(solution)/shard_map/reduce_sum | solution.py:145
  76.9 11.2 %all-to-all-done.1 = f32[16,8,128,16]{2,3,1,0:T(8,128)S(1)} async-done(((f32[16,8,128,16]{2,3,1,0:T(8,128)}), f32[16,8,128,16]{2,3,1,0:T(8,128)S(1)}, u32[]{:S(2)}, u32[]{:S(2)}) %all-to-all-start.1) | async-done | bytes 1048608 | tf_op jit(solution)/shard_map/all_to_all | solution.py:169
  89.9 3.1 %collective-permute-done.1 = f32[8,2176]{1,0:T(8,128)S(1)} collective-permute-done((f32[8,2176]{1,0:T(8,128)S(1)}, f32[8,2176]{1,0:T(8,128)S(1)}, u32[]{:S(2)}, u32[]{:S(2)}) %collective-permute-start.1) | collective-permute-done | bytes 69664 | tf_op jit(solution)/shard_map/ppermute | solution.py:36
  95.0 2.4 %collective-permute-done.2 = f32[8,2176]{1,0:T(8,128)S(1)} collective-permute-done((f32[8,2176]{1,0:T(8,128)S(1)}, f32[8,2176]{1,0:T(8,128)S(1)}, u32[]{:S(2)}, u32[]{:S(2)}) %collective-permute-start.2) | collective-permute-done | bytes 69664 | tf_op jit(solution)/shard_map/ppermute | solution.py:36
  97.4 3.4 %collective-permute-start.3 = (f32[8,2176]{1,0:T(8,128)S(1)}, f32[8,2176]{1,0:T(8,128)S(1)}, u32[]{:S(2)}, u32[]{:S(2)}) collective-permute-start(f32[8,2176]{1,0:T(8,128)S(1)} %add.118), channel_id=1, source_target_pairs={{0,64},{32,96},{64,0},{96,32},{128,192},{160,224},{192,128},{224,1... | collective-permute-start | bytes 208904 | tf_op jit(solution)/shard_map/ppermute | solution.py:36
  100.8 2.3 %collective-permute-done.3 = f32[8,2176]{1,0:T(8,128)S(1)} collective-permute-done((f32[8,2176]{1,0:T(8,128)S(1)}, f32[8,2176]{1,0:T(8,128)S(1)}, u32[]{:S(2)}, u32[]{:S(2)}) %collective-permute-start.3) | collective-permute-done | bytes 69664 | tf_op jit(solution)/shard_map/ppermute | solution.py:36
  103.1 7.7 %collective-permute-start.4 = (f32[8,2176]{1,0:T(8,128)S(1)}, f32[8,2176]{1,0:T(8,128)S(1)}, u32[]{:S(2)}, u32[]{:S(2)}) collective-permute-start(f32[8,2176]{1,0:T(8,128)S(1)} %add.119), channel_id=1, source_target_pairs={{0,128},{32,160},{64,192},{96,224},{128,0},{160,32},{192,64},{224,... | collective-permute-start | bytes 208904 | tf_op jit(solution)/shard_map/ppermute | solution.py:36
  110.8 2.6 %collective-permute-done.4 = f32[8,2176]{1,0:T(8,128)S(1)} collective-permute-done((f32[8,2176]{1,0:T(8,128)S(1)}, f32[8,2176]{1,0:T(8,128)S(1)}, u32[]{:S(2)}, u32[]{:S(2)}) %collective-permute-start.4) | collective-permute-done | bytes 69664 | tf_op jit(solution)/shard_map/ppermute | solution.py:36
  114.8 6.6 %all-to-all-start.2 = ((bf16[16,8,128,16]{2,3,1,0:T(8,128)(2,1)}), bf16[16,8,128,16]{2,3,1,0:T(8,128)(2,1)S(1)}, u32[]{:S(2)}, u32[]{:S(2)}) async-start(bf16[16,8,128,16]{2,3,1,0:T(8,128)(2,1)} %broadcast_in_dim.34), calls=%async_computation.2 | async-start | bytes 1048576 | tf_op jit(solution)/shard_map/all_to_all | solution.py:127
  121.5 9.8 %all-to-all-done.2 = bf16[16,8,128,16]{2,3,1,0:T(8,128)(2,1)S(1)} async-done(((bf16[16,8,128,16]{2,3,1,0:T(8,128)(2,1)}), bf16[16,8,128,16]{2,3,1,0:T(8,128)(2,1)S(1)}, u32[]{:S(2)}, u32[]{:S(2)}) %all-to-all-start.2) | async-done | bytes 524320 | tf_op jit(solution)/shard_map/all_to_all | solution.py:127
  131.2 3.1 %copy.63 = bf16[16,8,128,16]{3,2,1,0:T(8,128)(2,1)} copy(bf16[16,8,128,16]{2,3,1,0:T(8,128)(2,1)S(1)} %all-to-all-done.2) | data formatting | bytes 1048576 | tf_op jit(solution)/shard_map/all_to_all | solution.py:127
  134.3 3.1 %copy.64 = bf16[8,8,16,2,8,16]{5,4,3,2,1,0:T(8,128)(2,1)S(1)} copy(bf16[8,8,16,2,8,16]{5,4,2,1,3,0:T(8,128)(2,1)} %bitcast.61) | data formatting | bytes 1048576 | tf_op jit(solution)/shard_map/transpose | solution.py:181
  147.0 4.3 %collective-permute-done.6 = f32[8,32,128]{2,1,0:T(8,128)S(1)} collective-permute-done((f32[8,32,128]{2,1,0:T(8,128)S(1)}, f32[8,32,128]{2,1,0:T(8,128)S(1)}, u32[]{:S(2)}, u32[]{:S(2)}) %collective-permute-start.6) | collective-permute-done | bytes 131104 | tf_op jit(solution)/shard_map/ppermute | solution.py:36
  151.5 4.2 %collective-permute-done.7 = f32[4,32,128]{2,1,0:T(8,128)S(1)} collective-permute-done((f32[4,32,128]{2,1,0:T(8,128)S(1)}, f32[4,32,128]{2,1,0:T(8,128)S(1)}, u32[]{:S(2)}, u32[]{:S(2)}) %collective-permute-start.7) | collective-permute-done | bytes 65568 | tf_op jit(solution)/shard_map/ppermute | solution.py:36
  156.8 3.9 %collective-permute-done.8 = f32[2,32,128]{2,1,0:T(8,128)S(1)} collective-permute-done((f32[2,32,128]{2,1,0:T(8,128)S(1)}, f32[2,32,128]{2,1,0:T(8,128)S(1)}, u32[]{:S(2)}, u32[]{:S(2)}) %collective-permute-start.8) | collective-permute-done | bytes 32800 | tf_op jit(solution)/shard_map/ppermute | solution.py:36
  160.6 6.0 %collective-permute-start.9 = (f32[1,32,128]{2,1,0:T(8,128)S(1)}, f32[1,32,128]{2,1,0:T(8,128)S(1)}, u32[]{:S(2)}, u32[]{:S(2)}) collective-permute-start(f32[1,32,128]{2,1,0:T(8,128)S(1)} %constant_dynamic-slice_fusion), channel_id=1, source_target_pairs={{0,128},{32,160},{64,192},{96,224},{128,0},{160,32},{192,64},{224,... | collective-permute-start | bytes 49160 | tf_op jit(solution)/shard_map/ppermute | solution.py:36
  (70 shorter events, 27.5 us)
Async XLA Ops:
  2.2 9.3 %copy-start.6 = (bf16[8,2560]{1,0:T(8,128)(2,1)}, bf16[8,2560]{1,0:T(8,128)(2,1)S(1)}, u32[]{:S(2)}) copy-start(bf16[8,2560]{1,0:T(8,128)(2,1)S(1)} %get-tuple-element.24.codes_ref) | copy-start | bytes 122884
  3.0 14.2 %all-to-all-start = ((bf16[8,8,2560]{2,1,0:T(8,128)(2,1)}), bf16[8,8,2560]{2,1,0:T(8,128)(2,1)S(1)}, u32[]{:S(2)}, u32[]{:S(2)}) async-start(bf16[8,8,2560]{2,1,0:T(8,128)(2,1)} %broadcast_in_dim.20), calls=%async_computation | async-start | bytes 655360 | tf_op jit(solution)/shard_map/all_to_all | solution.py:127
  17.2 0.7 copy-start.5
  40.7 3.5 %copy-start.1 = (bf16[64,256,128]{2,1,0:T(8,128)(2,1)S(1)}, bf16[64,256,128]{2,1,0:T(8,128)(2,1)}, u32[]{:S(2)}) copy-start(bf16[64,256,128]{2,1,0:T(8,128)(2,1)} %get-tuple-element.12) | copy-start | bytes 12582916
  44.2 2.2 %copy-start.3 = (bf16[64,256,128]{2,1,0:T(8,128)(2,1)S(1)}, bf16[64,256,128]{2,1,0:T(8,128)(2,1)}, u32[]{:S(2)}) copy-start(bf16[64,256,128]{2,1,0:T(8,128)(2,1)} %get-tuple-element.13) | copy-start | bytes 12582916
  66.0 22.1 %all-to-all-start.1 = ((f32[16,8,128,16]{2,3,1,0:T(8,128)}), f32[16,8,128,16]{2,3,1,0:T(8,128)S(1)}, u32[]{:S(2)}, u32[]{:S(2)}) async-start(f32[16,8,128,16]{2,3,1,0:T(8,128)} %copy.59), calls=%async_computation.1 | async-start | bytes 2097152 | tf_op jit(solution)/shard_map/all_to_all | solution.py:169
  72.7 48.7 %copy-start.7 = (s32[32]{0:T(128)S(1)}, s32[32]{0:T(128)}, u32[]{:S(2)}) copy-start(s32[32]{0:T(128)} %constant.101) | copy-start | bytes 388
  75.1 1.3 collective-permute-start
  88.6 4.4 %collective-permute-start.1 = (f32[8,2176]{1,0:T(8,128)S(1)}, f32[8,2176]{1,0:T(8,128)S(1)}, u32[]{:S(2)}, u32[]{:S(2)}) collective-permute-start(f32[8,2176]{1,0:T(8,128)S(1)} %constant_dynamic-update-slice_fusion), channel_id=1, source_target_pairs={{0,16},{16,0},{1,17},{17,1},{2,18},{18,2},{3,19},{19,3},{4,20},{20... | collective-permute-start | bytes 208904 | tf_op jit(solution)/shard_map/ppermute | solution.py:36
  93.0 4.4 %collective-permute-start.2 = (f32[8,2176]{1,0:T(8,128)S(1)}, f32[8,2176]{1,0:T(8,128)S(1)}, u32[]{:S(2)}, u32[]{:S(2)}) collective-permute-start(f32[8,2176]{1,0:T(8,128)S(1)} %add.117), channel_id=1, source_target_pairs={{0,32},{32,0},{64,96},{96,64},{128,160},{160,128},{192,224},{224,1... | collective-permute-start | bytes 208904 | tf_op jit(solution)/shard_map/ppermute | solution.py:36
  97.4 5.6 %collective-permute-start.3 = (f32[8,2176]{1,0:T(8,128)S(1)}, f32[8,2176]{1,0:T(8,128)S(1)}, u32[]{:S(2)}, u32[]{:S(2)}) collective-permute-start(f32[8,2176]{1,0:T(8,128)S(1)} %add.118), channel_id=1, source_target_pairs={{0,64},{32,96},{64,0},{96,32},{128,192},{160,224},{192,128},{224,1... | collective-permute-start | bytes 208904 | tf_op jit(solution)/shard_map/ppermute | solution.py:36
  103.1 10.2 %collective-permute-start.4 = (f32[8,2176]{1,0:T(8,128)S(1)}, f32[8,2176]{1,0:T(8,128)S(1)}, u32[]{:S(2)}, u32[]{:S(2)}) collective-permute-start(f32[8,2176]{1,0:T(8,128)S(1)} %add.119), channel_id=1, source_target_pairs={{0,128},{32,160},{64,192},{96,224},{128,0},{160,32},{192,64},{224,... | collective-permute-start | bytes 208904 | tf_op jit(solution)/shard_map/ppermute | solution.py:36
  114.8 16.4 %all-to-all-start.2 = ((bf16[16,8,128,16]{2,3,1,0:T(8,128)(2,1)}), bf16[16,8,128,16]{2,3,1,0:T(8,128)(2,1)S(1)}, u32[]{:S(2)}, u32[]{:S(2)}) async-start(bf16[16,8,128,16]{2,3,1,0:T(8,128)(2,1)} %broadcast_in_dim.34), calls=%async_computation.2 | async-start | bytes 1048576 | tf_op jit(solution)/shard_map/all_to_all | solution.py:127
  134.3 3.4 %copy-start = (bf16[64,256,128]{2,1,0:T(8,128)(2,1)S(1)}, bf16[64,256,128]{2,1,0:T(8,128)(2,1)}, u32[]{:S(2)}) copy-start(bf16[64,256,128]{2,1,0:T(8,128)(2,1)} %get-tuple-element.11) | copy-start | bytes 12582916
  137.7 2.2 %copy-start.2 = (bf16[64,256,128]{2,1,0:T(8,128)(2,1)S(1)}, bf16[64,256,128]{2,1,0:T(8,128)(2,1)}, u32[]{:S(2)}) copy-start(bf16[64,256,128]{2,1,0:T(8,128)(2,1)} %get-tuple-element.12) | copy-start | bytes 12582916
  139.9 2.2 %copy-start.4 = (bf16[64,256,128]{2,1,0:T(8,128)(2,1)S(1)}, bf16[64,256,128]{2,1,0:T(8,128)(2,1)}, u32[]{:S(2)}) copy-start(bf16[64,256,128]{2,1,0:T(8,128)(2,1)} %get-tuple-element.13) | copy-start | bytes 12582916
  144.0 1.6 collective-permute-start.5
  145.7 5.6 %collective-permute-start.6 = (f32[8,32,128]{2,1,0:T(8,128)S(1)}, f32[8,32,128]{2,1,0:T(8,128)S(1)}, u32[]{:S(2)}, u32[]{:S(2)}) collective-permute-start(f32[8,32,128]{2,1,0:T(8,128)S(1)} %dynamic-slice_bitcast_fusion.1), channel_id=1, source_target_pairs={{0,16},{16,0},{1,17},{17,1},{2,18},{18,2},{3,19},{19,3},{4,20},{20... | collective-permute-start | bytes 393224 | tf_op jit(solution)/shard_map/ppermute | solution.py:36
  151.3 4.4 %collective-permute-start.7 = (f32[4,32,128]{2,1,0:T(8,128)S(1)}, f32[4,32,128]{2,1,0:T(8,128)S(1)}, u32[]{:S(2)}, u32[]{:S(2)}) collective-permute-start(f32[4,32,128]{2,1,0:T(8,128)S(1)} %dynamic-slice_bitcast_fusion.2), channel_id=1, source_target_pairs={{0,32},{32,0},{64,96},{96,64},{128,160},{160,128},{192,224},{224,1... | collective-permute-start | bytes 196616 | tf_op jit(solution)/shard_map/ppermute | solution.py:36
  155.7 4.9 %collective-permute-start.8 = (f32[2,32,128]{2,1,0:T(8,128)S(1)}, f32[2,32,128]{2,1,0:T(8,128)S(1)}, u32[]{:S(2)}, u32[]{:S(2)}) collective-permute-start(f32[2,32,128]{2,1,0:T(8,128)S(1)} %dynamic-slice_bitcast_fusion.3), channel_id=1, source_target_pairs={{0,64},{32,96},{64,0},{96,32},{128,192},{160,224},{192,128},{224,1... | collective-permute-start | bytes 98312 | tf_op jit(solution)/shard_map/ppermute | solution.py:36
  160.6 7.7 %collective-permute-start.9 = (f32[1,32,128]{2,1,0:T(8,128)S(1)}, f32[1,32,128]{2,1,0:T(8,128)S(1)}, u32[]{:S(2)}, u32[]{:S(2)}) collective-permute-start(f32[1,32,128]{2,1,0:T(8,128)S(1)} %constant_dynamic-slice_fusion), channel_id=1, source_target_pairs={{0,128},{32,160},{64,192},{96,224},{128,0},{160,32},{192,64},{224,... | collective-permute-start | bytes 49160 | tf_op jit(solution)/shard_map/ppermute | solution.py:36

commit v16 on v15

--- a/solution.py
+++ b/solution.py
@@ -158,12 +158,10 @@
     if "c" in row_names:
         group_names = feat_names + ("c",)
         half = K // 2
+        core = lax.axis_index("c")
         counts = counts + lax.ppermute(counts, "c", [(0, 1), (1, 0)])
-        core = lax.axis_index("c")
-        counts = lax.dynamic_index_in_dim(
-            counts.reshape(groups, K // 16, 2, 8), core, 2, keepdims=False
-        ).reshape(groups, half)
-        parts = partial.reshape(n_feat, groups, K // 16, 2, 8, DS).transpose(0, 3, 1, 2, 4, 5)
+        counts = lax.dynamic_index_in_dim(counts.reshape(groups, 2, half), core, 1, keepdims=False)
+        parts = partial.reshape(n_feat, groups, 2, half, DS).transpose(0, 2, 1, 3, 4)
         parts = parts.reshape(2 * n_feat, groups, half, DS)
         sums = jnp.sum(
             lax.all_to_all(parts, group_names, split_axis=0, concat_axis=0, tiled=True), axis=0
@@ -173,12 +171,18 @@
         total_sums = packed[:, : half * DS].reshape(groups, half, DS)
         total_counts = packed[:, half * DS :]
         cents = total_sums / (total_counts[:, :, None] + 1.0)
-        centroids_all = cents.transpose(1, 0, 2).reshape(half, groups * DS)
+        centroids_half = cents.transpose(1, 0, 2).reshape(half, groups * DS)
         row_index = lax.axis_index(row_names)
         share = K // n_row
-        centroids = lax.dynamic_slice_in_dim(centroids_all, (row_index // 2) * share, share, 0)
+        per_half = half // share
+        mine = lax.dynamic_slice_in_dim(centroids_half, (row_index % per_half) * share, share, 0)
+        theirs = lax.dynamic_slice_in_dim(
+            centroids_half, ((row_index ^ 1) % per_half) * share, share, 0
+        )
+        got = lax.ppermute(theirs, "c", [(0, 1), (1, 0)])
+        centroids = jnp.where(core == row_index // per_half, mine, got)
         table = broadcast_over(cents.astype(jnp.bfloat16), group_names, 2 * n_feat)
-        table = table.reshape(n_feat, 2, groups, K // 16, 8, DS).transpose(0, 2, 3, 1, 4, 5)
+        table = table.reshape(n_feat, 2, groups, half, DS).transpose(0, 2, 1, 3, 4)
         table = table.reshape(m_all, K, DS)
     else:
         partial = partial.reshape(n_feat, groups, K, DS)

time: 171 us -> 149 us (0.87)
  local copies, waits for them, and re-layouts: 34.2 us -> 11.5 us
    transpose x3 -> x2, local copies, waits for them, and re-layouts: 11.1 us -> 0.7 us  [the longest x1 0.54 us: shards(): table = table.reshape(n_feat, 2, groups, half, DS).transpose(0, 2, 1, 3, 4)]
    add x1 -> x0, local copies, waits for them, and re-layouts: 4.61 us -> none  [shards(): sum((lax.dot_general(part, rot3, dims, preferred_element_type=jnp.float32...]
    reshape x3, local copies, waits for them, and re-layouts: 6.29 us -> 2.04 us  [the longest x2 1.7 us: shards(): partial.reshape(n_feat, groups, 2, half, DS).transpose(0, 2, 1, 3, 4)]
    all_to_all x1 -> x0, local copies, waits for them, and re-layouts: 3.07 us -> none  [broadcast_over(): lax.all_to_all(copies, names, split_axis=0, concat_axis=0, tiled=True)]
    unnamed x19 -> x16, local copies, waits for them, and re-layouts: 5.74 us -> 5.5 us
  transfers between devices with their start and end apart: 13 -> 14, of which waited for: 13 -> 13; matrix products, arithmetic and copies ran while one was open for 3% -> 3% of each run, Pallas kernels for 3% -> 4%
where the time goes in v16:
time: 149 us; the launch traced here: 147 us
  waiting for transfers between devices  47.8 us (32%)
  starting transfers between devices  44 us (30%)
  Pallas kernels  27.9 us (19%)
  local copies, waits for them, and re-layouts  11.5 us (8%)
  matrix products  10.3 us (7%)
  other arithmetic  4.34 us (3%)
  between operations  1.59 us (1%)
    pallas_call x2, Pallas kernels, codeword_means(): pl.pallas_call(means_kernel, grid_spec=pltpu.PrefetchScalarGridSpec(num_s...  27.9 us
    ppermute x9, waiting for transfers between devices, exchange(): return lax.ppermute(x, name, pairs)  24.9 us
    ppermute x9, starting transfers between devices, exchange(): return lax.ppermute(x, name, pairs)  22.8 us
    all_to_all x2, starting transfers between devices, broadcast_over(): lax.all_to_all(copies, names, split_axis=0, concat_axis=0, tiled=True)  14 us
    all_to_all x1, waiting for transfers between devices, shards(): lax.all_to_all(parts, group_names, split_axis=0, concat_axis=0, tiled=True)  11.6 us
    all_to_all x2, waiting for transfers between devices, broadcast_over(): lax.all_to_all(copies, names, split_axis=0, concat_axis=0, tiled=True)  10.2 us
    all_to_all x1, starting transfers between devices, shards(): lax.all_to_all(parts, group_names, split_axis=0, concat_axis=0, tiled=True)  6.69 us
    dot_general x3, matrix products, shards(): lax.dot_general(part, rot3, dims, preferred_element_type=jnp.float32)  5.92 us
  transfers between devices with their start and end apart: 14, of which 13 were waited for; matrix products, arithmetic and copies ran while one was open for 3% of the time, Pallas kernels for 4%

profile of v16, /device:TPU:4, one launch (start us, length us, event | category | flops | bytes accessed | tf_op | source)
XLA Modules:
  0.0 147.5 jit_solution(5843951554544303621)
XLA Ops:
  3.0 7.4 %all-to-all-start = ((bf16[8,8,2560]{2,1,0:T(8,128)(2,1)}), bf16[8,8,2560]{2,1,0:T(8,128)(2,1)S(1)}, u32[]{:S(2)}, u32[]{:S(2)}) async-start(bf16[8,8,2560]{2,1,0:T(8,128)(2,1)} %broadcast_in_dim.20), calls=%async_computation | async-start | bytes 655360 | tf_op jit(solution)/shard_map/all_to_all | solution.py:127
  11.6 5.2 %shard_map.77 = (bf16[64,256,128]{2,1,0:T(8,128)(2,1)}, bf16[64,256,128]{2,1,0:T(8,128)(2,1)}, bf16[64,256,128]{2,1,0:T(8,128)(2,1)}) custom-call(s32[1]{0:T(128)} %bitcast.block_ref, bf16[8,2560]{1,0:T(8,128)(2,1)} %copy-done.5, bf16[2560,128]{1,0:T(8,128)(2,1)} %vec_ref.3), custom_call_target="tpu_custom_call" | custom-call | flops 1342177280 | bytes 2269184 | tf_op jit(solution)/shard_map/pallas_call | solution.py:78
  18.0 22.8 %shard_map.78 = (bf16[64,256,128]{2,1,0:T(8,128)(2,1)}, bf16[64,256,128]{2,1,0:T(8,128)(2,1)}, bf16[64,256,128]{2,1,0:T(8,128)(2,1)}) custom-call(s32[1]{0:T(128)} %bitcast.block_ref, bf16[64,2560]{1,0:T(8,128)(2,1)} %bitcast.75, bf16[2560,128]{1,0:T(8,128)(2,1)} %vec_ref.3, ...), custom_call_target="tpu_custom_call", output_to_operand_aliasing={{0}: (3, {}), {1}: (4, {}), {2}: (5, {})} | custom-call | flops 9395240960 | bytes 11993088 | tf_op jit(solution)/shard_map/pallas_call | solution.py:101
  40.7 3.5 %fusion.4 = f32[64,256,16]{1,2,0:T(8,128)S(1)} fusion(bf16[64,256,128]{2,1,0:T(8,128)(2,1)} %get-tuple-element.11, bf16[64,128,16]{1,2,0:T(8,128)(2,1)S(1)} %bitcast.62), kind=kOutput, calls=%fused_computation.31 | convolution fusion | flops 67108864 | bytes 5505024 | tf_op jit(solution)/shard_map/dot_general | solution.py:155
  49.4 6.7 %all-to-all-start.1 = ((f32[16,8,128,16]{2,3,1,0:T(8,128)}), f32[16,8,128,16]{2,3,1,0:T(8,128)S(1)}, u32[]{:S(2)}, u32[]{:S(2)}) async-start(f32[16,8,128,16]{2,3,1,0:T(8,128)} %bitcast.8), calls=%async_computation.1 | async-start | bytes 2097152 | tf_op jit(solution)/shard_map/all_to_all | solution.py:167
  56.1 2.3 %convert_reduce_fusion = f32[8,256]{1,0:T(8,128)S(1)} fusion(s32[8,2560]{1,0:T(8,128)S(1)} %get-tuple-element.23), kind=kLoop, calls=%fused_computation.1 | loop fusion | flops 15726592 | bytes 90112 | tf_op jit(solution)/shard_map/reduce_sum | solution.py:145
  59.9 11.6 %all-to-all-done.1 = f32[16,8,128,16]{2,3,1,0:T(8,128)S(1)} async-done(((f32[16,8,128,16]{2,3,1,0:T(8,128)}), f32[16,8,128,16]{2,3,1,0:T(8,128)S(1)}, u32[]{:S(2)}, u32[]{:S(2)}) %all-to-all-start.1) | async-done | bytes 1048608 | tf_op jit(solution)/shard_map/all_to_all | solution.py:167
  73.3 3.1 %collective-permute-done.1 = f32[8,2176]{1,0:T(8,128)S(1)} collective-permute-done((f32[8,2176]{1,0:T(8,128)S(1)}, f32[8,2176]{1,0:T(8,128)S(1)}, u32[]{:S(2)}, u32[]{:S(2)}) %collective-permute-start.1) | collective-permute-done | bytes 69664 | tf_op jit(solution)/shard_map/ppermute | solution.py:36
  76.4 2.0 %collective-permute-start.2 = (f32[8,2176]{1,0:T(8,128)S(1)}, f32[8,2176]{1,0:T(8,128)S(1)}, u32[]{:S(2)}, u32[]{:S(2)}) collective-permute-start(f32[8,2176]{1,0:T(8,128)S(1)} %fusion.2), channel_id=1, source_target_pairs={{0,32},{32,0},{64,96},{96,64},{128,160},{160,128},{192,224},{224,1... | collective-permute-start | bytes 208904 | tf_op jit(solution)/shard_map/ppermute | solution.py:36
  78.4 2.4 %collective-permute-done.2 = f32[8,2176]{1,0:T(8,128)S(1)} collective-permute-done((f32[8,2176]{1,0:T(8,128)S(1)}, f32[8,2176]{1,0:T(8,128)S(1)}, u32[]{:S(2)}, u32[]{:S(2)}) %collective-permute-start.2) | collective-permute-done | bytes 69664 | tf_op jit(solution)/shard_map/ppermute | solution.py:36
  80.8 3.4 %collective-permute-start.3 = (f32[8,2176]{1,0:T(8,128)S(1)}, f32[8,2176]{1,0:T(8,128)S(1)}, u32[]{:S(2)}, u32[]{:S(2)}) collective-permute-start(f32[8,2176]{1,0:T(8,128)S(1)} %add.130), channel_id=1, source_target_pairs={{0,64},{32,96},{64,0},{96,32},{128,192},{160,224},{192,128},{224,1... | collective-permute-start | bytes 208904 | tf_op jit(solution)/shard_map/ppermute | solution.py:36
  84.2 2.3 %collective-permute-done.3 = f32[8,2176]{1,0:T(8,128)S(1)} collective-permute-done((f32[8,2176]{1,0:T(8,128)S(1)}, f32[8,2176]{1,0:T(8,128)S(1)}, u32[]{:S(2)}, u32[]{:S(2)}) %collective-permute-start.3) | collective-permute-done | bytes 69664 | tf_op jit(solution)/shard_map/ppermute | solution.py:36
  86.5 7.7 %collective-permute-start.4 = (f32[8,2176]{1,0:T(8,128)S(1)}, f32[8,2176]{1,0:T(8,128)S(1)}, u32[]{:S(2)}, u32[]{:S(2)}) collective-permute-start(f32[8,2176]{1,0:T(8,128)S(1)} %add.131), channel_id=1, source_target_pairs={{0,128},{32,160},{64,192},{96,224},{128,0},{160,32},{192,64},{224,... | collective-permute-start | bytes 208904 | tf_op jit(solution)/shard_map/ppermute | solution.py:36
  94.1 2.6 %collective-permute-done.4 = f32[8,2176]{1,0:T(8,128)S(1)} collective-permute-done((f32[8,2176]{1,0:T(8,128)S(1)}, f32[8,2176]{1,0:T(8,128)S(1)}, u32[]{:S(2)}, u32[]{:S(2)}) %collective-permute-start.4) | collective-permute-done | bytes 69664 | tf_op jit(solution)/shard_map/ppermute | solution.py:36
  98.2 6.6 %all-to-all-start.2 = ((bf16[16,8,128,16]{2,3,1,0:T(8,128)(2,1)}), bf16[16,8,128,16]{2,3,1,0:T(8,128)(2,1)S(1)}, u32[]{:S(2)}, u32[]{:S(2)}) async-start(bf16[16,8,128,16]{2,3,1,0:T(8,128)(2,1)} %broadcast_in_dim.34), calls=%async_computation.2 | async-start | bytes 1048576 | tf_op jit(solution)/shard_map/all_to_all | solution.py:127
  104.9 9.8 %all-to-all-done.2 = bf16[16,8,128,16]{2,3,1,0:T(8,128)(2,1)S(1)} async-done(((bf16[16,8,128,16]{2,3,1,0:T(8,128)(2,1)}), bf16[16,8,128,16]{2,3,1,0:T(8,128)(2,1)S(1)}, u32[]{:S(2)}, u32[]{:S(2)}) %all-to-all-start.2) | async-done | bytes 524320 | tf_op jit(solution)/shard_map/all_to_all | solution.py:127
  115.5 3.0 %fusion.5 = f32[64,16,128]{2,1,0:T(8,128)S(1)} fusion(bf16[64,256,16]{1,2,0:T(8,128)(2,1)S(1)} %reshape.80, bf16[64,256,128]{2,1,0:T(8,128)(2,1)} %get-tuple-element.11), kind=kOutput, calls=%fused_computation.32 | convolution fusion | flops 67108864 | bytes 5242880 | tf_op jit(solution)/shard_map/dot_general | solution.py:206
  119.6 1.5 %copy-done.3 = bf16[64,256,128]{2,1,0:T(8,128)(2,1)S(1)} copy-done((bf16[64,256,128]{2,1,0:T(8,128)(2,1)S(1)}, bf16[64,256,128]{2,1,0:T(8,128)(2,1)}, u32[]{:S(2)}) %copy-start.3) | copy-done | bytes 4194328
  122.7 1.4 collective-permute-done.6
  124.1 1.3 collective-permute-start.7
  125.5 4.3 %collective-permute-done.7 = f32[8,32,128]{2,1,0:T(8,128)S(1)} collective-permute-done((f32[8,32,128]{2,1,0:T(8,128)S(1)}, f32[8,32,128]{2,1,0:T(8,128)S(1)}, u32[]{:S(2)}, u32[]{:S(2)}) %collective-permute-start.7) | collective-permute-done | bytes 131104 | tf_op jit(solution)/shard_map/ppermute | solution.py:36
  130.1 4.0 %collective-permute-done.8 = f32[4,32,128]{2,1,0:T(8,128)S(1)} collective-permute-done((f32[4,32,128]{2,1,0:T(8,128)S(1)}, f32[4,32,128]{2,1,0:T(8,128)S(1)}, u32[]{:S(2)}, u32[]{:S(2)}) %collective-permute-start.8) | collective-permute-done | bytes 65568 | tf_op jit(solution)/shard_map/ppermute | solution.py:36
  135.2 3.9 %collective-permute-done.9 = f32[2,32,128]{2,1,0:T(8,128)S(1)} collective-permute-done((f32[2,32,128]{2,1,0:T(8,128)S(1)}, f32[2,32,128]{2,1,0:T(8,128)S(1)}, u32[]{:S(2)}, u32[]{:S(2)}) %collective-permute-start.9) | collective-permute-done | bytes 32800 | tf_op jit(solution)/shard_map/ppermute | solution.py:36
  139.1 6.0 %collective-permute-start.10 = (f32[1,32,128]{2,1,0:T(8,128)S(1)}, f32[1,32,128]{2,1,0:T(8,128)S(1)}, u32[]{:S(2)}, u32[]{:S(2)}) collective-permute-start(f32[1,32,128]{2,1,0:T(8,128)S(1)} %constant_dynamic-slice_fusion), channel_id=1, source_target_pairs={{0,128},{32,160},{64,192},{96,224},{128,0},{160,32},{192,64},{224,... | collective-permute-start | bytes 49160 | tf_op jit(solution)/shard_map/ppermute | solution.py:36
  (67 shorter events, 21.2 us)
Async XLA Ops:
  2.2 9.3 %copy-start.5 = (bf16[8,2560]{1,0:T(8,128)(2,1)}, bf16[8,2560]{1,0:T(8,128)(2,1)S(1)}, u32[]{:S(2)}) copy-start(bf16[8,2560]{1,0:T(8,128)(2,1)S(1)} %get-tuple-element.22.codes_ref) | copy-start | bytes 122884
  3.0 14.2 %all-to-all-start = ((bf16[8,8,2560]{2,1,0:T(8,128)(2,1)}), bf16[8,8,2560]{2,1,0:T(8,128)(2,1)S(1)}, u32[]{:S(2)}, u32[]{:S(2)}) async-start(bf16[8,8,2560]{2,1,0:T(8,128)(2,1)} %broadcast_in_dim.20), calls=%async_computation | async-start | bytes 655360 | tf_op jit(solution)/shard_map/all_to_all | solution.py:127
  17.2 0.7 copy-start.4
  40.7 3.5 %copy-start = (bf16[64,256,128]{2,1,0:T(8,128)(2,1)S(1)}, bf16[64,256,128]{2,1,0:T(8,128)(2,1)}, u32[]{:S(2)}) copy-start(bf16[64,256,128]{2,1,0:T(8,128)(2,1)} %get-tuple-element.12) | copy-start | bytes 12582916
  44.3 2.2 %copy-start.2 = (bf16[64,256,128]{2,1,0:T(8,128)(2,1)S(1)}, bf16[64,256,128]{2,1,0:T(8,128)(2,1)}, u32[]{:S(2)}) copy-start(bf16[64,256,128]{2,1,0:T(8,128)(2,1)} %get-tuple-element.13) | copy-start | bytes 12582916
  49.4 22.0 %all-to-all-start.1 = ((f32[16,8,128,16]{2,3,1,0:T(8,128)}), f32[16,8,128,16]{2,3,1,0:T(8,128)S(1)}, u32[]{:S(2)}, u32[]{:S(2)}) async-start(f32[16,8,128,16]{2,3,1,0:T(8,128)} %bitcast.8), calls=%async_computation.1 | async-start | bytes 2097152 | tf_op jit(solution)/shard_map/all_to_all | solution.py:167
  56.1 48.8 %copy-start.6 = (s32[32]{0:T(128)S(1)}, s32[32]{0:T(128)}, u32[]{:S(2)}) copy-start(s32[32]{0:T(128)} %constant.117) | copy-start | bytes 388
  58.4 1.4 collective-permute-start
  72.0 4.4 %collective-permute-start.1 = (f32[8,2176]{1,0:T(8,128)S(1)}, f32[8,2176]{1,0:T(8,128)S(1)}, u32[]{:S(2)}, u32[]{:S(2)}) collective-permute-start(f32[8,2176]{1,0:T(8,128)S(1)} %pad_maximum_fusion), channel_id=1, source_target_pairs={{0,16},{16,0},{1,17},{17,1},{2,18},{18,2},{3,19},{19,3},{4,20},{20... | collective-permute-start | bytes 208904 | tf_op jit(solution)/shard_map/ppermute | solution.py:36
  76.4 4.4 %collective-permute-start.2 = (f32[8,2176]{1,0:T(8,128)S(1)}, f32[8,2176]{1,0:T(8,128)S(1)}, u32[]{:S(2)}, u32[]{:S(2)}) collective-permute-start(f32[8,2176]{1,0:T(8,128)S(1)} %fusion.2), channel_id=1, source_target_pairs={{0,32},{32,0},{64,96},{96,64},{128,160},{160,128},{192,224},{224,1... | collective-permute-start | bytes 208904 | tf_op jit(solution)/shard_map/ppermute | solution.py:36
  80.8 5.6 %collective-permute-start.3 = (f32[8,2176]{1,0:T(8,128)S(1)}, f32[8,2176]{1,0:T(8,128)S(1)}, u32[]{:S(2)}, u32[]{:S(2)}) collective-permute-start(f32[8,2176]{1,0:T(8,128)S(1)} %add.130), channel_id=1, source_target_pairs={{0,64},{32,96},{64,0},{96,32},{128,192},{160,224},{192,128},{224,1... | collective-permute-start | bytes 208904 | tf_op jit(solution)/shard_map/ppermute | solution.py:36
  86.5 10.2 %collective-permute-start.4 = (f32[8,2176]{1,0:T(8,128)S(1)}, f32[8,2176]{1,0:T(8,128)S(1)}, u32[]{:S(2)}, u32[]{:S(2)}) collective-permute-start(f32[8,2176]{1,0:T(8,128)S(1)} %add.131), channel_id=1, source_target_pairs={{0,128},{32,160},{64,192},{96,224},{128,0},{160,32},{192,64},{224,... | collective-permute-start | bytes 208904 | tf_op jit(solution)/shard_map/ppermute | solution.py:36
  98.2 16.4 %all-to-all-start.2 = ((bf16[16,8,128,16]{2,3,1,0:T(8,128)(2,1)}), bf16[16,8,128,16]{2,3,1,0:T(8,128)(2,1)S(1)}, u32[]{:S(2)}, u32[]{:S(2)}) async-start(bf16[16,8,128,16]{2,3,1,0:T(8,128)(2,1)} %broadcast_in_dim.34), calls=%async_computation.2 | async-start | bytes 1048576 | tf_op jit(solution)/shard_map/all_to_all | solution.py:127
  115.5 3.5 %copy-start.1 = (bf16[64,256,128]{2,1,0:T(8,128)(2,1)S(1)}, bf16[64,256,128]{2,1,0:T(8,128)(2,1)}, u32[]{:S(2)}) copy-start(bf16[64,256,128]{2,1,0:T(8,128)(2,1)} %get-tuple-element.12) | copy-start | bytes 12582916
  119.0 2.2 %copy-start.3 = (bf16[64,256,128]{2,1,0:T(8,128)(2,1)S(1)}, bf16[64,256,128]{2,1,0:T(8,128)(2,1)}, u32[]{:S(2)}) copy-start(bf16[64,256,128]{2,1,0:T(8,128)(2,1)} %get-tuple-element.13) | copy-start | bytes 12582916
  122.5 1.6 %collective-permute-start.6 = (f32[16,32,128]{2,1,0:T(8,128)S(1)}, f32[16,32,128]{2,1,0:T(8,128)S(1)}, u32[]{:S(2)}, u32[]{:S(2)}) collective-permute-start(f32[16,32,128]{2,1,0:T(8,128)S(1)} %dynamic-slice_bitcast_fusion), channel_id=1, source_target_pairs={{0,8},{8,0},{1,9},{9,1},{2,10},{10,2},{3,11},{11,3},{4,12},{12,4},... | collective-permute-start | bytes 786440 | tf_op jit(solution)/shard_map/ppermute | solution.py:36
  124.1 5.6 %collective-permute-start.7 = (f32[8,32,128]{2,1,0:T(8,128)S(1)}, f32[8,32,128]{2,1,0:T(8,128)S(1)}, u32[]{:S(2)}, u32[]{:S(2)}) collective-permute-start(f32[8,32,128]{2,1,0:T(8,128)S(1)} %dynamic-slice_bitcast_fusion.1), channel_id=1, source_target_pairs={{0,16},{16,0},{1,17},{17,1},{2,18},{18,2},{3,19},{19,3},{4,20},{20... | collective-permute-start | bytes 393224 | tf_op jit(solution)/shard_map/ppermute | solution.py:36
  129.8 4.4 %collective-permute-start.8 = (f32[4,32,128]{2,1,0:T(8,128)S(1)}, f32[4,32,128]{2,1,0:T(8,128)S(1)}, u32[]{:S(2)}, u32[]{:S(2)}) collective-permute-start(f32[4,32,128]{2,1,0:T(8,128)S(1)} %dynamic-slice_bitcast_fusion.2), channel_id=1, source_target_pairs={{0,32},{32,0},{64,96},{96,64},{128,160},{160,128},{192,224},{224,1... | collective-permute-start | bytes 196616 | tf_op jit(solution)/shard_map/ppermute | solution.py:36
  134.2 4.9 %collective-permute-start.9 = (f32[2,32,128]{2,1,0:T(8,128)S(1)}, f32[2,32,128]{2,1,0:T(8,128)S(1)}, u32[]{:S(2)}, u32[]{:S(2)}) collective-permute-start(f32[2,32,128]{2,1,0:T(8,128)S(1)} %dynamic-slice_bitcast_fusion.3), channel_id=1, source_target_pairs={{0,64},{32,96},{64,0},{96,32},{128,192},{160,224},{192,128},{224,1... | collective-permute-start | bytes 98312 | tf_op jit(solution)/shard_map/ppermute | solution.py:36
  135.1 10.0 %collective-permute-start.5 = (f32[8,128]{0,1:T(8,128)S(1)}, f32[8,128]{0,1:T(8,128)S(1)}, u32[]{:S(2)}, u32[]{:S(2)}) collective-permute-start(f32[8,128]{0,1:T(8,128)S(1)} %constant_dynamic-slice_fusion.1), channel_id=1, source_target_pairs={{0,8},{8,0},{1,9},{9,1},{2,10},{10,2},{3,11},{11,3},{4,12},{12,4},... | collective-permute-start | bytes 12296 | tf_op jit(solution)/shard_map/ppermute | solution.py:182
  139.1 7.7 %collective-permute-start.10 = (f32[1,32,128]{2,1,0:T(8,128)S(1)}, f32[1,32,128]{2,1,0:T(8,128)S(1)}, u32[]{:S(2)}, u32[]{:S(2)}) collective-permute-start(f32[1,32,128]{2,1,0:T(8,128)S(1)} %constant_dynamic-slice_fusion), channel_id=1, source_target_pairs={{0,128},{32,160},{64,192},{96,224},{128,0},{160,32},{192,64},{224,... | collective-permute-start | bytes 49160 | tf_op jit(solution)/shard_map/ppermute | solution.py:36

commit v17 on v15

--- a/solution.py
+++ b/solution.py
@@ -156,29 +156,44 @@
     )
 
     if "c" in row_names:
-        group_names = feat_names + ("c",)
-        half = K // 2
-        counts = counts + lax.ppermute(counts, "c", [(0, 1), (1, 0)])
-        core = lax.axis_index("c")
+        sub = ("xl", "c")
+        group_names = feat_names + sub
+        n_sub = 4
+        part_k = K // n_sub
+        me_sub = lax.axis_index(sub)
+        def sub_perm(flip):
+            return [(i, i ^ flip) for i in range(n_sub)]
+        counts = sum(
+            [counts] + [lax.ppermute(counts, sub, sub_perm(t)) for t in range(1, n_sub)]
+        )
         counts = lax.dynamic_index_in_dim(
-            counts.reshape(groups, K // 16, 2, 8), core, 2, keepdims=False
-        ).reshape(groups, half)
-        parts = partial.reshape(n_feat, groups, K // 16, 2, 8, DS).transpose(0, 3, 1, 2, 4, 5)
-        parts = parts.reshape(2 * n_feat, groups, half, DS)
+            counts.reshape(groups, n_sub, part_k), me_sub, 1, keepdims=False
+        )
+        parts = partial.reshape(n_feat, groups, n_sub, part_k, DS).transpose(0, 2, 1, 3, 4)
+        parts = parts.reshape(n_sub * n_feat, groups, part_k, DS)
         sums = jnp.sum(
             lax.all_to_all(parts, group_names, split_axis=0, concat_axis=0, tiled=True), axis=0
         )
-        packed = jnp.concatenate([sums.reshape(groups, half * DS), counts], axis=1)
-        packed = row_psum(packed, [st for st in steps if st[0] != "c"])
-        total_sums = packed[:, : half * DS].reshape(groups, half, DS)
-        total_counts = packed[:, half * DS :]
+        packed = jnp.concatenate([sums.reshape(groups, part_k * DS), counts], axis=1)
+        packed = row_psum(packed, [st for st in steps if st[0] not in sub])
+        total_sums = packed[:, : part_k * DS].reshape(groups, part_k, DS)
+        total_counts = packed[:, part_k * DS :]
         cents = total_sums / (total_counts[:, :, None] + 1.0)
-        centroids_all = cents.transpose(1, 0, 2).reshape(half, groups * DS)
+        centroids_part = cents.transpose(1, 0, 2).reshape(part_k, groups * DS)
         row_index = lax.axis_index(row_names)
         share = K // n_row
-        centroids = lax.dynamic_slice_in_dim(centroids_all, (row_index // 2) * share, share, 0)
-        table = broadcast_over(cents.astype(jnp.bfloat16), group_names, 2 * n_feat)
-        table = table.reshape(n_feat, 2, groups, K // 16, 8, DS).transpose(0, 2, 3, 1, 4, 5)
+        per_part = part_k // share
+        base = (row_index // n_sub) % (per_part // n_sub) * n_sub
+        holder = row_index // per_part
+        centroids = lax.dynamic_slice_in_dim(centroids_part, (base + me_sub) * share, share, 0)
+        for t in range(1, n_sub):
+            theirs = lax.dynamic_slice_in_dim(
+                centroids_part, (base + (me_sub ^ t)) * share, share, 0
+            )
+            got = lax.ppermute(theirs, sub, sub_perm(t))
+            centroids = jnp.where((me_sub ^ t) == holder, got, centroids)
+        table = broadcast_over(cents.astype(jnp.bfloat16), group_names, n_sub * n_feat)
+        table = table.reshape(n_feat, n_sub, groups, part_k, DS).transpose(0, 2, 1, 3, 4)
         table = table.reshape(m_all, K, DS)
     else:
         partial = partial.reshape(n_feat, groups, K, DS)

time: 171 us -> 153 us (0.89)
  local copies, waits for them, and re-layouts: 34.2 us -> 19.5 us
  waiting for transfers between devices: 47.6 us -> 37.5 us
  starting transfers between devices: 43.8 us -> 47.2 us
  other arithmetic: 4.25 us -> 7.57 us
    all_to_all x1, waiting for transfers between devices: 11.2 us -> 1.35 us  [shards(): lax.all_to_all(parts, group_names, split_axis=0, concat_axis=0, tiled=True)]
    transpose x3 -> x2, local copies, waits for them, and re-layouts: 11.1 us -> 1.47 us  [the longest x1 1.36 us: shards(): table.reshape(n_feat, n_sub, groups, part_k, DS).transpose(0, 2, 1, 3, 4)]
    ppermute x9 -> x8, waiting for transfers between devices: 25.2 us -> 16.4 us  [exchange(): return lax.ppermute(x, name, pairs)]
    ppermute x1 -> x6, waiting for transfers between devices: 1.02 us -> 9.57 us  [the longest x3 9.56 us: shards(): lax.ppermute(counts, sub, sub_perm(t))]
    unnamed x19 -> x21, local copies, waits for them, and re-layouts: 5.74 us -> 12.3 us
    add x1 -> x0, local copies, waits for them, and re-layouts: 4.61 us -> none  [shards(): sum((lax.dot_general(part, rot3, dims, preferred_element_type=jnp.float32...]
    ppermute x1 -> x6, starting transfers between devices: 0.24 us -> 3.92 us  [the longest x3 1.97 us: shards(): got = lax.ppermute(theirs, sub, sub_perm(t))]
    reshape x5 -> x6, local copies, waits for them, and re-layouts: 6.76 us -> 3.52 us  [the longest x2 2.5 us: shards(): partial.reshape(n_feat, groups, n_sub, part_k, DS).transpose(0, 2, 1, 3, 4)]
  transfers between devices with their start and end apart: 13 -> 17, of which waited for: 13 -> 13; matrix products, arithmetic and copies ran while one was open for 3% -> 3% of each run, Pallas kernels for 3% -> 3%
where the time goes in v17:
time: 153 us; the launch traced here: 152 us
  starting transfers between devices  47.2 us (31%)
  waiting for transfers between devices  37.5 us (25%)
  Pallas kernels  27.9 us (18%)
  local copies, waits for them, and re-layouts  19.5 us (13%)
  matrix products  10.3 us (7%)
  other arithmetic  7.57 us (5%)
  between operations  1.59 us (1%)
    pallas_call x2, Pallas kernels, codeword_means(): pl.pallas_call(means_kernel, grid_spec=pltpu.PrefetchScalarGridSpec(num_s...  27.9 us
    ppermute x8, starting transfers between devices, exchange(): return lax.ppermute(x, name, pairs)  22.9 us
    ppermute x8, waiting for transfers between devices, exchange(): return lax.ppermute(x, name, pairs)  16.4 us
    all_to_all x2, starting transfers between devices, broadcast_over(): lax.all_to_all(copies, names, split_axis=0, concat_axis=0, tiled=True)  13.6 us
    unnamed x21, local copies, waits for them, and re-layouts  12.3 us
    all_to_all x2, waiting for transfers between devices, broadcast_over(): lax.all_to_all(copies, names, split_axis=0, concat_axis=0, tiled=True)  10.1 us
    ppermute x3, waiting for transfers between devices, shards(): lax.ppermute(counts, sub, sub_perm(t))  9.56 us
    all_to_all x1, starting transfers between devices, shards(): lax.all_to_all(parts, group_names, split_axis=0, concat_axis=0, tiled=True)  6.84 us
  transfers between devices with their start and end apart: 17, of which 13 were waited for; matrix products, arithmetic and copies ran while one was open for 3% of the time, Pallas kernels for 3%

profile of v17, /device:TPU:4, one launch (start us, length us, event | category | flops | bytes accessed | tf_op | source)
XLA Modules:
  0.0 151.6 jit_solution(11444184325133277245)
XLA Ops:
  3.0 7.4 %all-to-all-start = ((bf16[8,8,2560]{2,1,0:T(8,128)(2,1)}), bf16[8,8,2560]{2,1,0:T(8,128)(2,1)S(1)}, u32[]{:S(2)}, u32[]{:S(2)}) async-start(bf16[8,8,2560]{2,1,0:T(8,128)(2,1)} %broadcast_in_dim.20), calls=%async_computation | async-start | bytes 655360 | tf_op jit(solution)/shard_map/all_to_all | solution.py:127
  11.5 5.2 %shard_map.77 = (bf16[64,256,128]{2,1,0:T(8,128)(2,1)}, bf16[64,256,128]{2,1,0:T(8,128)(2,1)}, bf16[64,256,128]{2,1,0:T(8,128)(2,1)}) custom-call(s32[1]{0:T(128)} %bitcast.block_ref, bf16[8,2560]{1,0:T(8,128)(2,1)} %copy-done.5, bf16[2560,128]{1,0:T(8,128)(2,1)} %vec_ref.3), custom_call_target="tpu_custom_call" | custom-call | flops 1342177280 | bytes 2269184 | tf_op jit(solution)/shard_map/pallas_call | solution.py:78
  18.0 22.8 %shard_map.78 = (bf16[64,256,128]{2,1,0:T(8,128)(2,1)}, bf16[64,256,128]{2,1,0:T(8,128)(2,1)}, bf16[64,256,128]{2,1,0:T(8,128)(2,1)}) custom-call(s32[1]{0:T(128)} %bitcast.block_ref, bf16[64,2560]{1,0:T(8,128)(2,1)} %bitcast.79, bf16[2560,128]{1,0:T(8,128)(2,1)} %vec_ref.3, ...), custom_call_target="tpu_custom_call", output_to_operand_aliasing={{0}: (3, {}), {1}: (4, {}), {2}: (5, {})} | custom-call | flops 9395240960 | bytes 11993088 | tf_op jit(solution)/shard_map/pallas_call | solution.py:101
  40.7 3.5 %fusion.4 = f32[64,256,16]{1,2,0:T(8,128)S(1)} fusion(bf16[64,256,128]{2,1,0:T(8,128)(2,1)} %get-tuple-element.11, bf16[64,128,16]{1,2,0:T(8,128)(2,1)S(1)} %bitcast.67), kind=kOutput, calls=%fused_computation.35 | convolution fusion | flops 67108864 | bytes 5505024 | tf_op jit(solution)/shard_map/dot_general | solution.py:155
  50.1 3.4 %reshape.93 = f32[32,1,8192]{2,1,0:T(1,128)} reshape(f32[32,8,16,64]{3,2,1,0:T(8,128)} %bitcast.65) | data formatting | bytes 2097152
  53.6 6.8 %all-to-all-start.1 = ((f32[32,1,8192]{2,1,0:T(1,128)}), f32[32,1,8192]{2,1,0:T(1,128)S(1)}, u32[]{:S(2)}, u32[]{:S(2)}) async-start(f32[32,1,8192]{2,1,0:T(1,128)} %reshape.93), calls=%async_computation.1 | async-start | bytes 2097152 | tf_op jit(solution)/shard_map/all_to_all | solution.py:175
  60.4 2.3 %convert_reduce_fusion = f32[8,256]{1,0:T(8,128)S(1)} fusion(s32[8,2560]{1,0:T(8,128)S(1)} %get-tuple-element.23), kind=kLoop, calls=%fused_computation.1 | loop fusion | flops 15726592 | bytes 90112 | tf_op jit(solution)/shard_map/reduce_sum | solution.py:145
  64.7 8.9 %collective-permute-done.2 = f32[8,256]{1,0:T(8,128)S(1)} collective-permute-done((f32[8,256]{1,0:T(8,128)S(1)}, f32[8,256]{1,0:T(8,128)S(1)}, u32[]{:S(2)}, u32[]{:S(2)}) %collective-permute-start.2) | collective-permute-done | bytes 8224 | tf_op jit(solution)/shard_map/ppermute | solution.py:167
  76.2 3.2 %reduce = f32[32,8192]{1,0:T(8,128)S(1)} reduce(f32[32,1,8192]{2,1,0:T(1,128)S(1)} %all-to-all-done.1, f32[]{:T(128)} %broadcast.22), dimensions={1}, to_apply=%all_to_all.10.reduce_sub_computation | reduce | bytes 2097156 | tf_op jit(solution)/shard_map/all_to_all | solution.py:175
  80.8 2.0 %collective-permute-start.3 = (f32[8,1088]{1,0:T(8,128)S(1)}, f32[8,1088]{1,0:T(8,128)S(1)}, u32[]{:S(2)}, u32[]{:S(2)}) collective-permute-start(f32[8,1088]{1,0:T(8,128)S(1)} %pad_maximum_fusion), channel_id=1, source_target_pairs={{0,32},{32,0},{64,96},{96,64},{128,160},{160,128},{192,224},{224,1... | collective-permute-start | bytes 104456 | tf_op jit(solution)/shard_map/ppermute | solution.py:36
  82.8 2.0 %collective-permute-done.3 = f32[8,1088]{1,0:T(8,128)S(1)} collective-permute-done((f32[8,1088]{1,0:T(8,128)S(1)}, f32[8,1088]{1,0:T(8,128)S(1)}, u32[]{:S(2)}, u32[]{:S(2)}) %collective-permute-start.3) | collective-permute-done | bytes 34848 | tf_op jit(solution)/shard_map/ppermute | solution.py:36
  84.8 3.3 %collective-permute-start.4 = (f32[8,1088]{1,0:T(8,128)S(1)}, f32[8,1088]{1,0:T(8,128)S(1)}, u32[]{:S(2)}, u32[]{:S(2)}) collective-permute-start(f32[8,1088]{1,0:T(8,128)S(1)} %fusion.2), channel_id=1, source_target_pairs={{0,64},{32,96},{64,0},{96,32},{128,192},{160,224},{192,128},{224,1... | collective-permute-start | bytes 104456 | tf_op jit(solution)/shard_map/ppermute | solution.py:36
  88.1 1.9 %collective-permute-done.4 = f32[8,1088]{1,0:T(8,128)S(1)} collective-permute-done((f32[8,1088]{1,0:T(8,128)S(1)}, f32[8,1088]{1,0:T(8,128)S(1)}, u32[]{:S(2)}, u32[]{:S(2)}) %collective-permute-start.4) | collective-permute-done | bytes 34848 | tf_op jit(solution)/shard_map/ppermute | solution.py:36
  90.0 6.9 %collective-permute-start.5 = (f32[8,1088]{1,0:T(8,128)S(1)}, f32[8,1088]{1,0:T(8,128)S(1)}, u32[]{:S(2)}, u32[]{:S(2)}) collective-permute-start(f32[8,1088]{1,0:T(8,128)S(1)} %add.152), channel_id=1, source_target_pairs={{0,128},{32,160},{64,192},{96,224},{128,0},{160,32},{192,64},{224,... | collective-permute-start | bytes 104456 | tf_op jit(solution)/shard_map/ppermute | solution.py:36
  96.9 1.9 %collective-permute-done.5 = f32[8,1088]{1,0:T(8,128)S(1)} collective-permute-done((f32[8,1088]{1,0:T(8,128)S(1)}, f32[8,1088]{1,0:T(8,128)S(1)}, u32[]{:S(2)}, u32[]{:S(2)}) %collective-permute-start.5) | collective-permute-done | bytes 34848 | tf_op jit(solution)/shard_map/ppermute | solution.py:36
  101.1 6.1 %all-to-all-start.2 = ((bf16[32,2,4096]{2,1,0:T(2,128)(2,1)}), bf16[32,2,4096]{2,1,0:T(2,128)(2,1)S(1)}, u32[]{:S(2)}, u32[]{:S(2)}) async-start(bf16[32,2,4096]{2,1,0:T(2,128)(2,1)} %reshape.95), calls=%async_computation.2 | async-start | bytes 1048576 | tf_op jit(solution)/shard_map/all_to_all | solution.py:127
  107.3 9.7 %all-to-all-done.2 = bf16[32,2,4096]{2,1,0:T(2,128)(2,1)S(1)} async-done(((bf16[32,2,4096]{2,1,0:T(2,128)(2,1)}), bf16[32,2,4096]{2,1,0:T(2,128)(2,1)S(1)}, u32[]{:S(2)}, u32[]{:S(2)}) %all-to-all-start.2) | async-done | bytes 524320 | tf_op jit(solution)/shard_map/all_to_all | solution.py:127
  119.6 3.0 %fusion.5 = f32[64,16,128]{2,1,0:T(8,128)S(1)} fusion(bf16[64,256,16]{1,2,0:T(8,128)(2,1)S(1)} %reshape.80, bf16[64,256,128]{2,1,0:T(8,128)(2,1)} %get-tuple-element.11), kind=kOutput, calls=%fused_computation.36 | convolution fusion | flops 67108864 | bytes 5242880 | tf_op jit(solution)/shard_map/dot_general | solution.py:217
  128.3 1.6 %collective-permute-start.10 = (f32[8,32,128]{2,1,0:T(8,128)S(1)}, f32[8,32,128]{2,1,0:T(8,128)S(1)}, u32[]{:S(2)}, u32[]{:S(2)}) collective-permute-start(f32[8,32,128]{2,1,0:T(8,128)S(1)} %dynamic-slice_bitcast_fusion.1), channel_id=1, source_target_pairs={{0,16},{16,0},{1,17},{17,1},{2,18},{18,2},{3,19},{19,3},{4,20},{20... | collective-permute-start | bytes 393224 | tf_op jit(solution)/shard_map/ppermute | solution.py:36
  129.9 4.0 %collective-permute-done.10 = f32[8,32,128]{2,1,0:T(8,128)S(1)} collective-permute-done((f32[8,32,128]{2,1,0:T(8,128)S(1)}, f32[8,32,128]{2,1,0:T(8,128)S(1)}, u32[]{:S(2)}, u32[]{:S(2)}) %collective-permute-start.10) | collective-permute-done | bytes 131104 | tf_op jit(solution)/shard_map/ppermute | solution.py:36
  135.1 3.2 %collective-permute-done.11 = f32[4,32,128]{2,1,0:T(8,128)S(1)} collective-permute-done((f32[4,32,128]{2,1,0:T(8,128)S(1)}, f32[4,32,128]{2,1,0:T(8,128)S(1)}, u32[]{:S(2)}, u32[]{:S(2)}) %collective-permute-start.11) | collective-permute-done | bytes 65568 | tf_op jit(solution)/shard_map/ppermute | solution.py:36
  138.3 2.0 %collective-permute-start.12 = (f32[2,32,128]{2,1,0:T(8,128)S(1)}, f32[2,32,128]{2,1,0:T(8,128)S(1)}, u32[]{:S(2)}, u32[]{:S(2)}) collective-permute-start(f32[2,32,128]{2,1,0:T(8,128)S(1)} %dynamic-slice_bitcast_fusion.3), channel_id=1, source_target_pairs={{0,64},{32,96},{64,0},{96,32},{128,192},{160,224},{192,128},{224,1... | collective-permute-start | bytes 98312 | tf_op jit(solution)/shard_map/ppermute | solution.py:36
  140.6 1.8 %collective-permute-start.7 = (f32[8,128]{0,1:T(8,128)S(1)}, f32[8,128]{0,1:T(8,128)S(1)}, u32[]{:S(2)}, u32[]{:S(2)}) collective-permute-start(f32[8,128]{0,1:T(8,128)S(1)} %get-tuple-element.27), channel_id=1, source_target_pairs={{0,16},{8,24},{16,0},{24,8},{1,17},{9,25},{17,1},{25,9},{2,18},{10... | collective-permute-start | bytes 12296 | tf_op jit(solution)/shard_map/ppermute | solution.py:193
  143.2 6.0 %collective-permute-start.13 = (f32[1,32,128]{2,1,0:T(8,128)S(1)}, f32[1,32,128]{2,1,0:T(8,128)S(1)}, u32[]{:S(2)}, u32[]{:S(2)}) collective-permute-start(f32[1,32,128]{2,1,0:T(8,128)S(1)} %constant_dynamic-slice_fusion), channel_id=1, source_target_pairs={{0,128},{32,160},{64,192},{96,224},{128,0},{160,32},{192,64},{224,... | collective-permute-start | bytes 49160 | tf_op jit(solution)/shard_map/ppermute | solution.py:36
  (79 shorter events, 30.8 us)
Async XLA Ops:
  2.2 9.3 %copy-start.5 = (bf16[8,2560]{1,0:T(8,128)(2,1)}, bf16[8,2560]{1,0:T(8,128)(2,1)S(1)}, u32[]{:S(2)}) copy-start(bf16[8,2560]{1,0:T(8,128)(2,1)S(1)} %get-tuple-element.22.codes_ref) | copy-start | bytes 122884
  3.0 14.2 %all-to-all-start = ((bf16[8,8,2560]{2,1,0:T(8,128)(2,1)}), bf16[8,8,2560]{2,1,0:T(8,128)(2,1)S(1)}, u32[]{:S(2)}, u32[]{:S(2)}) async-start(bf16[8,8,2560]{2,1,0:T(8,128)(2,1)} %broadcast_in_dim.20), calls=%async_computation | async-start | bytes 655360 | tf_op jit(solution)/shard_map/all_to_all | solution.py:127
  17.2 0.7 copy-start.4
  40.7 3.5 %copy-start = (bf16[64,256,128]{2,1,0:T(8,128)(2,1)S(1)}, bf16[64,256,128]{2,1,0:T(8,128)(2,1)}, u32[]{:S(2)}) copy-start(bf16[64,256,128]{2,1,0:T(8,128)(2,1)} %get-tuple-element.12) | copy-start | bytes 12582916
  44.2 2.2 %copy-start.2 = (bf16[64,256,128]{2,1,0:T(8,128)(2,1)S(1)}, bf16[64,256,128]{2,1,0:T(8,128)(2,1)}, u32[]{:S(2)}) copy-start(bf16[64,256,128]{2,1,0:T(8,128)(2,1)} %get-tuple-element.13) | copy-start | bytes 12582916
  53.6 22.1 %all-to-all-start.1 = ((f32[32,1,8192]{2,1,0:T(1,128)}), f32[32,1,8192]{2,1,0:T(1,128)S(1)}, u32[]{:S(2)}, u32[]{:S(2)}) async-start(f32[32,1,8192]{2,1,0:T(1,128)} %reshape.93), calls=%async_computation.1 | async-start | bytes 2097152 | tf_op jit(solution)/shard_map/all_to_all | solution.py:175
  62.8 10.9 %collective-permute-start.2 = (f32[8,256]{1,0:T(8,128)S(1)}, f32[8,256]{1,0:T(8,128)S(1)}, u32[]{:S(2)}, u32[]{:S(2)}) collective-permute-start(f32[8,256]{1,0:T(8,128)S(1)} %convert_reduce_fusion), channel_id=1, source_target_pairs={{0,24},{8,16},{16,8},{24,0},{1,25},{9,17},{17,9},{25,1},{2,26},{10... | collective-permute-start | bytes 24584 | tf_op jit(solution)/shard_map/ppermute | solution.py:167
  63.8 10.5 %collective-permute-start.1 = (f32[8,256]{1,0:T(8,128)S(1)}, f32[8,256]{1,0:T(8,128)S(1)}, u32[]{:S(2)}, u32[]{:S(2)}) collective-permute-start(f32[8,256]{1,0:T(8,128)S(1)} %convert_reduce_fusion), channel_id=1, source_target_pairs={{0,16},{8,24},{16,0},{24,8},{1,17},{9,25},{17,1},{25,9},{2,18},{10... | collective-permute-start | bytes 24584 | tf_op jit(solution)/shard_map/ppermute | solution.py:167
  64.7 9.6 %collective-permute-start = (f32[8,256]{1,0:T(8,128)S(1)}, f32[8,256]{1,0:T(8,128)S(1)}, u32[]{:S(2)}, u32[]{:S(2)}) collective-permute-start(f32[8,256]{1,0:T(8,128)S(1)} %convert_reduce_fusion), channel_id=1, source_target_pairs={{0,8},{8,0},{16,24},{24,16},{1,9},{9,1},{17,25},{25,17},{2,10},{10... | collective-permute-start | bytes 24584 | tf_op jit(solution)/shard_map/ppermute | solution.py:167
  80.3 26.9 %copy-start.6 = (s32[32]{0:T(128)S(1)}, s32[32]{0:T(128)}, u32[]{:S(2)}) copy-start(s32[32]{0:T(128)} %constant.120) | copy-start | bytes 388
  80.8 4.0 %collective-permute-start.3 = (f32[8,1088]{1,0:T(8,128)S(1)}, f32[8,1088]{1,0:T(8,128)S(1)}, u32[]{:S(2)}, u32[]{:S(2)}) collective-permute-start(f32[8,1088]{1,0:T(8,128)S(1)} %pad_maximum_fusion), channel_id=1, source_target_pairs={{0,32},{32,0},{64,96},{96,64},{128,160},{160,128},{192,224},{224,1... | collective-permute-start | bytes 104456 | tf_op jit(solution)/shard_map/ppermute | solution.py:36
  84.8 5.2 %collective-permute-start.4 = (f32[8,1088]{1,0:T(8,128)S(1)}, f32[8,1088]{1,0:T(8,128)S(1)}, u32[]{:S(2)}, u32[]{:S(2)}) collective-permute-start(f32[8,1088]{1,0:T(8,128)S(1)} %fusion.2), channel_id=1, source_target_pairs={{0,64},{32,96},{64,0},{96,32},{128,192},{160,224},{192,128},{224,1... | collective-permute-start | bytes 104456 | tf_op jit(solution)/shard_map/ppermute | solution.py:36
  90.0 8.8 %collective-permute-start.5 = (f32[8,1088]{1,0:T(8,128)S(1)}, f32[8,1088]{1,0:T(8,128)S(1)}, u32[]{:S(2)}, u32[]{:S(2)}) collective-permute-start(f32[8,1088]{1,0:T(8,128)S(1)} %add.152), channel_id=1, source_target_pairs={{0,128},{32,160},{64,192},{96,224},{128,0},{160,32},{192,64},{224,... | collective-permute-start | bytes 104456 | tf_op jit(solution)/shard_map/ppermute | solution.py:36
  101.1 15.8 %all-to-all-start.2 = ((bf16[32,2,4096]{2,1,0:T(2,128)(2,1)}), bf16[32,2,4096]{2,1,0:T(2,128)(2,1)S(1)}, u32[]{:S(2)}, u32[]{:S(2)}) async-start(bf16[32,2,4096]{2,1,0:T(2,128)(2,1)} %reshape.95), calls=%async_computation.2 | async-start | bytes 1048576 | tf_op jit(solution)/shard_map/all_to_all | solution.py:127
  119.6 3.5 %copy-start.1 = (bf16[64,256,128]{2,1,0:T(8,128)(2,1)S(1)}, bf16[64,256,128]{2,1,0:T(8,128)(2,1)}, u32[]{:S(2)}) copy-start(bf16[64,256,128]{2,1,0:T(8,128)(2,1)} %get-tuple-element.12) | copy-start | bytes 12582916
  123.1 2.2 %copy-start.3 = (bf16[64,256,128]{2,1,0:T(8,128)(2,1)S(1)}, bf16[64,256,128]{2,1,0:T(8,128)(2,1)}, u32[]{:S(2)}) copy-start(bf16[64,256,128]{2,1,0:T(8,128)(2,1)} %get-tuple-element.13) | copy-start | bytes 12582916
  126.6 1.6 %collective-permute-start.9 = (f32[16,32,128]{2,1,0:T(8,128)S(1)}, f32[16,32,128]{2,1,0:T(8,128)S(1)}, u32[]{:S(2)}, u32[]{:S(2)}) collective-permute-start(f32[16,32,128]{2,1,0:T(8,128)S(1)} %dynamic-slice_bitcast_fusion), channel_id=1, source_target_pairs={{0,8},{8,0},{1,9},{9,1},{2,10},{10,2},{3,11},{11,3},{4,12},{12,4},... | collective-permute-start | bytes 786440 | tf_op jit(solution)/shard_map/ppermute | solution.py:36
  128.3 5.6 %collective-permute-start.10 = (f32[8,32,128]{2,1,0:T(8,128)S(1)}, f32[8,32,128]{2,1,0:T(8,128)S(1)}, u32[]{:S(2)}, u32[]{:S(2)}) collective-permute-start(f32[8,32,128]{2,1,0:T(8,128)S(1)} %dynamic-slice_bitcast_fusion.1), channel_id=1, source_target_pairs={{0,16},{16,0},{1,17},{17,1},{2,18},{18,2},{3,19},{19,3},{4,20},{20... | collective-permute-start | bytes 393224 | tf_op jit(solution)/shard_map/ppermute | solution.py:36
  133.9 4.4 %collective-permute-start.11 = (f32[4,32,128]{2,1,0:T(8,128)S(1)}, f32[4,32,128]{2,1,0:T(8,128)S(1)}, u32[]{:S(2)}, u32[]{:S(2)}) collective-permute-start(f32[4,32,128]{2,1,0:T(8,128)S(1)} %dynamic-slice_bitcast_fusion.2), channel_id=1, source_target_pairs={{0,32},{32,0},{64,96},{96,64},{128,160},{160,128},{192,224},{224,1... | collective-permute-start | bytes 196616 | tf_op jit(solution)/shard_map/ppermute | solution.py:36
  138.3 4.9 %collective-permute-start.12 = (f32[2,32,128]{2,1,0:T(8,128)S(1)}, f32[2,32,128]{2,1,0:T(8,128)S(1)}, u32[]{:S(2)}, u32[]{:S(2)}) collective-permute-start(f32[2,32,128]{2,1,0:T(8,128)S(1)} %dynamic-slice_bitcast_fusion.3), channel_id=1, source_target_pairs={{0,64},{32,96},{64,0},{96,32},{128,192},{160,224},{192,128},{224,1... | collective-permute-start | bytes 98312 | tf_op jit(solution)/shard_map/ppermute | solution.py:36
  140.5 8.8 %collective-permute-start.6 = (f32[8,128]{0,1:T(8,128)S(1)}, f32[8,128]{0,1:T(8,128)S(1)}, u32[]{:S(2)}, u32[]{:S(2)}) collective-permute-start(f32[8,128]{0,1:T(8,128)S(1)} %get-tuple-element.28), channel_id=1, source_target_pairs={{0,24},{8,16},{16,8},{24,0},{1,25},{9,17},{17,9},{25,1},{2,26},{10... | collective-permute-start | bytes 12296 | tf_op jit(solution)/shard_map/ppermute | solution.py:193
  140.6 8.7 %collective-permute-start.7 = (f32[8,128]{0,1:T(8,128)S(1)}, f32[8,128]{0,1:T(8,128)S(1)}, u32[]{:S(2)}, u32[]{:S(2)}) collective-permute-start(f32[8,128]{0,1:T(8,128)S(1)} %get-tuple-element.27), channel_id=1, source_target_pairs={{0,16},{8,24},{16,0},{24,8},{1,17},{9,25},{17,1},{25,9},{2,18},{10... | collective-permute-start | bytes 12296 | tf_op jit(solution)/shard_map/ppermute | solution.py:193
  142.4 6.9 %collective-permute-start.8 = (f32[8,128]{0,1:T(8,128)S(1)}, f32[8,128]{0,1:T(8,128)S(1)}, u32[]{:S(2)}, u32[]{:S(2)}) collective-permute-start(f32[8,128]{0,1:T(8,128)S(1)} %get-tuple-element.26), channel_id=1, source_target_pairs={{0,8},{8,0},{16,24},{24,16},{1,9},{9,1},{17,25},{25,17},{2,10},{10... | collective-permute-start | bytes 12296 | tf_op jit(solution)/shard_map/ppermute | solution.py:193
  143.2 7.7 %collective-permute-start.13 = (f32[1,32,128]{2,1,0:T(8,128)S(1)}, f32[1,32,128]{2,1,0:T(8,128)S(1)}, u32[]{:S(2)}, u32[]{:S(2)}) collective-permute-start(f32[1,32,128]{2,1,0:T(8,128)S(1)} %constant_dynamic-slice_fusion), channel_id=1, source_target_pairs={{0,128},{32,160},{64,192},{96,224},{128,0},{160,32},{192,64},{224,... | collective-permute-start | bytes 49160 | tf_op jit(solution)/shard_map/ppermute | solution.py:36

commit v18 on v16

--- a/solution.py
+++ b/solution.py
@@ -181,8 +181,11 @@
         )
         got = lax.ppermute(theirs, "c", [(0, 1), (1, 0)])
         centroids = jnp.where(core == row_index // per_half, mine, got)
-        table = broadcast_over(cents.astype(jnp.bfloat16), group_names, 2 * n_feat)
-        table = table.reshape(n_feat, 2, groups, half, DS).transpose(0, 2, 1, 3, 4)
+        mine_half = cents.astype(jnp.bfloat16)
+        other_half = lax.ppermute(mine_half, "c", [(0, 1), (1, 0)])
+        low = jnp.where(core == 0, mine_half, other_half)
+        high = jnp.where(core == 0, other_half, mine_half)
+        table = broadcast_over(jnp.concatenate([low, high], axis=1), feat_names, n_feat)
         table = table.reshape(m_all, K, DS)
     else:
         partial = partial.reshape(n_feat, groups, K, DS)

time: 149 us -> 150 us (level)
    ppermute x0 -> x1, waiting for transfers between devices: none -> 1.52 us  [shards(): other_half = lax.ppermute(mine_half, 'c', [(0, 1), (1, 0)])]
  transfers between devices with their start and end apart: 14 -> 15, of which waited for: 13 -> 14; matrix products, arithmetic and copies ran while one was open for 3% -> 3% of each run, Pallas kernels for 4% -> 3%
where the time goes in v18:
time: 150 us; the launch traced here: 148 us
  waiting for transfers between devices  49.2 us (33%)
  starting transfers between devices  44.1 us (29%)
  Pallas kernels  27.9 us (19%)
  local copies, waits for them, and re-layouts  10.7 us (7%)
  matrix products  10.3 us (7%)
  other arithmetic  4.39 us (3%)
  between operations  1.6 us (1%)
    pallas_call x2, Pallas kernels, codeword_means(): pl.pallas_call(means_kernel, grid_spec=pltpu.PrefetchScalarGridSpec(num_s...  27.9 us
    ppermute x9, waiting for transfers between devices, exchange(): return lax.ppermute(x, name, pairs)  25 us
    ppermute x9, starting transfers between devices, exchange(): return lax.ppermute(x, name, pairs)  22.7 us
    all_to_all x2, starting transfers between devices, broadcast_over(): lax.all_to_all(copies, names, split_axis=0, concat_axis=0, tiled=True)  14.1 us
    all_to_all x1, waiting for transfers between devices, shards(): lax.all_to_all(parts, group_names, split_axis=0, concat_axis=0, tiled=True)  11.6 us
    all_to_all x2, waiting for transfers between devices, broadcast_over(): lax.all_to_all(copies, names, split_axis=0, concat_axis=0, tiled=True)  10 us
    all_to_all x1, starting transfers between devices, shards(): lax.all_to_all(parts, group_names, split_axis=0, concat_axis=0, tiled=True)  6.71 us
    dot_general x3, matrix products, shards(): lax.dot_general(part, rot3, dims, preferred_element_type=jnp.float32)  5.92 us
  transfers between devices with their start and end apart: 15, of which 14 were waited for; matrix products, arithmetic and copies ran while one was open for 3% of the time, Pallas kernels for 3%

profile of v18, /device:TPU:4, one launch (start us, length us, event | category | flops | bytes accessed | tf_op | source)
XLA Modules:
  0.0 148.1 jit_solution(12524904360103763949)
XLA Ops:
  3.0 7.4 %all-to-all-start = ((bf16[8,8,2560]{2,1,0:T(8,128)(2,1)}), bf16[8,8,2560]{2,1,0:T(8,128)(2,1)S(1)}, u32[]{:S(2)}, u32[]{:S(2)}) async-start(bf16[8,8,2560]{2,1,0:T(8,128)(2,1)} %broadcast_in_dim.20), calls=%async_computation | async-start | bytes 655360 | tf_op jit(solution)/shard_map/all_to_all | solution.py:127
  11.5 5.2 %shard_map.77 = (bf16[64,256,128]{2,1,0:T(8,128)(2,1)}, bf16[64,256,128]{2,1,0:T(8,128)(2,1)}, bf16[64,256,128]{2,1,0:T(8,128)(2,1)}) custom-call(s32[1]{0:T(128)} %bitcast.block_ref, bf16[8,2560]{1,0:T(8,128)(2,1)} %copy-done.5, bf16[2560,128]{1,0:T(8,128)(2,1)} %vec_ref.3), custom_call_target="tpu_custom_call" | custom-call | flops 1342177280 | bytes 2269184 | tf_op jit(solution)/shard_map/pallas_call | solution.py:78
  17.9 22.8 %shard_map.78 = (bf16[64,256,128]{2,1,0:T(8,128)(2,1)}, bf16[64,256,128]{2,1,0:T(8,128)(2,1)}, bf16[64,256,128]{2,1,0:T(8,128)(2,1)}) custom-call(s32[1]{0:T(128)} %bitcast.block_ref, bf16[64,2560]{1,0:T(8,128)(2,1)} %bitcast.73, bf16[2560,128]{1,0:T(8,128)(2,1)} %vec_ref.3, ...), custom_call_target="tpu_custom_call", output_to_operand_aliasing={{0}: (3, {}), {1}: (4, {}), {2}: (5, {})} | custom-call | flops 9395240960 | bytes 11993088 | tf_op jit(solution)/shard_map/pallas_call | solution.py:101
  40.7 3.5 %fusion.4 = f32[64,256,16]{1,2,0:T(8,128)S(1)} fusion(bf16[64,256,128]{2,1,0:T(8,128)(2,1)} %get-tuple-element.11, bf16[64,128,16]{1,2,0:T(8,128)(2,1)S(1)} %bitcast.61), kind=kOutput, calls=%fused_computation.34 | convolution fusion | flops 67108864 | bytes 5505024 | tf_op jit(solution)/shard_map/dot_general | solution.py:155
  49.3 6.7 %all-to-all-start.1 = ((f32[16,8,128,16]{2,3,1,0:T(8,128)}), f32[16,8,128,16]{2,3,1,0:T(8,128)S(1)}, u32[]{:S(2)}, u32[]{:S(2)}) async-start(f32[16,8,128,16]{2,3,1,0:T(8,128)} %bitcast.8), calls=%async_computation.1 | async-start | bytes 2097152 | tf_op jit(solution)/shard_map/all_to_all | solution.py:167
  56.1 2.3 %convert_reduce_fusion = f32[8,256]{1,0:T(8,128)S(1)} fusion(s32[8,2560]{1,0:T(8,128)S(1)} %get-tuple-element.23), kind=kLoop, calls=%fused_computation.1 | loop fusion | flops 15726592 | bytes 90112 | tf_op jit(solution)/shard_map/reduce_sum | solution.py:145
  59.8 11.6 %all-to-all-done.1 = f32[16,8,128,16]{2,3,1,0:T(8,128)S(1)} async-done(((f32[16,8,128,16]{2,3,1,0:T(8,128)}), f32[16,8,128,16]{2,3,1,0:T(8,128)S(1)}, u32[]{:S(2)}, u32[]{:S(2)}) %all-to-all-start.1) | async-done | bytes 1048608 | tf_op jit(solution)/shard_map/all_to_all | solution.py:167
  73.2 3.1 %collective-permute-done.1 = f32[8,2176]{1,0:T(8,128)S(1)} collective-permute-done((f32[8,2176]{1,0:T(8,128)S(1)}, f32[8,2176]{1,0:T(8,128)S(1)}, u32[]{:S(2)}, u32[]{:S(2)}) %collective-permute-start.1) | collective-permute-done | bytes 69664 | tf_op jit(solution)/shard_map/ppermute | solution.py:36
  76.4 2.0 %collective-permute-start.2 = (f32[8,2176]{1,0:T(8,128)S(1)}, f32[8,2176]{1,0:T(8,128)S(1)}, u32[]{:S(2)}, u32[]{:S(2)}) collective-permute-start(f32[8,2176]{1,0:T(8,128)S(1)} %fusion.2), channel_id=1, source_target_pairs={{0,32},{32,0},{64,96},{96,64},{128,160},{160,128},{192,224},{224,1... | collective-permute-start | bytes 208904 | tf_op jit(solution)/shard_map/ppermute | solution.py:36
  78.4 2.4 %collective-permute-done.2 = f32[8,2176]{1,0:T(8,128)S(1)} collective-permute-done((f32[8,2176]{1,0:T(8,128)S(1)}, f32[8,2176]{1,0:T(8,128)S(1)}, u32[]{:S(2)}, u32[]{:S(2)}) %collective-permute-start.2) | collective-permute-done | bytes 69664 | tf_op jit(solution)/shard_map/ppermute | solution.py:36
  80.8 3.4 %collective-permute-start.3 = (f32[8,2176]{1,0:T(8,128)S(1)}, f32[8,2176]{1,0:T(8,128)S(1)}, u32[]{:S(2)}, u32[]{:S(2)}) collective-permute-start(f32[8,2176]{1,0:T(8,128)S(1)} %add.130), channel_id=1, source_target_pairs={{0,64},{32,96},{64,0},{96,32},{128,192},{160,224},{192,128},{224,1... | collective-permute-start | bytes 208904 | tf_op jit(solution)/shard_map/ppermute | solution.py:36
  84.1 2.3 %collective-permute-done.3 = f32[8,2176]{1,0:T(8,128)S(1)} collective-permute-done((f32[8,2176]{1,0:T(8,128)S(1)}, f32[8,2176]{1,0:T(8,128)S(1)}, u32[]{:S(2)}, u32[]{:S(2)}) %collective-permute-start.3) | collective-permute-done | bytes 69664 | tf_op jit(solution)/shard_map/ppermute | solution.py:36
  86.4 7.7 %collective-permute-start.4 = (f32[8,2176]{1,0:T(8,128)S(1)}, f32[8,2176]{1,0:T(8,128)S(1)}, u32[]{:S(2)}, u32[]{:S(2)}) collective-permute-start(f32[8,2176]{1,0:T(8,128)S(1)} %add.131), channel_id=1, source_target_pairs={{0,128},{32,160},{64,192},{96,224},{128,0},{160,32},{192,64},{224,... | collective-permute-start | bytes 208904 | tf_op jit(solution)/shard_map/ppermute | solution.py:36
  94.1 2.6 %collective-permute-done.4 = f32[8,2176]{1,0:T(8,128)S(1)} collective-permute-done((f32[8,2176]{1,0:T(8,128)S(1)}, f32[8,2176]{1,0:T(8,128)S(1)}, u32[]{:S(2)}, u32[]{:S(2)}) %collective-permute-start.4) | collective-permute-done | bytes 69664 | tf_op jit(solution)/shard_map/ppermute | solution.py:36
  97.2 1.5 %collective-permute-done.6 = bf16[8,128,16]{2,1,0:T(8,128)(2,1)S(1)} collective-permute-done((bf16[8,128,16]{2,1,0:T(8,128)(2,1)S(1)}, bf16[8,128,16]{2,1,0:T(8,128)(2,1)S(1)}, u32[]{:S(2)}, u32[]{:S(2)}) %collective-permute-start.6) | collective-permute-done | bytes 32800 | tf_op jit(solution)/shard_map/ppermute | solution.py:185
  100.0 6.6 %all-to-all-start.2 = ((bf16[8,8,256,16]{2,3,1,0:T(8,128)(2,1)}), bf16[8,8,256,16]{2,3,1,0:T(8,128)(2,1)S(1)}, u32[]{:S(2)}, u32[]{:S(2)}) async-start(bf16[8,8,256,16]{2,3,1,0:T(8,128)(2,1)} %broadcast_in_dim.34), calls=%async_computation.2 | async-start | bytes 1048576 | tf_op jit(solution)/shard_map/all_to_all | solution.py:127
  106.6 9.5 %all-to-all-done.2 = bf16[8,8,256,16]{2,3,1,0:T(8,128)(2,1)S(1)} async-done(((bf16[8,8,256,16]{2,3,1,0:T(8,128)(2,1)}), bf16[8,8,256,16]{2,3,1,0:T(8,128)(2,1)S(1)}, u32[]{:S(2)}, u32[]{:S(2)}) %all-to-all-start.2) | async-done | bytes 524320 | tf_op jit(solution)/shard_map/all_to_all | solution.py:127
  116.1 3.0 %fusion.5 = f32[64,16,128]{2,1,0:T(8,128)S(1)} fusion(bf16[64,256,16]{1,2,0:T(8,128)(2,1)S(1)} %bitcast.58, bf16[64,256,128]{2,1,0:T(8,128)(2,1)} %get-tuple-element.11), kind=kOutput, calls=%fused_computation.35 | convolution fusion | flops 67108864 | bytes 5242880 | tf_op jit(solution)/shard_map/dot_general | solution.py:209
  120.2 1.5 %copy-done.3 = bf16[64,256,128]{2,1,0:T(8,128)(2,1)S(1)} copy-done((bf16[64,256,128]{2,1,0:T(8,128)(2,1)S(1)}, bf16[64,256,128]{2,1,0:T(8,128)(2,1)}, u32[]{:S(2)}) %copy-start.3) | copy-done | bytes 4194328
  123.2 1.5 %collective-permute-done.7 = f32[16,32,128]{2,1,0:T(8,128)S(1)} collective-permute-done((f32[16,32,128]{2,1,0:T(8,128)S(1)}, f32[16,32,128]{2,1,0:T(8,128)S(1)}, u32[]{:S(2)}, u32[]{:S(2)}) %collective-permute-start.7) | collective-permute-done | bytes 262176 | tf_op jit(solution)/shard_map/ppermute | solution.py:36
  126.1 4.3 %collective-permute-done.8 = f32[8,32,128]{2,1,0:T(8,128)S(1)} collective-permute-done((f32[8,32,128]{2,1,0:T(8,128)S(1)}, f32[8,32,128]{2,1,0:T(8,128)S(1)}, u32[]{:S(2)}, u32[]{:S(2)}) %collective-permute-start.8) | collective-permute-done | bytes 131104 | tf_op jit(solution)/shard_map/ppermute | solution.py:36
  130.7 4.0 %collective-permute-done.9 = f32[4,32,128]{2,1,0:T(8,128)S(1)} collective-permute-done((f32[4,32,128]{2,1,0:T(8,128)S(1)}, f32[4,32,128]{2,1,0:T(8,128)S(1)}, u32[]{:S(2)}, u32[]{:S(2)}) %collective-permute-start.9) | collective-permute-done | bytes 65568 | tf_op jit(solution)/shard_map/ppermute | solution.py:36
  135.8 3.9 %collective-permute-done.10 = f32[2,32,128]{2,1,0:T(8,128)S(1)} collective-permute-done((f32[2,32,128]{2,1,0:T(8,128)S(1)}, f32[2,32,128]{2,1,0:T(8,128)S(1)}, u32[]{:S(2)}, u32[]{:S(2)}) %collective-permute-start.10) | collective-permute-done | bytes 32800 | tf_op jit(solution)/shard_map/ppermute | solution.py:36
  139.7 6.0 %collective-permute-start.11 = (f32[1,32,128]{2,1,0:T(8,128)S(1)}, f32[1,32,128]{2,1,0:T(8,128)S(1)}, u32[]{:S(2)}, u32[]{:S(2)}) collective-permute-start(f32[1,32,128]{2,1,0:T(8,128)S(1)} %constant_dynamic-slice_fusion), channel_id=1, source_target_pairs={{0,128},{32,160},{64,192},{96,224},{128,0},{160,32},{192,64},{224,... | collective-permute-start | bytes 49160 | tf_op jit(solution)/shard_map/ppermute | solution.py:36
  (70 shorter events, 21.7 us)
Async XLA Ops:
  2.2 9.3 %copy-start.5 = (bf16[8,2560]{1,0:T(8,128)(2,1)}, bf16[8,2560]{1,0:T(8,128)(2,1)S(1)}, u32[]{:S(2)}) copy-start(bf16[8,2560]{1,0:T(8,128)(2,1)S(1)} %get-tuple-element.22.codes_ref) | copy-start | bytes 122884
  3.0 14.2 %all-to-all-start = ((bf16[8,8,2560]{2,1,0:T(8,128)(2,1)}), bf16[8,8,2560]{2,1,0:T(8,128)(2,1)S(1)}, u32[]{:S(2)}, u32[]{:S(2)}) async-start(bf16[8,8,2560]{2,1,0:T(8,128)(2,1)} %broadcast_in_dim.20), calls=%async_computation | async-start | bytes 655360 | tf_op jit(solution)/shard_map/all_to_all | solution.py:127
  17.2 0.7 copy-start.4
  40.7 3.5 %copy-start = (bf16[64,256,128]{2,1,0:T(8,128)(2,1)S(1)}, bf16[64,256,128]{2,1,0:T(8,128)(2,1)}, u32[]{:S(2)}) copy-start(bf16[64,256,128]{2,1,0:T(8,128)(2,1)} %get-tuple-element.12) | copy-start | bytes 12582916
  44.2 2.2 %copy-start.2 = (bf16[64,256,128]{2,1,0:T(8,128)(2,1)S(1)}, bf16[64,256,128]{2,1,0:T(8,128)(2,1)}, u32[]{:S(2)}) copy-start(bf16[64,256,128]{2,1,0:T(8,128)(2,1)} %get-tuple-element.13) | copy-start | bytes 12582916
  49.3 22.1 %all-to-all-start.1 = ((f32[16,8,128,16]{2,3,1,0:T(8,128)}), f32[16,8,128,16]{2,3,1,0:T(8,128)S(1)}, u32[]{:S(2)}, u32[]{:S(2)}) async-start(f32[16,8,128,16]{2,3,1,0:T(8,128)} %bitcast.8), calls=%async_computation.1 | async-start | bytes 2097152 | tf_op jit(solution)/shard_map/all_to_all | solution.py:167
  58.4 1.4 collective-permute-start
  59.8 46.8 %copy-start.6 = (s32[32]{0:T(128)S(1)}, s32[32]{0:T(128)}, u32[]{:S(2)}) copy-start(s32[32]{0:T(128)} %constant.117) | copy-start | bytes 388
  72.0 4.4 %collective-permute-start.1 = (f32[8,2176]{1,0:T(8,128)S(1)}, f32[8,2176]{1,0:T(8,128)S(1)}, u32[]{:S(2)}, u32[]{:S(2)}) collective-permute-start(f32[8,2176]{1,0:T(8,128)S(1)} %pad_maximum_fusion), channel_id=1, source_target_pairs={{0,16},{16,0},{1,17},{17,1},{2,18},{18,2},{3,19},{19,3},{4,20},{20... | collective-permute-start | bytes 208904 | tf_op jit(solution)/shard_map/ppermute | solution.py:36
  76.4 4.4 %collective-permute-start.2 = (f32[8,2176]{1,0:T(8,128)S(1)}, f32[8,2176]{1,0:T(8,128)S(1)}, u32[]{:S(2)}, u32[]{:S(2)}) collective-permute-start(f32[8,2176]{1,0:T(8,128)S(1)} %fusion.2), channel_id=1, source_target_pairs={{0,32},{32,0},{64,96},{96,64},{128,160},{160,128},{192,224},{224,1... | collective-permute-start | bytes 208904 | tf_op jit(solution)/shard_map/ppermute | solution.py:36
  80.8 5.6 %collective-permute-start.3 = (f32[8,2176]{1,0:T(8,128)S(1)}, f32[8,2176]{1,0:T(8,128)S(1)}, u32[]{:S(2)}, u32[]{:S(2)}) collective-permute-start(f32[8,2176]{1,0:T(8,128)S(1)} %add.130), channel_id=1, source_target_pairs={{0,64},{32,96},{64,0},{96,32},{128,192},{160,224},{192,128},{224,1... | collective-permute-start | bytes 208904 | tf_op jit(solution)/shard_map/ppermute | solution.py:36
  86.4 10.2 %collective-permute-start.4 = (f32[8,2176]{1,0:T(8,128)S(1)}, f32[8,2176]{1,0:T(8,128)S(1)}, u32[]{:S(2)}, u32[]{:S(2)}) collective-permute-start(f32[8,2176]{1,0:T(8,128)S(1)} %add.131), channel_id=1, source_target_pairs={{0,128},{32,160},{64,192},{96,224},{128,0},{160,32},{192,64},{224,... | collective-permute-start | bytes 208904 | tf_op jit(solution)/shard_map/ppermute | solution.py:36
  97.1 1.6 %collective-permute-start.6 = (bf16[8,128,16]{2,1,0:T(8,128)(2,1)S(1)}, bf16[8,128,16]{2,1,0:T(8,128)(2,1)S(1)}, u32[]{:S(2)}, u32[]{:S(2)}) collective-permute-start(bf16[8,128,16]{2,1,0:T(8,128)(2,1)S(1)} %get-tuple-element.24), channel_id=1, source_target_pairs={{0,8},{8,0},{1,9},{9,1},{2,10},{10,2},{3,11},{11,3},{4,12},{12,4},... | collective-permute-start | bytes 98312 | tf_op jit(solution)/shard_map/ppermute | solution.py:185
  100.0 16.2 %all-to-all-start.2 = ((bf16[8,8,256,16]{2,3,1,0:T(8,128)(2,1)}), bf16[8,8,256,16]{2,3,1,0:T(8,128)(2,1)S(1)}, u32[]{:S(2)}, u32[]{:S(2)}) async-start(bf16[8,8,256,16]{2,3,1,0:T(8,128)(2,1)} %broadcast_in_dim.34), calls=%async_computation.2 | async-start | bytes 1048576 | tf_op jit(solution)/shard_map/all_to_all | solution.py:127
  116.1 3.4 %copy-start.1 = (bf16[64,256,128]{2,1,0:T(8,128)(2,1)S(1)}, bf16[64,256,128]{2,1,0:T(8,128)(2,1)}, u32[]{:S(2)}) copy-start(bf16[64,256,128]{2,1,0:T(8,128)(2,1)} %get-tuple-element.12) | copy-start | bytes 12582916
  119.6 2.2 %copy-start.3 = (bf16[64,256,128]{2,1,0:T(8,128)(2,1)S(1)}, bf16[64,256,128]{2,1,0:T(8,128)(2,1)}, u32[]{:S(2)}) copy-start(bf16[64,256,128]{2,1,0:T(8,128)(2,1)} %get-tuple-element.13) | copy-start | bytes 12582916
  123.1 1.6 %collective-permute-start.7 = (f32[16,32,128]{2,1,0:T(8,128)S(1)}, f32[16,32,128]{2,1,0:T(8,128)S(1)}, u32[]{:S(2)}, u32[]{:S(2)}) collective-permute-start(f32[16,32,128]{2,1,0:T(8,128)S(1)} %dynamic-slice_bitcast_fusion), channel_id=1, source_target_pairs={{0,8},{8,0},{1,9},{9,1},{2,10},{10,2},{3,11},{11,3},{4,12},{12,4},... | collective-permute-start | bytes 786440 | tf_op jit(solution)/shard_map/ppermute | solution.py:36
  124.8 5.6 %collective-permute-start.8 = (f32[8,32,128]{2,1,0:T(8,128)S(1)}, f32[8,32,128]{2,1,0:T(8,128)S(1)}, u32[]{:S(2)}, u32[]{:S(2)}) collective-permute-start(f32[8,32,128]{2,1,0:T(8,128)S(1)} %dynamic-slice_bitcast_fusion.1), channel_id=1, source_target_pairs={{0,16},{16,0},{1,17},{17,1},{2,18},{18,2},{3,19},{19,3},{4,20},{20... | collective-permute-start | bytes 393224 | tf_op jit(solution)/shard_map/ppermute | solution.py:36
  130.4 4.4 %collective-permute-start.9 = (f32[4,32,128]{2,1,0:T(8,128)S(1)}, f32[4,32,128]{2,1,0:T(8,128)S(1)}, u32[]{:S(2)}, u32[]{:S(2)}) collective-permute-start(f32[4,32,128]{2,1,0:T(8,128)S(1)} %dynamic-slice_bitcast_fusion.2), channel_id=1, source_target_pairs={{0,32},{32,0},{64,96},{96,64},{128,160},{160,128},{192,224},{224,1... | collective-permute-start | bytes 196616 | tf_op jit(solution)/shard_map/ppermute | solution.py:36
  134.8 4.9 %collective-permute-start.10 = (f32[2,32,128]{2,1,0:T(8,128)S(1)}, f32[2,32,128]{2,1,0:T(8,128)S(1)}, u32[]{:S(2)}, u32[]{:S(2)}) collective-permute-start(f32[2,32,128]{2,1,0:T(8,128)S(1)} %dynamic-slice_bitcast_fusion.3), channel_id=1, source_target_pairs={{0,64},{32,96},{64,0},{96,32},{128,192},{160,224},{192,128},{224,1... | collective-permute-start | bytes 98312 | tf_op jit(solution)/shard_map/ppermute | solution.py:36
  135.8 10.0 %collective-permute-start.5 = (f32[8,128]{0,1:T(8,128)S(1)}, f32[8,128]{0,1:T(8,128)S(1)}, u32[]{:S(2)}, u32[]{:S(2)}) collective-permute-start(f32[8,128]{0,1:T(8,128)S(1)} %constant_dynamic-slice_fusion.1), channel_id=1, source_target_pairs={{0,8},{8,0},{1,9},{9,1},{2,10},{10,2},{3,11},{11,3},{4,12},{12,4},... | collective-permute-start | bytes 12296 | tf_op jit(solution)/shard_map/ppermute | solution.py:182
  139.7 7.7 %collective-permute-start.11 = (f32[1,32,128]{2,1,0:T(8,128)S(1)}, f32[1,32,128]{2,1,0:T(8,128)S(1)}, u32[]{:S(2)}, u32[]{:S(2)}) collective-permute-start(f32[1,32,128]{2,1,0:T(8,128)S(1)} %constant_dynamic-slice_fusion), channel_id=1, source_target_pairs={{0,128},{32,160},{64,192},{96,224},{128,0},{160,32},{192,64},{224,... | collective-permute-start | bytes 49160 | tf_op jit(solution)/shard_map/ppermute | solution.py:36
